TPU v7x, 32 devices: a whole 2x2x4 slice. The times are simulated.
32 devices in a mesh: pipe: 1, seq: 32 (over z, y, x, core).
Axes of the slice: x: 2, y: 2, z: 4, core: 2. Of those that a mesh axis runs over, the one named last changes fastest.
Arguments:
- queries: bfloat16 [1, 4096, 4096], P('pipe', 'seq'), may hold values from -42 to 42
- key_rows: bfloat16 [1, 4096, 2048], P('pipe', 'seq'), may hold values from -14 to 14
- value_rows: bfloat16 [1, 4096, 2048], P('pipe', 'seq'), may hold values from -6 to 6
- arriving_grad: bfloat16 [1, 4096, 4096], P('pipe', 'seq'), may hold values from -6 to 6
- doc_blocks: int32 [1, 32], P('pipe'), may hold values from 0 to 3, never falling along the last dimension, each value on 1 to 16 neighbouring positions
Outputs:
- grad_query: bfloat16 [1, 4096, 4096], P('pipe', 'seq')
- grad_key: bfloat16 [1, 4096, 2048], P('pipe', 'seq')
- grad_value: bfloat16 [1, 4096, 2048], P('pipe', 'seq')
Inputs may be any that keep to these rules, and one draw needn't show every extreme that they name: `doc_blocks`: in each section the document ids never fall from block to block, and each document covers 1 to 16 blocks, and at least one document of each section covers exactly 16.
All inputs are finite; a program needn't handle non-finite values.
Results may differ from a plain program's by a relative error of at most 0.015.
Values may be sent and summed in bfloat16 or wider, within the bound.
No kernel may reach another device: no remote copies, remote signals or barrier semaphores. Data moves between devices by JAX's collectives and lax.ppermute only.
A program may use at most 192 MiB of HBM per device.

v0:
```python
import jax
import jax.numpy as jnp
from jax import lax
from jax.experimental import pallas as pl
from jax.sharding import PartitionSpec as P

HEADS = 32
KV_HEADS = 16
HEAD_DIM = 128
WINDOW = 1024
MBLK = 128


SCORE_SCALE = 168.0 ** (-0.5)
MASKED_SCORE = -1e30


def passed_along(value, axis, steps):
    count = lax.axis_size(axis)
    pairs = [(source, (source + steps) % count) for source in range(count)]
    return lax.ppermute(value, axis, pairs)


def moved(value, pairs):
    return lax.ppermute(value, "seq", pairs)


def reverse(pairs):
    return [(t, s) for (s, t) in pairs]


class Routes:
    def __init__(self, count, reach):
        self.reach = reach
        self.chips = reach // 2
        group_chip = lambda i: (i % reach) // 2
        self.hop = [(i, i + reach) for i in range(count - reach)]
        self.up = []
        self.down = []
        for e in range(1, self.chips):
            self.up.append([(i, i + 2 * e) for i in range(count) if group_chip(i) + e < self.chips])
            self.down.append(
                [(i, i + 2 * e - reach) for i in range(count) if group_chip(i) + e >= self.chips]
            )
        self.sibling = [(i, i ^ 1) for i in range(count)]


def gather_window(own, routes, chip_in_group, core):
    prev = moved(own, routes.hop)
    direct = [own]
    for e in range(1, routes.chips):
        up = moved(own, routes.up[e - 1])
        down = moved(prev, routes.down[e - 1])
        direct.append(jnp.where(chip_in_group >= e, up, down))
    later = direct[1:] + [prev]
    sent = jnp.where(core == 0, jnp.stack(direct), jnp.stack(later))
    sib = moved(sent, routes.sibling)
    return prev, direct, sib


def scatter_window(prev, direct, sib, routes, chip_in_group, core):
    chips = routes.chips
    link = jnp.bfloat16
    back = moved(sib, routes.sibling).astype(jnp.float32)
    is_even = core == 0
    own = direct[0] + jnp.where(is_even, back[0], 0.0)
    prev = prev + jnp.where(is_even, 0.0, back[chips - 1])
    sums = [direct[e] + jnp.where(is_even, back[e], back[e - 1]) for e in range(1, chips)]
    for e in range(1, chips):
        sent = sums[e - 1].astype(link)
        prev = prev + moved(sent, reverse(routes.down[e - 1])).astype(jnp.float32)
    for e in range(1, chips):
        sent = sums[e - 1].astype(link)
        own = own + moved(sent, reverse(routes.up[e - 1])).astype(jnp.float32)
    own = own + moved(prev.astype(link), reverse(routes.hop)).astype(jnp.float32)
    return own


def attention_kernel(chips, mask_ref, q_ref, do_ref, prev_ref, *refs):
    direct_refs = refs[:chips]
    sib_ref = refs[chips]
    dq_ref, dprev_ref = refs[chips + 1], refs[chips + 2]
    ddirect_refs = refs[chips + 3 : 2 * chips + 3]
    dsib_ref = refs[2 * chips + 3]
    tokens = q_ref.shape[0]
    blocks = [prev_ref]
    for k in range(chips - 1, -1, -1):
        blocks.append(sib_ref.at[k])
        blocks.append(direct_refs[k])
    k = jnp.concatenate([b[0] for b in blocks], axis=0)
    v = jnp.concatenate([b[1] for b in blocks], axis=0)
    visible = mask_ref[...] > 0.0
    visible = jnp.concatenate([visible, visible], axis=0)
    q = q_ref[...]
    do = do_ref[...]
    qs = jnp.concatenate([q[:, :HEAD_DIM], q[:, HEAD_DIM:]], axis=0)
    dos = jnp.concatenate([do[:, :HEAD_DIM], do[:, HEAD_DIM:]], axis=0)
    contract_last = (((1,), (1,)), ((), ()))
    contract_first = (((0,), (0,)), ((), ()))
    scores = lax.dot_general(qs, k, contract_last, preferred_element_type=jnp.float32) * SCORE_SCALE
    scores = jnp.where(visible, scores, MASKED_SCORE)
    largest = jnp.max(scores, axis=1, keepdims=True)
    unscaled = jnp.where(visible, jnp.exp(scores - largest), 0.0)
    attn = unscaled * (1.0 / jnp.sum(unscaled, axis=1, keepdims=True))
    dattn = lax.dot_general(dos, v, contract_last, preferred_element_type=jnp.float32)
    row_delta = jnp.sum(attn * dattn, axis=1, keepdims=True)
    dscores = (attn * (dattn - row_delta)).astype(jnp.bfloat16)
    grad_q = jnp.dot(dscores, k, preferred_element_type=jnp.float32) * SCORE_SCALE
    dq_ref[:, :HEAD_DIM] = grad_q[:tokens].astype(dq_ref.dtype)
    dq_ref[:, HEAD_DIM:] = grad_q[tokens:].astype(dq_ref.dtype)
    grad_k = (
        lax.dot_general(dscores, qs, contract_first, preferred_element_type=jnp.float32)
        * SCORE_SCALE
    )
    grad_v = lax.dot_general(
        attn.astype(jnp.bfloat16), dos, contract_first, preferred_element_type=jnp.float32
    )
    outs = [dprev_ref]
    for kk in range(chips - 1, -1, -1):
        outs.append(dsib_ref.at[kk])
        outs.append(ddirect_refs[kk])
    for j, out in enumerate(outs):
        rows = slice(j * tokens, (j + 1) * tokens)
        out[0] = grad_k[rows].astype(out.dtype)
        out[1] = grad_v[rows].astype(out.dtype)


def attention_grads(mask, queries, grad_out, prev, direct, sib):
    tokens = queries.shape[0]
    chips = len(direct)
    key_count = mask.shape[1]
    width = prev.shape[2]
    heads = width // HEAD_DIM
    pair = 2 * HEAD_DIM
    block = pl.BlockSpec((2, tokens, HEAD_DIM), lambda g: (0, 0, g))
    sib_block = pl.BlockSpec((chips, 2, tokens, HEAD_DIM), lambda g: (0, 0, 0, g))
    pair_block = pl.BlockSpec((tokens, pair), lambda g: (0, g))
    part = jax.ShapeDtypeStruct(prev.shape, jnp.float32)
    flops = 2 * 5 * (2 * tokens) * key_count * HEAD_DIM * heads
    moved_bytes = 2 * 3 * queries.size + 2 * 2 * key_count * width * 3 + mask.size * 4
    return pl.pallas_call(
        lambda *refs: attention_kernel(chips, *refs),
        grid=(heads,),
        in_specs=[pl.BlockSpec((tokens, key_count), lambda g: (0, 0)), pair_block, pair_block]
        + [block] * (chips + 1)
        + [sib_block],
        out_specs=[pair_block] + [block] * (chips + 1) + [sib_block],
        out_shape=[jax.ShapeDtypeStruct(queries.shape, jnp.bfloat16)]
        + [part] * (chips + 1)
        + [jax.ShapeDtypeStruct(sib.shape, jnp.bfloat16)],
        cost_estimate=pl.CostEstimate(
            flops=flops, transcendentals=2 * tokens * key_count * heads, bytes_accessed=moved_bytes
        ),
    )(mask, queries, grad_out, prev, *direct, sib)


def local(queries, key_rows, value_rows, arriving_grad, doc_blocks):
    tokens = queries.shape[1]
    count = lax.axis_size("seq")
    grad_out = passed_along(arriving_grad, "pipe", -1)[0]
    position = lax.axis_index("seq")
    reach_back = (WINDOW - 1) // tokens + 1
    assert reach_back % 2 == 0 and count % reach_back == 0 and WINDOW % tokens == 0
    routes = Routes(count, reach_back)
    chip_in_group = (position % reach_back) // 2
    core = position % 2
    key_count = (reach_back + 1) * tokens
    token_doc = jnp.repeat(doc_blocks[0], MBLK)
    doc_pad = jnp.concatenate([jnp.full((reach_back * tokens,), -1, jnp.int32), token_doc])
    key_doc = lax.dynamic_slice_in_dim(doc_pad, position * tokens, key_count, 0)
    key_pos = (position - reach_back) * tokens + jnp.arange(key_count, dtype=jnp.int32)
    query_pos = position * tokens + jnp.arange(tokens, dtype=jnp.int32)
    query_doc = lax.dynamic_slice_in_dim(token_doc, position * tokens, tokens, 0)
    distance = query_pos[:, None] - key_pos[None, :]
    allowed = (distance >= 0) & (distance < WINDOW) & (query_doc[:, None] == key_doc[None, :])
    mask = allowed.astype(jnp.float32)
    packed = jnp.stack([key_rows[0], value_rows[0]])
    prev, direct, sib = gather_window(packed, routes, chip_in_group, core)
    outs = attention_grads(mask, queries[0], grad_out, prev, direct, sib)
    grad_query, dprev, ddirect, dsib = outs[0], outs[1], outs[2 : 2 + routes.chips], outs[-1]
    summed = scatter_window(dprev, ddirect, dsib, routes, chip_in_group, core)
    return (
        grad_query[None],
        summed[0].astype(jnp.bfloat16)[None],
        summed[1].astype(jnp.bfloat16)[None],
    )


def solution(mesh):
    placed = (
        P("pipe", "seq", None),
        P("pipe", "seq", None),
        P("pipe", "seq", None),
        P("pipe", "seq", None),
        P("pipe", None),
    )
    return jax.shard_map(
        local,
        mesh=mesh,
        in_specs=placed,
        out_specs=(P("pipe", "seq", None), P("pipe", "seq", None), P("pipe", "seq", None)),
        check_vma=False,
    )
```

profile of v0, /device:TPU:7, one launch (start us, length us, event | category | flops | bytes accessed | tf_op | source)
XLA Modules:
  0.0 215.2 jit_solution(6524982636948650854)
XLA Ops:
  0.6 0.0 copy-start
  0.6 1.1 constant_dynamic-update-slice_fusion.1
  1.7 1.1 constant_dynamic-update-slice_fusion.refs_4_
  2.8 0.0 copy-start.4
  2.8 3.3 %collective-permute-start.1 = (bf16[2,128,2048]{2,1,0:T(8,128)(2,1)S(1)}, bf16[2,128,2048]{2,1,0:T(8,128)(2,1)S(1)}, u32[]{:S(2)}, u32[]{:S(2)}) collective-permute-start(bf16[2,128,2048]{2,1,0:T(8,128)(2,1)S(1)} %constant_dynamic-update-slice_fusion.refs_4_), channel_id=1, source_target_pairs={{0,8},{1,9},{2,10},{3,11},{4,12},{5,13},{6,14},{7,15},{8,16},{9,17... | collective-permute-start | bytes 3145736 | tf_op jit(solution)/shard_map/ppermute | solution.py:25
  6.1 1.3 collective-permute-start.6
  7.4 20.4 %collective-permute-done.1.refs_3_ = bf16[2,128,2048]{2,1,0:T(8,128)(2,1)S(1)} collective-permute-done((bf16[2,128,2048]{2,1,0:T(8,128)(2,1)S(1)}, bf16[2,128,2048]{2,1,0:T(8,128)(2,1)S(1)}, u32[]{:S(2)}, u32[]{:S(2)}) %collective-permute-start.1) | collective-permute-done | bytes 1048608 | tf_op jit(solution)/shard_map/ppermute | solution.py:25
  27.8 3.1 %collective-permute-start.7 = (bf16[2,128,2048]{2,1,0:T(8,128)(2,1)S(1)}, bf16[2,128,2048]{2,1,0:T(8,128)(2,1)}, u32[]{:S(2)}, u32[]{:S(2)}) collective-permute-start(bf16[2,128,2048]{2,1,0:T(8,128)(2,1)S(1)} %collective-permute-done.1.refs_3_), channel_id=1, source_target_pairs={{2,0},{3,1},{4,2},{5,3},{6,4},{7,5},{10,8},{11,9},{12,10},{13,11},... | collective-permute-start | bytes 3145736 | tf_op jit(solution)/shard_map/ppermute | solution.py:25
  31.0 1.3 collective-permute-start.4
  32.3 5.9 %collective-permute-start.5 = (bf16[2,128,2048]{2,1,0:T(8,128)(2,1)S(1)}, bf16[2,128,2048]{2,1,0:T(8,128)(2,1)}, u32[]{:S(2)}, u32[]{:S(2)}) collective-permute-start(bf16[2,128,2048]{2,1,0:T(8,128)(2,1)S(1)} %collective-permute-done.1.refs_3_), channel_id=1, source_target_pairs={{4,0},{5,1},{6,2},{7,3},{12,8},{13,9},{14,10},{15,11},{20,16},{21,... | collective-permute-start | bytes 3145736 | tf_op jit(solution)/shard_map/ppermute | solution.py:25
  38.2 1.3 collective-permute-start.2
  39.5 0.0 collective-permute-done.6
  39.5 2.3 %collective-permute-start.3 = (bf16[2,128,2048]{2,1,0:T(8,128)(2,1)S(1)}, bf16[2,128,2048]{2,1,0:T(8,128)(2,1)S(1)}, u32[]{:S(2)}, u32[]{:S(2)}) collective-permute-start(bf16[2,128,2048]{2,1,0:T(8,128)(2,1)S(1)} %collective-permute-done.1.refs_3_), channel_id=1, source_target_pairs={{6,0},{7,1},{14,8},{15,9},{22,16},{23,17},{30,24},{31,25}} | collective-permute-start | bytes 3145736 | tf_op jit(solution)/shard_map/ppermute | solution.py:25
  41.8 9.1 %collective-permute-done.7 = bf16[2,128,2048]{2,1,0:T(8,128)(2,1)} collective-permute-done((bf16[2,128,2048]{2,1,0:T(8,128)(2,1)S(1)}, bf16[2,128,2048]{2,1,0:T(8,128)(2,1)}, u32[]{:S(2)}, u32[]{:S(2)}) %collective-permute-start.7) | collective-permute-done | bytes 1048608 | tf_op jit(solution)/shard_map/ppermute | solution.py:25
  50.9 1.3 broadcast_select_fusion.refs_7_
  52.2 0.0 copy-start.1
  52.2 3.6 %collective-permute-done.4 = bf16[2,128,2048]{2,1,0:T(8,128)(2,1)} collective-permute-done((bf16[2,128,2048]{2,1,0:T(8,128)(2,1)S(1)}, bf16[2,128,2048]{2,1,0:T(8,128)(2,1)}, u32[]{:S(2)}, u32[]{:S(2)}) %collective-permute-start.4) | collective-permute-done | bytes 1048608 | tf_op jit(solution)/shard_map/ppermute | solution.py:25
  55.8 20.4 %collective-permute-done.5 = bf16[2,128,2048]{2,1,0:T(8,128)(2,1)} collective-permute-done((bf16[2,128,2048]{2,1,0:T(8,128)(2,1)S(1)}, bf16[2,128,2048]{2,1,0:T(8,128)(2,1)}, u32[]{:S(2)}, u32[]{:S(2)}) %collective-permute-start.5) | collective-permute-done | bytes 1048608 | tf_op jit(solution)/shard_map/ppermute | solution.py:25
  76.2 1.3 broadcast_select_fusion.1.refs_6_
  77.5 0.0 copy-done.4
  77.6 0.0 copy-start.2
  77.6 0.0 collective-permute-done.2
  77.6 0.0 copy-start.5
  77.6 0.0 collective-permute-done.3
  77.6 0.1 broadcast_select_fusion.2.refs_5_
  77.7 0.0 copy-start.3
  77.7 0.0 copy-done.11
  77.7 0.0 copy-done.1
  77.7 1.8 copy-done.5
  79.6 2.5 %maximum_select_fusion = bf16[4,2,128,2048]{3,2,1,0:T(8,128)(2,1)} fusion(bf16[1,2,128,2048]{3,2,1,0:T(8,128)(2,1)S(1)} %bitcast.46, bf16[1,2,128,2048]{3,2,1,0:T(8,128)(2,1)S(1)} %bitcast.47, bf16[1,2,128,2048]{3,2,1,0:T(8,128)(2,1)S(1)} %bitcast.48, bf16[1,2,128,2048]{3,2,1,0:T(8,128)(2,1)S(1)} %bitcast.49, bf16[1,2,128,2048]{3,2,1,0:T(8,128)(2,1)S(1)} %bitcast.50, ...), kind=kLoop, calls=%fused_computation | loop fusion | flops 14680064 | bytes 9437185 | tf_op jit(solution)/shard_map/jit(_where)/select_n | solution.py:56
  82.1 0.0 copy-done.2
  82.1 0.0 copy-done.3
  82.1 0.5 collective-permute-start.8
  82.6 0.0 copy-done.12
  82.6 0.1 collective-permute-start
  82.7 0.0 copy-done
  82.7 0.1 broadcast_bitcast_fusion
  82.7 0.1 dynamic_slice.6
  82.8 0.1 pad_dynamic-slice_fusion
  82.9 1.1 fusion.14.refs_0_
  84.0 0.0 collective-permute-done
  84.0 5.7 %collective-permute-done.8.refs_8_ = bf16[4,2,128,2048]{3,2,1,0:T(8,128)(2,1)} collective-permute-done((bf16[4,2,128,2048]{3,2,1,0:T(8,128)(2,1)}, bf16[4,2,128,2048]{3,2,1,0:T(8,128)(2,1)}, u32[]{:S(2)}, u32[]{:S(2)}) %collective-permute-start.8) | collective-permute-done | bytes 4194336 | tf_op jit(solution)/shard_map/ppermute | solution.py:25
  89.7 27.7 %shard_map.76 = (bf16[128,4096]{1,0:T(8,128)(2,1)}, f32[2,128,2048]{2,1,0:T(8,128)}, f32[2,128,2048]{2,1,0:T(8,128)}, f32[2,128,2048]{2,1,0:T(8,128)}, f32[2,128...) custom-call(f32[128,1152]{1,0:T(8,128)} %fusion.14.refs_0_, ...), custom_call_target="tpu_custom_call" | custom-call | flops 6039797760 | bytes 32047104 | tf_op jit(solution)/shard_map/pallas_call | solution.py:141
  117.4 0.4 collective-permute-start.9
  117.8 7.0 %collective-permute-done.9 = bf16[4,2,128,2048]{3,2,1,0:T(8,128)(2,1)S(1)} collective-permute-done((bf16[4,2,128,2048]{3,2,1,0:T(8,128)(2,1)}, bf16[4,2,128,2048]{3,2,1,0:T(8,128)(2,1)S(1)}, u32[]{:S(2)}, u32[]{:S(2)}) %collective-permute-start.9) | collective-permute-done | bytes 4194336 | tf_op jit(solution)/shard_map/ppermute | solution.py:25
  124.8 1.1 convert_element_type.47
  125.9 2.8 %fusion.6 = (bf16[2,128,2048]{2,1,0:T(8,128)(2,1)}, bf16[2,128,2048]{2,1,0:T(8,128)(2,1)S(1)}, bf16[2,128,2048]{2,1,0:T(8,128)(2,1)S(1)}) fusion(f32[2,128,2048]{2,1,0:T(8,128)S(1)} %copy-done.7, f32[4,2,128,2048]{3,2,1,0:T(8,128)S(1)} %convert_element_type.47, pred[]{:T(512)S(6)} %eq.23, f32[2,128,2048]{2,1,0:T(8,128)S(1)} %copy-done.9, ...), kind=kLoop, calls=%fused_computation.11 | loop fusion | flops 4718592 | bytes 17825792 | tf_op jit(solution)/shard_map/convert_element_type | solution.py:73
  128.8 1.3 collective-permute-start.13
  130.1 1.3 collective-permute-start.15
  131.4 1.3 collective-permute-start.14
  132.7 8.6 %collective-permute-start.10 = (bf16[2,128,2048]{2,1,0:T(8,128)(2,1)}, bf16[2,128,2048]{2,1,0:T(8,128)(2,1)S(1)}, u32[]{:S(2)}, u32[]{:S(2)}) collective-permute-start(bf16[2,128,2048]{2,1,0:T(8,128)(2,1)} %get-tuple-element.17), channel_id=1, source_target_pairs={{2,0},{3,1},{4,2},{5,3},{6,4},{7,5},{10,8},{11,9},{12,10},{13,11},... | collective-permute-start | bytes 3145736 | tf_op jit(solution)/shard_map/ppermute | solution.py:25
  141.3 3.4 %collective-permute-start.12 = (bf16[2,128,2048]{2,1,0:T(8,128)(2,1)S(1)}, bf16[2,128,2048]{2,1,0:T(8,128)(2,1)S(1)}, u32[]{:S(2)}, u32[]{:S(2)}) collective-permute-start(bf16[2,128,2048]{2,1,0:T(8,128)(2,1)S(1)} %get-tuple-element.18), channel_id=1, source_target_pairs={{6,0},{7,1},{14,8},{15,9},{22,16},{23,17},{30,24},{31,25}} | collective-permute-start | bytes 3145736 | tf_op jit(solution)/shard_map/ppermute | solution.py:25
  144.7 17.4 %collective-permute-done.13 = bf16[2,128,2048]{2,1,0:T(8,128)(2,1)S(1)} collective-permute-done((bf16[2,128,2048]{2,1,0:T(8,128)(2,1)}, bf16[2,128,2048]{2,1,0:T(8,128)(2,1)S(1)}, u32[]{:S(2)}, u32[]{:S(2)}) %collective-permute-start.13) | collective-permute-done | bytes 1048608 | tf_op jit(solution)/shard_map/ppermute | solution.py:25
  162.1 1.3 collective-permute-start.11
  163.5 0.0 collective-permute-done.15
  163.5 21.5 %collective-permute-done.14 = bf16[2,128,2048]{2,1,0:T(8,128)(2,1)S(1)} collective-permute-done((bf16[2,128,2048]{2,1,0:T(8,128)(2,1)S(1)}, bf16[2,128,2048]{2,1,0:T(8,128)(2,1)S(1)}, u32[]{:S(2)}, u32[]{:S(2)}) %collective-permute-start.14) | collective-permute-done | bytes 1048608 | tf_op jit(solution)/shard_map/ppermute | solution.py:25
  184.9 0.9 fusion.3
  185.9 1.3 collective-permute-start.16
  187.2 0.0 collective-permute-done.10
  187.2 0.0 collective-permute-done.12
  187.2 18.3 %collective-permute-done.11 = bf16[2,128,2048]{2,1,0:T(8,128)(2,1)S(1)} collective-permute-done((bf16[2,128,2048]{2,1,0:T(8,128)(2,1)S(1)}, bf16[2,128,2048]{2,1,0:T(8,128)(2,1)S(1)}, u32[]{:S(2)}, u32[]{:S(2)}) %collective-permute-start.11) | collective-permute-done | bytes 1048608 | tf_op jit(solution)/shard_map/ppermute | solution.py:25
  205.5 7.6 %collective-permute-done.16 = bf16[2,128,2048]{2,1,0:T(8,128)(2,1)S(1)} collective-permute-done((bf16[2,128,2048]{2,1,0:T(8,128)(2,1)S(1)}, bf16[2,128,2048]{2,1,0:T(8,128)(2,1)S(1)}, u32[]{:S(2)}, u32[]{:S(2)}) %collective-permute-start.16) | collective-permute-done | bytes 1048608 | tf_op jit(solution)/shard_map/ppermute | solution.py:25
  213.1 1.0 fusion.11
  214.1 1.1 fusion.15
  (15 shorter events, 0.0 us)
Async XLA Ops:
  0.6 82.0 %copy-start = (s32[1,32]{1,0:T(1,128)S(1)}, s32[1,32]{1,0:T(1,128)}, u32[]{:S(2)}) copy-start(s32[1,32]{1,0:T(1,128)} %param.9) | copy-start | bytes 388
  2.8 74.7 %copy-start.4 = (bf16[2,128,2048]{2,1,0:T(8,128)(2,1)}, bf16[2,128,2048]{2,1,0:T(8,128)(2,1)S(1)}, u32[]{:S(2)}) copy-start(bf16[2,128,2048]{2,1,0:T(8,128)(2,1)S(1)} %constant_dynamic-update-slice_fusion.refs_4_) | copy-start | bytes 3145732
  2.8 25.0 %collective-permute-start.1 = (bf16[2,128,2048]{2,1,0:T(8,128)(2,1)S(1)}, bf16[2,128,2048]{2,1,0:T(8,128)(2,1)S(1)}, u32[]{:S(2)}, u32[]{:S(2)}) collective-permute-start(bf16[2,128,2048]{2,1,0:T(8,128)(2,1)S(1)} %constant_dynamic-update-slice_fusion.refs_4_), channel_id=1, source_target_pairs={{0,8},{1,9},{2,10},{3,11},{4,12},{5,13},{6,14},{7,15},{8,16},{9,17... | collective-permute-start | bytes 3145736 | tf_op jit(solution)/shard_map/ppermute | solution.py:25
  6.1 33.4 %collective-permute-start.6 = (bf16[2,128,2048]{2,1,0:T(8,128)(2,1)S(1)}, bf16[2,128,2048]{2,1,0:T(8,128)(2,1)}, u32[]{:S(2)}, u32[]{:S(2)}) collective-permute-start(bf16[2,128,2048]{2,1,0:T(8,128)(2,1)S(1)} %constant_dynamic-update-slice_fusion.refs_4_), channel_id=1, source_target_pairs={{0,6},{1,7},{8,14},{9,15},{16,22},{17,23},{24,30},{25,31}} | collective-permute-start | bytes 3145736 | tf_op jit(solution)/shard_map/ppermute | solution.py:25
  27.8 49.9 %copy-start.11 = (bf16[2,128,2048]{2,1,0:T(8,128)(2,1)}, bf16[2,128,2048]{2,1,0:T(8,128)(2,1)S(1)}, u32[]{:S(2)}) copy-start(bf16[2,128,2048]{2,1,0:T(8,128)(2,1)S(1)} %collective-permute-done.1.refs_3_) | copy-start | bytes 3145732
  27.8 23.0 %collective-permute-start.7 = (bf16[2,128,2048]{2,1,0:T(8,128)(2,1)S(1)}, bf16[2,128,2048]{2,1,0:T(8,128)(2,1)}, u32[]{:S(2)}, u32[]{:S(2)}) collective-permute-start(bf16[2,128,2048]{2,1,0:T(8,128)(2,1)S(1)} %collective-permute-done.1.refs_3_), channel_id=1, source_target_pairs={{2,0},{3,1},{4,2},{5,3},{6,4},{7,5},{10,8},{11,9},{12,10},{13,11},... | collective-permute-start | bytes 3145736 | tf_op jit(solution)/shard_map/ppermute | solution.py:25
  31.0 24.8 %collective-permute-start.4 = (bf16[2,128,2048]{2,1,0:T(8,128)(2,1)S(1)}, bf16[2,128,2048]{2,1,0:T(8,128)(2,1)}, u32[]{:S(2)}, u32[]{:S(2)}) collective-permute-start(bf16[2,128,2048]{2,1,0:T(8,128)(2,1)S(1)} %constant_dynamic-update-slice_fusion.refs_4_), channel_id=1, source_target_pairs={{0,4},{1,5},{2,6},{3,7},{8,12},{9,13},{10,14},{11,15},{16,20},{17,... | collective-permute-start | bytes 3145736 | tf_op jit(solution)/shard_map/ppermute | solution.py:25
  32.3 43.9 %collective-permute-start.5 = (bf16[2,128,2048]{2,1,0:T(8,128)(2,1)S(1)}, bf16[2,128,2048]{2,1,0:T(8,128)(2,1)}, u32[]{:S(2)}, u32[]{:S(2)}) collective-permute-start(bf16[2,128,2048]{2,1,0:T(8,128)(2,1)S(1)} %collective-permute-done.1.refs_3_), channel_id=1, source_target_pairs={{4,0},{5,1},{6,2},{7,3},{12,8},{13,9},{14,10},{15,11},{20,16},{21,... | collective-permute-start | bytes 3145736 | tf_op jit(solution)/shard_map/ppermute | solution.py:25
  38.2 39.4 %collective-permute-start.2 = (bf16[2,128,2048]{2,1,0:T(8,128)(2,1)S(1)}, bf16[2,128,2048]{2,1,0:T(8,128)(2,1)S(1)}, u32[]{:S(2)}, u32[]{:S(2)}) collective-permute-start(bf16[2,128,2048]{2,1,0:T(8,128)(2,1)S(1)} %constant_dynamic-update-slice_fusion.refs_4_), channel_id=1, source_target_pairs={{0,2},{1,3},{2,4},{3,5},{4,6},{5,7},{8,10},{9,11},{10,12},{11,13},... | collective-permute-start | bytes 3145736 | tf_op jit(solution)/shard_map/ppermute | solution.py:25
  39.5 38.0 %collective-permute-start.3 = (bf16[2,128,2048]{2,1,0:T(8,128)(2,1)S(1)}, bf16[2,128,2048]{2,1,0:T(8,128)(2,1)S(1)}, u32[]{:S(2)}, u32[]{:S(2)}) collective-permute-start(bf16[2,128,2048]{2,1,0:T(8,128)(2,1)S(1)} %collective-permute-done.1.refs_3_), channel_id=1, source_target_pairs={{6,0},{7,1},{14,8},{15,9},{22,16},{23,17},{30,24},{31,25}} | collective-permute-start | bytes 3145736 | tf_op jit(solution)/shard_map/ppermute | solution.py:25
  52.2 25.5 %copy-start.1 = (bf16[2,128,2048]{2,1,0:T(8,128)(2,1)}, bf16[2,128,2048]{2,1,0:T(8,128)(2,1)S(1)}, u32[]{:S(2)}) copy-start(bf16[2,128,2048]{2,1,0:T(8,128)(2,1)S(1)} %broadcast_select_fusion.refs_7_) | copy-start | bytes 3145732
  77.6 4.5 %copy-start.2 = (bf16[2,128,2048]{2,1,0:T(8,128)(2,1)}, bf16[2,128,2048]{2,1,0:T(8,128)(2,1)S(1)}, u32[]{:S(2)}) copy-start(bf16[2,128,2048]{2,1,0:T(8,128)(2,1)S(1)} %broadcast_select_fusion.1.refs_6_) | copy-start | bytes 3145732
  77.6 2.0 copy-start.5
  77.7 4.4 %copy-start.3 = (bf16[2,128,2048]{2,1,0:T(8,128)(2,1)}, bf16[2,128,2048]{2,1,0:T(8,128)(2,1)S(1)}, u32[]{:S(2)}) copy-start(bf16[2,128,2048]{2,1,0:T(8,128)(2,1)S(1)} %broadcast_select_fusion.2.refs_5_) | copy-start | bytes 3145732
  79.6 3.0 %copy-start.12 = (bf16[1,128,4096]{2,1,0:T(8,128)(2,1)S(1)}, bf16[1,128,4096]{2,1,0:T(8,128)(2,1)}, u32[]{:S(2)}) copy-start(bf16[1,128,4096]{2,1,0:T(8,128)(2,1)} %param.8) | copy-start | bytes 3145732
  82.1 7.6 %collective-permute-start.8 = (bf16[4,2,128,2048]{3,2,1,0:T(8,128)(2,1)}, bf16[4,2,128,2048]{3,2,1,0:T(8,128)(2,1)}, u32[]{:S(2)}, u32[]{:S(2)}) collective-permute-start(bf16[4,2,128,2048]{3,2,1,0:T(8,128)(2,1)} %maximum_select_fusion), channel_id=1, source_target_pairs={{0,1},{1,0},{2,3},{3,2},{4,5},{5,4},{6,7},{7,6},{8,9},{9,8},{10,11... | collective-permute-start | bytes 12582920 | tf_op jit(solution)/shard_map/ppermute | solution.py:25
  82.6 1.4 collective-permute-start
  84.0 5.7 %copy-start.13 = (bf16[1,128,4096]{2,1,0:T(8,128)(2,1)}, bf16[1,128,4096]{2,1,0:T(8,128)(2,1)S(1)}, u32[]{:S(2)}) copy-start(bf16[1,128,4096]{2,1,0:T(8,128)(2,1)S(1)} %collective-permute-done) | copy-start | bytes 3145732
  117.4 8.5 %copy-start.7 = (f32[2,128,2048]{2,1,0:T(8,128)S(1)}, f32[2,128,2048]{2,1,0:T(8,128)}, u32[]{:S(2)}) copy-start(f32[2,128,2048]{2,1,0:T(8,128)} %get-tuple-element.13) | copy-start | bytes 6291460
  117.4 8.5 %copy-start.8 = (f32[2,128,2048]{2,1,0:T(8,128)S(1)}, f32[2,128,2048]{2,1,0:T(8,128)}, u32[]{:S(2)}) copy-start(f32[2,128,2048]{2,1,0:T(8,128)} %get-tuple-element.14) | copy-start | bytes 6291460
  117.4 8.5 %copy-start.9 = (f32[2,128,2048]{2,1,0:T(8,128)S(1)}, f32[2,128,2048]{2,1,0:T(8,128)}, u32[]{:S(2)}) copy-start(f32[2,128,2048]{2,1,0:T(8,128)} %get-tuple-element.15) | copy-start | bytes 6291460
  117.4 7.4 %collective-permute-start.9 = (bf16[4,2,128,2048]{3,2,1,0:T(8,128)(2,1)}, bf16[4,2,128,2048]{3,2,1,0:T(8,128)(2,1)S(1)}, u32[]{:S(2)}, u32[]{:S(2)}) collective-permute-start(bf16[4,2,128,2048]{3,2,1,0:T(8,128)(2,1)} %get-tuple-element.12), channel_id=1, source_target_pairs={{0,1},{1,0},{2,3},{3,2},{4,5},{5,4},{6,7},{7,6},{8,9},{9,8},{10,11... | collective-permute-start | bytes 12582920 | tf_op jit(solution)/shard_map/ppermute | solution.py:25
  125.9 59.0 %copy-start.10 = (f32[2,128,2048]{2,1,0:T(8,128)S(1)}, f32[2,128,2048]{2,1,0:T(8,128)}, u32[]{:S(2)}) copy-start(f32[2,128,2048]{2,1,0:T(8,128)} %get-tuple-element.16) | copy-start | bytes 6291460
  128.8 33.3 %collective-permute-start.13 = (bf16[2,128,2048]{2,1,0:T(8,128)(2,1)}, bf16[2,128,2048]{2,1,0:T(8,128)(2,1)S(1)}, u32[]{:S(2)}, u32[]{:S(2)}) collective-permute-start(bf16[2,128,2048]{2,1,0:T(8,128)(2,1)} %get-tuple-element.17), channel_id=1, source_target_pairs={{0,6},{1,7},{8,14},{9,15},{16,22},{17,23},{24,30},{25,31}} | collective-permute-start | bytes 3145736 | tf_op jit(solution)/shard_map/ppermute | solution.py:25
  130.1 33.4 %collective-permute-start.15 = (bf16[2,128,2048]{2,1,0:T(8,128)(2,1)S(1)}, bf16[2,128,2048]{2,1,0:T(8,128)(2,1)S(1)}, u32[]{:S(2)}, u32[]{:S(2)}) collective-permute-start(bf16[2,128,2048]{2,1,0:T(8,128)(2,1)S(1)} %get-tuple-element.18), channel_id=1, source_target_pairs={{0,2},{1,3},{2,4},{3,5},{4,6},{5,7},{8,10},{9,11},{10,12},{11,13},... | collective-permute-start | bytes 3145736 | tf_op jit(solution)/shard_map/ppermute | solution.py:25
  131.4 53.6 %collective-permute-start.14 = (bf16[2,128,2048]{2,1,0:T(8,128)(2,1)S(1)}, bf16[2,128,2048]{2,1,0:T(8,128)(2,1)S(1)}, u32[]{:S(2)}, u32[]{:S(2)}) collective-permute-start(bf16[2,128,2048]{2,1,0:T(8,128)(2,1)S(1)} %get-tuple-element.19), channel_id=1, source_target_pairs={{0,4},{1,5},{2,6},{3,7},{8,12},{9,13},{10,14},{11,15},{16,20},{17,... | collective-permute-start | bytes 3145736 | tf_op jit(solution)/shard_map/ppermute | solution.py:25
  132.7 54.5 %collective-permute-start.10 = (bf16[2,128,2048]{2,1,0:T(8,128)(2,1)}, bf16[2,128,2048]{2,1,0:T(8,128)(2,1)S(1)}, u32[]{:S(2)}, u32[]{:S(2)}) collective-permute-start(bf16[2,128,2048]{2,1,0:T(8,128)(2,1)} %get-tuple-element.17), channel_id=1, source_target_pairs={{2,0},{3,1},{4,2},{5,3},{6,4},{7,5},{10,8},{11,9},{12,10},{13,11},... | collective-permute-start | bytes 3145736 | tf_op jit(solution)/shard_map/ppermute | solution.py:25
  141.3 45.9 %collective-permute-start.12 = (bf16[2,128,2048]{2,1,0:T(8,128)(2,1)S(1)}, bf16[2,128,2048]{2,1,0:T(8,128)(2,1)S(1)}, u32[]{:S(2)}, u32[]{:S(2)}) collective-permute-start(bf16[2,128,2048]{2,1,0:T(8,128)(2,1)S(1)} %get-tuple-element.18), channel_id=1, source_target_pairs={{6,0},{7,1},{14,8},{15,9},{22,16},{23,17},{30,24},{31,25}} | collective-permute-start | bytes 3145736 | tf_op jit(solution)/shard_map/ppermute | solution.py:25
  162.1 43.4 %collective-permute-start.11 = (bf16[2,128,2048]{2,1,0:T(8,128)(2,1)S(1)}, bf16[2,128,2048]{2,1,0:T(8,128)(2,1)S(1)}, u32[]{:S(2)}, u32[]{:S(2)}) collective-permute-start(bf16[2,128,2048]{2,1,0:T(8,128)(2,1)S(1)} %get-tuple-element.19), channel_id=1, source_target_pairs={{4,0},{5,1},{6,2},{7,3},{12,8},{13,9},{14,10},{15,11},{20,16},{21,... | collective-permute-start | bytes 3145736 | tf_op jit(solution)/shard_map/ppermute | solution.py:25
  184.9 28.2 %copy-start.6 = (f32[2,128,2048]{2,1,0:T(8,128)S(1)}, f32[2,128,2048]{2,1,0:T(8,128)}, u32[]{:S(2)}) copy-start(f32[2,128,2048]{2,1,0:T(8,128)} %get-tuple-element.11) | copy-start | bytes 6291460
  185.9 27.2 %collective-permute-start.16 = (bf16[2,128,2048]{2,1,0:T(8,128)(2,1)S(1)}, bf16[2,128,2048]{2,1,0:T(8,128)(2,1)S(1)}, u32[]{:S(2)}, u32[]{:S(2)}) collective-permute-start(bf16[2,128,2048]{2,1,0:T(8,128)(2,1)S(1)} %fusion.3), channel_id=1, source_target_pairs={{8,0},{9,1},{10,2},{11,3},{12,4},{13,5},{14,6},{15,7},{16,8},{17,9... | collective-permute-start | bytes 3145736 | tf_op jit(solution)/shard_map/ppermute | solution.py:25
where the time goes:
time: 218 us; the launch traced here: 215 us
  waiting for transfers between devices  131 us (60%)
  starting transfers between devices  38 us (17%)
  Pallas kernels  27.7 us (13%)
  other arithmetic  12.4 us (6%)
  local copies, waits for them, and re-layouts  5.25 us (2%)
    ppermute x16, waiting for transfers between devices, moved(): return lax.ppermute(value, 'seq', pairs)  131 us
    ppermute x16, starting transfers between devices, moved(): return lax.ppermute(value, 'seq', pairs)  37.9 us
    pallas_call x1, Pallas kernels, attention_grads(): pl.pallas_call(lambda *refs: attention_kernel(chips, *refs), grid=(heads,...  27.7 us
  transfers between devices with their start and end apart: 17, of which 10 were waited for; matrix products, arithmetic and copies ran while one was open for 2% of the time, Pallas kernels for 0%

commit v1 on v0

--- a/solution.py
+++ b/solution.py
@@ -9,6 +9,7 @@
 HEAD_DIM = 128
 WINDOW = 1024
 MBLK = 128
+CHUNKS = 2
 
 
 SCORE_SCALE = 168.0 ** (-0.5)
@@ -174,15 +175,27 @@
     distance = query_pos[:, None] - key_pos[None, :]
     allowed = (distance >= 0) & (distance < WINDOW) & (query_doc[:, None] == key_doc[None, :])
     mask = allowed.astype(jnp.float32)
-    packed = jnp.stack([key_rows[0], value_rows[0]])
-    prev, direct, sib = gather_window(packed, routes, chip_in_group, core)
-    outs = attention_grads(mask, queries[0], grad_out, prev, direct, sib)
-    grad_query, dprev, ddirect, dsib = outs[0], outs[1], outs[2 : 2 + routes.chips], outs[-1]
-    summed = scatter_window(dprev, ddirect, dsib, routes, chip_in_group, core)
+    width = KV_HEADS * HEAD_DIM // CHUNKS
+    query_parts, key_parts, value_parts = [], [], []
+    for chunk in range(CHUNKS):
+        keys = slice(chunk * width, (chunk + 1) * width)
+        pairs = slice(2 * chunk * width, 2 * (chunk + 1) * width)
+        packed = jnp.stack([key_rows[0][:, keys], value_rows[0][:, keys]])
+        if chunk > 0:
+            packed, _ = lax.optimization_barrier((packed, outs[0]))
+        prev, direct, sib = gather_window(packed, routes, chip_in_group, core)
+        if chunk > 0:
+            (prev, direct, sib), _ = lax.optimization_barrier(((prev, direct, sib), summed))
+        outs = attention_grads(mask, queries[0][:, pairs], grad_out[:, pairs], prev, direct, sib)
+        dprev, ddirect, dsib = outs[1], outs[2 : 2 + routes.chips], outs[-1]
+        summed = scatter_window(dprev, ddirect, dsib, routes, chip_in_group, core)
+        query_parts.append(outs[0])
+        key_parts.append(summed[0].astype(jnp.bfloat16))
+        value_parts.append(summed[1].astype(jnp.bfloat16))
     return (
-        grad_query[None],
-        summed[0].astype(jnp.bfloat16)[None],
-        summed[1].astype(jnp.bfloat16)[None],
+        jnp.concatenate(query_parts, axis=1)[None],
+        jnp.concatenate(key_parts, axis=1)[None],
+        jnp.concatenate(value_parts, axis=1)[None],
     )
 
 

time: 218 us -> 248 us (1.14)
  starting transfers between devices: 38 us -> 90 us
  waiting for transfers between devices: 131 us -> 103 us
    ppermute x16 -> x32, starting transfers between devices: 37.9 us -> 81.2 us  [moved(): return lax.ppermute(value, 'seq', pairs)]
    ppermute x16 -> x32, waiting for transfers between devices: 131 us -> 103 us  [moved(): return lax.ppermute(value, 'seq', pairs)]
    ppermute x1, starting transfers between devices: 0.07 us -> 8.83 us  [passed_along(): return lax.ppermute(value, axis, pairs)]
    slice x1 -> x2, local copies, waits for them, and re-layouts: 1.08 us -> 4.54 us  [the longest x1 2.27 us: local(): queries[0][:, pairs]]
    broadcast_in_dim x0 -> x3, other arithmetic: none -> 2.7 us  [the longest x1 1.05 us: local(): jnp.concatenate(query_parts, axis=1)[None]]
    pallas_call x1 -> x2, Pallas kernels: 27.7 us -> 30 us  [attention_grads(): pl.pallas_call(lambda *refs: attention_kernel(chips, *refs), grid=(heads,...]
  transfers between devices with their start and end apart: 17 -> 33, of which waited for: 10 -> 18; matrix products, arithmetic and copies ran while one was open for 2% -> 5% of each run, Pallas kernels for 0% -> 0%
where the time goes in v1:
time: 248 us; the launch traced here: 245 us
  waiting for transfers between devices  103 us (42%)
  starting transfers between devices  90 us (36%)
  Pallas kernels  30 us (12%)
  other arithmetic  12.7 us (5%)
  local copies, waits for them, and re-layouts  7.69 us (3%)
    ppermute x32, waiting for transfers between devices, moved(): return lax.ppermute(value, 'seq', pairs)  103 us
    ppermute x32, starting transfers between devices, moved(): return lax.ppermute(value, 'seq', pairs)  81.2 us
    pallas_call x2, Pallas kernels, attention_grads(): pl.pallas_call(lambda *refs: attention_kernel(chips, *refs), grid=(heads,...  30 us
    ppermute x1, starting transfers between devices, passed_along(): return lax.ppermute(value, axis, pairs)  8.83 us
  transfers between devices with their start and end apart: 33, of which 18 were waited for; matrix products, arithmetic and copies ran while one was open for 5% of the time, Pallas kernels for 0%

profile of v1, /device:TPU:7, one launch (start us, length us, event | category | flops | bytes accessed | tf_op | source)
XLA Modules:
  0.0 245.0 jit_solution(2661725655528637858)
XLA Ops:
  0.6 1.3 slice_bitcast_fusion.6
  2.0 3.2 %collective-permute-start.1 = (bf16[2,128,1024]{2,1,0:T(8,128)(2,1)S(1)}, bf16[2,128,1024]{2,1,0:T(8,128)(2,1)S(1)}, u32[]{:S(2)}, u32[]{:S(2)}) collective-permute-start(bf16[2,128,1024]{2,1,0:T(8,128)(2,1)S(1)} %get-tuple-element.60.refs_4_), channel_id=1, source_target_pairs={{0,8},{1,9},{2,10},{3,11},{4,12},{5,13},{6,14},{7,15},{8,16},{9,17... | collective-permute-start | bytes 1572872 | tf_op jit(solution)/shard_map/ppermute | solution.py:26
  5.3 1.3 collective-permute-start.4
  6.6 9.2 %collective-permute-done.1.refs_3_ = bf16[2,128,1024]{2,1,0:T(8,128)(2,1)S(1)} collective-permute-done((bf16[2,128,1024]{2,1,0:T(8,128)(2,1)S(1)}, bf16[2,128,1024]{2,1,0:T(8,128)(2,1)S(1)}, u32[]{:S(2)}, u32[]{:S(2)}) %collective-permute-start.1) | collective-permute-done | bytes 524320 | tf_op jit(solution)/shard_map/ppermute | solution.py:26
  15.8 2.9 %collective-permute-start.5 = (bf16[2,128,1024]{2,1,0:T(8,128)(2,1)S(1)}, bf16[2,128,1024]{2,1,0:T(8,128)(2,1)}, u32[]{:S(2)}, u32[]{:S(2)}) collective-permute-start(bf16[2,128,1024]{2,1,0:T(8,128)(2,1)S(1)} %collective-permute-done.1.refs_3_), channel_id=1, source_target_pairs={{4,0},{5,1},{6,2},{7,3},{12,8},{13,9},{14,10},{15,11},{20,16},{21,... | collective-permute-start | bytes 1572872 | tf_op jit(solution)/shard_map/ppermute | solution.py:26
  18.7 1.3 collective-permute-start.6
  20.0 3.1 %collective-permute-start.7 = (bf16[2,128,1024]{2,1,0:T(8,128)(2,1)S(1)}, bf16[2,128,1024]{2,1,0:T(8,128)(2,1)}, u32[]{:S(2)}, u32[]{:S(2)}) collective-permute-start(bf16[2,128,1024]{2,1,0:T(8,128)(2,1)S(1)} %collective-permute-done.1.refs_3_), channel_id=1, source_target_pairs={{2,0},{3,1},{4,2},{5,3},{6,4},{7,5},{10,8},{11,9},{12,10},{13,11},... | collective-permute-start | bytes 1572872 | tf_op jit(solution)/shard_map/ppermute | solution.py:26
  23.1 1.3 collective-permute-start.2
  24.5 6.6 %collective-permute-start.3 = (bf16[2,128,1024]{2,1,0:T(8,128)(2,1)S(1)}, bf16[2,128,1024]{2,1,0:T(8,128)(2,1)S(1)}, u32[]{:S(2)}, u32[]{:S(2)}) collective-permute-start(bf16[2,128,1024]{2,1,0:T(8,128)(2,1)S(1)} %collective-permute-done.1.refs_3_), channel_id=1, source_target_pairs={{6,0},{7,1},{14,8},{15,9},{22,16},{23,17},{30,24},{31,25}} | collective-permute-start | bytes 1572872 | tf_op jit(solution)/shard_map/ppermute | solution.py:26
  31.1 7.7 %collective-permute-done.5 = bf16[2,128,1024]{2,1,0:T(8,128)(2,1)} collective-permute-done((bf16[2,128,1024]{2,1,0:T(8,128)(2,1)S(1)}, bf16[2,128,1024]{2,1,0:T(8,128)(2,1)}, u32[]{:S(2)}, u32[]{:S(2)}) %collective-permute-start.5) | collective-permute-done | bytes 524320 | tf_op jit(solution)/shard_map/ppermute | solution.py:26
  38.9 1.3 broadcast_select_fusion.1.refs_7_
  40.2 3.9 %collective-permute-done.2 = bf16[2,128,1024]{2,1,0:T(8,128)(2,1)S(1)} collective-permute-done((bf16[2,128,1024]{2,1,0:T(8,128)(2,1)S(1)}, bf16[2,128,1024]{2,1,0:T(8,128)(2,1)S(1)}, u32[]{:S(2)}, u32[]{:S(2)}) %collective-permute-start.2) | collective-permute-done | bytes 524320 | tf_op jit(solution)/shard_map/ppermute | solution.py:26
  44.2 1.7 maximum_select_fusion
  45.9 2.5 %collective-permute-start.8 = (bf16[4,2,128,1024]{3,2,1,0:T(8,128)(2,1)S(1)}, bf16[4,2,128,1024]{3,2,1,0:T(8,128)(2,1)}, u32[]{:S(2)}, u32[]{:S(2)}) collective-permute-start(bf16[4,2,128,1024]{3,2,1,0:T(8,128)(2,1)S(1)} %maximum_select_fusion), channel_id=1, source_target_pairs={{0,1},{1,0},{2,3},{3,2},{4,5},{5,4},{6,7},{7,6},{8,9},{9,8},{10,11... | collective-permute-start | bytes 6291464 | tf_op jit(solution)/shard_map/ppermute | solution.py:26
  48.4 8.8 %collective-permute-start = (bf16[1,128,4096]{2,1,0:T(8,128)(2,1)}, bf16[1,128,4096]{2,1,0:T(8,128)(2,1)}, u32[]{:S(2)}, u32[]{:S(2)}) collective-permute-start(bf16[1,128,4096]{2,1,0:T(8,128)(2,1)} %param.8), channel_id=1, source_target_pairs={{0,0},{1,1},{2,2},{3,3},{4,4},{5,5},{6,6},{7,7},{8,8},{9,9},{10,10... | collective-permute-start | bytes 3145736 | tf_op jit(solution)/shard_map/ppermute | solution.py:22
  57.5 1.0 fusion.25.refs_0_
  58.5 2.3 fusion.28
  60.8 2.3 fusion.27
  63.1 15.0 %shard_map.76 = (bf16[128,2048]{1,0:T(8,128)(2,1)}, f32[2,128,1024]{2,1,0:T(8,128)}, f32[2,128,1024]{2,1,0:T(8,128)}, f32[2,128,1024]{2,1,0:T(8,128)}, f32[2,128...) custom-call(f32[128,1152]{1,0:T(8,128)} %fusion.25.refs_0_, ...), custom_call_target="tpu_custom_call" | custom-call | flops 3019898880 | bytes 16318464 | tf_op jit(solution)/shard_map/pallas_call | solution.py:142
  78.1 4.1 %collective-permute-start.9 = (bf16[2,128,1024]{2,1,0:T(8,128)(2,1)S(1)}, bf16[2,128,1024]{2,1,0:T(8,128)(2,1)S(1)}, u32[]{:S(2)}, u32[]{:S(2)}) collective-permute-start(bf16[2,128,1024]{2,1,0:T(8,128)(2,1)S(1)} %pad_maximum_fusion.1.refs_4_), channel_id=1, source_target_pairs={{0,8},{1,9},{2,10},{3,11},{4,12},{5,13},{6,14},{7,15},{8,16},{9,17... | collective-permute-start | bytes 1572872 | tf_op jit(solution)/shard_map/ppermute | solution.py:26
  82.6 1.3 collective-permute-start.14
  83.9 9.6 %collective-permute-done.9.refs_3_ = bf16[2,128,1024]{2,1,0:T(8,128)(2,1)S(1)} collective-permute-done((bf16[2,128,1024]{2,1,0:T(8,128)(2,1)S(1)}, bf16[2,128,1024]{2,1,0:T(8,128)(2,1)S(1)}, u32[]{:S(2)}, u32[]{:S(2)}) %collective-permute-start.9) | collective-permute-done | bytes 524320 | tf_op jit(solution)/shard_map/ppermute | solution.py:26
  93.5 6.7 %collective-permute-start.15 = (bf16[2,128,1024]{2,1,0:T(8,128)(2,1)S(1)}, bf16[2,128,1024]{2,1,0:T(8,128)(2,1)S(1)}, u32[]{:S(2)}, u32[]{:S(2)}) collective-permute-start(bf16[2,128,1024]{2,1,0:T(8,128)(2,1)S(1)} %collective-permute-done.9.refs_3_), channel_id=1, source_target_pairs={{2,0},{3,1},{4,2},{5,3},{6,4},{7,5},{10,8},{11,9},{12,10},{13,11},... | collective-permute-start | bytes 1572872 | tf_op jit(solution)/shard_map/ppermute | solution.py:26
  100.2 1.3 collective-permute-start.12
  101.5 4.0 %collective-permute-start.13 = (bf16[2,128,1024]{2,1,0:T(8,128)(2,1)S(1)}, bf16[2,128,1024]{2,1,0:T(8,128)(2,1)S(1)}, u32[]{:S(2)}, u32[]{:S(2)}) collective-permute-start(bf16[2,128,1024]{2,1,0:T(8,128)(2,1)S(1)} %collective-permute-done.9.refs_3_), channel_id=1, source_target_pairs={{4,0},{5,1},{6,2},{7,3},{12,8},{13,9},{14,10},{15,11},{20,16},{21,... | collective-permute-start | bytes 1572872 | tf_op jit(solution)/shard_map/ppermute | solution.py:26
  105.6 1.3 collective-permute-start.10
  106.9 3.7 %collective-permute-done.15 = bf16[2,128,1024]{2,1,0:T(8,128)(2,1)S(1)} collective-permute-done((bf16[2,128,1024]{2,1,0:T(8,128)(2,1)S(1)}, bf16[2,128,1024]{2,1,0:T(8,128)(2,1)S(1)}, u32[]{:S(2)}, u32[]{:S(2)}) %collective-permute-start.15) | collective-permute-done | bytes 524320 | tf_op jit(solution)/shard_map/ppermute | solution.py:26
  110.6 2.2 collective-permute-start.11
  113.0 1.5 collective-permute-done.12
  114.5 8.3 %collective-permute-done.13 = bf16[2,128,1024]{2,1,0:T(8,128)(2,1)S(1)} collective-permute-done((bf16[2,128,1024]{2,1,0:T(8,128)(2,1)S(1)}, bf16[2,128,1024]{2,1,0:T(8,128)(2,1)S(1)}, u32[]{:S(2)}, u32[]{:S(2)}) %collective-permute-start.13) | collective-permute-done | bytes 524320 | tf_op jit(solution)/shard_map/ppermute | solution.py:26
  123.9 2.0 collective-permute-start.16
  126.4 1.0 fusion.18
  127.4 1.3 collective-permute-start.21
  128.7 1.3 collective-permute-start.22
  130.0 1.3 collective-permute-start.23
  131.3 6.0 %collective-permute-start.18 = (bf16[2,128,1024]{2,1,0:T(8,128)(2,1)S(1)}, bf16[2,128,1024]{2,1,0:T(8,128)(2,1)S(1)}, u32[]{:S(2)}, u32[]{:S(2)}) collective-permute-start(bf16[2,128,1024]{2,1,0:T(8,128)(2,1)S(1)} %get-tuple-element.48), channel_id=1, source_target_pairs={{2,0},{3,1},{4,2},{5,3},{6,4},{7,5},{10,8},{11,9},{12,10},{13,11},... | collective-permute-start | bytes 1572872 | tf_op jit(solution)/shard_map/ppermute | solution.py:26
  137.3 8.3 %collective-permute-done.21 = bf16[2,128,1024]{2,1,0:T(8,128)(2,1)S(1)} collective-permute-done((bf16[2,128,1024]{2,1,0:T(8,128)(2,1)S(1)}, bf16[2,128,1024]{2,1,0:T(8,128)(2,1)S(1)}, u32[]{:S(2)}, u32[]{:S(2)}) %collective-permute-start.21) | collective-permute-done | bytes 524320 | tf_op jit(solution)/shard_map/ppermute | solution.py:26
  145.6 1.3 collective-permute-start.19
  147.0 7.0 %collective-permute-done.22 = bf16[2,128,1024]{2,1,0:T(8,128)(2,1)S(1)} collective-permute-done((bf16[2,128,1024]{2,1,0:T(8,128)(2,1)S(1)}, bf16[2,128,1024]{2,1,0:T(8,128)(2,1)S(1)}, u32[]{:S(2)}, u32[]{:S(2)}) %collective-permute-start.22) | collective-permute-done | bytes 524320 | tf_op jit(solution)/shard_map/ppermute | solution.py:26
  153.9 5.4 %collective-permute-start.20 = (bf16[2,128,1024]{2,1,0:T(8,128)(2,1)S(1)}, bf16[2,128,1024]{2,1,0:T(8,128)(2,1)S(1)}, u32[]{:S(2)}, u32[]{:S(2)}) collective-permute-start(bf16[2,128,1024]{2,1,0:T(8,128)(2,1)S(1)} %get-tuple-element.49), channel_id=1, source_target_pairs={{6,0},{7,1},{14,8},{15,9},{22,16},{23,17},{30,24},{31,25}} | collective-permute-start | bytes 1572872 | tf_op jit(solution)/shard_map/ppermute | solution.py:26
  159.8 1.3 collective-permute-start.24
  161.1 7.0 %collective-permute-done.19 = bf16[2,128,1024]{2,1,0:T(8,128)(2,1)S(1)} collective-permute-done((bf16[2,128,1024]{2,1,0:T(8,128)(2,1)S(1)}, bf16[2,128,1024]{2,1,0:T(8,128)(2,1)S(1)}, u32[]{:S(2)}, u32[]{:S(2)}) %collective-permute-start.19) | collective-permute-done | bytes 524320 | tf_op jit(solution)/shard_map/ppermute | solution.py:26
  168.5 5.4 %collective-permute-done.24 = bf16[2,128,1024]{2,1,0:T(8,128)(2,1)S(1)} collective-permute-done((bf16[2,128,1024]{2,1,0:T(8,128)(2,1)S(1)}, bf16[2,128,1024]{2,1,0:T(8,128)(2,1)S(1)}, u32[]{:S(2)}, u32[]{:S(2)}) %collective-permute-start.24) | collective-permute-done | bytes 524320 | tf_op jit(solution)/shard_map/ppermute | solution.py:26
  173.9 0.6 fusion.22
  174.5 1.3 copy-done.24
  175.8 15.0 %shard_map.77 = (bf16[128,2048]{1,0:T(8,128)(2,1)}, f32[2,128,1024]{2,1,0:T(8,128)}, f32[2,128,1024]{2,1,0:T(8,128)}, f32[2,128,1024]{2,1,0:T(8,128)}, f32[2,128...) custom-call(f32[128,1152]{1,0:T(8,128)} %fusion.25.refs_0_, ...), custom_call_target="tpu_custom_call" | custom-call | flops 3019898880 | bytes 16318464 | tf_op jit(solution)/shard_map/pallas_call | solution.py:142
  190.8 2.9 %collective-permute-start.25 = (bf16[4,2,128,1024]{3,2,1,0:T(8,128)(2,1)}, bf16[4,2,128,1024]{3,2,1,0:T(8,128)(2,1)S(1)}, u32[]{:S(2)}, u32[]{:S(2)}) collective-permute-start(bf16[4,2,128,1024]{3,2,1,0:T(8,128)(2,1)} %get-tuple-element.40), channel_id=1, source_target_pairs={{0,1},{1,0},{2,3},{3,2},{4,5},{5,4},{6,7},{7,6},{8,9},{9,8},{10,11... | collective-permute-start | bytes 6291464 | tf_op jit(solution)/shard_map/ppermute | solution.py:26
  193.8 4.0 %collective-permute-done.25 = bf16[4,2,128,1024]{3,2,1,0:T(8,128)(2,1)S(1)} collective-permute-done((bf16[4,2,128,1024]{3,2,1,0:T(8,128)(2,1)}, bf16[4,2,128,1024]{3,2,1,0:T(8,128)(2,1)S(1)}, u32[]{:S(2)}, u32[]{:S(2)}) %collective-permute-start.25) | collective-permute-done | bytes 2097184 | tf_op jit(solution)/shard_map/ppermute | solution.py:26
  198.3 1.0 fusion.6
  199.3 1.3 collective-permute-start.29
  200.6 1.3 collective-permute-start.30
  201.9 1.3 collective-permute-start.31
  203.2 4.0 %collective-permute-start.26 = (bf16[2,128,1024]{2,1,0:T(8,128)(2,1)S(1)}, bf16[2,128,1024]{2,1,0:T(8,128)(2,1)S(1)}, u32[]{:S(2)}, u32[]{:S(2)}) collective-permute-start(bf16[2,128,1024]{2,1,0:T(8,128)(2,1)S(1)} %get-tuple-element.45), channel_id=1, source_target_pairs={{2,0},{3,1},{4,2},{5,3},{6,4},{7,5},{10,8},{11,9},{12,10},{13,11},... | collective-permute-start | bytes 1572872 | tf_op jit(solution)/shard_map/ppermute | solution.py:26
  207.2 4.0 %collective-permute-start.27 = (bf16[2,128,1024]{2,1,0:T(8,128)(2,1)S(1)}, bf16[2,128,1024]{2,1,0:T(8,128)(2,1)S(1)}, u32[]{:S(2)}, u32[]{:S(2)}) collective-permute-start(bf16[2,128,1024]{2,1,0:T(8,128)(2,1)S(1)} %get-tuple-element.47), channel_id=1, source_target_pairs={{4,0},{5,1},{6,2},{7,3},{12,8},{13,9},{14,10},{15,11},{20,16},{21,... | collective-permute-start | bytes 1572872 | tf_op jit(solution)/shard_map/ppermute | solution.py:26
  211.3 4.0 %collective-permute-done.29 = bf16[2,128,1024]{2,1,0:T(8,128)(2,1)S(1)} collective-permute-done((bf16[2,128,1024]{2,1,0:T(8,128)(2,1)S(1)}, bf16[2,128,1024]{2,1,0:T(8,128)(2,1)S(1)}, u32[]{:S(2)}, u32[]{:S(2)}) %collective-permute-start.29) | collective-permute-done | bytes 524320 | tf_op jit(solution)/shard_map/ppermute | solution.py:26
  215.3 1.3 collective-permute-start.28
  216.6 10.6 %collective-permute-done.30 = bf16[2,128,1024]{2,1,0:T(8,128)(2,1)S(1)} collective-permute-done((bf16[2,128,1024]{2,1,0:T(8,128)(2,1)S(1)}, bf16[2,128,1024]{2,1,0:T(8,128)(2,1)S(1)}, u32[]{:S(2)}, u32[]{:S(2)}) %collective-permute-start.30) | collective-permute-done | bytes 524320 | tf_op jit(solution)/shard_map/ppermute | solution.py:26
  227.7 1.4 collective-permute-start.32
  229.2 1.0 maximum_bitcast_fusion
  230.2 2.2 collective-permute-done.27
  232.4 10.3 %collective-permute-done.32 = bf16[2,128,1024]{2,1,0:T(8,128)(2,1)S(1)} collective-permute-done((bf16[2,128,1024]{2,1,0:T(8,128)(2,1)S(1)}, bf16[2,128,1024]{2,1,0:T(8,128)(2,1)S(1)}, u32[]{:S(2)}, u32[]{:S(2)}) %collective-permute-start.32) | collective-permute-done | bytes 524320 | tf_op jit(solution)/shard_map/ppermute | solution.py:26
  242.7 0.6 fusion.11
  243.3 0.8 maximum_bitcast_fusion.2
  244.2 0.8 maximum_bitcast_fusion.1
  (85 shorter events, 4.4 us)
Async XLA Ops:
  0.6 56.6 %copy-start = (s32[1,32]{1,0:T(1,128)S(1)}, s32[1,32]{1,0:T(1,128)}, u32[]{:S(2)}) copy-start(s32[1,32]{1,0:T(1,128)} %param.9) | copy-start | bytes 388
  2.0 42.1 %copy-start.19 = (bf16[2,128,1024]{2,1,0:T(8,128)(2,1)}, bf16[2,128,1024]{2,1,0:T(8,128)(2,1)S(1)}, u32[]{:S(2)}) copy-start(bf16[2,128,1024]{2,1,0:T(8,128)(2,1)S(1)} %get-tuple-element.60.refs_4_) | copy-start | bytes 1572868
  2.0 13.8 %collective-permute-start.1 = (bf16[2,128,1024]{2,1,0:T(8,128)(2,1)S(1)}, bf16[2,128,1024]{2,1,0:T(8,128)(2,1)S(1)}, u32[]{:S(2)}, u32[]{:S(2)}) collective-permute-start(bf16[2,128,1024]{2,1,0:T(8,128)(2,1)S(1)} %get-tuple-element.60.refs_4_), channel_id=1, source_target_pairs={{0,8},{1,9},{2,10},{3,11},{4,12},{5,13},{6,14},{7,15},{8,16},{9,17... | collective-permute-start | bytes 1572872 | tf_op jit(solution)/shard_map/ppermute | solution.py:26
  5.3 19.2 %collective-permute-start.4 = (bf16[2,128,1024]{2,1,0:T(8,128)(2,1)S(1)}, bf16[2,128,1024]{2,1,0:T(8,128)(2,1)S(1)}, u32[]{:S(2)}, u32[]{:S(2)}) collective-permute-start(bf16[2,128,1024]{2,1,0:T(8,128)(2,1)S(1)} %get-tuple-element.60.refs_4_), channel_id=1, source_target_pairs={{0,4},{1,5},{2,6},{3,7},{8,12},{9,13},{10,14},{11,15},{16,20},{17,... | collective-permute-start | bytes 1572872 | tf_op jit(solution)/shard_map/ppermute | solution.py:26
  15.8 28.3 %copy-start.20 = (bf16[2,128,1024]{2,1,0:T(8,128)(2,1)}, bf16[2,128,1024]{2,1,0:T(8,128)(2,1)S(1)}, u32[]{:S(2)}) copy-start(bf16[2,128,1024]{2,1,0:T(8,128)(2,1)S(1)} %collective-permute-done.1.refs_3_) | copy-start | bytes 1572868
  15.8 23.0 %collective-permute-start.5 = (bf16[2,128,1024]{2,1,0:T(8,128)(2,1)S(1)}, bf16[2,128,1024]{2,1,0:T(8,128)(2,1)}, u32[]{:S(2)}, u32[]{:S(2)}) collective-permute-start(bf16[2,128,1024]{2,1,0:T(8,128)(2,1)S(1)} %collective-permute-done.1.refs_3_), channel_id=1, source_target_pairs={{4,0},{5,1},{6,2},{7,3},{12,8},{13,9},{14,10},{15,11},{20,16},{21,... | collective-permute-start | bytes 1572872 | tf_op jit(solution)/shard_map/ppermute | solution.py:26
  18.7 20.2 %collective-permute-start.6 = (bf16[2,128,1024]{2,1,0:T(8,128)(2,1)S(1)}, bf16[2,128,1024]{2,1,0:T(8,128)(2,1)}, u32[]{:S(2)}, u32[]{:S(2)}) collective-permute-start(bf16[2,128,1024]{2,1,0:T(8,128)(2,1)S(1)} %get-tuple-element.60.refs_4_), channel_id=1, source_target_pairs={{0,6},{1,7},{8,14},{9,15},{16,22},{17,23},{24,30},{25,31}} | collective-permute-start | bytes 1572872 | tf_op jit(solution)/shard_map/ppermute | solution.py:26
  20.0 18.9 %collective-permute-start.7 = (bf16[2,128,1024]{2,1,0:T(8,128)(2,1)S(1)}, bf16[2,128,1024]{2,1,0:T(8,128)(2,1)}, u32[]{:S(2)}, u32[]{:S(2)}) collective-permute-start(bf16[2,128,1024]{2,1,0:T(8,128)(2,1)S(1)} %collective-permute-done.1.refs_3_), channel_id=1, source_target_pairs={{2,0},{3,1},{4,2},{5,3},{6,4},{7,5},{10,8},{11,9},{12,10},{13,11},... | collective-permute-start | bytes 1572872 | tf_op jit(solution)/shard_map/ppermute | solution.py:26
  23.1 20.9 %collective-permute-start.2 = (bf16[2,128,1024]{2,1,0:T(8,128)(2,1)S(1)}, bf16[2,128,1024]{2,1,0:T(8,128)(2,1)S(1)}, u32[]{:S(2)}, u32[]{:S(2)}) collective-permute-start(bf16[2,128,1024]{2,1,0:T(8,128)(2,1)S(1)} %get-tuple-element.60.refs_4_), channel_id=1, source_target_pairs={{0,2},{1,3},{2,4},{3,5},{4,6},{5,7},{8,10},{9,11},{10,12},{11,13},... | collective-permute-start | bytes 1572872 | tf_op jit(solution)/shard_map/ppermute | solution.py:26
  24.5 19.6 %collective-permute-start.3 = (bf16[2,128,1024]{2,1,0:T(8,128)(2,1)S(1)}, bf16[2,128,1024]{2,1,0:T(8,128)(2,1)S(1)}, u32[]{:S(2)}, u32[]{:S(2)}) collective-permute-start(bf16[2,128,1024]{2,1,0:T(8,128)(2,1)S(1)} %collective-permute-done.1.refs_3_), channel_id=1, source_target_pairs={{6,0},{7,1},{14,8},{15,9},{22,16},{23,17},{30,24},{31,25}} | collective-permute-start | bytes 1572872 | tf_op jit(solution)/shard_map/ppermute | solution.py:26
  38.9 7.0 %copy-start.6 = (bf16[2,128,1024]{2,1,0:T(8,128)(2,1)}, bf16[2,128,1024]{2,1,0:T(8,128)(2,1)S(1)}, u32[]{:S(2)}) copy-start(bf16[2,128,1024]{2,1,0:T(8,128)(2,1)S(1)} %broadcast_select_fusion.3.refs_6_) | copy-start | bytes 1572868
  40.2 5.6 %copy-start.7 = (bf16[2,128,1024]{2,1,0:T(8,128)(2,1)}, bf16[2,128,1024]{2,1,0:T(8,128)(2,1)S(1)}, u32[]{:S(2)}) copy-start(bf16[2,128,1024]{2,1,0:T(8,128)(2,1)S(1)} %broadcast_select_fusion.1.refs_7_) | copy-start | bytes 1572868
  44.2 1.7 copy-start.8
  45.9 17.2 %collective-permute-start.8 = (bf16[4,2,128,1024]{3,2,1,0:T(8,128)(2,1)S(1)}, bf16[4,2,128,1024]{3,2,1,0:T(8,128)(2,1)}, u32[]{:S(2)}, u32[]{:S(2)}) collective-permute-start(bf16[4,2,128,1024]{3,2,1,0:T(8,128)(2,1)S(1)} %maximum_select_fusion), channel_id=1, source_target_pairs={{0,1},{1,0},{2,3},{3,2},{4,5},{5,4},{6,7},{7,6},{8,9},{9,8},{10,11... | collective-permute-start | bytes 6291464 | tf_op jit(solution)/shard_map/ppermute | solution.py:26
  48.4 12.5 %collective-permute-start = (bf16[1,128,4096]{2,1,0:T(8,128)(2,1)}, bf16[1,128,4096]{2,1,0:T(8,128)(2,1)}, u32[]{:S(2)}, u32[]{:S(2)}) collective-permute-start(bf16[1,128,4096]{2,1,0:T(8,128)(2,1)} %param.8), channel_id=1, source_target_pairs={{0,0},{1,1},{2,2},{3,3},{4,4},{5,5},{6,6},{7,7},{8,8},{9,9},{10,10... | collective-permute-start | bytes 3145736 | tf_op jit(solution)/shard_map/ppermute | solution.py:22
  57.5 65.6 %copy-start.2 = (bf16[2,128,1024]{2,1,0:T(8,128)(2,1)}, bf16[2,128,1024]{2,1,0:T(8,128)(2,1)S(1)}, u32[]{:S(2)}) copy-start(bf16[2,128,1024]{2,1,0:T(8,128)(2,1)S(1)} %pad_maximum_fusion.1.refs_4_) | copy-start | bytes 1572868
  78.1 15.4 %collective-permute-start.9 = (bf16[2,128,1024]{2,1,0:T(8,128)(2,1)S(1)}, bf16[2,128,1024]{2,1,0:T(8,128)(2,1)S(1)}, u32[]{:S(2)}, u32[]{:S(2)}) collective-permute-start(bf16[2,128,1024]{2,1,0:T(8,128)(2,1)S(1)} %pad_maximum_fusion.1.refs_4_), channel_id=1, source_target_pairs={{0,8},{1,9},{2,10},{3,11},{4,12},{5,13},{6,14},{7,15},{8,16},{9,17... | collective-permute-start | bytes 1572872 | tf_op jit(solution)/shard_map/ppermute | solution.py:26
  82.2 43.7 %collective-permute-start.17 = (bf16[4,2,128,1024]{3,2,1,0:T(8,128)(2,1)}, bf16[4,2,128,1024]{3,2,1,0:T(8,128)(2,1)S(1)}, u32[]{:S(2)}, u32[]{:S(2)}) collective-permute-start(bf16[4,2,128,1024]{3,2,1,0:T(8,128)(2,1)} %get-tuple-element.27), channel_id=1, source_target_pairs={{0,1},{1,0},{2,3},{3,2},{4,5},{5,4},{6,7},{7,6},{8,9},{9,8},{10,11... | collective-permute-start | bytes 6291464 | tf_op jit(solution)/shard_map/ppermute | solution.py:26
  82.6 23.0 %collective-permute-start.14 = (bf16[2,128,1024]{2,1,0:T(8,128)(2,1)S(1)}, bf16[2,128,1024]{2,1,0:T(8,128)(2,1)S(1)}, u32[]{:S(2)}, u32[]{:S(2)}) collective-permute-start(bf16[2,128,1024]{2,1,0:T(8,128)(2,1)S(1)} %pad_maximum_fusion.1.refs_4_), channel_id=1, source_target_pairs={{0,6},{1,7},{8,14},{9,15},{16,22},{17,23},{24,30},{25,31}} | collective-permute-start | bytes 1572872 | tf_op jit(solution)/shard_map/ppermute | solution.py:26
  93.5 29.6 %copy-start.21 = (bf16[2,128,1024]{2,1,0:T(8,128)(2,1)}, bf16[2,128,1024]{2,1,0:T(8,128)(2,1)S(1)}, u32[]{:S(2)}) copy-start(bf16[2,128,1024]{2,1,0:T(8,128)(2,1)S(1)} %collective-permute-done.9.refs_3_) | copy-start | bytes 1572868
  93.5 17.1 %collective-permute-start.15 = (bf16[2,128,1024]{2,1,0:T(8,128)(2,1)S(1)}, bf16[2,128,1024]{2,1,0:T(8,128)(2,1)S(1)}, u32[]{:S(2)}, u32[]{:S(2)}) collective-permute-start(bf16[2,128,1024]{2,1,0:T(8,128)(2,1)S(1)} %collective-permute-done.9.refs_3_), channel_id=1, source_target_pairs={{2,0},{3,1},{4,2},{5,3},{6,4},{7,5},{10,8},{11,9},{12,10},{13,11},... | collective-permute-start | bytes 1572872 | tf_op jit(solution)/shard_map/ppermute | solution.py:26
  100.2 14.2 %collective-permute-start.12 = (bf16[2,128,1024]{2,1,0:T(8,128)(2,1)S(1)}, bf16[2,128,1024]{2,1,0:T(8,128)(2,1)S(1)}, u32[]{:S(2)}, u32[]{:S(2)}) collective-permute-start(bf16[2,128,1024]{2,1,0:T(8,128)(2,1)S(1)} %pad_maximum_fusion.1.refs_4_), channel_id=1, source_target_pairs={{0,4},{1,5},{2,6},{3,7},{8,12},{9,13},{10,14},{11,15},{16,20},{17,... | collective-permute-start | bytes 1572872 | tf_op jit(solution)/shard_map/ppermute | solution.py:26
  101.5 21.3 %collective-permute-start.13 = (bf16[2,128,1024]{2,1,0:T(8,128)(2,1)S(1)}, bf16[2,128,1024]{2,1,0:T(8,128)(2,1)S(1)}, u32[]{:S(2)}, u32[]{:S(2)}) collective-permute-start(bf16[2,128,1024]{2,1,0:T(8,128)(2,1)S(1)} %collective-permute-done.9.refs_3_), channel_id=1, source_target_pairs={{4,0},{5,1},{6,2},{7,3},{12,8},{13,9},{14,10},{15,11},{20,16},{21,... | collective-permute-start | bytes 1572872 | tf_op jit(solution)/shard_map/ppermute | solution.py:26
  105.6 17.4 %collective-permute-start.10 = (bf16[2,128,1024]{2,1,0:T(8,128)(2,1)S(1)}, bf16[2,128,1024]{2,1,0:T(8,128)(2,1)S(1)}, u32[]{:S(2)}, u32[]{:S(2)}) collective-permute-start(bf16[2,128,1024]{2,1,0:T(8,128)(2,1)S(1)} %pad_maximum_fusion.1.refs_4_), channel_id=1, source_target_pairs={{0,2},{1,3},{2,4},{3,5},{4,6},{5,7},{8,10},{9,11},{10,12},{11,13},... | collective-permute-start | bytes 1572872 | tf_op jit(solution)/shard_map/ppermute | solution.py:26
  110.6 12.3 %collective-permute-start.11 = (bf16[2,128,1024]{2,1,0:T(8,128)(2,1)S(1)}, bf16[2,128,1024]{2,1,0:T(8,128)(2,1)S(1)}, u32[]{:S(2)}, u32[]{:S(2)}) collective-permute-start(bf16[2,128,1024]{2,1,0:T(8,128)(2,1)S(1)} %collective-permute-done.9.refs_3_), channel_id=1, source_target_pairs={{6,0},{7,1},{14,8},{15,9},{22,16},{23,17},{30,24},{31,25}} | collective-permute-start | bytes 1572872 | tf_op jit(solution)/shard_map/ppermute | solution.py:26
  113.0 10.7 %copy-start.3 = (bf16[2,128,1024]{2,1,0:T(8,128)(2,1)}, bf16[2,128,1024]{2,1,0:T(8,128)(2,1)S(1)}, u32[]{:S(2)}) copy-start(bf16[2,128,1024]{2,1,0:T(8,128)(2,1)S(1)} %broadcast_select_fusion.refs_7_) | copy-start | bytes 1572868
  122.8 0.8 copy-start.4
  123.0 0.8 copy-start.5
  123.8 2.5 %copy-start.12 = (f32[2,128,1024]{2,1,0:T(8,128)S(1)}, f32[2,128,1024]{2,1,0:T(8,128)}, u32[]{:S(2)}) copy-start(f32[2,128,1024]{2,1,0:T(8,128)} %get-tuple-element.28) | copy-start | bytes 3145732
  123.8 2.5 %copy-start.13 = (f32[2,128,1024]{2,1,0:T(8,128)S(1)}, f32[2,128,1024]{2,1,0:T(8,128)}, u32[]{:S(2)}) copy-start(f32[2,128,1024]{2,1,0:T(8,128)} %get-tuple-element.29) | copy-start | bytes 3145732
  123.9 2.5 %copy-start.14 = (f32[2,128,1024]{2,1,0:T(8,128)S(1)}, f32[2,128,1024]{2,1,0:T(8,128)}, u32[]{:S(2)}) copy-start(f32[2,128,1024]{2,1,0:T(8,128)} %get-tuple-element.30) | copy-start | bytes 3145732
  123.9 50.6 %collective-permute-start.16 = (bf16[4,2,128,1024]{3,2,1,0:T(8,128)(2,1)S(1)}, bf16[4,2,128,1024]{3,2,1,0:T(8,128)(2,1)S(1)}, u32[]{:S(2)}, u32[]{:S(2)}) collective-permute-start(bf16[4,2,128,1024]{3,2,1,0:T(8,128)(2,1)S(1)} %maximum_select_fusion.1), channel_id=1, source_target_pairs={{0,1},{1,0},{2,3},{3,2},{4,5},{5,4},{6,7},{7,6},{8,9},{9,8},{10,11... | collective-permute-start | bytes 6291464 | tf_op jit(solution)/shard_map/ppermute | solution.py:26
  126.4 33.0 %copy-start.10 = (f32[2,128,1024]{2,1,0:T(8,128)S(1)}, f32[2,128,1024]{2,1,0:T(8,128)}, u32[]{:S(2)}) copy-start(f32[2,128,1024]{2,1,0:T(8,128)} %get-tuple-element.31) | copy-start | bytes 3145732
  127.4 18.2 %collective-permute-start.21 = (bf16[2,128,1024]{2,1,0:T(8,128)(2,1)S(1)}, bf16[2,128,1024]{2,1,0:T(8,128)(2,1)S(1)}, u32[]{:S(2)}, u32[]{:S(2)}) collective-permute-start(bf16[2,128,1024]{2,1,0:T(8,128)(2,1)S(1)} %get-tuple-element.48), channel_id=1, source_target_pairs={{0,6},{1,7},{8,14},{9,15},{16,22},{17,23},{24,30},{25,31}} | collective-permute-start | bytes 1572872 | tf_op jit(solution)/shard_map/ppermute | solution.py:26
  128.7 25.2 %collective-permute-start.22 = (bf16[2,128,1024]{2,1,0:T(8,128)(2,1)S(1)}, bf16[2,128,1024]{2,1,0:T(8,128)(2,1)S(1)}, u32[]{:S(2)}, u32[]{:S(2)}) collective-permute-start(bf16[2,128,1024]{2,1,0:T(8,128)(2,1)S(1)} %get-tuple-element.50), channel_id=1, source_target_pairs={{0,4},{1,5},{2,6},{3,7},{8,12},{9,13},{10,14},{11,15},{16,20},{17,... | collective-permute-start | bytes 1572872 | tf_op jit(solution)/shard_map/ppermute | solution.py:26
  130.0 29.3 %collective-permute-start.23 = (bf16[2,128,1024]{2,1,0:T(8,128)(2,1)S(1)}, bf16[2,128,1024]{2,1,0:T(8,128)(2,1)S(1)}, u32[]{:S(2)}, u32[]{:S(2)}) collective-permute-start(bf16[2,128,1024]{2,1,0:T(8,128)(2,1)S(1)} %get-tuple-element.49), channel_id=1, source_target_pairs={{0,2},{1,3},{2,4},{3,5},{4,6},{5,7},{8,10},{9,11},{10,12},{11,13},... | collective-permute-start | bytes 1572872 | tf_op jit(solution)/shard_map/ppermute | solution.py:26
  131.3 29.8 %collective-permute-start.18 = (bf16[2,128,1024]{2,1,0:T(8,128)(2,1)S(1)}, bf16[2,128,1024]{2,1,0:T(8,128)(2,1)S(1)}, u32[]{:S(2)}, u32[]{:S(2)}) collective-permute-start(bf16[2,128,1024]{2,1,0:T(8,128)(2,1)S(1)} %get-tuple-element.48), channel_id=1, source_target_pairs={{2,0},{3,1},{4,2},{5,3},{6,4},{7,5},{10,8},{11,9},{12,10},{13,11},... | collective-permute-start | bytes 1572872 | tf_op jit(solution)/shard_map/ppermute | solution.py:26
  145.6 22.5 %collective-permute-start.19 = (bf16[2,128,1024]{2,1,0:T(8,128)(2,1)S(1)}, bf16[2,128,1024]{2,1,0:T(8,128)(2,1)S(1)}, u32[]{:S(2)}, u32[]{:S(2)}) collective-permute-start(bf16[2,128,1024]{2,1,0:T(8,128)(2,1)S(1)} %get-tuple-element.50), channel_id=1, source_target_pairs={{4,0},{5,1},{6,2},{7,3},{12,8},{13,9},{14,10},{15,11},{20,16},{21,... | collective-permute-start | bytes 1572872 | tf_op jit(solution)/shard_map/ppermute | solution.py:26
  153.9 14.6 %collective-permute-start.20 = (bf16[2,128,1024]{2,1,0:T(8,128)(2,1)S(1)}, bf16[2,128,1024]{2,1,0:T(8,128)(2,1)S(1)}, u32[]{:S(2)}, u32[]{:S(2)}) collective-permute-start(bf16[2,128,1024]{2,1,0:T(8,128)(2,1)S(1)} %get-tuple-element.49), channel_id=1, source_target_pairs={{6,0},{7,1},{14,8},{15,9},{22,16},{23,17},{30,24},{31,25}} | collective-permute-start | bytes 1572872 | tf_op jit(solution)/shard_map/ppermute | solution.py:26
  159.4 14.6 %copy-start.9 = (f32[2,128,1024]{2,1,0:T(8,128)S(1)}, f32[2,128,1024]{2,1,0:T(8,128)}, u32[]{:S(2)}) copy-start(f32[2,128,1024]{2,1,0:T(8,128)} %get-tuple-element.26) | copy-start | bytes 3145732
  159.8 14.1 %collective-permute-start.24 = (bf16[2,128,1024]{2,1,0:T(8,128)(2,1)S(1)}, bf16[2,128,1024]{2,1,0:T(8,128)(2,1)S(1)}, u32[]{:S(2)}, u32[]{:S(2)}) collective-permute-start(bf16[2,128,1024]{2,1,0:T(8,128)(2,1)S(1)} %fusion.15), channel_id=1, source_target_pairs={{8,0},{9,1},{10,2},{11,3},{12,4},{13,5},{14,6},{15,7},{16,8},{17,9... | collective-permute-start | bytes 1572872 | tf_op jit(solution)/shard_map/ppermute | solution.py:26
  174.5 1.3 copy-start.24
  190.8 7.4 %copy-start.16 = (f32[2,128,1024]{2,1,0:T(8,128)S(1)}, f32[2,128,1024]{2,1,0:T(8,128)}, u32[]{:S(2)}) copy-start(f32[2,128,1024]{2,1,0:T(8,128)} %get-tuple-element.41) | copy-start | bytes 3145732
  190.8 7.4 %copy-start.17 = (f32[2,128,1024]{2,1,0:T(8,128)S(1)}, f32[2,128,1024]{2,1,0:T(8,128)}, u32[]{:S(2)}) copy-start(f32[2,128,1024]{2,1,0:T(8,128)} %get-tuple-element.42) | copy-start | bytes 3145732
  190.8 7.4 %copy-start.18 = (f32[2,128,1024]{2,1,0:T(8,128)S(1)}, f32[2,128,1024]{2,1,0:T(8,128)}, u32[]{:S(2)}) copy-start(f32[2,128,1024]{2,1,0:T(8,128)} %get-tuple-element.43) | copy-start | bytes 3145732
  190.8 6.9 %collective-permute-start.25 = (bf16[4,2,128,1024]{3,2,1,0:T(8,128)(2,1)}, bf16[4,2,128,1024]{3,2,1,0:T(8,128)(2,1)S(1)}, u32[]{:S(2)}, u32[]{:S(2)}) collective-permute-start(bf16[4,2,128,1024]{3,2,1,0:T(8,128)(2,1)} %get-tuple-element.40), channel_id=1, source_target_pairs={{0,1},{1,0},{2,3},{3,2},{4,5},{5,4},{6,7},{7,6},{8,9},{9,8},{10,11... | collective-permute-start | bytes 6291464 | tf_op jit(solution)/shard_map/ppermute | solution.py:26
  198.3 28.9 %copy-start.15 = (f32[2,128,1024]{2,1,0:T(8,128)S(1)}, f32[2,128,1024]{2,1,0:T(8,128)}, u32[]{:S(2)}) copy-start(f32[2,128,1024]{2,1,0:T(8,128)} %get-tuple-element.44) | copy-start | bytes 3145732
  199.3 16.0 %collective-permute-start.29 = (bf16[2,128,1024]{2,1,0:T(8,128)(2,1)S(1)}, bf16[2,128,1024]{2,1,0:T(8,128)(2,1)S(1)}, u32[]{:S(2)}, u32[]{:S(2)}) collective-permute-start(bf16[2,128,1024]{2,1,0:T(8,128)(2,1)S(1)} %get-tuple-element.45), channel_id=1, source_target_pairs={{0,6},{1,7},{8,14},{9,15},{16,22},{17,23},{24,30},{25,31}} | collective-permute-start | bytes 1572872 | tf_op jit(solution)/shard_map/ppermute | solution.py:26
  200.6 26.6 %collective-permute-start.30 = (bf16[2,128,1024]{2,1,0:T(8,128)(2,1)S(1)}, bf16[2,128,1024]{2,1,0:T(8,128)(2,1)S(1)}, u32[]{:S(2)}, u32[]{:S(2)}) collective-permute-start(bf16[2,128,1024]{2,1,0:T(8,128)(2,1)S(1)} %get-tuple-element.47), channel_id=1, source_target_pairs={{0,4},{1,5},{2,6},{3,7},{8,12},{9,13},{10,14},{11,15},{16,20},{17,... | collective-permute-start | bytes 1572872 | tf_op jit(solution)/shard_map/ppermute | solution.py:26
  201.9 25.3 %collective-permute-start.31 = (bf16[2,128,1024]{2,1,0:T(8,128)(2,1)S(1)}, bf16[2,128,1024]{2,1,0:T(8,128)(2,1)S(1)}, u32[]{:S(2)}, u32[]{:S(2)}) collective-permute-start(bf16[2,128,1024]{2,1,0:T(8,128)(2,1)S(1)} %get-tuple-element.46), channel_id=1, source_target_pairs={{0,2},{1,3},{2,4},{3,5},{4,6},{5,7},{8,10},{9,11},{10,12},{11,13},... | collective-permute-start | bytes 1572872 | tf_op jit(solution)/shard_map/ppermute | solution.py:26
  203.2 27.0 %collective-permute-start.26 = (bf16[2,128,1024]{2,1,0:T(8,128)(2,1)S(1)}, bf16[2,128,1024]{2,1,0:T(8,128)(2,1)S(1)}, u32[]{:S(2)}, u32[]{:S(2)}) collective-permute-start(bf16[2,128,1024]{2,1,0:T(8,128)(2,1)S(1)} %get-tuple-element.45), channel_id=1, source_target_pairs={{2,0},{3,1},{4,2},{5,3},{6,4},{7,5},{10,8},{11,9},{12,10},{13,11},... | collective-permute-start | bytes 1572872 | tf_op jit(solution)/shard_map/ppermute | solution.py:26
  207.2 25.2 %collective-permute-start.27 = (bf16[2,128,1024]{2,1,0:T(8,128)(2,1)S(1)}, bf16[2,128,1024]{2,1,0:T(8,128)(2,1)S(1)}, u32[]{:S(2)}, u32[]{:S(2)}) collective-permute-start(bf16[2,128,1024]{2,1,0:T(8,128)(2,1)S(1)} %get-tuple-element.47), channel_id=1, source_target_pairs={{4,0},{5,1},{6,2},{7,3},{12,8},{13,9},{14,10},{15,11},{20,16},{21,... | collective-permute-start | bytes 1572872 | tf_op jit(solution)/shard_map/ppermute | solution.py:26
  215.3 17.2 %collective-permute-start.28 = (bf16[2,128,1024]{2,1,0:T(8,128)(2,1)S(1)}, bf16[2,128,1024]{2,1,0:T(8,128)(2,1)S(1)}, u32[]{:S(2)}, u32[]{:S(2)}) collective-permute-start(bf16[2,128,1024]{2,1,0:T(8,128)(2,1)S(1)} %get-tuple-element.46), channel_id=1, source_target_pairs={{6,0},{7,1},{14,8},{15,9},{22,16},{23,17},{30,24},{31,25}} | collective-permute-start | bytes 1572872 | tf_op jit(solution)/shard_map/ppermute | solution.py:26
  227.2 2.0 copy-start.22
  227.2 2.0 copy-start.23
  227.7 15.1 %copy-start.11 = (f32[2,128,1024]{2,1,0:T(8,128)S(1)}, f32[2,128,1024]{2,1,0:T(8,128)}, u32[]{:S(2)}) copy-start(f32[2,128,1024]{2,1,0:T(8,128)} %get-tuple-element.39) | copy-start | bytes 3145732
  227.7 15.0 %collective-permute-start.32 = (bf16[2,128,1024]{2,1,0:T(8,128)(2,1)S(1)}, bf16[2,128,1024]{2,1,0:T(8,128)(2,1)S(1)}, u32[]{:S(2)}, u32[]{:S(2)}) collective-permute-start(bf16[2,128,1024]{2,1,0:T(8,128)(2,1)S(1)} %fusion.3), channel_id=1, source_target_pairs={{8,0},{9,1},{10,2},{11,3},{12,4},{13,5},{14,6},{15,7},{16,8},{17,9... | collective-permute-start | bytes 1572872 | tf_op jit(solution)/shard_map/ppermute | solution.py:26
  242.7 2.3 copy-start.1

commit v2 on v1

--- a/solution.py
+++ b/solution.py
@@ -9,7 +9,7 @@
 HEAD_DIM = 128
 WINDOW = 1024
 MBLK = 128
-CHUNKS = 2
+CHUNKS = 1
 
 
 SCORE_SCALE = 168.0 ** (-0.5)
@@ -91,31 +91,29 @@
     k = jnp.concatenate([b[0] for b in blocks], axis=0)
     v = jnp.concatenate([b[1] for b in blocks], axis=0)
     visible = mask_ref[...] > 0.0
-    visible = jnp.concatenate([visible, visible], axis=0)
+    visible = jnp.concatenate([visible, visible], axis=1)
     q = q_ref[...]
     do = do_ref[...]
     qs = jnp.concatenate([q[:, :HEAD_DIM], q[:, HEAD_DIM:]], axis=0)
     dos = jnp.concatenate([do[:, :HEAD_DIM], do[:, HEAD_DIM:]], axis=0)
     contract_last = (((1,), (1,)), ((), ()))
     contract_first = (((0,), (0,)), ((), ()))
-    scores = lax.dot_general(qs, k, contract_last, preferred_element_type=jnp.float32) * SCORE_SCALE
+    scores = lax.dot_general(k, qs, contract_last, preferred_element_type=jnp.float32) * SCORE_SCALE
     scores = jnp.where(visible, scores, MASKED_SCORE)
-    largest = jnp.max(scores, axis=1, keepdims=True)
+    largest = jnp.max(scores, axis=0, keepdims=True)
     unscaled = jnp.where(visible, jnp.exp(scores - largest), 0.0)
-    attn = unscaled * (1.0 / jnp.sum(unscaled, axis=1, keepdims=True))
-    dattn = lax.dot_general(dos, v, contract_last, preferred_element_type=jnp.float32)
-    row_delta = jnp.sum(attn * dattn, axis=1, keepdims=True)
+    attn = unscaled * (1.0 / jnp.sum(unscaled, axis=0, keepdims=True))
+    dattn = lax.dot_general(v, dos, contract_last, preferred_element_type=jnp.float32)
+    row_delta = jnp.sum(attn * dattn, axis=0, keepdims=True)
     dscores = (attn * (dattn - row_delta)).astype(jnp.bfloat16)
-    grad_q = jnp.dot(dscores, k, preferred_element_type=jnp.float32) * SCORE_SCALE
+    grad_q = (
+        lax.dot_general(dscores, k, contract_first, preferred_element_type=jnp.float32)
+        * SCORE_SCALE
+    )
     dq_ref[:, :HEAD_DIM] = grad_q[:tokens].astype(dq_ref.dtype)
     dq_ref[:, HEAD_DIM:] = grad_q[tokens:].astype(dq_ref.dtype)
-    grad_k = (
-        lax.dot_general(dscores, qs, contract_first, preferred_element_type=jnp.float32)
-        * SCORE_SCALE
-    )
-    grad_v = lax.dot_general(
-        attn.astype(jnp.bfloat16), dos, contract_first, preferred_element_type=jnp.float32
-    )
+    grad_k = jnp.dot(dscores, qs, preferred_element_type=jnp.float32) * SCORE_SCALE
+    grad_v = jnp.dot(attn.astype(jnp.bfloat16), dos, preferred_element_type=jnp.float32)
     outs = [dprev_ref]
     for kk in range(chips - 1, -1, -1):
         outs.append(dsib_ref.at[kk])
@@ -129,7 +127,7 @@
 def attention_grads(mask, queries, grad_out, prev, direct, sib):
     tokens = queries.shape[0]
     chips = len(direct)
-    key_count = mask.shape[1]
+    key_count = mask.shape[0]
     width = prev.shape[2]
     heads = width // HEAD_DIM
     pair = 2 * HEAD_DIM
@@ -142,7 +140,7 @@
     return pl.pallas_call(
         lambda *refs: attention_kernel(chips, *refs),
         grid=(heads,),
-        in_specs=[pl.BlockSpec((tokens, key_count), lambda g: (0, 0)), pair_block, pair_block]
+        in_specs=[pl.BlockSpec((key_count, tokens), lambda g: (0, 0)), pair_block, pair_block]
         + [block] * (chips + 1)
         + [sib_block],
         out_specs=[pair_block] + [block] * (chips + 1) + [sib_block],
@@ -174,7 +172,7 @@
     query_doc = lax.dynamic_slice_in_dim(token_doc, position * tokens, tokens, 0)
     distance = query_pos[:, None] - key_pos[None, :]
     allowed = (distance >= 0) & (distance < WINDOW) & (query_doc[:, None] == key_doc[None, :])
-    mask = allowed.astype(jnp.float32)
+    mask = allowed.T.astype(jnp.float32)
     width = KV_HEADS * HEAD_DIM // CHUNKS
     query_parts, key_parts, value_parts = [], [], []
     for chunk in range(CHUNKS):

time: 248 us -> 221 us (0.89)
  starting transfers between devices: 90 us -> 38.1 us
  waiting for transfers between devices: 103 us -> 131 us
    ppermute x32 -> x16, starting transfers between devices: 81.2 us -> 38.1 us  [moved(): return lax.ppermute(value, 'seq', pairs)]
    ppermute x32 -> x16, waiting for transfers between devices: 103 us -> 131 us  [moved(): return lax.ppermute(value, 'seq', pairs)]
    ppermute x1, starting transfers between devices: 8.83 us -> 0.07 us  [passed_along(): return lax.ppermute(value, axis, pairs)]
    slice x2 -> x1, local copies, waits for them, and re-layouts: 4.54 us -> 1.08 us  [local(): value_parts.append(summed[1].astype(jnp.bfloat16))]
    broadcast_in_dim x3 -> x0, other arithmetic: 2.7 us -> none  [the longest x1 1.05 us: local(): jnp.concatenate(query_parts, axis=1)[None]]
    pallas_call x2 -> x1, Pallas kernels: 30 us -> 30.8 us  [attention_grads(): pl.pallas_call(lambda *refs: attention_kernel(chips, *refs), grid=(heads,...]
  transfers between devices with their start and end apart: 33 -> 17, of which waited for: 18 -> 10; matrix products, arithmetic and copies ran while one was open for 5% -> 2% of each run, Pallas kernels for 0% -> 0%
where the time goes in v2:
time: 221 us; the launch traced here: 218 us
  waiting for transfers between devices  131 us (59%)
  starting transfers between devices  38.1 us (17%)
  Pallas kernels  30.8 us (14%)
  other arithmetic  12.7 us (6%)
  local copies, waits for them, and re-layouts  5.25 us (2%)
    ppermute x16, waiting for transfers between devices, moved(): return lax.ppermute(value, 'seq', pairs)  131 us
    ppermute x16, starting transfers between devices, moved(): return lax.ppermute(value, 'seq', pairs)  38.1 us
    pallas_call x1, Pallas kernels, attention_grads(): pl.pallas_call(lambda *refs: attention_kernel(chips, *refs), grid=(heads,...  30.8 us
  transfers between devices with their start and end apart: 17, of which 10 were waited for; matrix products, arithmetic and copies ran while one was open for 2% of the time, Pallas kernels for 0%

profile of v2, /device:TPU:7, one launch (start us, length us, event | category | flops | bytes accessed | tf_op | source)
XLA Modules:
  0.0 218.5 jit_solution(15851383719901097830)
XLA Ops:
  0.6 0.0 copy-start
  0.6 1.1 constant_dynamic-update-slice_fusion.1
  1.7 1.1 constant_dynamic-update-slice_fusion.refs_4_
  2.8 0.0 copy-start.4
  2.8 3.3 %collective-permute-start.1 = (bf16[2,128,2048]{2,1,0:T(8,128)(2,1)S(1)}, bf16[2,128,2048]{2,1,0:T(8,128)(2,1)S(1)}, u32[]{:S(2)}, u32[]{:S(2)}) collective-permute-start(bf16[2,128,2048]{2,1,0:T(8,128)(2,1)S(1)} %constant_dynamic-update-slice_fusion.refs_4_), channel_id=1, source_target_pairs={{0,8},{1,9},{2,10},{3,11},{4,12},{5,13},{6,14},{7,15},{8,16},{9,17... | collective-permute-start | bytes 3145736 | tf_op jit(solution)/shard_map/ppermute | solution.py:26
  6.1 1.3 collective-permute-start.6
  7.4 20.4 %collective-permute-done.1.refs_3_ = bf16[2,128,2048]{2,1,0:T(8,128)(2,1)S(1)} collective-permute-done((bf16[2,128,2048]{2,1,0:T(8,128)(2,1)S(1)}, bf16[2,128,2048]{2,1,0:T(8,128)(2,1)S(1)}, u32[]{:S(2)}, u32[]{:S(2)}) %collective-permute-start.1) | collective-permute-done | bytes 1048608 | tf_op jit(solution)/shard_map/ppermute | solution.py:26
  27.8 3.1 %collective-permute-start.7 = (bf16[2,128,2048]{2,1,0:T(8,128)(2,1)S(1)}, bf16[2,128,2048]{2,1,0:T(8,128)(2,1)}, u32[]{:S(2)}, u32[]{:S(2)}) collective-permute-start(bf16[2,128,2048]{2,1,0:T(8,128)(2,1)S(1)} %collective-permute-done.1.refs_3_), channel_id=1, source_target_pairs={{2,0},{3,1},{4,2},{5,3},{6,4},{7,5},{10,8},{11,9},{12,10},{13,11},... | collective-permute-start | bytes 3145736 | tf_op jit(solution)/shard_map/ppermute | solution.py:26
  31.0 1.3 collective-permute-start.4
  32.3 5.9 %collective-permute-start.5 = (bf16[2,128,2048]{2,1,0:T(8,128)(2,1)S(1)}, bf16[2,128,2048]{2,1,0:T(8,128)(2,1)}, u32[]{:S(2)}, u32[]{:S(2)}) collective-permute-start(bf16[2,128,2048]{2,1,0:T(8,128)(2,1)S(1)} %collective-permute-done.1.refs_3_), channel_id=1, source_target_pairs={{4,0},{5,1},{6,2},{7,3},{12,8},{13,9},{14,10},{15,11},{20,16},{21,... | collective-permute-start | bytes 3145736 | tf_op jit(solution)/shard_map/ppermute | solution.py:26
  38.2 1.3 collective-permute-start.2
  39.5 0.0 collective-permute-done.6
  39.5 2.3 %collective-permute-start.3 = (bf16[2,128,2048]{2,1,0:T(8,128)(2,1)S(1)}, bf16[2,128,2048]{2,1,0:T(8,128)(2,1)S(1)}, u32[]{:S(2)}, u32[]{:S(2)}) collective-permute-start(bf16[2,128,2048]{2,1,0:T(8,128)(2,1)S(1)} %collective-permute-done.1.refs_3_), channel_id=1, source_target_pairs={{6,0},{7,1},{14,8},{15,9},{22,16},{23,17},{30,24},{31,25}} | collective-permute-start | bytes 3145736 | tf_op jit(solution)/shard_map/ppermute | solution.py:26
  41.8 9.1 %collective-permute-done.7 = bf16[2,128,2048]{2,1,0:T(8,128)(2,1)} collective-permute-done((bf16[2,128,2048]{2,1,0:T(8,128)(2,1)S(1)}, bf16[2,128,2048]{2,1,0:T(8,128)(2,1)}, u32[]{:S(2)}, u32[]{:S(2)}) %collective-permute-start.7) | collective-permute-done | bytes 1048608 | tf_op jit(solution)/shard_map/ppermute | solution.py:26
  50.9 1.3 broadcast_select_fusion.refs_7_
  52.2 0.0 copy-start.1
  52.2 3.6 %collective-permute-done.4 = bf16[2,128,2048]{2,1,0:T(8,128)(2,1)} collective-permute-done((bf16[2,128,2048]{2,1,0:T(8,128)(2,1)S(1)}, bf16[2,128,2048]{2,1,0:T(8,128)(2,1)}, u32[]{:S(2)}, u32[]{:S(2)}) %collective-permute-start.4) | collective-permute-done | bytes 1048608 | tf_op jit(solution)/shard_map/ppermute | solution.py:26
  55.8 20.4 %collective-permute-done.5 = bf16[2,128,2048]{2,1,0:T(8,128)(2,1)} collective-permute-done((bf16[2,128,2048]{2,1,0:T(8,128)(2,1)S(1)}, bf16[2,128,2048]{2,1,0:T(8,128)(2,1)}, u32[]{:S(2)}, u32[]{:S(2)}) %collective-permute-start.5) | collective-permute-done | bytes 1048608 | tf_op jit(solution)/shard_map/ppermute | solution.py:26
  76.2 1.3 broadcast_select_fusion.1.refs_6_
  77.5 0.0 copy-done.4
  77.6 0.0 copy-start.2
  77.6 0.0 collective-permute-done.2
  77.6 0.0 copy-start.5
  77.6 0.0 collective-permute-done.3
  77.6 0.1 broadcast_select_fusion.2.refs_5_
  77.7 0.0 copy-start.3
  77.7 0.0 copy-done.11
  77.7 0.0 copy-done.1
  77.7 1.8 copy-done.5
  79.6 2.5 %maximum_select_fusion = bf16[4,2,128,2048]{3,2,1,0:T(8,128)(2,1)} fusion(bf16[1,2,128,2048]{3,2,1,0:T(8,128)(2,1)S(1)} %bitcast.46, bf16[1,2,128,2048]{3,2,1,0:T(8,128)(2,1)S(1)} %bitcast.47, bf16[1,2,128,2048]{3,2,1,0:T(8,128)(2,1)S(1)} %bitcast.48, bf16[1,2,128,2048]{3,2,1,0:T(8,128)(2,1)S(1)} %bitcast.49, bf16[1,2,128,2048]{3,2,1,0:T(8,128)(2,1)S(1)} %bitcast.50, ...), kind=kLoop, calls=%fused_computation | loop fusion | flops 14680064 | bytes 9437185 | tf_op jit(solution)/shard_map/jit(_where)/select_n | solution.py:57
  82.1 0.0 copy-done.2
  82.1 0.0 copy-done.3
  82.1 0.5 collective-permute-start.8
  82.6 0.0 copy-done.12
  82.6 0.1 collective-permute-start
  82.7 0.1 broadcast_bitcast_fusion
  82.7 0.1 dynamic_slice.6
  82.8 0.1 pad_dynamic-slice_fusion
  82.9 1.5 fusion.14.refs_0_
  84.4 0.0 collective-permute-done
  84.4 5.3 %collective-permute-done.8.refs_8_ = bf16[4,2,128,2048]{3,2,1,0:T(8,128)(2,1)} collective-permute-done((bf16[4,2,128,2048]{3,2,1,0:T(8,128)(2,1)}, bf16[4,2,128,2048]{3,2,1,0:T(8,128)(2,1)}, u32[]{:S(2)}, u32[]{:S(2)}) %collective-permute-start.8) | collective-permute-done | bytes 4194336 | tf_op jit(solution)/shard_map/ppermute | solution.py:26
  89.7 30.8 %shard_map.76 = (bf16[128,4096]{1,0:T(8,128)(2,1)}, f32[2,128,2048]{2,1,0:T(8,128)}, f32[2,128,2048]{2,1,0:T(8,128)}, f32[2,128,2048]{2,1,0:T(8,128)}, f32[2,128...) custom-call(f32[1152,128]{1,0:T(8,128)} %fusion.14.refs_0_, ...), custom_call_target="tpu_custom_call" | custom-call | flops 6039797760 | bytes 32047104 | tf_op jit(solution)/shard_map/pallas_call | solution.py:140
  120.5 0.6 collective-permute-start.9
  121.1 7.0 %collective-permute-done.9 = bf16[4,2,128,2048]{3,2,1,0:T(8,128)(2,1)S(1)} collective-permute-done((bf16[4,2,128,2048]{3,2,1,0:T(8,128)(2,1)}, bf16[4,2,128,2048]{3,2,1,0:T(8,128)(2,1)S(1)}, u32[]{:S(2)}, u32[]{:S(2)}) %collective-permute-start.9) | collective-permute-done | bytes 4194336 | tf_op jit(solution)/shard_map/ppermute | solution.py:26
  128.1 1.1 convert_element_type.47
  129.2 2.8 %fusion.6 = (bf16[2,128,2048]{2,1,0:T(8,128)(2,1)}, bf16[2,128,2048]{2,1,0:T(8,128)(2,1)S(1)}, bf16[2,128,2048]{2,1,0:T(8,128)(2,1)S(1)}) fusion(f32[2,128,2048]{2,1,0:T(8,128)S(1)} %copy-done.7, f32[4,2,128,2048]{3,2,1,0:T(8,128)S(1)} %convert_element_type.47, pred[]{:T(512)S(6)} %eq.24, f32[2,128,2048]{2,1,0:T(8,128)S(1)} %copy-done.9, ...), kind=kLoop, calls=%fused_computation.11 | loop fusion | flops 4718592 | bytes 17825792 | tf_op jit(solution)/shard_map/convert_element_type | solution.py:74
  132.0 1.3 collective-permute-start.13
  133.3 1.3 collective-permute-start.15
  134.6 1.3 collective-permute-start.14
  135.9 8.6 %collective-permute-start.10 = (bf16[2,128,2048]{2,1,0:T(8,128)(2,1)}, bf16[2,128,2048]{2,1,0:T(8,128)(2,1)S(1)}, u32[]{:S(2)}, u32[]{:S(2)}) collective-permute-start(bf16[2,128,2048]{2,1,0:T(8,128)(2,1)} %get-tuple-element.17), channel_id=1, source_target_pairs={{2,0},{3,1},{4,2},{5,3},{6,4},{7,5},{10,8},{11,9},{12,10},{13,11},... | collective-permute-start | bytes 3145736 | tf_op jit(solution)/shard_map/ppermute | solution.py:26
  144.5 3.4 %collective-permute-start.12 = (bf16[2,128,2048]{2,1,0:T(8,128)(2,1)S(1)}, bf16[2,128,2048]{2,1,0:T(8,128)(2,1)S(1)}, u32[]{:S(2)}, u32[]{:S(2)}) collective-permute-start(bf16[2,128,2048]{2,1,0:T(8,128)(2,1)S(1)} %get-tuple-element.18), channel_id=1, source_target_pairs={{6,0},{7,1},{14,8},{15,9},{22,16},{23,17},{30,24},{31,25}} | collective-permute-start | bytes 3145736 | tf_op jit(solution)/shard_map/ppermute | solution.py:26
  147.9 17.5 %collective-permute-done.13 = bf16[2,128,2048]{2,1,0:T(8,128)(2,1)S(1)} collective-permute-done((bf16[2,128,2048]{2,1,0:T(8,128)(2,1)}, bf16[2,128,2048]{2,1,0:T(8,128)(2,1)S(1)}, u32[]{:S(2)}, u32[]{:S(2)}) %collective-permute-start.13) | collective-permute-done | bytes 1048608 | tf_op jit(solution)/shard_map/ppermute | solution.py:26
  165.5 1.3 collective-permute-start.11
  166.8 0.0 collective-permute-done.15
  166.8 21.3 %collective-permute-done.14 = bf16[2,128,2048]{2,1,0:T(8,128)(2,1)S(1)} collective-permute-done((bf16[2,128,2048]{2,1,0:T(8,128)(2,1)S(1)}, bf16[2,128,2048]{2,1,0:T(8,128)(2,1)S(1)}, u32[]{:S(2)}, u32[]{:S(2)}) %collective-permute-start.14) | collective-permute-done | bytes 1048608 | tf_op jit(solution)/shard_map/ppermute | solution.py:26
  188.2 0.9 fusion.3
  189.1 1.3 collective-permute-start.16
  190.4 0.0 collective-permute-done.10
  190.4 0.0 collective-permute-done.12
  190.4 18.3 %collective-permute-done.11 = bf16[2,128,2048]{2,1,0:T(8,128)(2,1)S(1)} collective-permute-done((bf16[2,128,2048]{2,1,0:T(8,128)(2,1)S(1)}, bf16[2,128,2048]{2,1,0:T(8,128)(2,1)S(1)}, u32[]{:S(2)}, u32[]{:S(2)}) %collective-permute-start.11) | collective-permute-done | bytes 1048608 | tf_op jit(solution)/shard_map/ppermute | solution.py:26
  208.7 7.6 %collective-permute-done.16 = bf16[2,128,2048]{2,1,0:T(8,128)(2,1)S(1)} collective-permute-done((bf16[2,128,2048]{2,1,0:T(8,128)(2,1)S(1)}, bf16[2,128,2048]{2,1,0:T(8,128)(2,1)S(1)}, u32[]{:S(2)}, u32[]{:S(2)}) %collective-permute-start.16) | collective-permute-done | bytes 1048608 | tf_op jit(solution)/shard_map/ppermute | solution.py:26
  216.3 0.0 copy-done.6
  216.3 1.0 fusion.11
  217.4 1.1 fusion.15
  (15 shorter events, 0.0 us)
Async XLA Ops:
  0.6 82.0 %copy-start = (s32[1,32]{1,0:T(1,128)S(1)}, s32[1,32]{1,0:T(1,128)}, u32[]{:S(2)}) copy-start(s32[1,32]{1,0:T(1,128)} %param.9) | copy-start | bytes 388
  2.8 74.7 %copy-start.4 = (bf16[2,128,2048]{2,1,0:T(8,128)(2,1)}, bf16[2,128,2048]{2,1,0:T(8,128)(2,1)S(1)}, u32[]{:S(2)}) copy-start(bf16[2,128,2048]{2,1,0:T(8,128)(2,1)S(1)} %constant_dynamic-update-slice_fusion.refs_4_) | copy-start | bytes 3145732
  2.8 25.0 %collective-permute-start.1 = (bf16[2,128,2048]{2,1,0:T(8,128)(2,1)S(1)}, bf16[2,128,2048]{2,1,0:T(8,128)(2,1)S(1)}, u32[]{:S(2)}, u32[]{:S(2)}) collective-permute-start(bf16[2,128,2048]{2,1,0:T(8,128)(2,1)S(1)} %constant_dynamic-update-slice_fusion.refs_4_), channel_id=1, source_target_pairs={{0,8},{1,9},{2,10},{3,11},{4,12},{5,13},{6,14},{7,15},{8,16},{9,17... | collective-permute-start | bytes 3145736 | tf_op jit(solution)/shard_map/ppermute | solution.py:26
  6.1 33.4 %collective-permute-start.6 = (bf16[2,128,2048]{2,1,0:T(8,128)(2,1)S(1)}, bf16[2,128,2048]{2,1,0:T(8,128)(2,1)}, u32[]{:S(2)}, u32[]{:S(2)}) collective-permute-start(bf16[2,128,2048]{2,1,0:T(8,128)(2,1)S(1)} %constant_dynamic-update-slice_fusion.refs_4_), channel_id=1, source_target_pairs={{0,6},{1,7},{8,14},{9,15},{16,22},{17,23},{24,30},{25,31}} | collective-permute-start | bytes 3145736 | tf_op jit(solution)/shard_map/ppermute | solution.py:26
  27.8 49.9 %copy-start.11 = (bf16[2,128,2048]{2,1,0:T(8,128)(2,1)}, bf16[2,128,2048]{2,1,0:T(8,128)(2,1)S(1)}, u32[]{:S(2)}) copy-start(bf16[2,128,2048]{2,1,0:T(8,128)(2,1)S(1)} %collective-permute-done.1.refs_3_) | copy-start | bytes 3145732
  27.8 23.0 %collective-permute-start.7 = (bf16[2,128,2048]{2,1,0:T(8,128)(2,1)S(1)}, bf16[2,128,2048]{2,1,0:T(8,128)(2,1)}, u32[]{:S(2)}, u32[]{:S(2)}) collective-permute-start(bf16[2,128,2048]{2,1,0:T(8,128)(2,1)S(1)} %collective-permute-done.1.refs_3_), channel_id=1, source_target_pairs={{2,0},{3,1},{4,2},{5,3},{6,4},{7,5},{10,8},{11,9},{12,10},{13,11},... | collective-permute-start | bytes 3145736 | tf_op jit(solution)/shard_map/ppermute | solution.py:26
  31.0 24.8 %collective-permute-start.4 = (bf16[2,128,2048]{2,1,0:T(8,128)(2,1)S(1)}, bf16[2,128,2048]{2,1,0:T(8,128)(2,1)}, u32[]{:S(2)}, u32[]{:S(2)}) collective-permute-start(bf16[2,128,2048]{2,1,0:T(8,128)(2,1)S(1)} %constant_dynamic-update-slice_fusion.refs_4_), channel_id=1, source_target_pairs={{0,4},{1,5},{2,6},{3,7},{8,12},{9,13},{10,14},{11,15},{16,20},{17,... | collective-permute-start | bytes 3145736 | tf_op jit(solution)/shard_map/ppermute | solution.py:26
  32.3 43.9 %collective-permute-start.5 = (bf16[2,128,2048]{2,1,0:T(8,128)(2,1)S(1)}, bf16[2,128,2048]{2,1,0:T(8,128)(2,1)}, u32[]{:S(2)}, u32[]{:S(2)}) collective-permute-start(bf16[2,128,2048]{2,1,0:T(8,128)(2,1)S(1)} %collective-permute-done.1.refs_3_), channel_id=1, source_target_pairs={{4,0},{5,1},{6,2},{7,3},{12,8},{13,9},{14,10},{15,11},{20,16},{21,... | collective-permute-start | bytes 3145736 | tf_op jit(solution)/shard_map/ppermute | solution.py:26
  38.2 39.4 %collective-permute-start.2 = (bf16[2,128,2048]{2,1,0:T(8,128)(2,1)S(1)}, bf16[2,128,2048]{2,1,0:T(8,128)(2,1)S(1)}, u32[]{:S(2)}, u32[]{:S(2)}) collective-permute-start(bf16[2,128,2048]{2,1,0:T(8,128)(2,1)S(1)} %constant_dynamic-update-slice_fusion.refs_4_), channel_id=1, source_target_pairs={{0,2},{1,3},{2,4},{3,5},{4,6},{5,7},{8,10},{9,11},{10,12},{11,13},... | collective-permute-start | bytes 3145736 | tf_op jit(solution)/shard_map/ppermute | solution.py:26
  39.5 38.0 %collective-permute-start.3 = (bf16[2,128,2048]{2,1,0:T(8,128)(2,1)S(1)}, bf16[2,128,2048]{2,1,0:T(8,128)(2,1)S(1)}, u32[]{:S(2)}, u32[]{:S(2)}) collective-permute-start(bf16[2,128,2048]{2,1,0:T(8,128)(2,1)S(1)} %collective-permute-done.1.refs_3_), channel_id=1, source_target_pairs={{6,0},{7,1},{14,8},{15,9},{22,16},{23,17},{30,24},{31,25}} | collective-permute-start | bytes 3145736 | tf_op jit(solution)/shard_map/ppermute | solution.py:26
  52.2 25.5 %copy-start.1 = (bf16[2,128,2048]{2,1,0:T(8,128)(2,1)}, bf16[2,128,2048]{2,1,0:T(8,128)(2,1)S(1)}, u32[]{:S(2)}) copy-start(bf16[2,128,2048]{2,1,0:T(8,128)(2,1)S(1)} %broadcast_select_fusion.refs_7_) | copy-start | bytes 3145732
  77.6 4.5 %copy-start.2 = (bf16[2,128,2048]{2,1,0:T(8,128)(2,1)}, bf16[2,128,2048]{2,1,0:T(8,128)(2,1)S(1)}, u32[]{:S(2)}) copy-start(bf16[2,128,2048]{2,1,0:T(8,128)(2,1)S(1)} %broadcast_select_fusion.1.refs_6_) | copy-start | bytes 3145732
  77.6 2.0 copy-start.5
  77.7 4.4 %copy-start.3 = (bf16[2,128,2048]{2,1,0:T(8,128)(2,1)}, bf16[2,128,2048]{2,1,0:T(8,128)(2,1)S(1)}, u32[]{:S(2)}) copy-start(bf16[2,128,2048]{2,1,0:T(8,128)(2,1)S(1)} %broadcast_select_fusion.2.refs_5_) | copy-start | bytes 3145732
  79.6 3.0 %copy-start.12 = (bf16[1,128,4096]{2,1,0:T(8,128)(2,1)S(1)}, bf16[1,128,4096]{2,1,0:T(8,128)(2,1)}, u32[]{:S(2)}) copy-start(bf16[1,128,4096]{2,1,0:T(8,128)(2,1)} %param.8) | copy-start | bytes 3145732
  82.1 7.6 %collective-permute-start.8 = (bf16[4,2,128,2048]{3,2,1,0:T(8,128)(2,1)}, bf16[4,2,128,2048]{3,2,1,0:T(8,128)(2,1)}, u32[]{:S(2)}, u32[]{:S(2)}) collective-permute-start(bf16[4,2,128,2048]{3,2,1,0:T(8,128)(2,1)} %maximum_select_fusion), channel_id=1, source_target_pairs={{0,1},{1,0},{2,3},{3,2},{4,5},{5,4},{6,7},{7,6},{8,9},{9,8},{10,11... | collective-permute-start | bytes 12582920 | tf_op jit(solution)/shard_map/ppermute | solution.py:26
  82.6 1.8 collective-permute-start
  84.4 5.3 %copy-start.13 = (bf16[1,128,4096]{2,1,0:T(8,128)(2,1)}, bf16[1,128,4096]{2,1,0:T(8,128)(2,1)S(1)}, u32[]{:S(2)}) copy-start(bf16[1,128,4096]{2,1,0:T(8,128)(2,1)S(1)} %collective-permute-done) | copy-start | bytes 3145732
  120.5 8.7 %copy-start.7 = (f32[2,128,2048]{2,1,0:T(8,128)S(1)}, f32[2,128,2048]{2,1,0:T(8,128)}, u32[]{:S(2)}) copy-start(f32[2,128,2048]{2,1,0:T(8,128)} %get-tuple-element.13) | copy-start | bytes 6291460
  120.5 8.7 %copy-start.8 = (f32[2,128,2048]{2,1,0:T(8,128)S(1)}, f32[2,128,2048]{2,1,0:T(8,128)}, u32[]{:S(2)}) copy-start(f32[2,128,2048]{2,1,0:T(8,128)} %get-tuple-element.14) | copy-start | bytes 6291460
  120.5 8.7 %copy-start.9 = (f32[2,128,2048]{2,1,0:T(8,128)S(1)}, f32[2,128,2048]{2,1,0:T(8,128)}, u32[]{:S(2)}) copy-start(f32[2,128,2048]{2,1,0:T(8,128)} %get-tuple-element.15) | copy-start | bytes 6291460
  120.5 7.6 %collective-permute-start.9 = (bf16[4,2,128,2048]{3,2,1,0:T(8,128)(2,1)}, bf16[4,2,128,2048]{3,2,1,0:T(8,128)(2,1)S(1)}, u32[]{:S(2)}, u32[]{:S(2)}) collective-permute-start(bf16[4,2,128,2048]{3,2,1,0:T(8,128)(2,1)} %get-tuple-element.12), channel_id=1, source_target_pairs={{0,1},{1,0},{2,3},{3,2},{4,5},{5,4},{6,7},{7,6},{8,9},{9,8},{10,11... | collective-permute-start | bytes 12582920 | tf_op jit(solution)/shard_map/ppermute | solution.py:26
  129.2 59.0 %copy-start.10 = (f32[2,128,2048]{2,1,0:T(8,128)S(1)}, f32[2,128,2048]{2,1,0:T(8,128)}, u32[]{:S(2)}) copy-start(f32[2,128,2048]{2,1,0:T(8,128)} %get-tuple-element.16) | copy-start | bytes 6291460
  132.0 33.5 %collective-permute-start.13 = (bf16[2,128,2048]{2,1,0:T(8,128)(2,1)}, bf16[2,128,2048]{2,1,0:T(8,128)(2,1)S(1)}, u32[]{:S(2)}, u32[]{:S(2)}) collective-permute-start(bf16[2,128,2048]{2,1,0:T(8,128)(2,1)} %get-tuple-element.17), channel_id=1, source_target_pairs={{0,6},{1,7},{8,14},{9,15},{16,22},{17,23},{24,30},{25,31}} | collective-permute-start | bytes 3145736 | tf_op jit(solution)/shard_map/ppermute | solution.py:26
  133.3 33.5 %collective-permute-start.15 = (bf16[2,128,2048]{2,1,0:T(8,128)(2,1)S(1)}, bf16[2,128,2048]{2,1,0:T(8,128)(2,1)S(1)}, u32[]{:S(2)}, u32[]{:S(2)}) collective-permute-start(bf16[2,128,2048]{2,1,0:T(8,128)(2,1)S(1)} %get-tuple-element.18), channel_id=1, source_target_pairs={{0,2},{1,3},{2,4},{3,5},{4,6},{5,7},{8,10},{9,11},{10,12},{11,13},... | collective-permute-start | bytes 3145736 | tf_op jit(solution)/shard_map/ppermute | solution.py:26
  134.6 53.6 %collective-permute-start.14 = (bf16[2,128,2048]{2,1,0:T(8,128)(2,1)S(1)}, bf16[2,128,2048]{2,1,0:T(8,128)(2,1)S(1)}, u32[]{:S(2)}, u32[]{:S(2)}) collective-permute-start(bf16[2,128,2048]{2,1,0:T(8,128)(2,1)S(1)} %get-tuple-element.19), channel_id=1, source_target_pairs={{0,4},{1,5},{2,6},{3,7},{8,12},{9,13},{10,14},{11,15},{16,20},{17,... | collective-permute-start | bytes 3145736 | tf_op jit(solution)/shard_map/ppermute | solution.py:26
  135.9 54.5 %collective-permute-start.10 = (bf16[2,128,2048]{2,1,0:T(8,128)(2,1)}, bf16[2,128,2048]{2,1,0:T(8,128)(2,1)S(1)}, u32[]{:S(2)}, u32[]{:S(2)}) collective-permute-start(bf16[2,128,2048]{2,1,0:T(8,128)(2,1)} %get-tuple-element.17), channel_id=1, source_target_pairs={{2,0},{3,1},{4,2},{5,3},{6,4},{7,5},{10,8},{11,9},{12,10},{13,11},... | collective-permute-start | bytes 3145736 | tf_op jit(solution)/shard_map/ppermute | solution.py:26
  144.5 46.0 %collective-permute-start.12 = (bf16[2,128,2048]{2,1,0:T(8,128)(2,1)S(1)}, bf16[2,128,2048]{2,1,0:T(8,128)(2,1)S(1)}, u32[]{:S(2)}, u32[]{:S(2)}) collective-permute-start(bf16[2,128,2048]{2,1,0:T(8,128)(2,1)S(1)} %get-tuple-element.18), channel_id=1, source_target_pairs={{6,0},{7,1},{14,8},{15,9},{22,16},{23,17},{30,24},{31,25}} | collective-permute-start | bytes 3145736 | tf_op jit(solution)/shard_map/ppermute | solution.py:26
  165.5 43.2 %collective-permute-start.11 = (bf16[2,128,2048]{2,1,0:T(8,128)(2,1)S(1)}, bf16[2,128,2048]{2,1,0:T(8,128)(2,1)S(1)}, u32[]{:S(2)}, u32[]{:S(2)}) collective-permute-start(bf16[2,128,2048]{2,1,0:T(8,128)(2,1)S(1)} %get-tuple-element.19), channel_id=1, source_target_pairs={{4,0},{5,1},{6,2},{7,3},{12,8},{13,9},{14,10},{15,11},{20,16},{21,... | collective-permute-start | bytes 3145736 | tf_op jit(solution)/shard_map/ppermute | solution.py:26
  188.2 28.1 %copy-start.6 = (f32[2,128,2048]{2,1,0:T(8,128)S(1)}, f32[2,128,2048]{2,1,0:T(8,128)}, u32[]{:S(2)}) copy-start(f32[2,128,2048]{2,1,0:T(8,128)} %get-tuple-element.11) | copy-start | bytes 6291460
  189.1 27.2 %collective-permute-start.16 = (bf16[2,128,2048]{2,1,0:T(8,128)(2,1)S(1)}, bf16[2,128,2048]{2,1,0:T(8,128)(2,1)S(1)}, u32[]{:S(2)}, u32[]{:S(2)}) collective-permute-start(bf16[2,128,2048]{2,1,0:T(8,128)(2,1)S(1)} %fusion.3), channel_id=1, source_target_pairs={{8,0},{9,1},{10,2},{11,3},{12,4},{13,5},{14,6},{15,7},{16,8},{17,9... | collective-permute-start | bytes 3145736 | tf_op jit(solution)/shard_map/ppermute | solution.py:26

commit v3 on v0

--- a/solution.py
+++ b/solution.py
@@ -76,7 +76,7 @@
     return own
 
 
-def attention_kernel(chips, mask_ref, q_ref, do_ref, prev_ref, *refs):
+def attention_kernel(chips, heads, bias_ref, q_ref, do_ref, prev_ref, *refs):
     direct_refs = refs[:chips]
     sib_ref = refs[chips]
     dq_ref, dprev_ref = refs[chips + 1], refs[chips + 2]
@@ -84,64 +84,62 @@
     dsib_ref = refs[2 * chips + 3]
     tokens = q_ref.shape[0]
     blocks = [prev_ref]
+    outs = [dprev_ref]
     for k in range(chips - 1, -1, -1):
-        blocks.append(sib_ref.at[k])
-        blocks.append(direct_refs[k])
-    k = jnp.concatenate([b[0] for b in blocks], axis=0)
-    v = jnp.concatenate([b[1] for b in blocks], axis=0)
-    visible = mask_ref[...] > 0.0
-    visible = jnp.concatenate([visible, visible], axis=0)
-    q = q_ref[...]
-    do = do_ref[...]
-    qs = jnp.concatenate([q[:, :HEAD_DIM], q[:, HEAD_DIM:]], axis=0)
-    dos = jnp.concatenate([do[:, :HEAD_DIM], do[:, HEAD_DIM:]], axis=0)
+        blocks += [sib_ref.at[k], direct_refs[k]]
+        outs += [dsib_ref.at[k], ddirect_refs[k]]
+    bias = bias_ref[...]
     contract_last = (((1,), (1,)), ((), ()))
     contract_first = (((0,), (0,)), ((), ()))
-    scores = lax.dot_general(qs, k, contract_last, preferred_element_type=jnp.float32) * SCORE_SCALE
-    scores = jnp.where(visible, scores, MASKED_SCORE)
-    largest = jnp.max(scores, axis=1, keepdims=True)
-    unscaled = jnp.where(visible, jnp.exp(scores - largest), 0.0)
-    attn = unscaled * (1.0 / jnp.sum(unscaled, axis=1, keepdims=True))
-    dattn = lax.dot_general(dos, v, contract_last, preferred_element_type=jnp.float32)
-    row_delta = jnp.sum(attn * dattn, axis=1, keepdims=True)
-    dscores = (attn * (dattn - row_delta)).astype(jnp.bfloat16)
-    grad_q = jnp.dot(dscores, k, preferred_element_type=jnp.float32) * SCORE_SCALE
-    dq_ref[:, :HEAD_DIM] = grad_q[:tokens].astype(dq_ref.dtype)
-    dq_ref[:, HEAD_DIM:] = grad_q[tokens:].astype(dq_ref.dtype)
-    grad_k = (
-        lax.dot_general(dscores, qs, contract_first, preferred_element_type=jnp.float32)
-        * SCORE_SCALE
-    )
-    grad_v = lax.dot_general(
-        attn.astype(jnp.bfloat16), dos, contract_first, preferred_element_type=jnp.float32
-    )
-    outs = [dprev_ref]
-    for kk in range(chips - 1, -1, -1):
-        outs.append(dsib_ref.at[kk])
-        outs.append(ddirect_refs[kk])
-    for j, out in enumerate(outs):
-        rows = slice(j * tokens, (j + 1) * tokens)
-        out[0] = grad_k[rows].astype(out.dtype)
-        out[1] = grad_v[rows].astype(out.dtype)
-
-
-def attention_grads(mask, queries, grad_out, prev, direct, sib):
+    for h in range(heads):
+        cols = slice(h * HEAD_DIM, (h + 1) * HEAD_DIM)
+        pair = slice(2 * h * HEAD_DIM, (2 * h + 1) * HEAD_DIM)
+        pair2 = slice((2 * h + 1) * HEAD_DIM, (2 * h + 2) * HEAD_DIM)
+        k = jnp.concatenate([b[0, :, cols] for b in blocks], axis=0)
+        v = jnp.concatenate([b[1, :, cols] for b in blocks], axis=0)
+        qs = jnp.concatenate([q_ref[:, pair], q_ref[:, pair2]], axis=0)
+        dos = jnp.concatenate([do_ref[:, pair], do_ref[:, pair2]], axis=0)
+        scores = lax.dot_general(qs, k, contract_last, preferred_element_type=jnp.float32)
+        scores = scores * SCORE_SCALE + bias
+        largest = jnp.max(scores, axis=1, keepdims=True)
+        unscaled = jnp.exp(scores - largest)
+        attn = unscaled * (1.0 / jnp.sum(unscaled, axis=1, keepdims=True))
+        dattn = lax.dot_general(dos, v, contract_last, preferred_element_type=jnp.float32)
+        row_delta = jnp.sum(attn * dattn, axis=1, keepdims=True)
+        dscores = (attn * (dattn - row_delta)).astype(jnp.bfloat16)
+        grad_q = jnp.dot(dscores, k, preferred_element_type=jnp.float32) * SCORE_SCALE
+        dq_ref[:, pair] = grad_q[:tokens].astype(dq_ref.dtype)
+        dq_ref[:, pair2] = grad_q[tokens:].astype(dq_ref.dtype)
+        grad_k = (
+            lax.dot_general(dscores, qs, contract_first, preferred_element_type=jnp.float32)
+            * SCORE_SCALE
+        )
+        grad_v = lax.dot_general(
+            attn.astype(jnp.bfloat16), dos, contract_first, preferred_element_type=jnp.float32
+        )
+        for j, out in enumerate(outs):
+            rows = slice(j * tokens, (j + 1) * tokens)
+            out[0, :, cols] = grad_k[rows].astype(out.dtype)
+            out[1, :, cols] = grad_v[rows].astype(out.dtype)
+
+
+def attention_grads(bias, queries, grad_out, prev, direct, sib, per_step=2):
     tokens = queries.shape[0]
     chips = len(direct)
-    key_count = mask.shape[1]
+    key_count = bias.shape[1]
     width = prev.shape[2]
     heads = width // HEAD_DIM
-    pair = 2 * HEAD_DIM
-    block = pl.BlockSpec((2, tokens, HEAD_DIM), lambda g: (0, 0, g))
-    sib_block = pl.BlockSpec((chips, 2, tokens, HEAD_DIM), lambda g: (0, 0, 0, g))
-    pair_block = pl.BlockSpec((tokens, pair), lambda g: (0, g))
+    cols = per_step * HEAD_DIM
+    block = pl.BlockSpec((2, tokens, cols), lambda g: (0, 0, g))
+    sib_block = pl.BlockSpec((chips, 2, tokens, cols), lambda g: (0, 0, 0, g))
+    pair_block = pl.BlockSpec((tokens, 2 * cols), lambda g: (0, g))
     part = jax.ShapeDtypeStruct(prev.shape, jnp.float32)
     flops = 2 * 5 * (2 * tokens) * key_count * HEAD_DIM * heads
-    moved_bytes = 2 * 3 * queries.size + 2 * 2 * key_count * width * 3 + mask.size * 4
+    moved_bytes = 2 * 3 * queries.size + 2 * 2 * key_count * width * 3 + bias.size * 4
     return pl.pallas_call(
-        lambda *refs: attention_kernel(chips, *refs),
-        grid=(heads,),
-        in_specs=[pl.BlockSpec((tokens, key_count), lambda g: (0, 0)), pair_block, pair_block]
+        lambda *refs: attention_kernel(chips, per_step, *refs),
+        grid=(heads // per_step,),
+        in_specs=[pl.BlockSpec(bias.shape, lambda g: (0, 0)), pair_block, pair_block]
         + [block] * (chips + 1)
         + [sib_block],
         out_specs=[pair_block] + [block] * (chips + 1) + [sib_block],
@@ -151,7 +149,7 @@
         cost_estimate=pl.CostEstimate(
             flops=flops, transcendentals=2 * tokens * key_count * heads, bytes_accessed=moved_bytes
         ),
-    )(mask, queries, grad_out, prev, *direct, sib)
+    )(bias, queries, grad_out, prev, *direct, sib)
 
 
 def local(queries, key_rows, value_rows, arriving_grad, doc_blocks):
@@ -173,10 +171,11 @@
     query_doc = lax.dynamic_slice_in_dim(token_doc, position * tokens, tokens, 0)
     distance = query_pos[:, None] - key_pos[None, :]
     allowed = (distance >= 0) & (distance < WINDOW) & (query_doc[:, None] == key_doc[None, :])
-    mask = allowed.astype(jnp.float32)
+    bias = jnp.where(allowed, 0.0, MASKED_SCORE).astype(jnp.float32)
+    bias = jnp.concatenate([bias, bias], axis=0)
     packed = jnp.stack([key_rows[0], value_rows[0]])
     prev, direct, sib = gather_window(packed, routes, chip_in_group, core)
-    outs = attention_grads(mask, queries[0], grad_out, prev, direct, sib)
+    outs = attention_grads(bias, queries[0], grad_out, prev, direct, sib)
     grad_query, dprev, ddirect, dsib = outs[0], outs[1], outs[2 : 2 + routes.chips], outs[-1]
     summed = scatter_window(dprev, ddirect, dsib, routes, chip_in_group, core)
     return (

time: 218 us -> 217 us (level)
  Pallas kernels: 27.7 us -> 25.1 us
    pallas_call x1, Pallas kernels: 27.7 us -> 25.1 us  [attention_grads(): pl.pallas_call(lambda *refs: attention_kernel(chips, per_step, *refs), gr...]
where the time goes in v3:
time: 217 us; the launch traced here: 214 us
  waiting for transfers between devices  131 us (60%)
  starting transfers between devices  38.8 us (18%)
  Pallas kernels  25.1 us (12%)
  other arithmetic  12.6 us (6%)
  local copies, waits for them, and re-layouts  5.27 us (2%)
    ppermute x16, waiting for transfers between devices, moved(): return lax.ppermute(value, 'seq', pairs)  131 us
    ppermute x16, starting transfers between devices, moved(): return lax.ppermute(value, 'seq', pairs)  38.7 us
    pallas_call x1, Pallas kernels, attention_grads(): pl.pallas_call(lambda *refs: attention_kernel(chips, per_step, *refs), gr...  25.1 us
  transfers between devices with their start and end apart: 17, of which 10 were waited for; matrix products, arithmetic and copies ran while one was open for 2% of the time, Pallas kernels for 0%

profile of v3, /device:TPU:7, one launch (start us, length us, event | category | flops | bytes accessed | tf_op | source)
XLA Modules:
  0.0 214.1 jit_solution(4751532897921956308)
XLA Ops:
  0.6 0.0 copy-start
  0.6 1.1 constant_dynamic-update-slice_fusion.1
  1.7 1.1 constant_dynamic-update-slice_fusion.refs_4_
  2.8 0.0 copy-start.5
  2.8 4.2 %collective-permute-start.1 = (bf16[2,128,2048]{2,1,0:T(8,128)(2,1)S(1)}, bf16[2,128,2048]{2,1,0:T(8,128)(2,1)}, u32[]{:S(2)}, u32[]{:S(2)}) collective-permute-start(bf16[2,128,2048]{2,1,0:T(8,128)(2,1)S(1)} %constant_dynamic-update-slice_fusion.refs_4_), channel_id=1, source_target_pairs={{0,8},{1,9},{2,10},{3,11},{4,12},{5,13},{6,14},{7,15},{8,16},{9,17... | collective-permute-start | bytes 3145736 | tf_op jit(solution)/shard_map/ppermute | solution.py:25
  7.0 1.3 collective-permute-start.6
  8.3 19.5 %collective-permute-done.1.refs_3_ = bf16[2,128,2048]{2,1,0:T(8,128)(2,1)} collective-permute-done((bf16[2,128,2048]{2,1,0:T(8,128)(2,1)S(1)}, bf16[2,128,2048]{2,1,0:T(8,128)(2,1)}, u32[]{:S(2)}, u32[]{:S(2)}) %collective-permute-start.1) | collective-permute-done | bytes 1048608 | tf_op jit(solution)/shard_map/ppermute | solution.py:25
  27.8 3.2 %collective-permute-start.7 = (bf16[2,128,2048]{2,1,0:T(8,128)(2,1)}, bf16[2,128,2048]{2,1,0:T(8,128)(2,1)}, u32[]{:S(2)}, u32[]{:S(2)}) collective-permute-start(bf16[2,128,2048]{2,1,0:T(8,128)(2,1)} %collective-permute-done.1.refs_3_), channel_id=1, source_target_pairs={{2,0},{3,1},{4,2},{5,3},{6,4},{7,5},{10,8},{11,9},{12,10},{13,11},... | collective-permute-start | bytes 3145736 | tf_op jit(solution)/shard_map/ppermute | solution.py:25
  31.0 1.3 collective-permute-start.4
  32.3 5.9 %collective-permute-start.5 = (bf16[2,128,2048]{2,1,0:T(8,128)(2,1)}, bf16[2,128,2048]{2,1,0:T(8,128)(2,1)}, u32[]{:S(2)}, u32[]{:S(2)}) collective-permute-start(bf16[2,128,2048]{2,1,0:T(8,128)(2,1)} %collective-permute-done.1.refs_3_), channel_id=1, source_target_pairs={{4,0},{5,1},{6,2},{7,3},{12,8},{13,9},{14,10},{15,11},{20,16},{21,... | collective-permute-start | bytes 3145736 | tf_op jit(solution)/shard_map/ppermute | solution.py:25
  38.2 1.3 collective-permute-start.2
  39.6 0.0 collective-permute-done.6
  39.6 2.3 %collective-permute-start.3 = (bf16[2,128,2048]{2,1,0:T(8,128)(2,1)}, bf16[2,128,2048]{2,1,0:T(8,128)(2,1)S(1)}, u32[]{:S(2)}, u32[]{:S(2)}) collective-permute-start(bf16[2,128,2048]{2,1,0:T(8,128)(2,1)} %collective-permute-done.1.refs_3_), channel_id=1, source_target_pairs={{6,0},{7,1},{14,8},{15,9},{22,16},{23,17},{30,24},{31,25}} | collective-permute-start | bytes 3145736 | tf_op jit(solution)/shard_map/ppermute | solution.py:25
  41.8 9.4 %collective-permute-done.7 = bf16[2,128,2048]{2,1,0:T(8,128)(2,1)} collective-permute-done((bf16[2,128,2048]{2,1,0:T(8,128)(2,1)}, bf16[2,128,2048]{2,1,0:T(8,128)(2,1)}, u32[]{:S(2)}, u32[]{:S(2)}) %collective-permute-start.7) | collective-permute-done | bytes 1048608 | tf_op jit(solution)/shard_map/ppermute | solution.py:25
  51.2 0.1 broadcast_select_fusion.refs_7_
  51.3 0.0 copy-start.2
  51.3 4.5 %collective-permute-done.4 = bf16[2,128,2048]{2,1,0:T(8,128)(2,1)} collective-permute-done((bf16[2,128,2048]{2,1,0:T(8,128)(2,1)S(1)}, bf16[2,128,2048]{2,1,0:T(8,128)(2,1)}, u32[]{:S(2)}, u32[]{:S(2)}) %collective-permute-start.4) | collective-permute-done | bytes 1048608 | tf_op jit(solution)/shard_map/ppermute | solution.py:25
  55.8 20.7 %collective-permute-done.5 = bf16[2,128,2048]{2,1,0:T(8,128)(2,1)} collective-permute-done((bf16[2,128,2048]{2,1,0:T(8,128)(2,1)}, bf16[2,128,2048]{2,1,0:T(8,128)(2,1)}, u32[]{:S(2)}, u32[]{:S(2)}) %collective-permute-start.5) | collective-permute-done | bytes 1048608 | tf_op jit(solution)/shard_map/ppermute | solution.py:25
  76.5 1.3 broadcast_select_fusion.1.refs_6_
  77.9 0.0 collective-permute-done.2
  77.9 0.0 collective-permute-done.3
  77.9 0.1 broadcast_select_fusion.2.refs_5_
  78.0 1.8 copy-done.6
  79.9 3.7 %maximum_select_fusion = bf16[4,2,128,2048]{3,2,1,0:T(8,128)(2,1)} fusion(bf16[1,2,128,2048]{3,2,1,0:T(8,128)(2,1)S(1)} %bitcast.46, bf16[1,2,128,2048]{3,2,1,0:T(8,128)(2,1)S(1)} %bitcast.47, bf16[1,2,128,2048]{3,2,1,0:T(8,128)(2,1)S(1)} %bitcast.48, bf16[1,2,128,2048]{3,2,1,0:T(8,128)(2,1)S(1)} %bitcast.49, bf16[1,2,128,2048]{3,2,1,0:T(8,128)(2,1)} %bitcast.8, ...), kind=kLoop, calls=%fused_computation | loop fusion | flops 14680064 | bytes 9437185 | tf_op jit(solution)/shard_map/jit(_where)/select_n | solution.py:56
  83.5 0.0 copy-done.4
  83.6 0.5 collective-permute-start.8
  84.0 0.1 collective-permute-start
  84.1 0.0 copy-done
  84.1 0.1 broadcast_bitcast_fusion
  84.2 0.1 dynamic_slice.6
  84.3 0.1 pad_dynamic-slice_fusion
  84.4 0.2 fusion.14
  84.6 1.1 pad_maximum_fusion.refs_0_
  85.8 0.0 collective-permute-done
  85.8 5.4 %collective-permute-done.8.refs_8_ = bf16[4,2,128,2048]{3,2,1,0:T(8,128)(2,1)} collective-permute-done((bf16[4,2,128,2048]{3,2,1,0:T(8,128)(2,1)}, bf16[4,2,128,2048]{3,2,1,0:T(8,128)(2,1)}, u32[]{:S(2)}, u32[]{:S(2)}) %collective-permute-start.8) | collective-permute-done | bytes 4194336 | tf_op jit(solution)/shard_map/ppermute | solution.py:25
  91.2 25.1 %shard_map.76 = (bf16[128,4096]{1,0:T(8,128)(2,1)}, f32[2,128,2048]{2,1,0:T(8,128)}, f32[2,128,2048]{2,1,0:T(8,128)}, f32[2,128,2048]{2,1,0:T(8,128)}, f32[2,128...) custom-call(f32[256,1152]{1,0:T(8,128)} %pad_maximum_fusion.refs_0_, ...), custom_call_target="tpu_custom_call" | custom-call | flops 6039797760 | bytes 32636928 | tf_op jit(solution)/shard_map/pallas_call | solution.py:139
  116.3 0.0 copy-start.8
  116.3 0.0 copy-start.9
  116.3 0.0 copy-start.10
  116.3 0.4 collective-permute-start.9
  116.7 7.0 %collective-permute-done.9 = bf16[4,2,128,2048]{3,2,1,0:T(8,128)(2,1)S(1)} collective-permute-done((bf16[4,2,128,2048]{3,2,1,0:T(8,128)(2,1)}, bf16[4,2,128,2048]{3,2,1,0:T(8,128)(2,1)S(1)}, u32[]{:S(2)}, u32[]{:S(2)}) %collective-permute-start.9) | collective-permute-done | bytes 4194336 | tf_op jit(solution)/shard_map/ppermute | solution.py:25
  123.7 1.1 convert_element_type.43
  124.8 0.0 copy-done.8
  124.8 0.0 copy-done.9
  124.8 0.0 copy-done.10
  124.8 0.0 copy-start.11
  124.8 2.8 %fusion.6 = (bf16[2,128,2048]{2,1,0:T(8,128)(2,1)}, bf16[2,128,2048]{2,1,0:T(8,128)(2,1)S(1)}, bf16[2,128,2048]{2,1,0:T(8,128)(2,1)S(1)}) fusion(f32[2,128,2048]{2,1,0:T(8,128)S(1)} %copy-done.8, f32[4,2,128,2048]{3,2,1,0:T(8,128)S(1)} %convert_element_type.43, pred[]{:T(512)S(6)} %eq.23, f32[2,128,2048]{2,1,0:T(8,128)S(1)} %copy-done.10, ...), kind=kLoop, calls=%fused_computation.11 | loop fusion | flops 4718592 | bytes 17825792 | tf_op jit(solution)/shard_map/convert_element_type | solution.py:73
  127.7 1.3 collective-permute-start.13
  129.0 1.3 collective-permute-start.15
  130.3 1.3 collective-permute-start.14
  131.6 8.6 %collective-permute-start.10 = (bf16[2,128,2048]{2,1,0:T(8,128)(2,1)}, bf16[2,128,2048]{2,1,0:T(8,128)(2,1)S(1)}, u32[]{:S(2)}, u32[]{:S(2)}) collective-permute-start(bf16[2,128,2048]{2,1,0:T(8,128)(2,1)} %get-tuple-element.17), channel_id=1, source_target_pairs={{2,0},{3,1},{4,2},{5,3},{6,4},{7,5},{10,8},{11,9},{12,10},{13,11},... | collective-permute-start | bytes 3145736 | tf_op jit(solution)/shard_map/ppermute | solution.py:25
  140.2 3.3 %collective-permute-start.12 = (bf16[2,128,2048]{2,1,0:T(8,128)(2,1)S(1)}, bf16[2,128,2048]{2,1,0:T(8,128)(2,1)S(1)}, u32[]{:S(2)}, u32[]{:S(2)}) collective-permute-start(bf16[2,128,2048]{2,1,0:T(8,128)(2,1)S(1)} %get-tuple-element.18), channel_id=1, source_target_pairs={{6,0},{7,1},{14,8},{15,9},{22,16},{23,17},{30,24},{31,25}} | collective-permute-start | bytes 3145736 | tf_op jit(solution)/shard_map/ppermute | solution.py:25
  143.5 17.4 %collective-permute-done.13 = bf16[2,128,2048]{2,1,0:T(8,128)(2,1)S(1)} collective-permute-done((bf16[2,128,2048]{2,1,0:T(8,128)(2,1)}, bf16[2,128,2048]{2,1,0:T(8,128)(2,1)S(1)}, u32[]{:S(2)}, u32[]{:S(2)}) %collective-permute-start.13) | collective-permute-done | bytes 1048608 | tf_op jit(solution)/shard_map/ppermute | solution.py:25
  160.9 1.3 collective-permute-start.11
  162.3 0.0 collective-permute-done.15
  162.3 21.5 %collective-permute-done.14 = bf16[2,128,2048]{2,1,0:T(8,128)(2,1)S(1)} collective-permute-done((bf16[2,128,2048]{2,1,0:T(8,128)(2,1)S(1)}, bf16[2,128,2048]{2,1,0:T(8,128)(2,1)S(1)}, u32[]{:S(2)}, u32[]{:S(2)}) %collective-permute-start.14) | collective-permute-done | bytes 1048608 | tf_op jit(solution)/shard_map/ppermute | solution.py:25
  183.7 0.9 fusion.3
  184.7 1.3 collective-permute-start.16
  186.0 0.0 collective-permute-done.10
  186.0 0.0 collective-permute-done.12
  186.0 18.4 %collective-permute-done.11 = bf16[2,128,2048]{2,1,0:T(8,128)(2,1)S(1)} collective-permute-done((bf16[2,128,2048]{2,1,0:T(8,128)(2,1)S(1)}, bf16[2,128,2048]{2,1,0:T(8,128)(2,1)S(1)}, u32[]{:S(2)}, u32[]{:S(2)}) %collective-permute-start.11) | collective-permute-done | bytes 1048608 | tf_op jit(solution)/shard_map/ppermute | solution.py:25
  204.4 7.6 %collective-permute-done.16 = bf16[2,128,2048]{2,1,0:T(8,128)(2,1)S(1)} collective-permute-done((bf16[2,128,2048]{2,1,0:T(8,128)(2,1)S(1)}, bf16[2,128,2048]{2,1,0:T(8,128)(2,1)S(1)}, u32[]{:S(2)}, u32[]{:S(2)}) %collective-permute-start.16) | collective-permute-done | bytes 1048608 | tf_op jit(solution)/shard_map/ppermute | solution.py:25
  212.0 1.0 fusion.11
  213.0 1.1 fusion.15
  (16 shorter events, 0.0 us)
Async XLA Ops:
  0.6 83.5 %copy-start = (s32[1,32]{1,0:T(1,128)S(1)}, s32[1,32]{1,0:T(1,128)}, u32[]{:S(2)}) copy-start(s32[1,32]{1,0:T(1,128)} %param.9) | copy-start | bytes 388
  2.8 75.0 %copy-start.5 = (bf16[2,128,2048]{2,1,0:T(8,128)(2,1)}, bf16[2,128,2048]{2,1,0:T(8,128)(2,1)S(1)}, u32[]{:S(2)}) copy-start(bf16[2,128,2048]{2,1,0:T(8,128)(2,1)S(1)} %constant_dynamic-update-slice_fusion.refs_4_) | copy-start | bytes 3145732
  2.8 25.0 %collective-permute-start.1 = (bf16[2,128,2048]{2,1,0:T(8,128)(2,1)S(1)}, bf16[2,128,2048]{2,1,0:T(8,128)(2,1)}, u32[]{:S(2)}, u32[]{:S(2)}) collective-permute-start(bf16[2,128,2048]{2,1,0:T(8,128)(2,1)S(1)} %constant_dynamic-update-slice_fusion.refs_4_), channel_id=1, source_target_pairs={{0,8},{1,9},{2,10},{3,11},{4,12},{5,13},{6,14},{7,15},{8,16},{9,17... | collective-permute-start | bytes 3145736 | tf_op jit(solution)/shard_map/ppermute | solution.py:25
  7.0 32.5 %collective-permute-start.6 = (bf16[2,128,2048]{2,1,0:T(8,128)(2,1)S(1)}, bf16[2,128,2048]{2,1,0:T(8,128)(2,1)S(1)}, u32[]{:S(2)}, u32[]{:S(2)}) collective-permute-start(bf16[2,128,2048]{2,1,0:T(8,128)(2,1)S(1)} %constant_dynamic-update-slice_fusion.refs_4_), channel_id=1, source_target_pairs={{0,6},{1,7},{8,14},{9,15},{16,22},{17,23},{24,30},{25,31}} | collective-permute-start | bytes 3145736 | tf_op jit(solution)/shard_map/ppermute | solution.py:25
  27.8 23.4 %collective-permute-start.7 = (bf16[2,128,2048]{2,1,0:T(8,128)(2,1)}, bf16[2,128,2048]{2,1,0:T(8,128)(2,1)}, u32[]{:S(2)}, u32[]{:S(2)}) collective-permute-start(bf16[2,128,2048]{2,1,0:T(8,128)(2,1)} %collective-permute-done.1.refs_3_), channel_id=1, source_target_pairs={{2,0},{3,1},{4,2},{5,3},{6,4},{7,5},{10,8},{11,9},{12,10},{13,11},... | collective-permute-start | bytes 3145736 | tf_op jit(solution)/shard_map/ppermute | solution.py:25
  31.0 24.8 %collective-permute-start.4 = (bf16[2,128,2048]{2,1,0:T(8,128)(2,1)S(1)}, bf16[2,128,2048]{2,1,0:T(8,128)(2,1)}, u32[]{:S(2)}, u32[]{:S(2)}) collective-permute-start(bf16[2,128,2048]{2,1,0:T(8,128)(2,1)S(1)} %constant_dynamic-update-slice_fusion.refs_4_), channel_id=1, source_target_pairs={{0,4},{1,5},{2,6},{3,7},{8,12},{9,13},{10,14},{11,15},{16,20},{17,... | collective-permute-start | bytes 3145736 | tf_op jit(solution)/shard_map/ppermute | solution.py:25
  32.3 44.2 %collective-permute-start.5 = (bf16[2,128,2048]{2,1,0:T(8,128)(2,1)}, bf16[2,128,2048]{2,1,0:T(8,128)(2,1)}, u32[]{:S(2)}, u32[]{:S(2)}) collective-permute-start(bf16[2,128,2048]{2,1,0:T(8,128)(2,1)} %collective-permute-done.1.refs_3_), channel_id=1, source_target_pairs={{4,0},{5,1},{6,2},{7,3},{12,8},{13,9},{14,10},{15,11},{20,16},{21,... | collective-permute-start | bytes 3145736 | tf_op jit(solution)/shard_map/ppermute | solution.py:25
  38.2 39.7 %collective-permute-start.2 = (bf16[2,128,2048]{2,1,0:T(8,128)(2,1)S(1)}, bf16[2,128,2048]{2,1,0:T(8,128)(2,1)S(1)}, u32[]{:S(2)}, u32[]{:S(2)}) collective-permute-start(bf16[2,128,2048]{2,1,0:T(8,128)(2,1)S(1)} %constant_dynamic-update-slice_fusion.refs_4_), channel_id=1, source_target_pairs={{0,2},{1,3},{2,4},{3,5},{4,6},{5,7},{8,10},{9,11},{10,12},{11,13},... | collective-permute-start | bytes 3145736 | tf_op jit(solution)/shard_map/ppermute | solution.py:25
  39.6 38.3 %collective-permute-start.3 = (bf16[2,128,2048]{2,1,0:T(8,128)(2,1)}, bf16[2,128,2048]{2,1,0:T(8,128)(2,1)S(1)}, u32[]{:S(2)}, u32[]{:S(2)}) collective-permute-start(bf16[2,128,2048]{2,1,0:T(8,128)(2,1)} %collective-permute-done.1.refs_3_), channel_id=1, source_target_pairs={{6,0},{7,1},{14,8},{15,9},{22,16},{23,17},{30,24},{31,25}} | collective-permute-start | bytes 3145736 | tf_op jit(solution)/shard_map/ppermute | solution.py:25
  51.3 26.7 %copy-start.2 = (bf16[2,128,2048]{2,1,0:T(8,128)(2,1)}, bf16[2,128,2048]{2,1,0:T(8,128)(2,1)S(1)}, u32[]{:S(2)}) copy-start(bf16[2,128,2048]{2,1,0:T(8,128)(2,1)S(1)} %broadcast_select_fusion.refs_7_) | copy-start | bytes 3145732
  77.9 5.7 %copy-start.3 = (bf16[2,128,2048]{2,1,0:T(8,128)(2,1)}, bf16[2,128,2048]{2,1,0:T(8,128)(2,1)S(1)}, u32[]{:S(2)}) copy-start(bf16[2,128,2048]{2,1,0:T(8,128)(2,1)S(1)} %broadcast_select_fusion.1.refs_6_) | copy-start | bytes 3145732
  77.9 2.0 copy-start.6
  78.0 5.5 %copy-start.4 = (bf16[2,128,2048]{2,1,0:T(8,128)(2,1)}, bf16[2,128,2048]{2,1,0:T(8,128)(2,1)S(1)}, u32[]{:S(2)}) copy-start(bf16[2,128,2048]{2,1,0:T(8,128)(2,1)S(1)} %broadcast_select_fusion.2.refs_5_) | copy-start | bytes 3145732
  79.9 4.2 %copy-start.12 = (bf16[1,128,4096]{2,1,0:T(8,128)(2,1)S(1)}, bf16[1,128,4096]{2,1,0:T(8,128)(2,1)}, u32[]{:S(2)}) copy-start(bf16[1,128,4096]{2,1,0:T(8,128)(2,1)} %param.8) | copy-start | bytes 3145732
  83.6 7.6 %collective-permute-start.8 = (bf16[4,2,128,2048]{3,2,1,0:T(8,128)(2,1)}, bf16[4,2,128,2048]{3,2,1,0:T(8,128)(2,1)}, u32[]{:S(2)}, u32[]{:S(2)}) collective-permute-start(bf16[4,2,128,2048]{3,2,1,0:T(8,128)(2,1)} %maximum_select_fusion), channel_id=1, source_target_pairs={{0,1},{1,0},{2,3},{3,2},{4,5},{5,4},{6,7},{7,6},{8,9},{9,8},{10,11... | collective-permute-start | bytes 12582920 | tf_op jit(solution)/shard_map/ppermute | solution.py:25
  84.0 1.7 collective-permute-start
  85.8 5.4 %copy-start.13 = (bf16[1,128,4096]{2,1,0:T(8,128)(2,1)}, bf16[1,128,4096]{2,1,0:T(8,128)(2,1)S(1)}, u32[]{:S(2)}) copy-start(bf16[1,128,4096]{2,1,0:T(8,128)(2,1)S(1)} %collective-permute-done) | copy-start | bytes 3145732
  116.3 8.5 %copy-start.8 = (f32[2,128,2048]{2,1,0:T(8,128)S(1)}, f32[2,128,2048]{2,1,0:T(8,128)}, u32[]{:S(2)}) copy-start(f32[2,128,2048]{2,1,0:T(8,128)} %get-tuple-element.13) | copy-start | bytes 6291460
  116.3 8.5 %copy-start.9 = (f32[2,128,2048]{2,1,0:T(8,128)S(1)}, f32[2,128,2048]{2,1,0:T(8,128)}, u32[]{:S(2)}) copy-start(f32[2,128,2048]{2,1,0:T(8,128)} %get-tuple-element.14) | copy-start | bytes 6291460
  116.3 8.5 %copy-start.10 = (f32[2,128,2048]{2,1,0:T(8,128)S(1)}, f32[2,128,2048]{2,1,0:T(8,128)}, u32[]{:S(2)}) copy-start(f32[2,128,2048]{2,1,0:T(8,128)} %get-tuple-element.15) | copy-start | bytes 6291460
  116.3 7.4 %collective-permute-start.9 = (bf16[4,2,128,2048]{3,2,1,0:T(8,128)(2,1)}, bf16[4,2,128,2048]{3,2,1,0:T(8,128)(2,1)S(1)}, u32[]{:S(2)}, u32[]{:S(2)}) collective-permute-start(bf16[4,2,128,2048]{3,2,1,0:T(8,128)(2,1)} %get-tuple-element.12), channel_id=1, source_target_pairs={{0,1},{1,0},{2,3},{3,2},{4,5},{5,4},{6,7},{7,6},{8,9},{9,8},{10,11... | collective-permute-start | bytes 12582920 | tf_op jit(solution)/shard_map/ppermute | solution.py:25
  124.8 58.9 %copy-start.11 = (f32[2,128,2048]{2,1,0:T(8,128)S(1)}, f32[2,128,2048]{2,1,0:T(8,128)}, u32[]{:S(2)}) copy-start(f32[2,128,2048]{2,1,0:T(8,128)} %get-tuple-element.16) | copy-start | bytes 6291460
  127.7 33.2 %collective-permute-start.13 = (bf16[2,128,2048]{2,1,0:T(8,128)(2,1)}, bf16[2,128,2048]{2,1,0:T(8,128)(2,1)S(1)}, u32[]{:S(2)}, u32[]{:S(2)}) collective-permute-start(bf16[2,128,2048]{2,1,0:T(8,128)(2,1)} %get-tuple-element.17), channel_id=1, source_target_pairs={{0,6},{1,7},{8,14},{9,15},{16,22},{17,23},{24,30},{25,31}} | collective-permute-start | bytes 3145736 | tf_op jit(solution)/shard_map/ppermute | solution.py:25
  129.0 33.3 %collective-permute-start.15 = (bf16[2,128,2048]{2,1,0:T(8,128)(2,1)S(1)}, bf16[2,128,2048]{2,1,0:T(8,128)(2,1)S(1)}, u32[]{:S(2)}, u32[]{:S(2)}) collective-permute-start(bf16[2,128,2048]{2,1,0:T(8,128)(2,1)S(1)} %get-tuple-element.18), channel_id=1, source_target_pairs={{0,2},{1,3},{2,4},{3,5},{4,6},{5,7},{8,10},{9,11},{10,12},{11,13},... | collective-permute-start | bytes 3145736 | tf_op jit(solution)/shard_map/ppermute | solution.py:25
  130.3 53.5 %collective-permute-start.14 = (bf16[2,128,2048]{2,1,0:T(8,128)(2,1)S(1)}, bf16[2,128,2048]{2,1,0:T(8,128)(2,1)S(1)}, u32[]{:S(2)}, u32[]{:S(2)}) collective-permute-start(bf16[2,128,2048]{2,1,0:T(8,128)(2,1)S(1)} %get-tuple-element.19), channel_id=1, source_target_pairs={{0,4},{1,5},{2,6},{3,7},{8,12},{9,13},{10,14},{11,15},{16,20},{17,... | collective-permute-start | bytes 3145736 | tf_op jit(solution)/shard_map/ppermute | solution.py:25
  131.6 54.4 %collective-permute-start.10 = (bf16[2,128,2048]{2,1,0:T(8,128)(2,1)}, bf16[2,128,2048]{2,1,0:T(8,128)(2,1)S(1)}, u32[]{:S(2)}, u32[]{:S(2)}) collective-permute-start(bf16[2,128,2048]{2,1,0:T(8,128)(2,1)} %get-tuple-element.17), channel_id=1, source_target_pairs={{2,0},{3,1},{4,2},{5,3},{6,4},{7,5},{10,8},{11,9},{12,10},{13,11},... | collective-permute-start | bytes 3145736 | tf_op jit(solution)/shard_map/ppermute | solution.py:25
  140.2 45.8 %collective-permute-start.12 = (bf16[2,128,2048]{2,1,0:T(8,128)(2,1)S(1)}, bf16[2,128,2048]{2,1,0:T(8,128)(2,1)S(1)}, u32[]{:S(2)}, u32[]{:S(2)}) collective-permute-start(bf16[2,128,2048]{2,1,0:T(8,128)(2,1)S(1)} %get-tuple-element.18), channel_id=1, source_target_pairs={{6,0},{7,1},{14,8},{15,9},{22,16},{23,17},{30,24},{31,25}} | collective-permute-start | bytes 3145736 | tf_op jit(solution)/shard_map/ppermute | solution.py:25
  160.9 43.5 %collective-permute-start.11 = (bf16[2,128,2048]{2,1,0:T(8,128)(2,1)S(1)}, bf16[2,128,2048]{2,1,0:T(8,128)(2,1)S(1)}, u32[]{:S(2)}, u32[]{:S(2)}) collective-permute-start(bf16[2,128,2048]{2,1,0:T(8,128)(2,1)S(1)} %get-tuple-element.19), channel_id=1, source_target_pairs={{4,0},{5,1},{6,2},{7,3},{12,8},{13,9},{14,10},{15,11},{20,16},{21,... | collective-permute-start | bytes 3145736 | tf_op jit(solution)/shard_map/ppermute | solution.py:25
  183.7 28.3 %copy-start.7 = (f32[2,128,2048]{2,1,0:T(8,128)S(1)}, f32[2,128,2048]{2,1,0:T(8,128)}, u32[]{:S(2)}) copy-start(f32[2,128,2048]{2,1,0:T(8,128)} %get-tuple-element.11) | copy-start | bytes 6291460
  184.7 27.3 %collective-permute-start.16 = (bf16[2,128,2048]{2,1,0:T(8,128)(2,1)S(1)}, bf16[2,128,2048]{2,1,0:T(8,128)(2,1)S(1)}, u32[]{:S(2)}, u32[]{:S(2)}) collective-permute-start(bf16[2,128,2048]{2,1,0:T(8,128)(2,1)S(1)} %fusion.3), channel_id=1, source_target_pairs={{8,0},{9,1},{10,2},{11,3},{12,4},{13,5},{14,6},{15,7},{16,8},{17,9... | collective-permute-start | bytes 3145736 | tf_op jit(solution)/shard_map/ppermute | solution.py:25
  212.0 2.1 copy-start.1

commit v4 on v3

--- a/solution.py
+++ b/solution.py
@@ -68,10 +68,10 @@
     sums = [direct[e] + jnp.where(is_even, back[e], back[e - 1]) for e in range(1, chips)]
     for e in range(1, chips):
         sent = sums[e - 1].astype(link)
-        prev = prev + moved(sent, reverse(routes.down[e - 1])).astype(jnp.float32)
-    for e in range(1, chips):
-        sent = sums[e - 1].astype(link)
-        own = own + moved(sent, reverse(routes.up[e - 1])).astype(jnp.float32)
+        got = moved(sent, reverse(routes.up[e - 1] + routes.down[e - 1])).astype(jnp.float32)
+        upward = chip_in_group + e < chips
+        own = own + jnp.where(upward, got, 0.0)
+        prev = prev + jnp.where(upward, 0.0, got)
     own = own + moved(prev.astype(link), reverse(routes.hop)).astype(jnp.float32)
     return own
 
@@ -155,7 +155,9 @@
 def local(queries, key_rows, value_rows, arriving_grad, doc_blocks):
     tokens = queries.shape[1]
     count = lax.axis_size("seq")
-    grad_out = passed_along(arriving_grad, "pipe", -1)[0]
+    if lax.axis_size("pipe") > 1:
+        arriving_grad = passed_along(arriving_grad, "pipe", -1)
+    grad_out = arriving_grad[0]
     position = lax.axis_index("seq")
     reach_back = (WINDOW - 1) // tokens + 1
     assert reach_back % 2 == 0 and count % reach_back == 0 and WINDOW % tokens == 0

time: 217 us -> 220 us (1.014)
  starting transfers between devices: 38.8 us -> 30.3 us
  other arithmetic: 12.6 us -> 18.1 us
  waiting for transfers between devices: 131 us -> 136 us
    ppermute x16 -> x13, starting transfers between devices: 38.7 us -> 30.3 us  [moved(): return lax.ppermute(value, 'seq', pairs)]
    ppermute x16 -> x13, waiting for transfers between devices: 131 us -> 136 us  [moved(): return lax.ppermute(value, 'seq', pairs)]
    convert_element_type x1, other arithmetic: 0.93 us -> 3.34 us  [scatter_window(): prev.astype(link)]
  transfers between devices with their start and end apart: 17 -> 13, of which waited for: 10 -> 9; matrix products, arithmetic and copies ran while one was open for 2% -> 2% of each run, Pallas kernels for 0% -> 0%
where the time goes in v4:
time: 220 us; the launch traced here: 216 us
  waiting for transfers between devices  136 us (62%)
  starting transfers between devices  30.3 us (14%)
  Pallas kernels  25.1 us (11%)
  other arithmetic  18.1 us (8%)
  local copies, waits for them, and re-layouts  5.23 us (2%)
    ppermute x13, waiting for transfers between devices, moved(): return lax.ppermute(value, 'seq', pairs)  136 us
    ppermute x13, starting transfers between devices, moved(): return lax.ppermute(value, 'seq', pairs)  30.3 us
    pallas_call x1, Pallas kernels, attention_grads(): pl.pallas_call(lambda *refs: attention_kernel(chips, per_step, *refs), gr...  25.1 us
  transfers between devices with their start and end apart: 13, of which 9 were waited for; matrix products, arithmetic and copies ran while one was open for 2% of the time, Pallas kernels for 0%

profile of v4, /device:TPU:7, one launch (start us, length us, event | category | flops | bytes accessed | tf_op | source)
XLA Modules:
  0.0 215.6 jit_solution(7573692241070527938)
XLA Ops:
  0.6 0.0 copy-start
  0.6 1.1 constant_dynamic-update-slice_fusion.1
  1.7 1.1 constant_dynamic-update-slice_fusion.refs_4_
  2.8 0.0 copy-start.5
  2.8 3.3 %collective-permute-start = (bf16[2,128,2048]{2,1,0:T(8,128)(2,1)S(1)}, bf16[2,128,2048]{2,1,0:T(8,128)(2,1)S(1)}, u32[]{:S(2)}, u32[]{:S(2)}) collective-permute-start(bf16[2,128,2048]{2,1,0:T(8,128)(2,1)S(1)} %constant_dynamic-update-slice_fusion.refs_4_), channel_id=1, source_target_pairs={{0,8},{1,9},{2,10},{3,11},{4,12},{5,13},{6,14},{7,15},{8,16},{9,17... | collective-permute-start | bytes 3145736 | tf_op jit(solution)/shard_map/ppermute | solution.py:25
  6.1 1.3 collective-permute-start.3
  7.4 20.4 %collective-permute-done.refs_3_ = bf16[2,128,2048]{2,1,0:T(8,128)(2,1)S(1)} collective-permute-done((bf16[2,128,2048]{2,1,0:T(8,128)(2,1)S(1)}, bf16[2,128,2048]{2,1,0:T(8,128)(2,1)S(1)}, u32[]{:S(2)}, u32[]{:S(2)}) %collective-permute-start) | collective-permute-done | bytes 1048608 | tf_op jit(solution)/shard_map/ppermute | solution.py:25
  27.8 3.1 %collective-permute-start.4 = (bf16[2,128,2048]{2,1,0:T(8,128)(2,1)S(1)}, bf16[2,128,2048]{2,1,0:T(8,128)(2,1)}, u32[]{:S(2)}, u32[]{:S(2)}) collective-permute-start(bf16[2,128,2048]{2,1,0:T(8,128)(2,1)S(1)} %collective-permute-done.refs_3_), channel_id=1, source_target_pairs={{4,0},{5,1},{6,2},{7,3},{12,8},{13,9},{14,10},{15,11},{20,16},{21,... | collective-permute-start | bytes 3145736 | tf_op jit(solution)/shard_map/ppermute | solution.py:25
  30.9 1.3 collective-permute-start.5
  32.2 3.5 %collective-permute-start.6 = (bf16[2,128,2048]{2,1,0:T(8,128)(2,1)S(1)}, bf16[2,128,2048]{2,1,0:T(8,128)(2,1)}, u32[]{:S(2)}, u32[]{:S(2)}) collective-permute-start(bf16[2,128,2048]{2,1,0:T(8,128)(2,1)S(1)} %collective-permute-done.refs_3_), channel_id=1, source_target_pairs={{2,0},{3,1},{4,2},{5,3},{6,4},{7,5},{10,8},{11,9},{12,10},{13,11},... | collective-permute-start | bytes 3145736 | tf_op jit(solution)/shard_map/ppermute | solution.py:25
  35.7 1.3 collective-permute-start.1
  37.0 0.0 collective-permute-done.3
  37.0 6.5 %collective-permute-start.2 = (bf16[2,128,2048]{2,1,0:T(8,128)(2,1)S(1)}, bf16[2,128,2048]{2,1,0:T(8,128)(2,1)S(1)}, u32[]{:S(2)}, u32[]{:S(2)}) collective-permute-start(bf16[2,128,2048]{2,1,0:T(8,128)(2,1)S(1)} %collective-permute-done.refs_3_), channel_id=1, source_target_pairs={{6,0},{7,1},{14,8},{15,9},{22,16},{23,17},{30,24},{31,25}} | collective-permute-start | bytes 3145736 | tf_op jit(solution)/shard_map/ppermute | solution.py:25
  43.5 29.8 %collective-permute-done.4 = bf16[2,128,2048]{2,1,0:T(8,128)(2,1)} collective-permute-done((bf16[2,128,2048]{2,1,0:T(8,128)(2,1)S(1)}, bf16[2,128,2048]{2,1,0:T(8,128)(2,1)}, u32[]{:S(2)}, u32[]{:S(2)}) %collective-permute-start.4) | collective-permute-done | bytes 1048608 | tf_op jit(solution)/shard_map/ppermute | solution.py:25
  73.3 1.3 broadcast_select_fusion.1.refs_6_
  74.7 0.0 copy-start.2
  74.7 0.0 collective-permute-done.5
  74.7 0.0 collective-permute-done.6
  74.7 1.7 broadcast_select_fusion.refs_7_
  76.4 0.0 copy-done.5
  76.4 0.0 copy-start.3
  76.4 2.5 %collective-permute-done.1 = bf16[2,128,2048]{2,1,0:T(8,128)(2,1)S(1)} collective-permute-done((bf16[2,128,2048]{2,1,0:T(8,128)(2,1)S(1)}, bf16[2,128,2048]{2,1,0:T(8,128)(2,1)S(1)}, u32[]{:S(2)}, u32[]{:S(2)}) %collective-permute-start.1) | collective-permute-done | bytes 1048608 | tf_op jit(solution)/shard_map/ppermute | solution.py:25
  78.9 0.0 collective-permute-done.2
  78.9 0.1 broadcast_select_fusion.2.refs_5_
  79.0 0.0 copy-start.4
  79.0 0.0 copy-done.11
  79.0 0.0 copy-done.2
  79.0 1.5 copy-done.6
  80.5 2.5 %maximum_select_fusion = bf16[4,2,128,2048]{3,2,1,0:T(8,128)(2,1)} fusion(bf16[1,2,128,2048]{3,2,1,0:T(8,128)(2,1)S(1)} %bitcast.33, bf16[1,2,128,2048]{3,2,1,0:T(8,128)(2,1)S(1)} %bitcast.32, bf16[1,2,128,2048]{3,2,1,0:T(8,128)(2,1)S(1)} %bitcast.34, bf16[1,2,128,2048]{3,2,1,0:T(8,128)(2,1)S(1)} %bitcast.35, bf16[1,2,128,2048]{3,2,1,0:T(8,128)(2,1)S(1)} %bitcast.36, ...), kind=kLoop, calls=%fused_computation | loop fusion | flops 14680064 | bytes 9437185 | tf_op jit(solution)/shard_map/jit(_where)/select_n | solution.py:56
  83.0 0.0 copy-done.3
  83.0 0.0 copy-done.4
  83.0 2.4 %collective-permute-start.7 = (bf16[4,2,128,2048]{3,2,1,0:T(8,128)(2,1)}, bf16[4,2,128,2048]{3,2,1,0:T(8,128)(2,1)}, u32[]{:S(2)}, u32[]{:S(2)}) collective-permute-start(bf16[4,2,128,2048]{3,2,1,0:T(8,128)(2,1)} %maximum_select_fusion), channel_id=1, source_target_pairs={{0,1},{1,0},{2,3},{3,2},{4,5},{5,4},{6,7},{7,6},{8,9},{9,8},{10,11... | collective-permute-start | bytes 12582920 | tf_op jit(solution)/shard_map/ppermute | solution.py:25
  85.5 0.0 copy-done
  85.5 0.1 broadcast_bitcast_fusion
  85.5 0.1 dynamic_slice.6
  85.6 0.1 pad_dynamic-slice_fusion
  85.7 0.2 fusion.14
  86.0 1.1 pad_maximum_fusion.refs_0_
  87.1 5.5 %collective-permute-done.7.refs_8_ = bf16[4,2,128,2048]{3,2,1,0:T(8,128)(2,1)} collective-permute-done((bf16[4,2,128,2048]{3,2,1,0:T(8,128)(2,1)}, bf16[4,2,128,2048]{3,2,1,0:T(8,128)(2,1)}, u32[]{:S(2)}, u32[]{:S(2)}) %collective-permute-start.7) | collective-permute-done | bytes 4194336 | tf_op jit(solution)/shard_map/ppermute | solution.py:25
  92.6 25.1 %shard_map.76 = (bf16[128,4096]{1,0:T(8,128)(2,1)}, f32[2,128,2048]{2,1,0:T(8,128)}, f32[2,128,2048]{2,1,0:T(8,128)}, f32[2,128,2048]{2,1,0:T(8,128)}, f32[2,128...) custom-call(f32[256,1152]{1,0:T(8,128)} %pad_maximum_fusion.refs_0_, ...), custom_call_target="tpu_custom_call" | custom-call | flops 6039797760 | bytes 32636928 | tf_op jit(solution)/shard_map/pallas_call | solution.py:139
  117.7 0.0 copy-start.8
  117.7 0.0 copy-start.9
  117.7 0.0 copy-start.10
  117.7 0.4 collective-permute-start.8
  118.2 7.0 %collective-permute-done.8 = bf16[4,2,128,2048]{3,2,1,0:T(8,128)(2,1)S(1)} collective-permute-done((bf16[4,2,128,2048]{3,2,1,0:T(8,128)(2,1)}, bf16[4,2,128,2048]{3,2,1,0:T(8,128)(2,1)S(1)}, u32[]{:S(2)}, u32[]{:S(2)}) %collective-permute-start.8) | collective-permute-done | bytes 4194336 | tf_op jit(solution)/shard_map/ppermute | solution.py:25
  125.2 1.0 convert_element_type.31
  126.2 0.0 copy-start.1
  126.2 0.0 copy-done.8
  126.2 0.0 copy-done.9
  126.3 0.0 copy-done.10
  126.3 3.9 %fusion.9 = (bf16[2,128,2048]{2,1,0:T(8,128)(2,1)}, bf16[2,128,2048]{2,1,0:T(8,128)(2,1)}, bf16[2,128,2048]{2,1,0:T(8,128)(2,1)}) fusion(f32[2,128,2048]{2,1,0:T(8,128)S(1)} %copy-done.10, f32[4,2,128,2048]{3,2,1,0:T(8,128)S(1)} %convert_element_type.31, pred[]{:T(512)S(6)} %eq.23, f32[2,128,2048]{2,1,0:T(8,128)S(1)} %copy-done.9, ...), kind=kLoop, calls=%fused_computation.18 | loop fusion | flops 4718592 | bytes 17825792 | tf_op jit(solution)/shard_map/convert_element_type | solution.py:70
  130.2 0.3 copy-done.1
  130.5 2.8 %collective-permute-start.10 = (bf16[2,128,2048]{2,1,0:T(8,128)(2,1)}, bf16[2,128,2048]{2,1,0:T(8,128)(2,1)S(1)}, u32[]{:S(2)}, u32[]{:S(2)}) collective-permute-start(bf16[2,128,2048]{2,1,0:T(8,128)(2,1)} %get-tuple-element.18), channel_id=1, source_target_pairs={{4,0},{5,1},{6,2},{7,3},{12,8},{13,9},{14,10},{15,11},{20,16},{21,... | collective-permute-start | bytes 3145736 | tf_op jit(solution)/shard_map/ppermute | solution.py:25
  133.4 3.1 %collective-permute-start.11 = (bf16[2,128,2048]{2,1,0:T(8,128)(2,1)}, bf16[2,128,2048]{2,1,0:T(8,128)(2,1)S(1)}, u32[]{:S(2)}, u32[]{:S(2)}) collective-permute-start(bf16[2,128,2048]{2,1,0:T(8,128)(2,1)} %get-tuple-element.17), channel_id=1, source_target_pairs={{6,0},{7,1},{14,8},{15,9},{22,16},{23,17},{30,24},{31,25},{0,2},{1... | collective-permute-start | bytes 3145736 | tf_op jit(solution)/shard_map/ppermute | solution.py:25
  136.5 0.0 collective-permute-start.9
  136.5 20.3 %collective-permute-done.10 = bf16[2,128,2048]{2,1,0:T(8,128)(2,1)S(1)} collective-permute-done((bf16[2,128,2048]{2,1,0:T(8,128)(2,1)}, bf16[2,128,2048]{2,1,0:T(8,128)(2,1)S(1)}, u32[]{:S(2)}, u32[]{:S(2)}) %collective-permute-start.10) | collective-permute-done | bytes 1048608 | tf_op jit(solution)/shard_map/ppermute | solution.py:25
  156.8 2.0 collective-permute-done.11
  158.8 23.3 %collective-permute-done.9 = bf16[2,128,2048]{2,1,0:T(8,128)(2,1)S(1)} collective-permute-done((bf16[2,128,2048]{2,1,0:T(8,128)(2,1)}, bf16[2,128,2048]{2,1,0:T(8,128)(2,1)S(1)}, u32[]{:S(2)}, u32[]{:S(2)}) %collective-permute-start.9) | collective-permute-done | bytes 1048608 | tf_op jit(solution)/shard_map/ppermute | solution.py:25
  182.1 3.3 %fusion.8 = bf16[2,128,2048]{2,1,0:T(8,128)(2,1)S(1)} fusion(bf16[2,128,2048]{2,1,0:T(8,128)(2,1)S(1)} %collective-permute-done.9, bf16[2,128,2048]{2,1,0:T(8,128)(2,1)S(1)} %collective-permute-done.10, bf16[2,128,2048]{2,1,0:T(8,128)(2,1)S(1)} %collective-permute-done.11, f32[2,128,2048]{2,1,0:T(8,128)} %get-tuple-element.16, ...), kind=kLoop, calls=%fused_computation.15 | loop fusion | flops 6291456 | bytes 8388612 | tf_op jit(solution)/shard_map/convert_element_type | solution.py:75
  185.4 1.3 collective-permute-start.12
  186.7 25.1 %collective-permute-done.12 = bf16[2,128,2048]{2,1,0:T(8,128)(2,1)S(1)} collective-permute-done((bf16[2,128,2048]{2,1,0:T(8,128)(2,1)S(1)}, bf16[2,128,2048]{2,1,0:T(8,128)(2,1)S(1)}, u32[]{:S(2)}, u32[]{:S(2)}) %collective-permute-start.12) | collective-permute-done | bytes 1048608 | tf_op jit(solution)/shard_map/ppermute | solution.py:25
  211.8 0.0 copy-done.7
  211.8 2.7 %fusion.4 = bf16[2,128,2048]{2,1,0:T(8,128)(2,1)S(1)} fusion(bf16[2,128,2048]{2,1,0:T(8,128)(2,1)S(1)} %collective-permute-done.9, bf16[2,128,2048]{2,1,0:T(8,128)(2,1)S(1)} %collective-permute-done.10, bf16[2,128,2048]{2,1,0:T(8,128)(2,1)S(1)} %collective-permute-done.11, f32[2,128,2048]{2,1,0:T(8,128)S(1)} %copy-done.7, ...), kind=kLoop, calls=%fused_computation.11 | loop fusion | flops 7340032 | bytes 9437188 | tf_op jit(solution)/shard_map/convert.1
  214.5 1.1 fusion.15
  (4 shorter events, 0.0 us)
Async XLA Ops:
  0.6 84.8 %copy-start = (s32[1,32]{1,0:T(1,128)S(1)}, s32[1,32]{1,0:T(1,128)}, u32[]{:S(2)}) copy-start(s32[1,32]{1,0:T(1,128)} %param.9) | copy-start | bytes 388
  2.8 73.6 %copy-start.5 = (bf16[2,128,2048]{2,1,0:T(8,128)(2,1)}, bf16[2,128,2048]{2,1,0:T(8,128)(2,1)S(1)}, u32[]{:S(2)}) copy-start(bf16[2,128,2048]{2,1,0:T(8,128)(2,1)S(1)} %constant_dynamic-update-slice_fusion.refs_4_) | copy-start | bytes 3145732
  2.8 25.0 %collective-permute-start = (bf16[2,128,2048]{2,1,0:T(8,128)(2,1)S(1)}, bf16[2,128,2048]{2,1,0:T(8,128)(2,1)S(1)}, u32[]{:S(2)}, u32[]{:S(2)}) collective-permute-start(bf16[2,128,2048]{2,1,0:T(8,128)(2,1)S(1)} %constant_dynamic-update-slice_fusion.refs_4_), channel_id=1, source_target_pairs={{0,8},{1,9},{2,10},{3,11},{4,12},{5,13},{6,14},{7,15},{8,16},{9,17... | collective-permute-start | bytes 3145736 | tf_op jit(solution)/shard_map/ppermute | solution.py:25
  6.1 30.9 %collective-permute-start.3 = (bf16[2,128,2048]{2,1,0:T(8,128)(2,1)S(1)}, bf16[2,128,2048]{2,1,0:T(8,128)(2,1)}, u32[]{:S(2)}, u32[]{:S(2)}) collective-permute-start(bf16[2,128,2048]{2,1,0:T(8,128)(2,1)S(1)} %constant_dynamic-update-slice_fusion.refs_4_), channel_id=1, source_target_pairs={{0,4},{1,5},{2,6},{3,7},{8,12},{9,13},{10,14},{11,15},{16,20},{17,... | collective-permute-start | bytes 3145736 | tf_op jit(solution)/shard_map/ppermute | solution.py:25
  27.8 51.2 %copy-start.11 = (bf16[2,128,2048]{2,1,0:T(8,128)(2,1)}, bf16[2,128,2048]{2,1,0:T(8,128)(2,1)S(1)}, u32[]{:S(2)}) copy-start(bf16[2,128,2048]{2,1,0:T(8,128)(2,1)S(1)} %collective-permute-done.refs_3_) | copy-start | bytes 3145732
  27.8 45.5 %collective-permute-start.4 = (bf16[2,128,2048]{2,1,0:T(8,128)(2,1)S(1)}, bf16[2,128,2048]{2,1,0:T(8,128)(2,1)}, u32[]{:S(2)}, u32[]{:S(2)}) collective-permute-start(bf16[2,128,2048]{2,1,0:T(8,128)(2,1)S(1)} %collective-permute-done.refs_3_), channel_id=1, source_target_pairs={{4,0},{5,1},{6,2},{7,3},{12,8},{13,9},{14,10},{15,11},{20,16},{21,... | collective-permute-start | bytes 3145736 | tf_op jit(solution)/shard_map/ppermute | solution.py:25
  30.9 43.7 %collective-permute-start.5 = (bf16[2,128,2048]{2,1,0:T(8,128)(2,1)S(1)}, bf16[2,128,2048]{2,1,0:T(8,128)(2,1)}, u32[]{:S(2)}, u32[]{:S(2)}) collective-permute-start(bf16[2,128,2048]{2,1,0:T(8,128)(2,1)S(1)} %constant_dynamic-update-slice_fusion.refs_4_), channel_id=1, source_target_pairs={{0,6},{1,7},{8,14},{9,15},{16,22},{17,23},{24,30},{25,31}} | collective-permute-start | bytes 3145736 | tf_op jit(solution)/shard_map/ppermute | solution.py:25
  32.2 42.5 %collective-permute-start.6 = (bf16[2,128,2048]{2,1,0:T(8,128)(2,1)S(1)}, bf16[2,128,2048]{2,1,0:T(8,128)(2,1)}, u32[]{:S(2)}, u32[]{:S(2)}) collective-permute-start(bf16[2,128,2048]{2,1,0:T(8,128)(2,1)S(1)} %collective-permute-done.refs_3_), channel_id=1, source_target_pairs={{2,0},{3,1},{4,2},{5,3},{6,4},{7,5},{10,8},{11,9},{12,10},{13,11},... | collective-permute-start | bytes 3145736 | tf_op jit(solution)/shard_map/ppermute | solution.py:25
  35.7 43.2 %collective-permute-start.1 = (bf16[2,128,2048]{2,1,0:T(8,128)(2,1)S(1)}, bf16[2,128,2048]{2,1,0:T(8,128)(2,1)S(1)}, u32[]{:S(2)}, u32[]{:S(2)}) collective-permute-start(bf16[2,128,2048]{2,1,0:T(8,128)(2,1)S(1)} %constant_dynamic-update-slice_fusion.refs_4_), channel_id=1, source_target_pairs={{0,2},{1,3},{2,4},{3,5},{4,6},{5,7},{8,10},{9,11},{10,12},{11,13},... | collective-permute-start | bytes 3145736 | tf_op jit(solution)/shard_map/ppermute | solution.py:25
  37.0 41.9 %collective-permute-start.2 = (bf16[2,128,2048]{2,1,0:T(8,128)(2,1)S(1)}, bf16[2,128,2048]{2,1,0:T(8,128)(2,1)S(1)}, u32[]{:S(2)}, u32[]{:S(2)}) collective-permute-start(bf16[2,128,2048]{2,1,0:T(8,128)(2,1)S(1)} %collective-permute-done.refs_3_), channel_id=1, source_target_pairs={{6,0},{7,1},{14,8},{15,9},{22,16},{23,17},{30,24},{31,25}} | collective-permute-start | bytes 3145736 | tf_op jit(solution)/shard_map/ppermute | solution.py:25
  74.7 4.4 %copy-start.2 = (bf16[2,128,2048]{2,1,0:T(8,128)(2,1)}, bf16[2,128,2048]{2,1,0:T(8,128)(2,1)S(1)}, u32[]{:S(2)}) copy-start(bf16[2,128,2048]{2,1,0:T(8,128)(2,1)S(1)} %broadcast_select_fusion.1.refs_6_) | copy-start | bytes 3145732
  76.4 6.6 %copy-start.3 = (bf16[2,128,2048]{2,1,0:T(8,128)(2,1)}, bf16[2,128,2048]{2,1,0:T(8,128)(2,1)S(1)}, u32[]{:S(2)}) copy-start(bf16[2,128,2048]{2,1,0:T(8,128)(2,1)S(1)} %broadcast_select_fusion.refs_7_) | copy-start | bytes 3145732
  78.9 1.6 copy-start.6
  79.0 4.0 %copy-start.4 = (bf16[2,128,2048]{2,1,0:T(8,128)(2,1)}, bf16[2,128,2048]{2,1,0:T(8,128)(2,1)S(1)}, u32[]{:S(2)}) copy-start(bf16[2,128,2048]{2,1,0:T(8,128)(2,1)S(1)} %broadcast_select_fusion.2.refs_5_) | copy-start | bytes 3145732
  83.0 9.6 %collective-permute-start.7 = (bf16[4,2,128,2048]{3,2,1,0:T(8,128)(2,1)}, bf16[4,2,128,2048]{3,2,1,0:T(8,128)(2,1)}, u32[]{:S(2)}, u32[]{:S(2)}) collective-permute-start(bf16[4,2,128,2048]{3,2,1,0:T(8,128)(2,1)} %maximum_select_fusion), channel_id=1, source_target_pairs={{0,1},{1,0},{2,3},{3,2},{4,5},{5,4},{6,7},{7,6},{8,9},{9,8},{10,11... | collective-permute-start | bytes 12582920 | tf_op jit(solution)/shard_map/ppermute | solution.py:25
  117.7 8.5 %copy-start.8 = (f32[2,128,2048]{2,1,0:T(8,128)S(1)}, f32[2,128,2048]{2,1,0:T(8,128)}, u32[]{:S(2)}) copy-start(f32[2,128,2048]{2,1,0:T(8,128)} %get-tuple-element.13) | copy-start | bytes 6291460
  117.7 8.5 %copy-start.9 = (f32[2,128,2048]{2,1,0:T(8,128)S(1)}, f32[2,128,2048]{2,1,0:T(8,128)}, u32[]{:S(2)}) copy-start(f32[2,128,2048]{2,1,0:T(8,128)} %get-tuple-element.14) | copy-start | bytes 6291460
  117.7 8.5 %copy-start.10 = (f32[2,128,2048]{2,1,0:T(8,128)S(1)}, f32[2,128,2048]{2,1,0:T(8,128)}, u32[]{:S(2)}) copy-start(f32[2,128,2048]{2,1,0:T(8,128)} %get-tuple-element.15) | copy-start | bytes 6291460
  117.7 7.4 %collective-permute-start.8 = (bf16[4,2,128,2048]{3,2,1,0:T(8,128)(2,1)}, bf16[4,2,128,2048]{3,2,1,0:T(8,128)(2,1)S(1)}, u32[]{:S(2)}, u32[]{:S(2)}) collective-permute-start(bf16[4,2,128,2048]{3,2,1,0:T(8,128)(2,1)} %get-tuple-element.12), channel_id=1, source_target_pairs={{0,1},{1,0},{2,3},{3,2},{4,5},{5,4},{6,7},{7,6},{8,9},{9,8},{10,11... | collective-permute-start | bytes 12582920 | tf_op jit(solution)/shard_map/ppermute | solution.py:25
  126.2 4.3 %copy-start.1 = (f32[4,2,128,2048]{3,2,1,0:T(8,128)}, f32[4,2,128,2048]{3,2,1,0:T(8,128)S(1)}, u32[]{:S(2)}) copy-start(f32[4,2,128,2048]{3,2,1,0:T(8,128)S(1)} %convert_element_type.31) | copy-start | bytes 25165828
  130.5 26.3 %collective-permute-start.10 = (bf16[2,128,2048]{2,1,0:T(8,128)(2,1)}, bf16[2,128,2048]{2,1,0:T(8,128)(2,1)S(1)}, u32[]{:S(2)}, u32[]{:S(2)}) collective-permute-start(bf16[2,128,2048]{2,1,0:T(8,128)(2,1)} %get-tuple-element.18), channel_id=1, source_target_pairs={{4,0},{5,1},{6,2},{7,3},{12,8},{13,9},{14,10},{15,11},{20,16},{21,... | collective-permute-start | bytes 3145736 | tf_op jit(solution)/shard_map/ppermute | solution.py:25
  133.4 25.4 %collective-permute-start.11 = (bf16[2,128,2048]{2,1,0:T(8,128)(2,1)}, bf16[2,128,2048]{2,1,0:T(8,128)(2,1)S(1)}, u32[]{:S(2)}, u32[]{:S(2)}) collective-permute-start(bf16[2,128,2048]{2,1,0:T(8,128)(2,1)} %get-tuple-element.17), channel_id=1, source_target_pairs={{6,0},{7,1},{14,8},{15,9},{22,16},{23,17},{30,24},{31,25},{0,2},{1... | collective-permute-start | bytes 3145736 | tf_op jit(solution)/shard_map/ppermute | solution.py:25
  136.5 45.6 %collective-permute-start.9 = (bf16[2,128,2048]{2,1,0:T(8,128)(2,1)}, bf16[2,128,2048]{2,1,0:T(8,128)(2,1)S(1)}, u32[]{:S(2)}, u32[]{:S(2)}) collective-permute-start(bf16[2,128,2048]{2,1,0:T(8,128)(2,1)} %get-tuple-element.19), channel_id=1, source_target_pairs={{2,0},{3,1},{4,2},{5,3},{6,4},{7,5},{10,8},{11,9},{12,10},{13,11},... | collective-permute-start | bytes 3145736 | tf_op jit(solution)/shard_map/ppermute | solution.py:25
  182.1 29.7 %copy-start.7 = (f32[2,128,2048]{2,1,0:T(8,128)S(1)}, f32[2,128,2048]{2,1,0:T(8,128)}, u32[]{:S(2)}) copy-start(f32[2,128,2048]{2,1,0:T(8,128)} %get-tuple-element.11) | copy-start | bytes 6291460
  185.4 26.4 %collective-permute-start.12 = (bf16[2,128,2048]{2,1,0:T(8,128)(2,1)S(1)}, bf16[2,128,2048]{2,1,0:T(8,128)(2,1)S(1)}, u32[]{:S(2)}, u32[]{:S(2)}) collective-permute-start(bf16[2,128,2048]{2,1,0:T(8,128)(2,1)S(1)} %fusion.8), channel_id=1, source_target_pairs={{8,0},{9,1},{10,2},{11,3},{12,4},{13,5},{14,6},{15,7},{16,8},{17,9... | collective-permute-start | bytes 3145736 | tf_op jit(solution)/shard_map/ppermute | solution.py:25

commit v5 on v4

--- a/solution.py
+++ b/solution.py
@@ -45,13 +45,21 @@
         self.sibling = [(i, i ^ 1) for i in range(count)]
 
 
+def halves(value):
+    width = value.shape[-1] // 2
+    return [value[..., :width], value[..., width:]]
+
+
 def gather_window(own, routes, chip_in_group, core):
-    prev = moved(own, routes.hop)
+    prev_parts = [moved(part, routes.hop) for part in halves(own)]
     direct = [own]
     for e in range(1, routes.chips):
         up = moved(own, routes.up[e - 1])
-        down = moved(prev, routes.down[e - 1])
+        down = jnp.concatenate(
+            [moved(part, routes.down[e - 1]) for part in prev_parts], axis=-1
+        )
         direct.append(jnp.where(chip_in_group >= e, up, down))
+    prev = jnp.concatenate(prev_parts, axis=-1)
     later = direct[1:] + [prev]
     sent = jnp.where(core == 0, jnp.stack(direct), jnp.stack(later))
     sib = moved(sent, routes.sibling)
@@ -66,14 +74,16 @@
     own = direct[0] + jnp.where(is_even, back[0], 0.0)
     prev = prev + jnp.where(is_even, 0.0, back[chips - 1])
     sums = [direct[e] + jnp.where(is_even, back[e], back[e - 1]) for e in range(1, chips)]
+    sent = [total.astype(link) for total in sums]
+    prev_parts = halves(prev)
     for e in range(1, chips):
-        sent = sums[e - 1].astype(link)
-        got = moved(sent, reverse(routes.up[e - 1] + routes.down[e - 1])).astype(jnp.float32)
-        upward = chip_in_group + e < chips
-        own = own + jnp.where(upward, got, 0.0)
-        prev = prev + jnp.where(upward, 0.0, got)
-    own = own + moved(prev.astype(link), reverse(routes.hop)).astype(jnp.float32)
-    return own
+        for x, part in enumerate(halves(sent[e - 1])):
+            got = moved(part, reverse(routes.down[e - 1]))
+            prev_parts[x] = prev_parts[x] + got.astype(jnp.float32)
+    for e in range(1, chips):
+        own = own + moved(sent[e - 1], reverse(routes.up[e - 1])).astype(jnp.float32)
+    hopped = [moved(part.astype(link), reverse(routes.hop)) for part in prev_parts]
+    return own + jnp.concatenate(hopped, axis=-1).astype(jnp.float32)
 
 
 def attention_kernel(chips, heads, bias_ref, q_ref, do_ref, prev_ref, *refs):

time: 220 us -> 223 us (1.014)
  starting transfers between devices: 30.3 us -> 43.6 us
  waiting for transfers between devices: 136 us -> 126 us
    ppermute x13 -> x24, starting transfers between devices: 30.3 us -> 43.6 us  [moved(): return lax.ppermute(value, 'seq', pairs)]
    ppermute x13 -> x24, waiting for transfers between devices: 136 us -> 126 us  [moved(): return lax.ppermute(value, 'seq', pairs)]
    add x0 -> x1, other arithmetic: none -> 6.88 us  [scatter_window(): prev = prev + jnp.where(is_even, 0.0, back[chips - 1])]
    convert_element_type x2 -> x1, other arithmetic: 7.27 us -> 0.84 us  [scatter_window(): part.astype(link)]
  transfers between devices with their start and end apart: 13 -> 24, of which waited for: 9 -> 13; matrix products, arithmetic and copies ran while one was open for 2% -> 4% of each run, Pallas kernels for 0% -> 0%
where the time goes in v5:
time: 223 us; the launch traced here: 220 us
  waiting for transfers between devices  126 us (57%)
  starting transfers between devices  43.6 us (20%)
  Pallas kernels  25.1 us (11%)
  other arithmetic  17.1 us (8%)
  local copies, waits for them, and re-layouts  7.09 us (3%)
    ppermute x24, waiting for transfers between devices, moved(): return lax.ppermute(value, 'seq', pairs)  126 us
    ppermute x24, starting transfers between devices, moved(): return lax.ppermute(value, 'seq', pairs)  43.6 us
    pallas_call x1, Pallas kernels, attention_grads(): pl.pallas_call(lambda *refs: attention_kernel(chips, per_step, *refs), gr...  25.1 us
    add x1, other arithmetic, scatter_window(): prev = prev + jnp.where(is_even, 0.0, back[chips - 1])  6.88 us
  transfers between devices with their start and end apart: 24, of which 13 were waited for; matrix products, arithmetic and copies ran while one was open for 4% of the time, Pallas kernels for 0%

profile of v5, /device:TPU:7, one launch (start us, length us, event | category | flops | bytes accessed | tf_op | source)
XLA Modules:
  0.0 219.8 jit_solution(3705496676901844811)
XLA Ops:
  0.6 0.0 copy-start
  0.6 1.1 constant_dynamic-update-slice_fusion.1
  1.7 1.1 constant_dynamic-update-slice_fusion.refs_4_
  2.8 0.1 fusion.21
  2.9 4.0 %collective-permute-start.1 = (bf16[2,128,1024]{2,1,0:T(8,128)(2,1)S(1)}, bf16[2,128,1024]{2,1,0:T(8,128)(2,1)}, u32[]{:S(2)}, u32[]{:S(2)}) collective-permute-start(bf16[2,128,1024]{2,1,0:T(8,128)(2,1)S(1)} %get-tuple-element.31), channel_id=1, source_target_pairs={{0,8},{1,9},{2,10},{3,11},{4,12},{5,13},{6,14},{7,15},{8,16},{9,17... | collective-permute-start | bytes 1572872 | tf_op jit(solution)/shard_map/ppermute | solution.py:25
  6.9 3.2 %collective-permute-start = (bf16[2,128,1024]{2,1,0:T(8,128)(2,1)S(1)}, bf16[2,128,1024]{2,1,0:T(8,128)(2,1)}, u32[]{:S(2)}, u32[]{:S(2)}) collective-permute-start(bf16[2,128,1024]{2,1,0:T(8,128)(2,1)S(1)} %get-tuple-element.32), channel_id=1, source_target_pairs={{0,8},{1,9},{2,10},{3,11},{4,12},{5,13},{6,14},{7,15},{8,16},{9,17... | collective-permute-start | bytes 1572872 | tf_op jit(solution)/shard_map/ppermute | solution.py:25
  10.1 1.3 collective-permute-start.8
  11.4 5.3 %collective-permute-done.1 = bf16[2,128,1024]{2,1,0:T(8,128)(2,1)} collective-permute-done((bf16[2,128,1024]{2,1,0:T(8,128)(2,1)S(1)}, bf16[2,128,1024]{2,1,0:T(8,128)(2,1)}, u32[]{:S(2)}, u32[]{:S(2)}) %collective-permute-start.1) | collective-permute-done | bytes 524320 | tf_op jit(solution)/shard_map/ppermute | solution.py:25
  16.7 3.0 %collective-permute-start.10 = (bf16[2,128,1024]{2,1,0:T(8,128)(2,1)}, bf16[2,128,1024]{2,1,0:T(8,128)(2,1)}, u32[]{:S(2)}, u32[]{:S(2)}) collective-permute-start(bf16[2,128,1024]{2,1,0:T(8,128)(2,1)} %collective-permute-done.1), channel_id=1, source_target_pairs={{2,0},{3,1},{4,2},{5,3},{6,4},{7,5},{10,8},{11,9},{12,10},{13,11},... | collective-permute-start | bytes 1572872 | tf_op jit(solution)/shard_map/ppermute | solution.py:25
  19.7 2.1 collective-permute-start.7
  21.8 1.3 collective-permute-start.5
  23.1 4.9 %collective-permute-done = bf16[2,128,1024]{2,1,0:T(8,128)(2,1)} collective-permute-done((bf16[2,128,1024]{2,1,0:T(8,128)(2,1)S(1)}, bf16[2,128,1024]{2,1,0:T(8,128)(2,1)}, u32[]{:S(2)}, u32[]{:S(2)}) %collective-permute-start) | collective-permute-done | bytes 524320 | tf_op jit(solution)/shard_map/ppermute | solution.py:25
  27.9 3.0 %collective-permute-start.9 = (bf16[2,128,1024]{2,1,0:T(8,128)(2,1)}, bf16[2,128,1024]{2,1,0:T(8,128)(2,1)}, u32[]{:S(2)}, u32[]{:S(2)}) collective-permute-start(bf16[2,128,1024]{2,1,0:T(8,128)(2,1)} %collective-permute-done), channel_id=1, source_target_pairs={{2,0},{3,1},{4,2},{5,3},{6,4},{7,5},{10,8},{11,9},{12,10},{13,11},... | collective-permute-start | bytes 1572872 | tf_op jit(solution)/shard_map/ppermute | solution.py:25
  30.9 1.1 constant_dynamic-update-slice_fusion.3
  32.0 1.3 collective-permute-start.2
  33.3 20.9 %collective-permute-done.7 = bf16[2,128,1024]{2,1,0:T(8,128)(2,1)} collective-permute-done((bf16[2,128,1024]{2,1,0:T(8,128)(2,1)}, bf16[2,128,1024]{2,1,0:T(8,128)(2,1)}, u32[]{:S(2)}, u32[]{:S(2)}) %collective-permute-start.7) | collective-permute-done | bytes 524320 | tf_op jit(solution)/shard_map/ppermute | solution.py:25
  54.1 4.1 %collective-permute-start.6 = (bf16[2,128,1024]{2,1,0:T(8,128)(2,1)}, bf16[2,128,1024]{2,1,0:T(8,128)(2,1)S(1)}, u32[]{:S(2)}, u32[]{:S(2)}) collective-permute-start(bf16[2,128,1024]{2,1,0:T(8,128)(2,1)} %collective-permute-done), channel_id=1, source_target_pairs={{4,0},{5,1},{6,2},{7,3},{12,8},{13,9},{14,10},{15,11},{20,16},{21,... | collective-permute-start | bytes 1572872 | tf_op jit(solution)/shard_map/ppermute | solution.py:25
  58.3 1.1 constant_dynamic-update-slice_fusion.2.refs_3_
  59.4 0.0 collective-permute-done.9
  59.4 1.3 collective-permute-start.4
  60.7 0.0 collective-permute-done.8
  60.7 1.3 collective-permute-start.3
  62.0 1.6 maximum_select_fusion.3.refs_7_
  63.6 5.7 %collective-permute-done.6 = bf16[2,128,1024]{2,1,0:T(8,128)(2,1)S(1)} collective-permute-done((bf16[2,128,1024]{2,1,0:T(8,128)(2,1)}, bf16[2,128,1024]{2,1,0:T(8,128)(2,1)S(1)}, u32[]{:S(2)}, u32[]{:S(2)}) %collective-permute-start.6) | collective-permute-done | bytes 524320 | tf_op jit(solution)/shard_map/ppermute | solution.py:25
  69.3 1.4 maximum_select_fusion.2.refs_6_
  70.8 1.0 collective-permute-done.4
  71.8 11.2 %collective-permute-done.3 = bf16[2,128,1024]{2,1,0:T(8,128)(2,1)S(1)} collective-permute-done((bf16[2,128,1024]{2,1,0:T(8,128)(2,1)}, bf16[2,128,1024]{2,1,0:T(8,128)(2,1)S(1)}, u32[]{:S(2)}, u32[]{:S(2)}) %collective-permute-start.3) | collective-permute-done | bytes 524320 | tf_op jit(solution)/shard_map/ppermute | solution.py:25
  83.0 0.0 collective-permute-done.2
  83.0 0.4 maximum_select_fusion.1.refs_5_
  83.5 2.5 %maximum_select_fusion = bf16[4,2,128,2048]{3,2,1,0:T(8,128)(2,1)} fusion(bf16[1,2,128,2048]{3,2,1,0:T(8,128)(2,1)S(1)} %bitcast.39, bf16[1,2,128,2048]{3,2,1,0:T(8,128)(2,1)S(1)} %bitcast.40, bf16[1,2,128,2048]{3,2,1,0:T(8,128)(2,1)S(1)} %bitcast.41, bf16[1,2,128,2048]{3,2,1,0:T(8,128)(2,1)S(1)} %bitcast.38, bf16[1,2,128,2048]{3,2,1,0:T(8,128)(2,1)S(1)} %bitcast.42, ...), kind=kLoop, calls=%fused_computation | loop fusion | flops 14680064 | bytes 9437185 | tf_op jit(solution)/shard_map/jit(_where)/select_n | solution.py:64
  86.0 1.3 collective-permute-start.11
  87.3 0.1 broadcast_bitcast_fusion
  87.4 0.1 dynamic_slice.6
  87.5 0.1 pad_dynamic-slice_fusion
  87.6 0.2 fusion.16
  87.8 1.1 pad_maximum_fusion.refs_0_
  88.9 5.5 %collective-permute-done.11.refs_8_ = bf16[4,2,128,2048]{3,2,1,0:T(8,128)(2,1)} collective-permute-done((bf16[4,2,128,2048]{3,2,1,0:T(8,128)(2,1)}, bf16[4,2,128,2048]{3,2,1,0:T(8,128)(2,1)}, u32[]{:S(2)}, u32[]{:S(2)}) %collective-permute-start.11) | collective-permute-done | bytes 4194336 | tf_op jit(solution)/shard_map/ppermute | solution.py:25
  94.5 25.1 %shard_map.76 = (bf16[128,4096]{1,0:T(8,128)(2,1)}, f32[2,128,2048]{2,1,0:T(8,128)}, f32[2,128,2048]{2,1,0:T(8,128)}, f32[2,128,2048]{2,1,0:T(8,128)}, f32[2,128...) custom-call(f32[256,1152]{1,0:T(8,128)} %pad_maximum_fusion.refs_0_, ...), custom_call_target="tpu_custom_call" | custom-call | flops 6039797760 | bytes 32636928 | tf_op jit(solution)/shard_map/pallas_call | solution.py:149
  119.6 0.4 collective-permute-start.12
  120.0 7.0 %collective-permute-done.12 = bf16[4,2,128,2048]{3,2,1,0:T(8,128)(2,1)S(1)} collective-permute-done((bf16[4,2,128,2048]{3,2,1,0:T(8,128)(2,1)}, bf16[4,2,128,2048]{3,2,1,0:T(8,128)(2,1)S(1)}, u32[]{:S(2)}, u32[]{:S(2)}) %collective-permute-start.12) | collective-permute-done | bytes 4194336 | tf_op jit(solution)/shard_map/ppermute | solution.py:25
  127.0 1.0 convert_element_type.52
  128.1 6.9 %bitcast_add_fusion = (f32[2,128,2048]{2,1,0:T(8,128)S(1)}, bf16[2,128,2048]{2,1,0:T(8,128)(2,1)}, bf16[2,128,2048]{2,1,0:T(8,128)(2,1)S(1)}, bf16[2,128,2048]{2,1,0:T(8,128)(2,1)S(1)}) fusion(f32[2,128,2048]{2,1,0:T(8,128)} %get-tuple-element.16, f32[4,2,128,2048]{3,2,1,0:T(8,128)S(1)} %convert_element_type.52, pred[]{:T(512)S(6)} %eq.23, ...), kind=kLoop, calls=%fused_computation.1 | loop fusion | flops 5767168 | bytes 22020096 | tf_op jit(solution)/shard_map/add | solution.py:75
  134.9 1.3 fusion.20
  136.2 1.3 collective-permute-start.18
  137.5 1.3 collective-permute-start.22
  138.8 0.1 fusion.19
  138.9 1.4 collective-permute-start.17
  140.3 1.3 collective-permute-start.21
  141.6 0.1 fusion.18
  141.7 1.3 collective-permute-start.16
  143.0 8.2 %collective-permute-done.18 = bf16[2,128,1024]{2,1,0:T(8,128)(2,1)S(1)} collective-permute-done((bf16[2,128,1024]{2,1,0:T(8,128)(2,1)S(1)}, bf16[2,128,1024]{2,1,0:T(8,128)(2,1)S(1)}, u32[]{:S(2)}, u32[]{:S(2)}) %collective-permute-start.18) | collective-permute-done | bytes 524320 | tf_op jit(solution)/shard_map/ppermute | solution.py:25
  151.3 1.3 collective-permute-start.20
  152.5 9.9 %collective-permute-done.22 = bf16[2,128,1024]{2,1,0:T(8,128)(2,1)S(1)} collective-permute-done((bf16[2,128,1024]{2,1,0:T(8,128)(2,1)S(1)}, bf16[2,128,1024]{2,1,0:T(8,128)(2,1)S(1)}, u32[]{:S(2)}, u32[]{:S(2)}) %collective-permute-start.22) | collective-permute-done | bytes 524320 | tf_op jit(solution)/shard_map/ppermute | solution.py:25
  162.5 2.4 %collective-permute-start.15 = (bf16[2,128,2048]{2,1,0:T(8,128)(2,1)S(1)}, bf16[2,128,2048]{2,1,0:T(8,128)(2,1)S(1)}, u32[]{:S(2)}, u32[]{:S(2)}) collective-permute-start(bf16[2,128,2048]{2,1,0:T(8,128)(2,1)S(1)} %copy-done.3), channel_id=1, source_target_pairs={{6,0},{7,1},{14,8},{15,9},{22,16},{23,17},{30,24},{31,25}} | collective-permute-start | bytes 3145736 | tf_op jit(solution)/shard_map/ppermute | solution.py:25
  165.0 1.7 collective-permute-start.14
  166.7 22.6 %collective-permute-done.21 = bf16[2,128,1024]{2,1,0:T(8,128)(2,1)S(1)} collective-permute-done((bf16[2,128,1024]{2,1,0:T(8,128)(2,1)S(1)}, bf16[2,128,1024]{2,1,0:T(8,128)(2,1)S(1)}, u32[]{:S(2)}, u32[]{:S(2)}) %collective-permute-start.21) | collective-permute-done | bytes 524320 | tf_op jit(solution)/shard_map/ppermute | solution.py:25
  189.3 1.3 collective-permute-start.13
  190.7 0.8 fusion.13
  191.5 1.3 collective-permute-start.19
  192.8 1.3 collective-permute-start.23
  194.1 17.6 %collective-permute-done.13 = bf16[2,128,2048]{2,1,0:T(8,128)(2,1)S(1)} collective-permute-done((bf16[2,128,2048]{2,1,0:T(8,128)(2,1)S(1)}, bf16[2,128,2048]{2,1,0:T(8,128)(2,1)S(1)}, u32[]{:S(2)}, u32[]{:S(2)}) %collective-permute-start.13) | collective-permute-done | bytes 1048608 | tf_op jit(solution)/shard_map/ppermute | solution.py:25
  211.8 5.9 %collective-permute-done.23 = bf16[2,128,1024]{2,1,0:T(8,128)(2,1)S(1)} collective-permute-done((bf16[2,128,1024]{2,1,0:T(8,128)(2,1)S(1)}, bf16[2,128,1024]{2,1,0:T(8,128)(2,1)S(1)}, u32[]{:S(2)}, u32[]{:S(2)}) %collective-permute-start.23) | collective-permute-done | bytes 524320 | tf_op jit(solution)/shard_map/ppermute | solution.py:25
  217.7 1.0 fusion.7
  218.7 1.1 fusion.17
  (26 shorter events, 0.1 us)
Async XLA Ops:
  0.6 86.7 %copy-start = (s32[1,32]{1,0:T(1,128)S(1)}, s32[1,32]{1,0:T(1,128)}, u32[]{:S(2)}) copy-start(s32[1,32]{1,0:T(1,128)} %param.9) | copy-start | bytes 388
  2.8 80.6 %copy-start.2 = (bf16[2,128,2048]{2,1,0:T(8,128)(2,1)}, bf16[2,128,2048]{2,1,0:T(8,128)(2,1)S(1)}, u32[]{:S(2)}) copy-start(bf16[2,128,2048]{2,1,0:T(8,128)(2,1)S(1)} %constant_dynamic-update-slice_fusion.refs_4_) | copy-start | bytes 3145732
  2.9 13.8 %collective-permute-start.1 = (bf16[2,128,1024]{2,1,0:T(8,128)(2,1)S(1)}, bf16[2,128,1024]{2,1,0:T(8,128)(2,1)}, u32[]{:S(2)}, u32[]{:S(2)}) collective-permute-start(bf16[2,128,1024]{2,1,0:T(8,128)(2,1)S(1)} %get-tuple-element.31), channel_id=1, source_target_pairs={{0,8},{1,9},{2,10},{3,11},{4,12},{5,13},{6,14},{7,15},{8,16},{9,17... | collective-permute-start | bytes 1572872 | tf_op jit(solution)/shard_map/ppermute | solution.py:25
  6.9 21.0 %collective-permute-start = (bf16[2,128,1024]{2,1,0:T(8,128)(2,1)S(1)}, bf16[2,128,1024]{2,1,0:T(8,128)(2,1)}, u32[]{:S(2)}, u32[]{:S(2)}) collective-permute-start(bf16[2,128,1024]{2,1,0:T(8,128)(2,1)S(1)} %get-tuple-element.32), channel_id=1, source_target_pairs={{0,8},{1,9},{2,10},{3,11},{4,12},{5,13},{6,14},{7,15},{8,16},{9,17... | collective-permute-start | bytes 1572872 | tf_op jit(solution)/shard_map/ppermute | solution.py:25
  10.1 50.6 %collective-permute-start.8 = (bf16[2,128,2048]{2,1,0:T(8,128)(2,1)S(1)}, bf16[2,128,2048]{2,1,0:T(8,128)(2,1)S(1)}, u32[]{:S(2)}, u32[]{:S(2)}) collective-permute-start(bf16[2,128,2048]{2,1,0:T(8,128)(2,1)S(1)} %constant_dynamic-update-slice_fusion.refs_4_), channel_id=1, source_target_pairs={{0,6},{1,7},{8,14},{9,15},{16,22},{17,23},{24,30},{25,31}} | collective-permute-start | bytes 3145736 | tf_op jit(solution)/shard_map/ppermute | solution.py:25
  16.7 15.3 %collective-permute-start.10 = (bf16[2,128,1024]{2,1,0:T(8,128)(2,1)}, bf16[2,128,1024]{2,1,0:T(8,128)(2,1)}, u32[]{:S(2)}, u32[]{:S(2)}) collective-permute-start(bf16[2,128,1024]{2,1,0:T(8,128)(2,1)} %collective-permute-done.1), channel_id=1, source_target_pairs={{2,0},{3,1},{4,2},{5,3},{6,4},{7,5},{10,8},{11,9},{12,10},{13,11},... | collective-permute-start | bytes 1572872 | tf_op jit(solution)/shard_map/ppermute | solution.py:25
  19.7 34.5 %collective-permute-start.7 = (bf16[2,128,1024]{2,1,0:T(8,128)(2,1)}, bf16[2,128,1024]{2,1,0:T(8,128)(2,1)}, u32[]{:S(2)}, u32[]{:S(2)}) collective-permute-start(bf16[2,128,1024]{2,1,0:T(8,128)(2,1)} %collective-permute-done.1), channel_id=1, source_target_pairs={{4,0},{5,1},{6,2},{7,3},{12,8},{13,9},{14,10},{15,11},{20,16},{21,... | collective-permute-start | bytes 1572872 | tf_op jit(solution)/shard_map/ppermute | solution.py:25
  21.8 47.6 %collective-permute-start.5 = (bf16[2,128,2048]{2,1,0:T(8,128)(2,1)S(1)}, bf16[2,128,2048]{2,1,0:T(8,128)(2,1)S(1)}, u32[]{:S(2)}, u32[]{:S(2)}) collective-permute-start(bf16[2,128,2048]{2,1,0:T(8,128)(2,1)S(1)} %constant_dynamic-update-slice_fusion.refs_4_), channel_id=1, source_target_pairs={{0,4},{1,5},{2,6},{3,7},{8,12},{9,13},{10,14},{11,15},{16,20},{17,... | collective-permute-start | bytes 3145736 | tf_op jit(solution)/shard_map/ppermute | solution.py:25
  27.9 31.4 %collective-permute-start.9 = (bf16[2,128,1024]{2,1,0:T(8,128)(2,1)}, bf16[2,128,1024]{2,1,0:T(8,128)(2,1)}, u32[]{:S(2)}, u32[]{:S(2)}) collective-permute-start(bf16[2,128,1024]{2,1,0:T(8,128)(2,1)} %collective-permute-done), channel_id=1, source_target_pairs={{2,0},{3,1},{4,2},{5,3},{6,4},{7,5},{10,8},{11,9},{12,10},{13,11},... | collective-permute-start | bytes 1572872 | tf_op jit(solution)/shard_map/ppermute | solution.py:25
  32.0 51.0 %collective-permute-start.2 = (bf16[2,128,2048]{2,1,0:T(8,128)(2,1)S(1)}, bf16[2,128,2048]{2,1,0:T(8,128)(2,1)S(1)}, u32[]{:S(2)}, u32[]{:S(2)}) collective-permute-start(bf16[2,128,2048]{2,1,0:T(8,128)(2,1)S(1)} %constant_dynamic-update-slice_fusion.refs_4_), channel_id=1, source_target_pairs={{0,2},{1,3},{2,4},{3,5},{4,6},{5,7},{8,10},{9,11},{10,12},{11,13},... | collective-permute-start | bytes 3145736 | tf_op jit(solution)/shard_map/ppermute | solution.py:25
  54.1 15.2 %collective-permute-start.6 = (bf16[2,128,1024]{2,1,0:T(8,128)(2,1)}, bf16[2,128,1024]{2,1,0:T(8,128)(2,1)S(1)}, u32[]{:S(2)}, u32[]{:S(2)}) collective-permute-start(bf16[2,128,1024]{2,1,0:T(8,128)(2,1)} %collective-permute-done), channel_id=1, source_target_pairs={{4,0},{5,1},{6,2},{7,3},{12,8},{13,9},{14,10},{15,11},{20,16},{21,... | collective-permute-start | bytes 1572872 | tf_op jit(solution)/shard_map/ppermute | solution.py:25
  59.4 24.1 %copy-start.7 = (bf16[2,128,2048]{2,1,0:T(8,128)(2,1)}, bf16[2,128,2048]{2,1,0:T(8,128)(2,1)S(1)}, u32[]{:S(2)}) copy-start(bf16[2,128,2048]{2,1,0:T(8,128)(2,1)S(1)} %constant_dynamic-update-slice_fusion.2.refs_3_) | copy-start | bytes 3145732
  59.4 12.4 %collective-permute-start.4 = (bf16[2,128,1024]{2,1,0:T(8,128)(2,1)}, bf16[2,128,1024]{2,1,0:T(8,128)(2,1)S(1)}, u32[]{:S(2)}, u32[]{:S(2)}) collective-permute-start(bf16[2,128,1024]{2,1,0:T(8,128)(2,1)} %collective-permute-done.1), channel_id=1, source_target_pairs={{6,0},{7,1},{14,8},{15,9},{22,16},{23,17},{30,24},{31,25}} | collective-permute-start | bytes 1572872 | tf_op jit(solution)/shard_map/ppermute | solution.py:25
  60.7 22.3 %collective-permute-start.3 = (bf16[2,128,1024]{2,1,0:T(8,128)(2,1)}, bf16[2,128,1024]{2,1,0:T(8,128)(2,1)S(1)}, u32[]{:S(2)}, u32[]{:S(2)}) collective-permute-start(bf16[2,128,1024]{2,1,0:T(8,128)(2,1)} %collective-permute-done), channel_id=1, source_target_pairs={{6,0},{7,1},{14,8},{15,9},{22,16},{23,17},{30,24},{31,25}} | collective-permute-start | bytes 1572872 | tf_op jit(solution)/shard_map/ppermute | solution.py:25
  63.6 19.8 %copy-start.4 = (bf16[2,128,2048]{2,1,0:T(8,128)(2,1)}, bf16[2,128,2048]{2,1,0:T(8,128)(2,1)S(1)}, u32[]{:S(2)}) copy-start(bf16[2,128,2048]{2,1,0:T(8,128)(2,1)S(1)} %maximum_select_fusion.3.refs_7_) | copy-start | bytes 3145732
  70.8 15.2 %copy-start.5 = (bf16[2,128,2048]{2,1,0:T(8,128)(2,1)}, bf16[2,128,2048]{2,1,0:T(8,128)(2,1)S(1)}, u32[]{:S(2)}) copy-start(bf16[2,128,2048]{2,1,0:T(8,128)(2,1)S(1)} %maximum_select_fusion.2.refs_6_) | copy-start | bytes 3145732
  83.4 2.6 %copy-start.6 = (bf16[2,128,2048]{2,1,0:T(8,128)(2,1)}, bf16[2,128,2048]{2,1,0:T(8,128)(2,1)S(1)}, u32[]{:S(2)}) copy-start(bf16[2,128,2048]{2,1,0:T(8,128)(2,1)S(1)} %maximum_select_fusion.1.refs_5_) | copy-start | bytes 3145732
  86.0 8.5 %collective-permute-start.11 = (bf16[4,2,128,2048]{3,2,1,0:T(8,128)(2,1)}, bf16[4,2,128,2048]{3,2,1,0:T(8,128)(2,1)}, u32[]{:S(2)}, u32[]{:S(2)}) collective-permute-start(bf16[4,2,128,2048]{3,2,1,0:T(8,128)(2,1)} %maximum_select_fusion), channel_id=1, source_target_pairs={{0,1},{1,0},{2,3},{3,2},{4,5},{5,4},{6,7},{7,6},{8,9},{9,8},{10,11... | collective-permute-start | bytes 12582920 | tf_op jit(solution)/shard_map/ppermute | solution.py:25
  119.6 7.4 %collective-permute-start.12 = (bf16[4,2,128,2048]{3,2,1,0:T(8,128)(2,1)}, bf16[4,2,128,2048]{3,2,1,0:T(8,128)(2,1)S(1)}, u32[]{:S(2)}, u32[]{:S(2)}) collective-permute-start(bf16[4,2,128,2048]{3,2,1,0:T(8,128)(2,1)} %get-tuple-element.12), channel_id=1, source_target_pairs={{0,1},{1,0},{2,3},{3,2},{4,5},{5,4},{6,7},{7,6},{8,9},{9,8},{10,11... | collective-permute-start | bytes 12582920 | tf_op jit(solution)/shard_map/ppermute | solution.py:25
  136.2 15.0 %collective-permute-start.18 = (bf16[2,128,1024]{2,1,0:T(8,128)(2,1)S(1)}, bf16[2,128,1024]{2,1,0:T(8,128)(2,1)S(1)}, u32[]{:S(2)}, u32[]{:S(2)}) collective-permute-start(bf16[2,128,1024]{2,1,0:T(8,128)(2,1)S(1)} %get-tuple-element.29), channel_id=1, source_target_pairs={{0,2},{1,3},{2,4},{3,5},{4,6},{5,7},{8,10},{9,11},{10,12},{11,13},... | collective-permute-start | bytes 1572872 | tf_op jit(solution)/shard_map/ppermute | solution.py:25
  137.5 25.0 %collective-permute-start.22 = (bf16[2,128,1024]{2,1,0:T(8,128)(2,1)S(1)}, bf16[2,128,1024]{2,1,0:T(8,128)(2,1)S(1)}, u32[]{:S(2)}, u32[]{:S(2)}) collective-permute-start(bf16[2,128,1024]{2,1,0:T(8,128)(2,1)S(1)} %get-tuple-element.30), channel_id=1, source_target_pairs={{0,2},{1,3},{2,4},{3,5},{4,6},{5,7},{8,10},{9,11},{10,12},{11,13},... | collective-permute-start | bytes 1572872 | tf_op jit(solution)/shard_map/ppermute | solution.py:25
  138.8 23.7 %copy-start.3 = (bf16[2,128,2048]{2,1,0:T(8,128)(2,1)S(1)}, bf16[2,128,2048]{2,1,0:T(8,128)(2,1)}, u32[]{:S(2)}) copy-start(bf16[2,128,2048]{2,1,0:T(8,128)(2,1)} %get-tuple-element.18) | copy-start | bytes 3145732
  138.9 26.0 %collective-permute-start.17 = (bf16[2,128,1024]{2,1,0:T(8,128)(2,1)S(1)}, bf16[2,128,1024]{2,1,0:T(8,128)(2,1)S(1)}, u32[]{:S(2)}, u32[]{:S(2)}) collective-permute-start(bf16[2,128,1024]{2,1,0:T(8,128)(2,1)S(1)} %get-tuple-element.27), channel_id=1, source_target_pairs={{0,4},{1,5},{2,6},{3,7},{8,12},{9,13},{10,14},{11,15},{16,20},{17,... | collective-permute-start | bytes 1572872 | tf_op jit(solution)/shard_map/ppermute | solution.py:25
  140.3 48.9 %collective-permute-start.21 = (bf16[2,128,1024]{2,1,0:T(8,128)(2,1)S(1)}, bf16[2,128,1024]{2,1,0:T(8,128)(2,1)S(1)}, u32[]{:S(2)}, u32[]{:S(2)}) collective-permute-start(bf16[2,128,1024]{2,1,0:T(8,128)(2,1)S(1)} %get-tuple-element.28), channel_id=1, source_target_pairs={{0,4},{1,5},{2,6},{3,7},{8,12},{9,13},{10,14},{11,15},{16,20},{17,... | collective-permute-start | bytes 1572872 | tf_op jit(solution)/shard_map/ppermute | solution.py:25
  141.7 48.9 %collective-permute-start.16 = (bf16[2,128,1024]{2,1,0:T(8,128)(2,1)S(1)}, bf16[2,128,1024]{2,1,0:T(8,128)(2,1)S(1)}, u32[]{:S(2)}, u32[]{:S(2)}) collective-permute-start(bf16[2,128,1024]{2,1,0:T(8,128)(2,1)S(1)} %get-tuple-element.25), channel_id=1, source_target_pairs={{0,6},{1,7},{8,14},{9,15},{16,22},{17,23},{24,30},{25,31}} | collective-permute-start | bytes 1572872 | tf_op jit(solution)/shard_map/ppermute | solution.py:25
  151.3 39.4 %collective-permute-start.20 = (bf16[2,128,1024]{2,1,0:T(8,128)(2,1)S(1)}, bf16[2,128,1024]{2,1,0:T(8,128)(2,1)S(1)}, u32[]{:S(2)}, u32[]{:S(2)}) collective-permute-start(bf16[2,128,1024]{2,1,0:T(8,128)(2,1)S(1)} %get-tuple-element.26), channel_id=1, source_target_pairs={{0,6},{1,7},{8,14},{9,15},{16,22},{17,23},{24,30},{25,31}} | collective-permute-start | bytes 1572872 | tf_op jit(solution)/shard_map/ppermute | solution.py:25
  162.5 31.6 %collective-permute-start.15 = (bf16[2,128,2048]{2,1,0:T(8,128)(2,1)S(1)}, bf16[2,128,2048]{2,1,0:T(8,128)(2,1)S(1)}, u32[]{:S(2)}, u32[]{:S(2)}) collective-permute-start(bf16[2,128,2048]{2,1,0:T(8,128)(2,1)S(1)} %copy-done.3), channel_id=1, source_target_pairs={{6,0},{7,1},{14,8},{15,9},{22,16},{23,17},{30,24},{31,25}} | collective-permute-start | bytes 3145736 | tf_op jit(solution)/shard_map/ppermute | solution.py:25
  165.0 29.2 %collective-permute-start.14 = (bf16[2,128,2048]{2,1,0:T(8,128)(2,1)S(1)}, bf16[2,128,2048]{2,1,0:T(8,128)(2,1)S(1)}, u32[]{:S(2)}, u32[]{:S(2)}) collective-permute-start(bf16[2,128,2048]{2,1,0:T(8,128)(2,1)S(1)} %get-tuple-element.19), channel_id=1, source_target_pairs={{4,0},{5,1},{6,2},{7,3},{12,8},{13,9},{14,10},{15,11},{20,16},{21,... | collective-permute-start | bytes 3145736 | tf_op jit(solution)/shard_map/ppermute | solution.py:25
  189.3 22.5 %collective-permute-start.13 = (bf16[2,128,2048]{2,1,0:T(8,128)(2,1)S(1)}, bf16[2,128,2048]{2,1,0:T(8,128)(2,1)S(1)}, u32[]{:S(2)}, u32[]{:S(2)}) collective-permute-start(bf16[2,128,2048]{2,1,0:T(8,128)(2,1)S(1)} %get-tuple-element.20), channel_id=1, source_target_pairs={{2,0},{3,1},{4,2},{5,3},{6,4},{7,5},{10,8},{11,9},{12,10},{13,11},... | collective-permute-start | bytes 3145736 | tf_op jit(solution)/shard_map/ppermute | solution.py:25
  190.7 27.0 %copy-start.8 = (f32[2,128,2048]{2,1,0:T(8,128)S(1)}, f32[2,128,2048]{2,1,0:T(8,128)}, u32[]{:S(2)}) copy-start(f32[2,128,2048]{2,1,0:T(8,128)} %get-tuple-element.11) | copy-start | bytes 6291460
  191.5 20.3 %collective-permute-start.19 = (bf16[2,128,1024]{2,1,0:T(8,128)(2,1)S(1)}, bf16[2,128,1024]{2,1,0:T(8,128)(2,1)S(1)}, u32[]{:S(2)}, u32[]{:S(2)}) collective-permute-start(bf16[2,128,1024]{2,1,0:T(8,128)(2,1)S(1)} %get-tuple-element.21), channel_id=1, source_target_pairs={{8,0},{9,1},{10,2},{11,3},{12,4},{13,5},{14,6},{15,7},{16,8},{17,9... | collective-permute-start | bytes 1572872 | tf_op jit(solution)/shard_map/ppermute | solution.py:25
  192.8 24.8 %collective-permute-start.23 = (bf16[2,128,1024]{2,1,0:T(8,128)(2,1)S(1)}, bf16[2,128,1024]{2,1,0:T(8,128)(2,1)S(1)}, u32[]{:S(2)}, u32[]{:S(2)}) collective-permute-start(bf16[2,128,1024]{2,1,0:T(8,128)(2,1)S(1)} %get-tuple-element.22), channel_id=1, source_target_pairs={{8,0},{9,1},{10,2},{11,3},{12,4},{13,5},{14,6},{15,7},{16,8},{17,9... | collective-permute-start | bytes 1572872 | tf_op jit(solution)/shard_map/ppermute | solution.py:25
  217.7 2.1 copy-start.1

commit v6 on v0

v6 whole, which is shorter than its diff:
```python
import jax
import jax.numpy as jnp
from jax import lax
from jax.experimental import pallas as pl
from jax.experimental.pallas import tpu as pltpu
from jax.sharding import PartitionSpec as P

HEADS = 32
KV_HEADS = 16
HEAD_DIM = 128
WINDOW = 1024
MBLK = 128


SCORE_SCALE = 168.0 ** (-0.5)
MASKED_SCORE = -1e30


def passed_along(value, axis, steps):
    count = lax.axis_size(axis)
    pairs = [(source, (source + steps) % count) for source in range(count)]
    return lax.ppermute(value, axis, pairs)


def moved(value, pairs):
    return lax.ppermute(value, "seq", pairs)


def reverse(pairs):
    return [(t, s) for (s, t) in pairs]


class Routes:
    def __init__(self, count, reach):
        self.reach = reach
        self.chips = reach // 2
        group_chip = lambda i: (i % reach) // 2
        self.hop = [(i, i + reach) for i in range(count - reach)]
        self.up = []
        self.down = []
        for e in range(1, self.chips):
            self.up.append([(i, i + 2 * e) for i in range(count) if group_chip(i) + e < self.chips])
            self.down.append(
                [(i, i + 2 * e - reach) for i in range(count) if group_chip(i) + e >= self.chips]
            )
        self.sibling = [(i, i ^ 1) for i in range(count)]


def gather_window(own, routes, chip_in_group):
    prev = moved(own, routes.hop)
    recv = []
    for e in range(1, routes.chips):
        up = moved(own, routes.up[e - 1])
        down = moved(prev, routes.down[e - 1])
        recv.append(jnp.where(chip_in_group >= e, up, down))
    return [prev] + recv[::-1] + [own]


def scatter_window(parts, routes):
    link = jnp.bfloat16
    chips = routes.chips
    prev, own = parts[0], parts[-1]
    recv = parts[1:-1][::-1]
    sent = [r.astype(link) for r in recv]
    for e in range(1, chips):
        prev = prev + moved(sent[e - 1], reverse(routes.down[e - 1])).astype(jnp.float32)
    for e in range(1, chips):
        own = own + moved(sent[e - 1], reverse(routes.up[e - 1])).astype(jnp.float32)
    return own + moved(prev.astype(link), reverse(routes.hop)).astype(jnp.float32)


def attention_kernel(chips, core_ref, bias_ref, qm_ref, qs_ref, dm_ref, ds_ref, *refs):
    del core_ref
    kv_refs = refs[:chips]
    dqm_ref, dqs_ref = refs[chips], refs[chips + 1]
    part_refs = refs[chips + 2 :]
    tokens = qm_ref.shape[0]
    d = HEAD_DIM
    k = jnp.concatenate([r[0, s] for r in kv_refs for s in range(2)], axis=0)
    v = jnp.concatenate([r[1, s] for r in kv_refs for s in range(2)], axis=0)
    qs = jnp.concatenate([qm_ref[:, :d], qs_ref[:, :d], qm_ref[:, d:], qs_ref[:, d:]], axis=0)
    dos = jnp.concatenate([dm_ref[:, :d], ds_ref[:, :d], dm_ref[:, d:], ds_ref[:, d:]], axis=0)
    contract_last = (((1,), (1,)), ((), ()))
    contract_first = (((0,), (0,)), ((), ()))
    scores = lax.dot_general(qs, k, contract_last, preferred_element_type=jnp.float32)
    scores = scores * SCORE_SCALE + bias_ref[...]
    largest = jnp.max(scores, axis=1, keepdims=True)
    unscaled = jnp.exp(scores - largest)
    attn = unscaled * (1.0 / jnp.sum(unscaled, axis=1, keepdims=True))
    dattn = lax.dot_general(dos, v, contract_last, preferred_element_type=jnp.float32)
    row_delta = jnp.sum(attn * dattn, axis=1, keepdims=True)
    dscores = (attn * (dattn - row_delta)).astype(jnp.bfloat16)
    grad_q = jnp.dot(dscores, k, preferred_element_type=jnp.float32) * SCORE_SCALE
    rows = lambda j: slice(j * tokens, (j + 1) * tokens)
    dqm_ref[:, :d] = grad_q[rows(0)].astype(dqm_ref.dtype)
    dqs_ref[:, :d] = grad_q[rows(1)].astype(dqs_ref.dtype)
    dqm_ref[:, d:] = grad_q[rows(2)].astype(dqm_ref.dtype)
    dqs_ref[:, d:] = grad_q[rows(3)].astype(dqs_ref.dtype)
    grad_k = (
        lax.dot_general(dscores, qs, contract_first, preferred_element_type=jnp.float32)
        * SCORE_SCALE
    )
    grad_v = lax.dot_general(
        attn.astype(jnp.bfloat16), dos, contract_first, preferred_element_type=jnp.float32
    )
    for j, out in enumerate(part_refs):
        for s in range(2):
            out[0, s] = grad_k[rows(2 * j + s)]
            out[1, s] = grad_v[rows(2 * j + s)]


def attention_grads(core, bias, queries, query_sib, grad_out, grad_sib, payloads):
    tokens = queries.shape[0]
    chips = len(payloads)
    key_count = bias.shape[1]
    half = payloads[0].shape[3]
    heads = half // HEAD_DIM
    pair = 2 * HEAD_DIM
    mine = pl.BlockSpec((tokens, pair), lambda g, c: (0, c[0] * heads + g))
    other = pl.BlockSpec((tokens, pair), lambda g, c: (0, g))
    chip = pl.BlockSpec((2, 2, tokens, HEAD_DIM), lambda g, c: (0, 0, 0, g))
    part = jax.ShapeDtypeStruct(payloads[0].shape, jnp.float32)
    rows = 4 * tokens
    flops = 2 * 5 * rows * key_count * HEAD_DIM * heads
    moved_bytes = 2 * 6 * tokens * half * 2 + 2 * 2 * key_count * half * 3 + bias.size * 4
    grid_spec = pltpu.PrefetchScalarGridSpec(
        num_scalar_prefetch=1,
        grid=(heads,),
        in_specs=[pl.BlockSpec(bias.shape, lambda g, c: (0, 0)), mine, other, mine, other]
        + [chip] * chips,
        out_specs=[other, other] + [chip] * chips,
    )
    return pl.pallas_call(
        lambda *refs: attention_kernel(chips, *refs),
        grid_spec=grid_spec,
        out_shape=[jax.ShapeDtypeStruct(query_sib.shape, jnp.bfloat16)] * 2 + [part] * chips,
        cost_estimate=pl.CostEstimate(
            flops=flops, transcendentals=rows * key_count * heads, bytes_accessed=moved_bytes
        ),
    )(core, bias, queries, query_sib, grad_out, grad_sib, *payloads)


def in_core_order(core, mine, theirs):
    return jnp.where(core == 0, jnp.concatenate([mine, theirs], -1), jnp.concatenate([theirs, mine], -1))


def local(queries, key_rows, value_rows, arriving_grad, doc_blocks):
    tokens = queries.shape[1]
    count = lax.axis_size("seq")
    if lax.axis_size("pipe") > 1:
        arriving_grad = passed_along(arriving_grad, "pipe", -1)
    grad_out = arriving_grad[0]
    position = lax.axis_index("seq")
    reach_back = (WINDOW - 1) // tokens + 1
    assert reach_back % 2 == 0 and count % reach_back == 0 and WINDOW % tokens == 0
    routes = Routes(count, reach_back)
    chips = routes.chips
    chip_in_group = (position % reach_back) // 2
    core = position % 2
    other = 1 - core
    key_width = key_rows.shape[2] // 2
    query_width = queries.shape[2] // 2
    keys, values = key_rows[0], value_rows[0]
    kv_sent = jnp.stack(
        [lax.dynamic_slice_in_dim(keys, other * key_width, key_width, 1),
         lax.dynamic_slice_in_dim(values, other * key_width, key_width, 1)]
    )
    kv_sib = moved(kv_sent, routes.sibling)
    kv_mine = jnp.stack(
        [lax.dynamic_slice_in_dim(keys, core * key_width, key_width, 1),
         lax.dynamic_slice_in_dim(values, core * key_width, key_width, 1)]
    )
    own = jnp.stack([kv_mine, kv_sib], axis=1)
    qd_sent = jnp.stack(
        [lax.dynamic_slice_in_dim(queries[0], other * query_width, query_width, 1),
         lax.dynamic_slice_in_dim(grad_out, other * query_width, query_width, 1)]
    )
    qd_sib = moved(qd_sent, routes.sibling)
    payloads = gather_window(own, routes, chip_in_group)

    chip = position // 2
    block_of = lambda m, s: 2 * m + jnp.where(s == 0, core, other)
    key_blocks = [block_of(chip - chips + j, s) for j in range(chips + 1) for s in range(2)]
    token_doc = jnp.repeat(doc_blocks[0], MBLK)
    pad = (reach_back + 2) * tokens
    doc_pad = jnp.concatenate([jnp.full((pad,), -1, jnp.int32), token_doc])
    key_doc = jnp.concatenate(
        [lax.dynamic_slice_in_dim(doc_pad, b * tokens + pad, tokens, 0) for b in key_blocks]
    )
    offsets = jnp.arange(tokens, dtype=jnp.int32)
    key_pos = jnp.concatenate([b * tokens + offsets for b in key_blocks])
    masks = []
    for block in (position, position ^ 1):
        query_pos = block * tokens + offsets
        query_doc = lax.dynamic_slice_in_dim(token_doc, block * tokens, tokens, 0)
        distance = query_pos[:, None] - key_pos[None, :]
        allowed = (distance >= 0) & (distance < WINDOW) & (query_doc[:, None] == key_doc[None, :])
        masks.append(jnp.where(allowed, 0.0, MASKED_SCORE).astype(jnp.float32))
    bias = jnp.concatenate(masks + masks, axis=0)

    outs = attention_grads(
        core[None].astype(jnp.int32), bias, queries[0], qd_sib[0], grad_out, qd_sib[1], payloads
    )
    dq_mine, dq_sib, parts = outs[0], outs[1], outs[2:]
    summed = scatter_window(parts, routes)
    sent = jnp.concatenate(
        [summed[0, 1].astype(jnp.bfloat16), summed[1, 1].astype(jnp.bfloat16), dq_sib], axis=-1
    )
    got = moved(sent, routes.sibling)
    grad_key = in_core_order(core, summed[0, 0].astype(jnp.bfloat16), got[:, :key_width])
    grad_value = in_core_order(
        core, summed[1, 0].astype(jnp.bfloat16), got[:, key_width : 2 * key_width]
    )
    grad_query = in_core_order(core, dq_mine, got[:, 2 * key_width :])
    return (grad_query[None], grad_key[None], grad_value[None])


def solution(mesh):
    placed = (
        P("pipe", "seq", None),
        P("pipe", "seq", None),
        P("pipe", "seq", None),
        P("pipe", "seq", None),
        P("pipe", None),
    )
    return jax.shard_map(
        local,
        mesh=mesh,
        in_specs=placed,
        out_specs=(P("pipe", "seq", None), P("pipe", "seq", None), P("pipe", "seq", None)),
        check_vma=False,
    )
```

time: 218 us -> 202 us (0.927); the launches traced: 215 us -> 201 us
  waiting for transfers between devices: 131 us -> 121 us
  starting transfers between devices: 38 us -> 32.8 us
  other arithmetic: 12.4 us -> 16.3 us
  Pallas kernels: 27.7 us -> 25.4 us
    ppermute x16 -> x17, waiting for transfers between devices: 131 us -> 121 us  [moved(): return lax.ppermute(value, 'seq', pairs)]
    ppermute x16 -> x17, starting transfers between devices: 37.9 us -> 32.8 us  [moved(): return lax.ppermute(value, 'seq', pairs)]
    convert_element_type x3, other arithmetic: 4.99 us -> 2.2 us  [scatter_window(): sent = [r.astype(link) for r in recv]]
    select_n x4 -> x7, other arithmetic: 5.3 us -> 8.05 us  [the longest x3 4.53 us: gather_window(): recv.append(jnp.where(chip_in_group >= e, up, down))]
    pallas_call x1, Pallas kernels: 27.7 us -> 25.4 us  [attention_grads(): pl.pallas_call(lambda *refs: attention_kernel(chips, *refs), grid_spec=gr...]
    another operation x1 -> x5, other arithmetic: 1.05 us -> 3.32 us  [the longest x2 2.16 us: local(): own = jnp.stack([kv_mine, kv_sib], axis=1)]
  transfers between devices with their start and end apart: 17 -> 17, of which waited for: 10 -> 10; matrix products, arithmetic and copies ran while one was open for 2% -> 5% of each run, Pallas kernels for 0% -> 0%
where the time goes in v6:
time: 202 us; the launch traced here: 201 us
  waiting for transfers between devices  121 us (60%)
  starting transfers between devices  32.8 us (16%)
  Pallas kernels  25.4 us (13%)
  other arithmetic  16.3 us (8%)
  local copies, waits for them, and re-layouts  4.47 us (2%)
    ppermute x17, waiting for transfers between devices, moved(): return lax.ppermute(value, 'seq', pairs)  121 us
    ppermute x17, starting transfers between devices, moved(): return lax.ppermute(value, 'seq', pairs)  32.8 us
    pallas_call x1, Pallas kernels, attention_grads(): pl.pallas_call(lambda *refs: attention_kernel(chips, *refs), grid_spec=gr...  25.4 us
    select_n x3, other arithmetic, gather_window(): recv.append(jnp.where(chip_in_group >= e, up, down))  4.53 us
  transfers between devices with their start and end apart: 17, of which 10 were waited for; matrix products, arithmetic and copies ran while one was open for 5% of the time, Pallas kernels for 0%

profile of v6, /device:TPU:7, one launch (start us, length us, event | category | flops | bytes accessed | tf_op | source)
XLA Modules:
  0.0 201.5 jit_solution(7519690589233687259)
XLA Ops:
  0.6 0.0 copy-start
  0.6 0.0 copy-start.7
  0.7 1.4 constant_dynamic-slice_fusion.2
  2.1 0.1 pad_maximum_fusion.4
  2.2 0.7 collective-permute-start.1
  2.9 0.1 constant_dynamic-slice_fusion.4
  3.0 0.1 pad_maximum_fusion.1
  3.1 0.3 collective-permute-start
  3.6 0.1 broadcast_bitcast_fusion
  3.6 0.1 constant_dynamic-update-slice_fusion.19
  3.7 0.1 fusion.6
  3.8 0.1 maximum_bitcast_fusion
  3.8 0.8 collective-permute-done.1
  4.6 2.1 %pad_maximum_fusion.2.refs_10_ = bf16[2,2,128,1024]{3,2,1,0:T(8,128)(2,1)} fusion(bf16[2,1,128,1024]{3,2,1,0:T(8,128)(2,1)} %bitcast.8, bf16[2,1,128,1024]{3,2,1,0:T(8,128)(2,1)S(1)} %maximum_bitcast_fusion), kind=kLoop, calls=%fused_computation.4 | loop fusion | flops 524288 | bytes 2097152 | tf_op jit(solution)/shard_map/stack | solution.py:173
  6.7 4.2 %collective-permute-start.2 = (bf16[2,2,128,1024]{3,2,1,0:T(8,128)(2,1)}, bf16[2,2,128,1024]{3,2,1,0:T(8,128)(2,1)}, u32[]{:S(2)}, u32[]{:S(2)}) collective-permute-start(bf16[2,2,128,1024]{3,2,1,0:T(8,128)(2,1)} %pad_maximum_fusion.2.refs_10_), channel_id=1, source_target_pairs={{0,8},{1,9},{2,10},{3,11},{4,12},{5,13},{6,14},{7,15},{8,16},{9,17... | collective-permute-start | bytes 3145736 | tf_op jit(solution)/shard_map/ppermute | solution.py:26
  10.9 0.1 constant_dynamic-update-slice_fusion.15
  11.0 0.1 constant_dynamic-update-slice_fusion.13
  11.0 0.1 constant_dynamic-update-slice_fusion.11
  11.1 0.1 constant_dynamic-update-slice_fusion.9
  11.2 0.1 constant_dynamic-update-slice_fusion.7
  11.3 0.1 constant_dynamic-update-slice_fusion.5
  11.4 1.3 collective-permute-start.7
  12.7 0.1 constant_dynamic-update-slice_fusion.3
  12.7 0.1 constant_dynamic-update-slice_fusion
  12.8 19.5 %collective-permute-done.2.refs_6_ = bf16[2,2,128,1024]{3,2,1,0:T(8,128)(2,1)} collective-permute-done((bf16[2,2,128,1024]{3,2,1,0:T(8,128)(2,1)}, bf16[2,2,128,1024]{3,2,1,0:T(8,128)(2,1)}, u32[]{:S(2)}, u32[]{:S(2)}) %collective-permute-start.2) | collective-permute-done | bytes 1048608 | tf_op jit(solution)/shard_map/ppermute | solution.py:26
  32.4 3.1 %collective-permute-start.8 = (bf16[2,2,128,1024]{3,2,1,0:T(8,128)(2,1)}, bf16[2,2,128,1024]{3,2,1,0:T(8,128)(2,1)}, u32[]{:S(2)}, u32[]{:S(2)}) collective-permute-start(bf16[2,2,128,1024]{3,2,1,0:T(8,128)(2,1)} %collective-permute-done.2.refs_6_), channel_id=1, source_target_pairs={{6,0},{7,1},{14,8},{15,9},{22,16},{23,17},{30,24},{31,25}} | collective-permute-start | bytes 3145736 | tf_op jit(solution)/shard_map/ppermute | solution.py:26
  35.4 0.4 fusion.2
  35.9 1.3 collective-permute-start.5
  37.2 4.1 %collective-permute-start.6 = (bf16[2,2,128,1024]{3,2,1,0:T(8,128)(2,1)}, bf16[2,2,128,1024]{3,2,1,0:T(8,128)(2,1)S(1)}, u32[]{:S(2)}, u32[]{:S(2)}) collective-permute-start(bf16[2,2,128,1024]{3,2,1,0:T(8,128)(2,1)} %collective-permute-done.2.refs_6_), channel_id=1, source_target_pairs={{4,0},{5,1},{6,2},{7,3},{12,8},{13,9},{14,10},{15,11},{20,16},{21,... | collective-permute-start | bytes 3145736 | tf_op jit(solution)/shard_map/ppermute | solution.py:26
  41.4 1.7 pad_maximum_fusion.refs_1_
  43.1 1.3 collective-permute-start.3
  44.4 1.4 collective-permute-start.4
  45.7 1.0 slice_bitcast_fusion.1
  46.8 9.3 %collective-permute-done.8 = bf16[2,2,128,1024]{3,2,1,0:T(8,128)(2,1)} collective-permute-done((bf16[2,2,128,1024]{3,2,1,0:T(8,128)(2,1)}, bf16[2,2,128,1024]{3,2,1,0:T(8,128)(2,1)}, u32[]{:S(2)}, u32[]{:S(2)}) %collective-permute-start.8) | collective-permute-done | bytes 1048608 | tf_op jit(solution)/shard_map/ppermute | solution.py:26
  56.1 2.3 %broadcast_select_fusion.refs_9_ = bf16[2,2,128,1024]{3,2,1,0:T(8,128)(2,1)} fusion(bf16[2,2,128,1024]{3,2,1,0:T(8,128)(2,1)} %collective-permute-done.7, bf16[2,2,128,1024]{3,2,1,0:T(8,128)(2,1)} %collective-permute-done.8, pred[]{:T(512)S(6)} %ge.19), kind=kLoop, calls=%fused_computation.7 | loop fusion | flops 524288 | bytes 3145729 | tf_op jit(solution)/shard_map/jit(_where)/select_n | solution.py:55
  58.4 25.3 %collective-permute-done.5 = bf16[2,2,128,1024]{3,2,1,0:T(8,128)(2,1)S(1)} collective-permute-done((bf16[2,2,128,1024]{3,2,1,0:T(8,128)(2,1)}, bf16[2,2,128,1024]{3,2,1,0:T(8,128)(2,1)S(1)}, u32[]{:S(2)}, u32[]{:S(2)}) %collective-permute-start.5) | collective-permute-done | bytes 1048608 | tf_op jit(solution)/shard_map/ppermute | solution.py:26
  83.7 1.1 collective-permute-done.6
  84.8 1.1 broadcast_select_fusion.1.refs_8_
  85.8 1.1 broadcast_select_fusion.2.refs_7_
  87.0 25.4 %shard_map.76 = (bf16[128,2048]{1,0:T(8,128)(2,1)}, bf16[128,2048]{1,0:T(8,128)(2,1)}, f32[2,2,128,1024]{3,2,1,0:T(8,128)}, f32[2,2,128,1024]{3,2,1,0:T(8,128)},...) custom-call(s32[1]{0:T(128)} %bitcast.refs_0_, ...), custom_call_target="tpu_custom_call" | custom-call | flops 6710886400 | bytes 21495808 | tf_op jit(solution)/shard_map/pallas_call | solution.py:133
  112.3 1.9 convert_element_type.63
  114.2 1.4 collective-permute-start.12
  115.7 0.2 convert_element_type.65
  115.9 1.4 collective-permute-start.13
  117.3 0.2 convert_element_type.67
  117.5 1.3 collective-permute-start.14
  118.8 4.7 %collective-permute-start.10 = (bf16[2,2,128,1024]{3,2,1,0:T(8,128)(2,1)S(1)}, bf16[2,2,128,1024]{3,2,1,0:T(8,128)(2,1)S(1)}, u32[]{:S(2)}, u32[]{:S(2)}) collective-permute-start(bf16[2,2,128,1024]{3,2,1,0:T(8,128)(2,1)S(1)} %convert_element_type.65), channel_id=1, source_target_pairs={{4,0},{5,1},{6,2},{7,3},{12,8},{13,9},{14,10},{15,11},{20,16},{21,... | collective-permute-start | bytes 3145736 | tf_op jit(solution)/shard_map/ppermute | solution.py:26
  123.5 2.5 %collective-permute-start.11 = (bf16[2,2,128,1024]{3,2,1,0:T(8,128)(2,1)S(1)}, bf16[2,2,128,1024]{3,2,1,0:T(8,128)(2,1)S(1)}, u32[]{:S(2)}, u32[]{:S(2)}) collective-permute-start(bf16[2,2,128,1024]{3,2,1,0:T(8,128)(2,1)S(1)} %convert_element_type.67), channel_id=1, source_target_pairs={{6,0},{7,1},{14,8},{15,9},{22,16},{23,17},{30,24},{31,25}} | collective-permute-start | bytes 3145736 | tf_op jit(solution)/shard_map/ppermute | solution.py:26
  126.0 13.2 %collective-permute-done.12 = bf16[2,2,128,1024]{3,2,1,0:T(8,128)(2,1)S(1)} collective-permute-done((bf16[2,2,128,1024]{3,2,1,0:T(8,128)(2,1)S(1)}, bf16[2,2,128,1024]{3,2,1,0:T(8,128)(2,1)S(1)}, u32[]{:S(2)}, u32[]{:S(2)}) %collective-permute-start.12) | collective-permute-done | bytes 1048608 | tf_op jit(solution)/shard_map/ppermute | solution.py:26
  139.2 1.3 collective-permute-start.9
  140.6 24.1 %collective-permute-done.13 = bf16[2,2,128,1024]{3,2,1,0:T(8,128)(2,1)S(1)} collective-permute-done((bf16[2,2,128,1024]{3,2,1,0:T(8,128)(2,1)S(1)}, bf16[2,2,128,1024]{3,2,1,0:T(8,128)(2,1)S(1)}, u32[]{:S(2)}, u32[]{:S(2)}) %collective-permute-start.13) | collective-permute-done | bytes 1048608 | tf_op jit(solution)/shard_map/ppermute | solution.py:26
  164.7 0.8 add_convert_fusion.1
  165.6 1.3 collective-permute-start.15
  166.9 0.8 collective-permute-done.9
  167.7 25.0 %collective-permute-done.15 = bf16[2,2,128,1024]{3,2,1,0:T(8,128)(2,1)S(1)} collective-permute-done((bf16[2,2,128,1024]{3,2,1,0:T(8,128)(2,1)S(1)}, bf16[2,2,128,1024]{3,2,1,0:T(8,128)(2,1)S(1)}, u32[]{:S(2)}, u32[]{:S(2)}) %collective-permute-start.15) | collective-permute-done | bytes 1048608 | tf_op jit(solution)/shard_map/ppermute | solution.py:26
  192.8 1.0 add_convert_fusion
  193.8 0.1 slice_bitcast_fusion.4
  193.9 0.9 copy-done.6
  194.8 0.1 pad_maximum_fusion.3
  194.9 1.1 collective-permute-start.16
  196.0 2.3 %collective-permute-done.16 = bf16[128,4096]{1,0:T(8,128)(2,1)S(1)} collective-permute-done((bf16[128,4096]{1,0:T(8,128)(2,1)S(1)}, bf16[128,4096]{1,0:T(8,128)(2,1)S(1)}, u32[]{:S(2)}, u32[]{:S(2)}) %collective-permute-start.16) | collective-permute-done | bytes 1048608 | tf_op jit(solution)/shard_map/ppermute | solution.py:26
  198.3 0.9 maximum_select_fusion.2
  199.3 0.9 maximum_select_fusion.1
  200.2 1.2 maximum_select_fusion
  (36 shorter events, 0.2 us)
Async XLA Ops:
  0.6 2.9 %copy-start = (s32[1,32]{1,0:T(1,128)S(1)}, s32[1,32]{1,0:T(1,128)}, u32[]{:S(2)}) copy-start(s32[1,32]{1,0:T(1,128)} %param.9) | copy-start | bytes 388
  0.6 2.3 %copy-start.7 = (bf16[1,128,4096]{2,1,0:T(8,128)(2,1)S(1)}, bf16[1,128,4096]{2,1,0:T(8,128)(2,1)}, u32[]{:S(2)}) copy-start(bf16[1,128,4096]{2,1,0:T(8,128)(2,1)} %param.5) | copy-start | bytes 3145732
  0.7 2.3 %copy-start.8 = (bf16[1,128,4096]{2,1,0:T(8,128)(2,1)S(1)}, bf16[1,128,4096]{2,1,0:T(8,128)(2,1)}, u32[]{:S(2)}) copy-start(bf16[1,128,4096]{2,1,0:T(8,128)(2,1)} %param.8) | copy-start | bytes 3145732
  2.2 2.4 %collective-permute-start.1 = (bf16[2,128,1024]{2,1,0:T(8,128)(2,1)S(1)}, bf16[2,128,1024]{2,1,0:T(8,128)(2,1)}, u32[]{:S(2)}, u32[]{:S(2)}) collective-permute-start(bf16[2,128,1024]{2,1,0:T(8,128)(2,1)S(1)} %pad_maximum_fusion.4), channel_id=1, source_target_pairs={{0,1},{1,0},{2,3},{3,2},{4,5},{5,4},{6,7},{7,6},{8,9},{9,8},{10,11... | collective-permute-start | bytes 1572872 | tf_op jit(solution)/shard_map/ppermute | solution.py:26
  3.1 39.9 %collective-permute-start = (bf16[2,128,2048]{2,1,0:T(8,128)(2,1)S(1)}, bf16[2,128,2048]{2,1,0:T(8,128)(2,1)S(1)}, u32[]{:S(2)}, u32[]{:S(2)}) collective-permute-start(bf16[2,128,2048]{2,1,0:T(8,128)(2,1)S(1)} %pad_maximum_fusion.1), channel_id=1, source_target_pairs={{0,1},{1,0},{2,3},{3,2},{4,5},{5,4},{6,7},{7,6},{8,9},{9,8},{10,11... | collective-permute-start | bytes 3145736 | tf_op jit(solution)/shard_map/ppermute | solution.py:26
  6.7 25.7 %collective-permute-start.2 = (bf16[2,2,128,1024]{3,2,1,0:T(8,128)(2,1)}, bf16[2,2,128,1024]{3,2,1,0:T(8,128)(2,1)}, u32[]{:S(2)}, u32[]{:S(2)}) collective-permute-start(bf16[2,2,128,1024]{3,2,1,0:T(8,128)(2,1)} %pad_maximum_fusion.2.refs_10_), channel_id=1, source_target_pairs={{0,8},{1,9},{2,10},{3,11},{4,12},{5,13},{6,14},{7,15},{8,16},{9,17... | collective-permute-start | bytes 3145736 | tf_op jit(solution)/shard_map/ppermute | solution.py:26
  11.4 33.0 %collective-permute-start.7 = (bf16[2,2,128,1024]{3,2,1,0:T(8,128)(2,1)}, bf16[2,2,128,1024]{3,2,1,0:T(8,128)(2,1)}, u32[]{:S(2)}, u32[]{:S(2)}) collective-permute-start(bf16[2,2,128,1024]{3,2,1,0:T(8,128)(2,1)} %pad_maximum_fusion.2.refs_10_), channel_id=1, source_target_pairs={{0,2},{1,3},{2,4},{3,5},{4,6},{5,7},{8,10},{9,11},{10,12},{11,13},... | collective-permute-start | bytes 3145736 | tf_op jit(solution)/shard_map/ppermute | solution.py:26
  32.4 23.7 %collective-permute-start.8 = (bf16[2,2,128,1024]{3,2,1,0:T(8,128)(2,1)}, bf16[2,2,128,1024]{3,2,1,0:T(8,128)(2,1)}, u32[]{:S(2)}, u32[]{:S(2)}) collective-permute-start(bf16[2,2,128,1024]{3,2,1,0:T(8,128)(2,1)} %collective-permute-done.2.refs_6_), channel_id=1, source_target_pairs={{6,0},{7,1},{14,8},{15,9},{22,16},{23,17},{30,24},{31,25}} | collective-permute-start | bytes 3145736 | tf_op jit(solution)/shard_map/ppermute | solution.py:26
  35.9 47.7 %collective-permute-start.5 = (bf16[2,2,128,1024]{3,2,1,0:T(8,128)(2,1)}, bf16[2,2,128,1024]{3,2,1,0:T(8,128)(2,1)S(1)}, u32[]{:S(2)}, u32[]{:S(2)}) collective-permute-start(bf16[2,2,128,1024]{3,2,1,0:T(8,128)(2,1)} %pad_maximum_fusion.2.refs_10_), channel_id=1, source_target_pairs={{0,4},{1,5},{2,6},{3,7},{8,12},{9,13},{10,14},{11,15},{16,20},{17,... | collective-permute-start | bytes 3145736 | tf_op jit(solution)/shard_map/ppermute | solution.py:26
  37.2 47.5 %collective-permute-start.6 = (bf16[2,2,128,1024]{3,2,1,0:T(8,128)(2,1)}, bf16[2,2,128,1024]{3,2,1,0:T(8,128)(2,1)S(1)}, u32[]{:S(2)}, u32[]{:S(2)}) collective-permute-start(bf16[2,2,128,1024]{3,2,1,0:T(8,128)(2,1)} %collective-permute-done.2.refs_6_), channel_id=1, source_target_pairs={{4,0},{5,1},{6,2},{7,3},{12,8},{13,9},{14,10},{15,11},{20,16},{21,... | collective-permute-start | bytes 3145736 | tf_op jit(solution)/shard_map/ppermute | solution.py:26
  43.1 42.8 %collective-permute-start.3 = (bf16[2,2,128,1024]{3,2,1,0:T(8,128)(2,1)}, bf16[2,2,128,1024]{3,2,1,0:T(8,128)(2,1)S(1)}, u32[]{:S(2)}, u32[]{:S(2)}) collective-permute-start(bf16[2,2,128,1024]{3,2,1,0:T(8,128)(2,1)} %pad_maximum_fusion.2.refs_10_), channel_id=1, source_target_pairs={{0,6},{1,7},{8,14},{9,15},{16,22},{17,23},{24,30},{25,31}} | collective-permute-start | bytes 3145736 | tf_op jit(solution)/shard_map/ppermute | solution.py:26
  44.4 41.5 %collective-permute-start.4 = (bf16[2,2,128,1024]{3,2,1,0:T(8,128)(2,1)}, bf16[2,2,128,1024]{3,2,1,0:T(8,128)(2,1)S(1)}, u32[]{:S(2)}, u32[]{:S(2)}) collective-permute-start(bf16[2,2,128,1024]{3,2,1,0:T(8,128)(2,1)} %collective-permute-done.2.refs_6_), channel_id=1, source_target_pairs={{2,0},{3,1},{4,2},{5,3},{6,4},{7,5},{10,8},{11,9},{12,10},{13,11},... | collective-permute-start | bytes 3145736 | tf_op jit(solution)/shard_map/ppermute | solution.py:26
  112.3 3.4 %copy-start.4 = (f32[2,2,128,1024]{3,2,1,0:T(8,128)S(1)}, f32[2,2,128,1024]{3,2,1,0:T(8,128)}, u32[]{:S(2)}) copy-start(f32[2,2,128,1024]{3,2,1,0:T(8,128)} %get-tuple-element.13) | copy-start | bytes 6291460
  114.2 3.1 %copy-start.3 = (f32[2,2,128,1024]{3,2,1,0:T(8,128)S(1)}, f32[2,2,128,1024]{3,2,1,0:T(8,128)}, u32[]{:S(2)}) copy-start(f32[2,2,128,1024]{3,2,1,0:T(8,128)} %get-tuple-element.14) | copy-start | bytes 6291460
  114.2 25.0 %collective-permute-start.12 = (bf16[2,2,128,1024]{3,2,1,0:T(8,128)(2,1)S(1)}, bf16[2,2,128,1024]{3,2,1,0:T(8,128)(2,1)S(1)}, u32[]{:S(2)}, u32[]{:S(2)}) collective-permute-start(bf16[2,2,128,1024]{3,2,1,0:T(8,128)(2,1)S(1)} %convert_element_type.63), channel_id=1, source_target_pairs={{0,6},{1,7},{8,14},{9,15},{16,22},{17,23},{24,30},{25,31}} | collective-permute-start | bytes 3145736 | tf_op jit(solution)/shard_map/ppermute | solution.py:26
  115.9 48.9 %copy-start.2 = (f32[2,2,128,1024]{3,2,1,0:T(8,128)S(1)}, f32[2,2,128,1024]{3,2,1,0:T(8,128)}, u32[]{:S(2)}) copy-start(f32[2,2,128,1024]{3,2,1,0:T(8,128)} %get-tuple-element.15) | copy-start | bytes 6291460
  115.9 48.9 %collective-permute-start.13 = (bf16[2,2,128,1024]{3,2,1,0:T(8,128)(2,1)S(1)}, bf16[2,2,128,1024]{3,2,1,0:T(8,128)(2,1)S(1)}, u32[]{:S(2)}, u32[]{:S(2)}) collective-permute-start(bf16[2,2,128,1024]{3,2,1,0:T(8,128)(2,1)S(1)} %convert_element_type.65), channel_id=1, source_target_pairs={{0,4},{1,5},{2,6},{3,7},{8,12},{9,13},{10,14},{11,15},{16,20},{17,... | collective-permute-start | bytes 3145736 | tf_op jit(solution)/shard_map/ppermute | solution.py:26
  117.5 47.3 %collective-permute-start.14 = (bf16[2,2,128,1024]{3,2,1,0:T(8,128)(2,1)S(1)}, bf16[2,2,128,1024]{3,2,1,0:T(8,128)(2,1)S(1)}, u32[]{:S(2)}, u32[]{:S(2)}) collective-permute-start(bf16[2,2,128,1024]{3,2,1,0:T(8,128)(2,1)S(1)} %convert_element_type.67), channel_id=1, source_target_pairs={{0,2},{1,3},{2,4},{3,5},{4,6},{5,7},{8,10},{9,11},{10,12},{11,13},... | collective-permute-start | bytes 3145736 | tf_op jit(solution)/shard_map/ppermute | solution.py:26
  118.8 48.1 %collective-permute-start.10 = (bf16[2,2,128,1024]{3,2,1,0:T(8,128)(2,1)S(1)}, bf16[2,2,128,1024]{3,2,1,0:T(8,128)(2,1)S(1)}, u32[]{:S(2)}, u32[]{:S(2)}) collective-permute-start(bf16[2,2,128,1024]{3,2,1,0:T(8,128)(2,1)S(1)} %convert_element_type.65), channel_id=1, source_target_pairs={{4,0},{5,1},{6,2},{7,3},{12,8},{13,9},{14,10},{15,11},{20,16},{21,... | collective-permute-start | bytes 3145736 | tf_op jit(solution)/shard_map/ppermute | solution.py:26
  123.5 43.4 %collective-permute-start.11 = (bf16[2,2,128,1024]{3,2,1,0:T(8,128)(2,1)S(1)}, bf16[2,2,128,1024]{3,2,1,0:T(8,128)(2,1)S(1)}, u32[]{:S(2)}, u32[]{:S(2)}) collective-permute-start(bf16[2,2,128,1024]{3,2,1,0:T(8,128)(2,1)S(1)} %convert_element_type.67), channel_id=1, source_target_pairs={{6,0},{7,1},{14,8},{15,9},{22,16},{23,17},{30,24},{31,25}} | collective-permute-start | bytes 3145736 | tf_op jit(solution)/shard_map/ppermute | solution.py:26
  139.2 28.5 %collective-permute-start.9 = (bf16[2,2,128,1024]{3,2,1,0:T(8,128)(2,1)S(1)}, bf16[2,2,128,1024]{3,2,1,0:T(8,128)(2,1)S(1)}, u32[]{:S(2)}, u32[]{:S(2)}) collective-permute-start(bf16[2,2,128,1024]{3,2,1,0:T(8,128)(2,1)S(1)} %convert_element_type.63), channel_id=1, source_target_pairs={{2,0},{3,1},{4,2},{5,3},{6,4},{7,5},{10,8},{11,9},{12,10},{13,11},... | collective-permute-start | bytes 3145736 | tf_op jit(solution)/shard_map/ppermute | solution.py:26
  164.7 28.0 %copy-start.1 = (f32[2,2,128,1024]{3,2,1,0:T(8,128)S(1)}, f32[2,2,128,1024]{3,2,1,0:T(8,128)}, u32[]{:S(2)}) copy-start(f32[2,2,128,1024]{3,2,1,0:T(8,128)} %get-tuple-element.11) | copy-start | bytes 6291460
  165.6 27.2 %collective-permute-start.15 = (bf16[2,2,128,1024]{3,2,1,0:T(8,128)(2,1)S(1)}, bf16[2,2,128,1024]{3,2,1,0:T(8,128)(2,1)S(1)}, u32[]{:S(2)}, u32[]{:S(2)}) collective-permute-start(bf16[2,2,128,1024]{3,2,1,0:T(8,128)(2,1)S(1)} %add_convert_fusion.1), channel_id=1, source_target_pairs={{8,0},{9,1},{10,2},{11,3},{12,4},{13,5},{14,6},{15,7},{16,8},{17,9... | collective-permute-start | bytes 3145736 | tf_op jit(solution)/shard_map/ppermute | solution.py:26
  193.8 1.0 copy-start.6
  194.9 3.4 %collective-permute-start.16 = (bf16[128,4096]{1,0:T(8,128)(2,1)S(1)}, bf16[128,4096]{1,0:T(8,128)(2,1)S(1)}, u32[]{:S(2)}, u32[]{:S(2)}) collective-permute-start(bf16[128,4096]{1,0:T(8,128)(2,1)S(1)} %pad_maximum_fusion.3), channel_id=1, source_target_pairs={{0,1},{1,0},{2,3},{3,2},{4,5},{5,4},{6,7},{7,6},{8,9},{9,8},{10,11... | collective-permute-start | bytes 3145736 | tf_op jit(solution)/shard_map/ppermute | solution.py:26
  196.0 4.2 %copy-start.5 = (bf16[128,2048]{1,0:T(8,128)(2,1)S(1)}, bf16[128,2048]{1,0:T(8,128)(2,1)}, u32[]{:S(2)}) copy-start(bf16[128,2048]{1,0:T(8,128)(2,1)} %get-tuple-element.10) | copy-start | bytes 1572868

commit v7 on v6

--- a/solution.py
+++ b/solution.py
@@ -36,6 +36,7 @@
         self.chips = reach // 2
         group_chip = lambda i: (i % reach) // 2
         self.hop = [(i, i + reach) for i in range(count - reach)]
+        self.hop_cross = [(i, (i + reach) ^ 1) for i in range(count - reach)]
         self.up = []
         self.down = []
         for e in range(1, self.chips):
@@ -46,8 +47,8 @@
         self.sibling = [(i, i ^ 1) for i in range(count)]
 
 
-def gather_window(own, routes, chip_in_group):
-    prev = moved(own, routes.hop)
+def gather_window(own, mine, theirs, routes, chip_in_group):
+    prev = jnp.stack([moved(mine, routes.hop), moved(theirs, routes.hop_cross)], axis=1)
     recv = []
     for e in range(1, routes.chips):
         up = moved(own, routes.up[e - 1])
@@ -176,7 +177,7 @@
          lax.dynamic_slice_in_dim(grad_out, other * query_width, query_width, 1)]
     )
     qd_sib = moved(qd_sent, routes.sibling)
-    payloads = gather_window(own, routes, chip_in_group)
+    payloads = gather_window(own, kv_mine, kv_sent, routes, chip_in_group)
 
     chip = position // 2
     block_of = lambda m, s: 2 * m + jnp.where(s == 0, core, other)
@@ -202,16 +203,11 @@
         core[None].astype(jnp.int32), bias, queries[0], qd_sib[0], grad_out, qd_sib[1], payloads
     )
     dq_mine, dq_sib, parts = outs[0], outs[1], outs[2:]
+    grad_query = in_core_order(core, dq_mine, moved(dq_sib, routes.sibling))
     summed = scatter_window(parts, routes)
-    sent = jnp.concatenate(
-        [summed[0, 1].astype(jnp.bfloat16), summed[1, 1].astype(jnp.bfloat16), dq_sib], axis=-1
-    )
-    got = moved(sent, routes.sibling)
-    grad_key = in_core_order(core, summed[0, 0].astype(jnp.bfloat16), got[:, :key_width])
-    grad_value = in_core_order(
-        core, summed[1, 0].astype(jnp.bfloat16), got[:, key_width : 2 * key_width]
-    )
-    grad_query = in_core_order(core, dq_mine, got[:, 2 * key_width :])
+    got = moved(summed[:, 1].astype(jnp.bfloat16), routes.sibling)
+    grad_key = in_core_order(core, summed[0, 0].astype(jnp.bfloat16), got[0])
+    grad_value = in_core_order(core, summed[1, 0].astype(jnp.bfloat16), got[1])
     return (grad_query[None], grad_key[None], grad_value[None])
 
 

time: 202 us -> 209 us (1.035)
  other arithmetic: 16.3 us -> 24.5 us
  waiting for transfers between devices: 121 us -> 113 us
  starting transfers between devices: 32.8 us -> 39.8 us
    ppermute x17 -> x19, waiting for transfers between devices: 121 us -> 113 us  [moved(): return lax.ppermute(value, 'seq', pairs)]
    ppermute x17 -> x19, starting transfers between devices: 32.8 us -> 39.8 us  [moved(): return lax.ppermute(value, 'seq', pairs)]
    another operation x1 -> x2, other arithmetic: 1.01 us -> 5.56 us
  transfers between devices with their start and end apart: 17 -> 19, of which waited for: 10 -> 9; matrix products, arithmetic and copies ran while one was open for 5% -> 10% of each run, Pallas kernels for 0% -> 0%
where the time goes in v7:
time: 209 us; the launch traced here: 207 us
  waiting for transfers between devices  113 us (54%)
  starting transfers between devices  39.8 us (19%)
  Pallas kernels  25.4 us (12%)
  other arithmetic  24.5 us (12%)
  local copies, waits for them, and re-layouts  3.46 us (2%)
    ppermute x19, waiting for transfers between devices, moved(): return lax.ppermute(value, 'seq', pairs)  113 us
    ppermute x19, starting transfers between devices, moved(): return lax.ppermute(value, 'seq', pairs)  39.8 us
    pallas_call x1, Pallas kernels, attention_grads(): pl.pallas_call(lambda *refs: attention_kernel(chips, *refs), grid_spec=gr...  25.4 us
    select_n x3, other arithmetic, gather_window(): recv.append(jnp.where(chip_in_group >= e, up, down))  4.56 us
  transfers between devices with their start and end apart: 19, of which 9 were waited for; matrix products, arithmetic and copies ran while one was open for 10% of the time, Pallas kernels for 0%

profile of v7, /device:TPU:7, one launch (start us, length us, event | category | flops | bytes accessed | tf_op | source)
XLA Modules:
  0.0 207.3 jit_solution(14717058054404504121)
XLA Ops:
  0.6 0.0 copy-start
  0.7 0.0 copy-start.6
  0.7 0.0 copy-start.7
  0.7 1.4 constant_dynamic-slice_fusion.2
  2.1 0.8 pad_maximum_fusion.5
  2.9 4.6 %collective-permute-start.2 = (bf16[2,128,1024]{2,1,0:T(8,128)(2,1)}, bf16[2,128,1024]{2,1,0:T(8,128)(2,1)}, u32[]{:S(2)}, u32[]{:S(2)}) collective-permute-start(bf16[2,128,1024]{2,1,0:T(8,128)(2,1)} %pad_maximum_fusion.5), channel_id=1, source_target_pairs={{0,9},{1,8},{2,11},{3,10},{4,13},{5,12},{6,15},{7,14},{8,17},{9,16... | collective-permute-start | bytes 1572872 | tf_op jit(solution)/shard_map/ppermute | solution.py:26
  7.5 0.1 fusion.6
  7.6 3.3 %collective-permute-start.1 = (bf16[2,128,1024]{2,1,0:T(8,128)(2,1)S(1)}, bf16[2,128,1024]{2,1,0:T(8,128)(2,1)}, u32[]{:S(2)}, u32[]{:S(2)}) collective-permute-start(bf16[2,128,1024]{2,1,0:T(8,128)(2,1)S(1)} %get-tuple-element.24), channel_id=1, source_target_pairs={{0,8},{1,9},{2,10},{3,11},{4,12},{5,13},{6,14},{7,15},{8,16},{9,17... | collective-permute-start | bytes 1572872 | tf_op jit(solution)/shard_map/ppermute | solution.py:26
  10.9 0.1 constant_dynamic-slice_fusion.4
  10.9 0.1 pad_maximum_fusion.1
  11.1 0.8 collective-permute-start
  11.9 0.1 broadcast_bitcast_fusion
  12.1 0.1 constant_dynamic-update-slice_fusion.19
  12.2 0.1 fusion.8
  12.3 0.1 constant_dynamic-update-slice_fusion.15
  12.3 0.1 constant_dynamic-update-slice_fusion.13
  12.4 0.1 constant_dynamic-update-slice_fusion.11
  12.5 0.1 constant_dynamic-update-slice_fusion.9
  12.6 0.1 constant_dynamic-update-slice_fusion.7
  12.7 0.1 constant_dynamic-update-slice_fusion.5
  12.7 0.1 constant_dynamic-update-slice_fusion.3
  12.8 17.0 %collective-permute-done.1 = bf16[2,128,1024]{2,1,0:T(8,128)(2,1)} collective-permute-done((bf16[2,128,1024]{2,1,0:T(8,128)(2,1)S(1)}, bf16[2,128,1024]{2,1,0:T(8,128)(2,1)}, u32[]{:S(2)}, u32[]{:S(2)}) %collective-permute-start.1) | collective-permute-done | bytes 524320 | tf_op jit(solution)/shard_map/ppermute | solution.py:26
  29.9 0.0 collective-permute-done.2
  29.9 2.3 %pad_maximum_fusion.2.refs_6_ = bf16[2,2,128,1024]{3,2,1,0:T(8,128)(2,1)} fusion(bf16[2,1,128,1024]{3,2,1,0:T(8,128)(2,1)} %bitcast.8, bf16[2,1,128,1024]{3,2,1,0:T(8,128)(2,1)} %bitcast.7), kind=kLoop, calls=%fused_computation.4 | loop fusion | flops 524288 | bytes 2097152 | tf_op jit(solution)/shard_map/stack | solution.py:51
  32.1 3.1 %collective-permute-start.9 = (bf16[2,2,128,1024]{3,2,1,0:T(8,128)(2,1)}, bf16[2,2,128,1024]{3,2,1,0:T(8,128)(2,1)}, u32[]{:S(2)}, u32[]{:S(2)}) collective-permute-start(bf16[2,2,128,1024]{3,2,1,0:T(8,128)(2,1)} %pad_maximum_fusion.2.refs_6_), channel_id=1, source_target_pairs={{6,0},{7,1},{14,8},{15,9},{22,16},{23,17},{30,24},{31,25}} | collective-permute-start | bytes 3145736 | tf_op jit(solution)/shard_map/ppermute | solution.py:26
  35.2 0.1 constant_dynamic-update-slice_fusion
  35.3 2.1 %pad_maximum_fusion.3.refs_10_ = bf16[2,2,128,1024]{3,2,1,0:T(8,128)(2,1)} fusion(bf16[2,1,128,1024]{3,2,1,0:T(8,128)(2,1)} %bitcast.12, bf16[2,1,128,1024]{3,2,1,0:T(8,128)(2,1)S(1)} %get-tuple-element.23), kind=kLoop, calls=%fused_computation.5 | loop fusion | flops 524288 | bytes 2097152 | tf_op jit(solution)/shard_map/stack | solution.py:174
  37.4 1.3 collective-permute-start.8
  38.7 0.5 fusion.2
  39.2 2.6 %collective-permute-start.7 = (bf16[2,2,128,1024]{3,2,1,0:T(8,128)(2,1)}, bf16[2,2,128,1024]{3,2,1,0:T(8,128)(2,1)S(1)}, u32[]{:S(2)}, u32[]{:S(2)}) collective-permute-start(bf16[2,2,128,1024]{3,2,1,0:T(8,128)(2,1)} %pad_maximum_fusion.2.refs_6_), channel_id=1, source_target_pairs={{4,0},{5,1},{6,2},{7,3},{12,8},{13,9},{14,10},{15,11},{20,16},{21,... | collective-permute-start | bytes 3145736 | tf_op jit(solution)/shard_map/ppermute | solution.py:26
  41.8 1.3 collective-permute-start.6
  43.1 1.7 pad_maximum_fusion.refs_1_
  44.8 3.2 %collective-permute-start.5 = (bf16[2,2,128,1024]{3,2,1,0:T(8,128)(2,1)}, bf16[2,2,128,1024]{3,2,1,0:T(8,128)(2,1)S(1)}, u32[]{:S(2)}, u32[]{:S(2)}) collective-permute-start(bf16[2,2,128,1024]{3,2,1,0:T(8,128)(2,1)} %pad_maximum_fusion.2.refs_6_), channel_id=1, source_target_pairs={{2,0},{3,1},{4,2},{5,3},{6,4},{7,5},{10,8},{11,9},{12,10},{13,11},... | collective-permute-start | bytes 3145736 | tf_op jit(solution)/shard_map/ppermute | solution.py:26
  48.0 8.7 %collective-permute-done.9 = bf16[2,2,128,1024]{3,2,1,0:T(8,128)(2,1)} collective-permute-done((bf16[2,2,128,1024]{3,2,1,0:T(8,128)(2,1)}, bf16[2,2,128,1024]{3,2,1,0:T(8,128)(2,1)}, u32[]{:S(2)}, u32[]{:S(2)}) %collective-permute-start.9) | collective-permute-done | bytes 1048608 | tf_op jit(solution)/shard_map/ppermute | solution.py:26
  56.7 1.3 collective-permute-start.4
  58.0 1.0 slice_bitcast_fusion.1
  59.0 4.6 %collective-permute-done.8 = bf16[2,2,128,1024]{3,2,1,0:T(8,128)(2,1)} collective-permute-done((bf16[2,2,128,1024]{3,2,1,0:T(8,128)(2,1)}, bf16[2,2,128,1024]{3,2,1,0:T(8,128)(2,1)}, u32[]{:S(2)}, u32[]{:S(2)}) %collective-permute-start.8) | collective-permute-done | bytes 1048608 | tf_op jit(solution)/shard_map/ppermute | solution.py:26
  63.6 2.3 %broadcast_select_fusion.refs_9_ = bf16[2,2,128,1024]{3,2,1,0:T(8,128)(2,1)} fusion(bf16[2,2,128,1024]{3,2,1,0:T(8,128)(2,1)} %collective-permute-done.8, bf16[2,2,128,1024]{3,2,1,0:T(8,128)(2,1)} %collective-permute-done.9, pred[]{:T(512)S(6)} %ge.19), kind=kLoop, calls=%fused_computation.7 | loop fusion | flops 524288 | bytes 3145729 | tf_op jit(solution)/shard_map/jit(_where)/select_n | solution.py:56
  66.0 24.1 %collective-permute-done.6 = bf16[2,2,128,1024]{3,2,1,0:T(8,128)(2,1)S(1)} collective-permute-done((bf16[2,2,128,1024]{3,2,1,0:T(8,128)(2,1)}, bf16[2,2,128,1024]{3,2,1,0:T(8,128)(2,1)S(1)}, u32[]{:S(2)}, u32[]{:S(2)}) %collective-permute-start.6) | collective-permute-done | bytes 1048608 | tf_op jit(solution)/shard_map/ppermute | solution.py:26
  90.0 1.1 broadcast_select_fusion.1.refs_8_
  91.1 1.1 broadcast_select_fusion.2.refs_7_
  92.3 25.4 %shard_map.76 = (bf16[128,2048]{1,0:T(8,128)(2,1)}, bf16[128,2048]{1,0:T(8,128)(2,1)}, f32[2,2,128,1024]{3,2,1,0:T(8,128)}, f32[2,2,128,1024]{3,2,1,0:T(8,128)},...) custom-call(s32[1]{0:T(128)} %bitcast.refs_0_, ...), custom_call_target="tpu_custom_call" | custom-call | flops 6710886400 | bytes 21495808 | tf_op jit(solution)/shard_map/pallas_call | solution.py:134
  117.7 1.9 convert_element_type.59
  119.6 1.4 collective-permute-start.14
  121.0 1.1 convert_element_type.61
  122.1 1.4 collective-permute-start.15
  123.6 1.1 convert_element_type.63
  124.7 1.3 collective-permute-start.16
  126.0 5.0 %collective-permute-start.11 = (bf16[2,2,128,1024]{3,2,1,0:T(8,128)(2,1)S(1)}, bf16[2,2,128,1024]{3,2,1,0:T(8,128)(2,1)}, u32[]{:S(2)}, u32[]{:S(2)}) collective-permute-start(bf16[2,2,128,1024]{3,2,1,0:T(8,128)(2,1)S(1)} %convert_element_type.59), channel_id=1, source_target_pairs={{2,0},{3,1},{4,2},{5,3},{6,4},{7,5},{10,8},{11,9},{12,10},{13,11},... | collective-permute-start | bytes 3145736 | tf_op jit(solution)/shard_map/ppermute | solution.py:26
  131.0 4.1 %collective-permute-start.12 = (bf16[2,2,128,1024]{3,2,1,0:T(8,128)(2,1)}, bf16[2,2,128,1024]{3,2,1,0:T(8,128)(2,1)}, u32[]{:S(2)}, u32[]{:S(2)}) collective-permute-start(bf16[2,2,128,1024]{3,2,1,0:T(8,128)(2,1)} %convert_element_type.61), channel_id=1, source_target_pairs={{4,0},{5,1},{6,2},{7,3},{12,8},{13,9},{14,10},{15,11},{20,16},{21,... | collective-permute-start | bytes 3145736 | tf_op jit(solution)/shard_map/ppermute | solution.py:26
  135.1 10.2 %collective-permute-done.14 = bf16[2,2,128,1024]{3,2,1,0:T(8,128)(2,1)S(1)} collective-permute-done((bf16[2,2,128,1024]{3,2,1,0:T(8,128)(2,1)S(1)}, bf16[2,2,128,1024]{3,2,1,0:T(8,128)(2,1)S(1)}, u32[]{:S(2)}, u32[]{:S(2)}) %collective-permute-start.14) | collective-permute-done | bytes 1048608 | tf_op jit(solution)/shard_map/ppermute | solution.py:26
  145.3 2.3 %collective-permute-start.13 = (bf16[2,2,128,1024]{3,2,1,0:T(8,128)(2,1)}, bf16[2,2,128,1024]{3,2,1,0:T(8,128)(2,1)}, u32[]{:S(2)}, u32[]{:S(2)}) collective-permute-start(bf16[2,2,128,1024]{3,2,1,0:T(8,128)(2,1)} %convert_element_type.63), channel_id=1, source_target_pairs={{6,0},{7,1},{14,8},{15,9},{22,16},{23,17},{30,24},{31,25}} | collective-permute-start | bytes 3145736 | tf_op jit(solution)/shard_map/ppermute | solution.py:26
  147.5 22.5 %collective-permute-done.15 = bf16[2,2,128,1024]{3,2,1,0:T(8,128)(2,1)S(1)} collective-permute-done((bf16[2,2,128,1024]{3,2,1,0:T(8,128)(2,1)}, bf16[2,2,128,1024]{3,2,1,0:T(8,128)(2,1)S(1)}, u32[]{:S(2)}, u32[]{:S(2)}) %collective-permute-start.15) | collective-permute-done | bytes 1048608 | tf_op jit(solution)/shard_map/ppermute | solution.py:26
  170.1 1.8 add_convert_fusion.1
  171.9 1.3 collective-permute-start.17
  173.1 0.6 collective-permute-start.10
  173.7 2.9 %collective-permute-done.12 = bf16[2,2,128,1024]{3,2,1,0:T(8,128)(2,1)} collective-permute-done((bf16[2,2,128,1024]{3,2,1,0:T(8,128)(2,1)}, bf16[2,2,128,1024]{3,2,1,0:T(8,128)(2,1)}, u32[]{:S(2)}, u32[]{:S(2)}) %collective-permute-start.12) | collective-permute-done | bytes 1048608 | tf_op jit(solution)/shard_map/ppermute | solution.py:26
  176.6 22.9 %collective-permute-done.17 = bf16[2,2,128,1024]{3,2,1,0:T(8,128)(2,1)} collective-permute-done((bf16[2,2,128,1024]{3,2,1,0:T(8,128)(2,1)}, bf16[2,2,128,1024]{3,2,1,0:T(8,128)(2,1)}, u32[]{:S(2)}, u32[]{:S(2)}) %collective-permute-start.17) | collective-permute-done | bytes 1048608 | tf_op jit(solution)/shard_map/ppermute | solution.py:26
  199.5 3.3 %add_convert_fusion = bf16[2,2,128,1024]{3,2,1,0:T(8,128)(2,1)S(1)} fusion(bf16[2,2,128,1024]{3,2,1,0:T(8,128)(2,1)} %collective-permute-done.17, bf16[2,2,128,1024]{3,2,1,0:T(8,128)(2,1)} %collective-permute-done.13, bf16[2,2,128,1024]{3,2,1,0:T(8,128)(2,1)} %collective-permute-done.12, f32[2,2,128,1024]{3,2,1,0:T(8,128)S(1)} %copy-done.1, ...), kind=kLoop, calls=%fused_computation.1 | loop fusion | flops 4718592 | bytes 7340032 | tf_op jit(solution)/shard_map/convert.2
  202.8 1.1 collective-permute-start.18
  203.9 1.2 maximum_select_fusion
  205.2 0.3 collective-permute-done.18
  205.5 0.9 maximum_select_fusion.2
  206.4 0.9 maximum_select_fusion.1
  (38 shorter events, 0.2 us)
Async XLA Ops:
  0.6 11.3 %copy-start = (s32[1,32]{1,0:T(1,128)S(1)}, s32[1,32]{1,0:T(1,128)}, u32[]{:S(2)}) copy-start(s32[1,32]{1,0:T(1,128)} %param.9) | copy-start | bytes 388
  0.7 10.2 %copy-start.6 = (bf16[1,128,4096]{2,1,0:T(8,128)(2,1)S(1)}, bf16[1,128,4096]{2,1,0:T(8,128)(2,1)}, u32[]{:S(2)}) copy-start(bf16[1,128,4096]{2,1,0:T(8,128)(2,1)} %param.5) | copy-start | bytes 3145732
  0.7 10.2 %copy-start.7 = (bf16[1,128,4096]{2,1,0:T(8,128)(2,1)S(1)}, bf16[1,128,4096]{2,1,0:T(8,128)(2,1)}, u32[]{:S(2)}) copy-start(bf16[1,128,4096]{2,1,0:T(8,128)(2,1)} %param.8) | copy-start | bytes 3145732
  2.9 26.9 %collective-permute-start.2 = (bf16[2,128,1024]{2,1,0:T(8,128)(2,1)}, bf16[2,128,1024]{2,1,0:T(8,128)(2,1)}, u32[]{:S(2)}, u32[]{:S(2)}) collective-permute-start(bf16[2,128,1024]{2,1,0:T(8,128)(2,1)} %pad_maximum_fusion.5), channel_id=1, source_target_pairs={{0,9},{1,8},{2,11},{3,10},{4,13},{5,12},{6,15},{7,14},{8,17},{9,16... | collective-permute-start | bytes 1572872 | tf_op jit(solution)/shard_map/ppermute | solution.py:26
  7.5 27.8 %collective-permute-start.3 = (bf16[2,128,1024]{2,1,0:T(8,128)(2,1)}, bf16[2,128,1024]{2,1,0:T(8,128)(2,1)}, u32[]{:S(2)}, u32[]{:S(2)}) collective-permute-start(bf16[2,128,1024]{2,1,0:T(8,128)(2,1)} %pad_maximum_fusion.5), channel_id=1, source_target_pairs={{0,1},{1,0},{2,3},{3,2},{4,5},{5,4},{6,7},{7,6},{8,9},{9,8},{10,11... | collective-permute-start | bytes 1572872 | tf_op jit(solution)/shard_map/ppermute | solution.py:26
  7.6 22.3 %collective-permute-start.1 = (bf16[2,128,1024]{2,1,0:T(8,128)(2,1)S(1)}, bf16[2,128,1024]{2,1,0:T(8,128)(2,1)}, u32[]{:S(2)}, u32[]{:S(2)}) collective-permute-start(bf16[2,128,1024]{2,1,0:T(8,128)(2,1)S(1)} %get-tuple-element.24), channel_id=1, source_target_pairs={{0,8},{1,9},{2,10},{3,11},{4,12},{5,13},{6,14},{7,15},{8,16},{9,17... | collective-permute-start | bytes 1572872 | tf_op jit(solution)/shard_map/ppermute | solution.py:26
  11.1 33.7 %collective-permute-start = (bf16[2,128,2048]{2,1,0:T(8,128)(2,1)S(1)}, bf16[2,128,2048]{2,1,0:T(8,128)(2,1)S(1)}, u32[]{:S(2)}, u32[]{:S(2)}) collective-permute-start(bf16[2,128,2048]{2,1,0:T(8,128)(2,1)S(1)} %pad_maximum_fusion.1), channel_id=1, source_target_pairs={{0,1},{1,0},{2,3},{3,2},{4,5},{5,4},{6,7},{7,6},{8,9},{9,8},{10,11... | collective-permute-start | bytes 3145736 | tf_op jit(solution)/shard_map/ppermute | solution.py:26
  32.1 24.6 %collective-permute-start.9 = (bf16[2,2,128,1024]{3,2,1,0:T(8,128)(2,1)}, bf16[2,2,128,1024]{3,2,1,0:T(8,128)(2,1)}, u32[]{:S(2)}, u32[]{:S(2)}) collective-permute-start(bf16[2,2,128,1024]{3,2,1,0:T(8,128)(2,1)} %pad_maximum_fusion.2.refs_6_), channel_id=1, source_target_pairs={{6,0},{7,1},{14,8},{15,9},{22,16},{23,17},{30,24},{31,25}} | collective-permute-start | bytes 3145736 | tf_op jit(solution)/shard_map/ppermute | solution.py:26
  37.4 26.2 %collective-permute-start.8 = (bf16[2,2,128,1024]{3,2,1,0:T(8,128)(2,1)}, bf16[2,2,128,1024]{3,2,1,0:T(8,128)(2,1)}, u32[]{:S(2)}, u32[]{:S(2)}) collective-permute-start(bf16[2,2,128,1024]{3,2,1,0:T(8,128)(2,1)} %pad_maximum_fusion.3.refs_10_), channel_id=1, source_target_pairs={{0,2},{1,3},{2,4},{3,5},{4,6},{5,7},{8,10},{9,11},{10,12},{11,13},... | collective-permute-start | bytes 3145736 | tf_op jit(solution)/shard_map/ppermute | solution.py:26
  39.2 26.8 %collective-permute-start.7 = (bf16[2,2,128,1024]{3,2,1,0:T(8,128)(2,1)}, bf16[2,2,128,1024]{3,2,1,0:T(8,128)(2,1)S(1)}, u32[]{:S(2)}, u32[]{:S(2)}) collective-permute-start(bf16[2,2,128,1024]{3,2,1,0:T(8,128)(2,1)} %pad_maximum_fusion.2.refs_6_), channel_id=1, source_target_pairs={{4,0},{5,1},{6,2},{7,3},{12,8},{13,9},{14,10},{15,11},{20,16},{21,... | collective-permute-start | bytes 3145736 | tf_op jit(solution)/shard_map/ppermute | solution.py:26
  41.8 48.3 %collective-permute-start.6 = (bf16[2,2,128,1024]{3,2,1,0:T(8,128)(2,1)}, bf16[2,2,128,1024]{3,2,1,0:T(8,128)(2,1)S(1)}, u32[]{:S(2)}, u32[]{:S(2)}) collective-permute-start(bf16[2,2,128,1024]{3,2,1,0:T(8,128)(2,1)} %pad_maximum_fusion.3.refs_10_), channel_id=1, source_target_pairs={{0,4},{1,5},{2,6},{3,7},{8,12},{9,13},{10,14},{11,15},{16,20},{17,... | collective-permute-start | bytes 3145736 | tf_op jit(solution)/shard_map/ppermute | solution.py:26
  44.8 46.3 %collective-permute-start.5 = (bf16[2,2,128,1024]{3,2,1,0:T(8,128)(2,1)}, bf16[2,2,128,1024]{3,2,1,0:T(8,128)(2,1)S(1)}, u32[]{:S(2)}, u32[]{:S(2)}) collective-permute-start(bf16[2,2,128,1024]{3,2,1,0:T(8,128)(2,1)} %pad_maximum_fusion.2.refs_6_), channel_id=1, source_target_pairs={{2,0},{3,1},{4,2},{5,3},{6,4},{7,5},{10,8},{11,9},{12,10},{13,11},... | collective-permute-start | bytes 3145736 | tf_op jit(solution)/shard_map/ppermute | solution.py:26
  56.7 34.5 %collective-permute-start.4 = (bf16[2,2,128,1024]{3,2,1,0:T(8,128)(2,1)}, bf16[2,2,128,1024]{3,2,1,0:T(8,128)(2,1)S(1)}, u32[]{:S(2)}, u32[]{:S(2)}) collective-permute-start(bf16[2,2,128,1024]{3,2,1,0:T(8,128)(2,1)} %pad_maximum_fusion.3.refs_10_), channel_id=1, source_target_pairs={{0,6},{1,7},{8,14},{9,15},{16,22},{17,23},{24,30},{25,31}} | collective-permute-start | bytes 3145736 | tf_op jit(solution)/shard_map/ppermute | solution.py:26
  117.7 3.3 %copy-start.4 = (f32[2,2,128,1024]{3,2,1,0:T(8,128)S(1)}, f32[2,2,128,1024]{3,2,1,0:T(8,128)}, u32[]{:S(2)}) copy-start(f32[2,2,128,1024]{3,2,1,0:T(8,128)} %get-tuple-element.14) | copy-start | bytes 6291460
  119.6 4.0 %copy-start.3 = (f32[2,2,128,1024]{3,2,1,0:T(8,128)S(1)}, f32[2,2,128,1024]{3,2,1,0:T(8,128)}, u32[]{:S(2)}) copy-start(f32[2,2,128,1024]{3,2,1,0:T(8,128)} %get-tuple-element.15) | copy-start | bytes 6291460
  119.6 25.7 %collective-permute-start.14 = (bf16[2,2,128,1024]{3,2,1,0:T(8,128)(2,1)S(1)}, bf16[2,2,128,1024]{3,2,1,0:T(8,128)(2,1)S(1)}, u32[]{:S(2)}, u32[]{:S(2)}) collective-permute-start(bf16[2,2,128,1024]{3,2,1,0:T(8,128)(2,1)S(1)} %convert_element_type.59), channel_id=1, source_target_pairs={{0,6},{1,7},{8,14},{9,15},{16,22},{17,23},{24,30},{25,31}} | collective-permute-start | bytes 3145736 | tf_op jit(solution)/shard_map/ppermute | solution.py:26
  122.1 47.9 %copy-start.2 = (f32[2,2,128,1024]{3,2,1,0:T(8,128)S(1)}, f32[2,2,128,1024]{3,2,1,0:T(8,128)}, u32[]{:S(2)}) copy-start(f32[2,2,128,1024]{3,2,1,0:T(8,128)} %get-tuple-element.16) | copy-start | bytes 6291460
  122.1 47.9 %collective-permute-start.15 = (bf16[2,2,128,1024]{3,2,1,0:T(8,128)(2,1)}, bf16[2,2,128,1024]{3,2,1,0:T(8,128)(2,1)S(1)}, u32[]{:S(2)}, u32[]{:S(2)}) collective-permute-start(bf16[2,2,128,1024]{3,2,1,0:T(8,128)(2,1)} %convert_element_type.61), channel_id=1, source_target_pairs={{0,4},{1,5},{2,6},{3,7},{8,12},{9,13},{10,14},{11,15},{16,20},{17,... | collective-permute-start | bytes 3145736 | tf_op jit(solution)/shard_map/ppermute | solution.py:26
  124.7 45.4 %collective-permute-start.16 = (bf16[2,2,128,1024]{3,2,1,0:T(8,128)(2,1)}, bf16[2,2,128,1024]{3,2,1,0:T(8,128)(2,1)S(1)}, u32[]{:S(2)}, u32[]{:S(2)}) collective-permute-start(bf16[2,2,128,1024]{3,2,1,0:T(8,128)(2,1)} %convert_element_type.63), channel_id=1, source_target_pairs={{0,2},{1,3},{2,4},{3,5},{4,6},{5,7},{8,10},{9,11},{10,12},{11,13},... | collective-permute-start | bytes 3145736 | tf_op jit(solution)/shard_map/ppermute | solution.py:26
  126.0 47.7 %collective-permute-start.11 = (bf16[2,2,128,1024]{3,2,1,0:T(8,128)(2,1)S(1)}, bf16[2,2,128,1024]{3,2,1,0:T(8,128)(2,1)}, u32[]{:S(2)}, u32[]{:S(2)}) collective-permute-start(bf16[2,2,128,1024]{3,2,1,0:T(8,128)(2,1)S(1)} %convert_element_type.59), channel_id=1, source_target_pairs={{2,0},{3,1},{4,2},{5,3},{6,4},{7,5},{10,8},{11,9},{12,10},{13,11},... | collective-permute-start | bytes 3145736 | tf_op jit(solution)/shard_map/ppermute | solution.py:26
  131.0 45.6 %collective-permute-start.12 = (bf16[2,2,128,1024]{3,2,1,0:T(8,128)(2,1)}, bf16[2,2,128,1024]{3,2,1,0:T(8,128)(2,1)}, u32[]{:S(2)}, u32[]{:S(2)}) collective-permute-start(bf16[2,2,128,1024]{3,2,1,0:T(8,128)(2,1)} %convert_element_type.61), channel_id=1, source_target_pairs={{4,0},{5,1},{6,2},{7,3},{12,8},{13,9},{14,10},{15,11},{20,16},{21,... | collective-permute-start | bytes 3145736 | tf_op jit(solution)/shard_map/ppermute | solution.py:26
  145.3 31.3 %collective-permute-start.13 = (bf16[2,2,128,1024]{3,2,1,0:T(8,128)(2,1)}, bf16[2,2,128,1024]{3,2,1,0:T(8,128)(2,1)}, u32[]{:S(2)}, u32[]{:S(2)}) collective-permute-start(bf16[2,2,128,1024]{3,2,1,0:T(8,128)(2,1)} %convert_element_type.63), channel_id=1, source_target_pairs={{6,0},{7,1},{14,8},{15,9},{22,16},{23,17},{30,24},{31,25}} | collective-permute-start | bytes 3145736 | tf_op jit(solution)/shard_map/ppermute | solution.py:26
  170.0 29.4 %copy-start.1 = (f32[2,2,128,1024]{3,2,1,0:T(8,128)S(1)}, f32[2,2,128,1024]{3,2,1,0:T(8,128)}, u32[]{:S(2)}) copy-start(f32[2,2,128,1024]{3,2,1,0:T(8,128)} %get-tuple-element.12) | copy-start | bytes 6291460
  171.9 27.6 %collective-permute-start.17 = (bf16[2,2,128,1024]{3,2,1,0:T(8,128)(2,1)}, bf16[2,2,128,1024]{3,2,1,0:T(8,128)(2,1)}, u32[]{:S(2)}, u32[]{:S(2)}) collective-permute-start(bf16[2,2,128,1024]{3,2,1,0:T(8,128)(2,1)} %add_convert_fusion.1), channel_id=1, source_target_pairs={{8,0},{9,1},{10,2},{11,3},{12,4},{13,5},{14,6},{15,7},{16,8},{17,9... | collective-permute-start | bytes 3145736 | tf_op jit(solution)/shard_map/ppermute | solution.py:26
  173.1 30.8 %collective-permute-start.10 = (bf16[128,2048]{1,0:T(8,128)(2,1)}, bf16[128,2048]{1,0:T(8,128)(2,1)S(1)}, u32[]{:S(2)}, u32[]{:S(2)}) collective-permute-start(bf16[128,2048]{1,0:T(8,128)(2,1)} %get-tuple-element.11), channel_id=1, source_target_pairs={{0,1},{1,0},{2,3},{3,2},{4,5},{5,4},{6,7},{7,6},{8,9},{9,8},{10,11... | collective-permute-start | bytes 1572872 | tf_op jit(solution)/shard_map/ppermute | solution.py:26
  199.5 4.4 %copy-start.5 = (bf16[128,2048]{1,0:T(8,128)(2,1)S(1)}, bf16[128,2048]{1,0:T(8,128)(2,1)}, u32[]{:S(2)}) copy-start(bf16[128,2048]{1,0:T(8,128)(2,1)} %get-tuple-element.10) | copy-start | bytes 1572868
  202.8 2.6 %collective-permute-start.18 = (bf16[2,128,1024]{2,1,0:T(8,128)(2,1)S(1)}, bf16[2,128,1024]{2,1,0:T(8,128)(2,1)S(1)}, u32[]{:S(2)}, u32[]{:S(2)}) collective-permute-start(bf16[2,128,1024]{2,1,0:T(8,128)(2,1)S(1)} %slice_bitcast_fusion), channel_id=1, source_target_pairs={{0,1},{1,0},{2,3},{3,2},{4,5},{5,4},{6,7},{7,6},{8,9},{9,8},{10,11... | collective-permute-start | bytes 1572872 | tf_op jit(solution)/shard_map/ppermute | solution.py:26

commit v8 on v6

--- a/solution.py
+++ b/solution.py
@@ -50,9 +50,8 @@
     prev = moved(own, routes.hop)
     recv = []
     for e in range(1, routes.chips):
-        up = moved(own, routes.up[e - 1])
-        down = moved(prev, routes.down[e - 1])
-        recv.append(jnp.where(chip_in_group >= e, up, down))
+        sent = jnp.where(chip_in_group + e < routes.chips, own, prev)
+        recv.append(moved(sent, routes.up[e - 1] + routes.down[e - 1]))
     return [prev] + recv[::-1] + [own]
 
 

time: 202 us -> 200 us (0.990)
  waiting for transfers between devices: 121 us -> 107 us
  starting transfers between devices: 32.8 us -> 44.1 us
  local copies, waits for them, and re-layouts: 4.47 us -> 7.57 us
  other arithmetic: 16.3 us -> 13.9 us
    ppermute x17 -> x14, waiting for transfers between devices: 121 us -> 107 us  [moved(): return lax.ppermute(value, 'seq', pairs)]
    ppermute x17 -> x14, starting transfers between devices: 32.8 us -> 44.1 us  [moved(): return lax.ppermute(value, 'seq', pairs)]
    select_n x3 -> x1, other arithmetic: 4.53 us -> 1.45 us  [gather_window(): sent = jnp.where(chip_in_group + e < routes.chips, own, prev)]
  transfers between devices with their start and end apart: 17 -> 14, of which waited for: 10 -> 9; matrix products, arithmetic and copies ran while one was open for 5% -> 5% of each run, Pallas kernels for 0% -> 0%
where the time goes in v8:
time: 200 us; the launch traced here: 199 us
  waiting for transfers between devices  107 us (54%)
  starting transfers between devices  44.1 us (22%)
  Pallas kernels  25.4 us (13%)
  other arithmetic  13.9 us (7%)
  local copies, waits for them, and re-layouts  7.57 us (4%)
    ppermute x14, waiting for transfers between devices, moved(): return lax.ppermute(value, 'seq', pairs)  107 us
    ppermute x14, starting transfers between devices, moved(): return lax.ppermute(value, 'seq', pairs)  44.1 us
    pallas_call x1, Pallas kernels, attention_grads(): pl.pallas_call(lambda *refs: attention_kernel(chips, *refs), grid_spec=gr...  25.4 us
  transfers between devices with their start and end apart: 14, of which 9 were waited for; matrix products, arithmetic and copies ran while one was open for 5% of the time, Pallas kernels for 0%

profile of v8, /device:TPU:7, one launch (start us, length us, event | category | flops | bytes accessed | tf_op | source)
XLA Modules:
  0.0 198.9 jit_solution(11936462073503682286)
XLA Ops:
  0.6 0.0 copy-start
  0.6 0.0 copy-start.7
  0.7 2.0 %constant_dynamic-slice_fusion.2 = (bf16[1,128,1024]{2,1,0:T(8,128)(2,1)S(1)}, bf16[1,128,1024]{2,1,0:T(8,128)(2,1)S(1)}, bf16[1,128,1024]{2,1,0:T(8,128)(2,1)S(1)}, bf16[1,128,1024]{2,1,0:T(8,128)(2,1)}) fusion(bf16[1,128,2048]{2,1,0:T(8,128)(2,1)} %param.7, s32[]{:T(128)S(6)} %select_n.163, s32[]{:T(128)S(6)} %select_n.164, bf16[1,128,2048]{2,1,0:T(8,128)(2,1)} %param.6), kind=kLoop, calls=%fused_computation.66 | loop fusion | bytes 2097160 | tf_op jit(solution)/shard_map/dynamic_slice | solution.py:170
  2.7 0.8 pad_maximum_fusion.4
  3.6 0.7 collective-permute-start.1
  4.2 1.2 constant_dynamic-slice_fusion.4
  5.5 0.1 pad_maximum_fusion.1
  5.6 0.1 collective-permute-start
  5.9 0.1 broadcast_bitcast_fusion
  6.0 0.1 constant_dynamic-update-slice_fusion.19
  6.1 0.1 fusion.6
  6.2 1.0 maximum_bitcast_fusion
  7.2 0.0 collective-permute-done.1
  7.2 1.1 pad_maximum_fusion.2.refs_10_
  8.2 4.2 %collective-permute-start.2 = (bf16[2,2,128,1024]{3,2,1,0:T(8,128)(2,1)}, bf16[2,2,128,1024]{3,2,1,0:T(8,128)(2,1)}, u32[]{:S(2)}, u32[]{:S(2)}) collective-permute-start(bf16[2,2,128,1024]{3,2,1,0:T(8,128)(2,1)} %pad_maximum_fusion.2.refs_10_), channel_id=1, source_target_pairs={{0,8},{1,9},{2,10},{3,11},{4,12},{5,13},{6,14},{7,15},{8,16},{9,17... | collective-permute-start | bytes 3145736 | tf_op jit(solution)/shard_map/ppermute | solution.py:26
  12.4 0.1 constant_dynamic-update-slice_fusion.15
  12.5 0.1 constant_dynamic-update-slice_fusion.13
  12.6 0.1 constant_dynamic-update-slice_fusion.11
  12.7 0.1 constant_dynamic-update-slice_fusion.9
  12.8 0.1 constant_dynamic-update-slice_fusion.7
  12.8 0.1 constant_dynamic-update-slice_fusion.5
  12.9 0.1 constant_dynamic-update-slice_fusion.3
  13.0 0.1 constant_dynamic-update-slice_fusion
  13.1 20.8 %collective-permute-done.2.refs_6_ = bf16[2,2,128,1024]{3,2,1,0:T(8,128)(2,1)} collective-permute-done((bf16[2,2,128,1024]{3,2,1,0:T(8,128)(2,1)}, bf16[2,2,128,1024]{3,2,1,0:T(8,128)(2,1)}, u32[]{:S(2)}, u32[]{:S(2)}) %collective-permute-start.2) | collective-permute-done | bytes 1048608 | tf_op jit(solution)/shard_map/ppermute | solution.py:26
  33.9 1.4 broadcast_select_fusion
  35.4 0.3 collective-permute-start.3
  35.7 0.2 collective-permute-start.4
  35.9 2.1 %collective-permute-start.5 = (bf16[2,2,128,1024]{3,2,1,0:T(8,128)(2,1)S(1)}, bf16[2,2,128,1024]{3,2,1,0:T(8,128)(2,1)S(1)}, u32[]{:S(2)}, u32[]{:S(2)}) collective-permute-start(bf16[2,2,128,1024]{3,2,1,0:T(8,128)(2,1)S(1)} %get-tuple-element.17), channel_id=1, source_target_pairs={{0,2},{1,3},{2,4},{3,5},{4,6},{5,7},{8,10},{9,11},{10,12},{11,13},... | collective-permute-start | bytes 3145736 | tf_op jit(solution)/shard_map/ppermute | solution.py:26
  38.0 0.5 fusion.2
  38.5 1.7 pad_maximum_fusion.refs_1_
  40.2 0.0 collective-permute-done
  40.2 1.1 slice_bitcast_fusion.1
  41.2 18.6 %collective-permute-done.3.refs_7_ = bf16[2,2,128,1024]{3,2,1,0:T(8,128)(2,1)S(1)} collective-permute-done((bf16[2,2,128,1024]{3,2,1,0:T(8,128)(2,1)S(1)}, bf16[2,2,128,1024]{3,2,1,0:T(8,128)(2,1)S(1)}, u32[]{:S(2)}, u32[]{:S(2)}) %collective-permute-start.3) | collective-permute-done | bytes 1048608 | tf_op jit(solution)/shard_map/ppermute | solution.py:26
  59.8 22.7 %collective-permute-done.4.refs_8_ = bf16[2,2,128,1024]{3,2,1,0:T(8,128)(2,1)S(1)} collective-permute-done((bf16[2,2,128,1024]{3,2,1,0:T(8,128)(2,1)S(1)}, bf16[2,2,128,1024]{3,2,1,0:T(8,128)(2,1)S(1)}, u32[]{:S(2)}, u32[]{:S(2)}) %collective-permute-start.4) | collective-permute-done | bytes 1048608 | tf_op jit(solution)/shard_map/ppermute | solution.py:26
  82.5 0.0 collective-permute-done.5.refs_9_
  82.5 1.0 copy-done.9
  83.5 0.3 copy-done.10
  83.8 25.4 %shard_map.76 = (bf16[128,2048]{1,0:T(8,128)(2,1)}, bf16[128,2048]{1,0:T(8,128)(2,1)}, f32[2,2,128,1024]{3,2,1,0:T(8,128)}, f32[2,2,128,1024]{3,2,1,0:T(8,128)},...) custom-call(s32[1]{0:T(128)} %bitcast.refs_0_, ...), custom_call_target="tpu_custom_call" | custom-call | flops 6710886400 | bytes 21495808 | tf_op jit(solution)/shard_map/pallas_call | solution.py:132
  109.2 1.9 convert_element_type.65
  111.1 1.4 collective-permute-start.10
  112.5 0.1 convert_element_type.67
  112.7 1.4 collective-permute-start.11
  114.1 0.2 convert_element_type.63
  114.3 1.3 collective-permute-start.9
  115.6 3.5 %collective-permute-start.6 = (bf16[2,2,128,1024]{3,2,1,0:T(8,128)(2,1)S(1)}, bf16[2,2,128,1024]{3,2,1,0:T(8,128)(2,1)S(1)}, u32[]{:S(2)}, u32[]{:S(2)}) collective-permute-start(bf16[2,2,128,1024]{3,2,1,0:T(8,128)(2,1)S(1)} %convert_element_type.63), channel_id=1, source_target_pairs={{2,0},{3,1},{4,2},{5,3},{6,4},{7,5},{10,8},{11,9},{12,10},{13,11},... | collective-permute-start | bytes 3145736 | tf_op jit(solution)/shard_map/ppermute | solution.py:26
  119.1 4.7 %collective-permute-start.7 = (bf16[2,2,128,1024]{3,2,1,0:T(8,128)(2,1)S(1)}, bf16[2,2,128,1024]{3,2,1,0:T(8,128)(2,1)S(1)}, u32[]{:S(2)}, u32[]{:S(2)}) collective-permute-start(bf16[2,2,128,1024]{3,2,1,0:T(8,128)(2,1)S(1)} %convert_element_type.65), channel_id=1, source_target_pairs={{4,0},{5,1},{6,2},{7,3},{12,8},{13,9},{14,10},{15,11},{20,16},{21,... | collective-permute-start | bytes 3145736 | tf_op jit(solution)/shard_map/ppermute | solution.py:26
  123.8 12.7 %collective-permute-done.10 = bf16[2,2,128,1024]{3,2,1,0:T(8,128)(2,1)S(1)} collective-permute-done((bf16[2,2,128,1024]{3,2,1,0:T(8,128)(2,1)S(1)}, bf16[2,2,128,1024]{3,2,1,0:T(8,128)(2,1)S(1)}, u32[]{:S(2)}, u32[]{:S(2)}) %collective-permute-start.10) | collective-permute-done | bytes 1048608 | tf_op jit(solution)/shard_map/ppermute | solution.py:26
  136.5 19.7 %collective-permute-start.8 = (bf16[2,2,128,1024]{3,2,1,0:T(8,128)(2,1)S(1)}, bf16[2,2,128,1024]{3,2,1,0:T(8,128)(2,1)S(1)}, u32[]{:S(2)}, u32[]{:S(2)}) collective-permute-start(bf16[2,2,128,1024]{3,2,1,0:T(8,128)(2,1)S(1)} %convert_element_type.67), channel_id=1, source_target_pairs={{6,0},{7,1},{14,8},{15,9},{22,16},{23,17},{30,24},{31,25}} | collective-permute-start | bytes 3145736 | tf_op jit(solution)/shard_map/ppermute | solution.py:26
  156.3 0.0 collective-permute-done.11
  156.3 5.9 %collective-permute-done.9 = bf16[2,2,128,1024]{3,2,1,0:T(8,128)(2,1)S(1)} collective-permute-done((bf16[2,2,128,1024]{3,2,1,0:T(8,128)(2,1)S(1)}, bf16[2,2,128,1024]{3,2,1,0:T(8,128)(2,1)S(1)}, u32[]{:S(2)}, u32[]{:S(2)}) %collective-permute-start.9) | collective-permute-done | bytes 1048608 | tf_op jit(solution)/shard_map/ppermute | solution.py:26
  162.2 0.8 add_convert_fusion.1
  163.0 1.3 collective-permute-start.12
  164.3 2.3 %collective-permute-done.7 = bf16[2,2,128,1024]{3,2,1,0:T(8,128)(2,1)S(1)} collective-permute-done((bf16[2,2,128,1024]{3,2,1,0:T(8,128)(2,1)S(1)}, bf16[2,2,128,1024]{3,2,1,0:T(8,128)(2,1)S(1)}, u32[]{:S(2)}, u32[]{:S(2)}) %collective-permute-start.7) | collective-permute-done | bytes 1048608 | tf_op jit(solution)/shard_map/ppermute | solution.py:26
  166.6 7.5 %collective-permute-done.8 = bf16[2,2,128,1024]{3,2,1,0:T(8,128)(2,1)S(1)} collective-permute-done((bf16[2,2,128,1024]{3,2,1,0:T(8,128)(2,1)S(1)}, bf16[2,2,128,1024]{3,2,1,0:T(8,128)(2,1)S(1)}, u32[]{:S(2)}, u32[]{:S(2)}) %collective-permute-start.8) | collective-permute-done | bytes 1048608 | tf_op jit(solution)/shard_map/ppermute | solution.py:26
  174.1 14.1 %collective-permute-done.12 = bf16[2,2,128,1024]{3,2,1,0:T(8,128)(2,1)S(1)} collective-permute-done((bf16[2,2,128,1024]{3,2,1,0:T(8,128)(2,1)S(1)}, bf16[2,2,128,1024]{3,2,1,0:T(8,128)(2,1)S(1)}, u32[]{:S(2)}, u32[]{:S(2)}) %collective-permute-start.12) | collective-permute-done | bytes 1048608 | tf_op jit(solution)/shard_map/ppermute | solution.py:26
  188.2 1.0 add_convert_fusion
  189.2 0.1 slice_bitcast_fusion.4
  189.3 1.0 copy-done.6
  190.3 0.1 pad_maximum_fusion.3
  190.4 3.1 %collective-permute-start.13 = (bf16[128,4096]{1,0:T(8,128)(2,1)S(1)}, bf16[128,4096]{1,0:T(8,128)(2,1)S(1)}, u32[]{:S(2)}, u32[]{:S(2)}) collective-permute-start(bf16[128,4096]{1,0:T(8,128)(2,1)S(1)} %pad_maximum_fusion.3), channel_id=1, source_target_pairs={{0,1},{1,0},{2,3},{3,2},{4,5},{5,4},{6,7},{7,6},{8,9},{9,8},{10,11... | collective-permute-start | bytes 3145736 | tf_op jit(solution)/shard_map/ppermute | solution.py:26
  193.5 2.3 %collective-permute-done.13 = bf16[128,4096]{1,0:T(8,128)(2,1)S(1)} collective-permute-done((bf16[128,4096]{1,0:T(8,128)(2,1)S(1)}, bf16[128,4096]{1,0:T(8,128)(2,1)S(1)}, u32[]{:S(2)}, u32[]{:S(2)}) %collective-permute-start.13) | collective-permute-done | bytes 1048608 | tf_op jit(solution)/shard_map/ppermute | solution.py:26
  195.8 0.9 maximum_select_fusion.2
  196.7 0.9 maximum_select_fusion.1
  197.7 1.2 maximum_select_fusion
  (32 shorter events, 0.2 us)
Async XLA Ops:
  0.6 5.3 %copy-start = (s32[1,32]{1,0:T(1,128)S(1)}, s32[1,32]{1,0:T(1,128)}, u32[]{:S(2)}) copy-start(s32[1,32]{1,0:T(1,128)} %param.9) | copy-start | bytes 388
  0.6 3.6 %copy-start.7 = (bf16[1,128,4096]{2,1,0:T(8,128)(2,1)S(1)}, bf16[1,128,4096]{2,1,0:T(8,128)(2,1)}, u32[]{:S(2)}) copy-start(bf16[1,128,4096]{2,1,0:T(8,128)(2,1)} %param.5) | copy-start | bytes 3145732
  3.6 3.6 %collective-permute-start.1 = (bf16[2,128,1024]{2,1,0:T(8,128)(2,1)}, bf16[2,128,1024]{2,1,0:T(8,128)(2,1)S(1)}, u32[]{:S(2)}, u32[]{:S(2)}) collective-permute-start(bf16[2,128,1024]{2,1,0:T(8,128)(2,1)} %pad_maximum_fusion.4), channel_id=1, source_target_pairs={{0,1},{1,0},{2,3},{3,2},{4,5},{5,4},{6,7},{7,6},{8,9},{9,8},{10,11... | collective-permute-start | bytes 1572872 | tf_op jit(solution)/shard_map/ppermute | solution.py:26
  5.6 34.5 %collective-permute-start = (bf16[2,128,2048]{2,1,0:T(8,128)(2,1)S(1)}, bf16[2,128,2048]{2,1,0:T(8,128)(2,1)S(1)}, u32[]{:S(2)}, u32[]{:S(2)}) collective-permute-start(bf16[2,128,2048]{2,1,0:T(8,128)(2,1)S(1)} %pad_maximum_fusion.1), channel_id=1, source_target_pairs={{0,1},{1,0},{2,3},{3,2},{4,5},{5,4},{6,7},{7,6},{8,9},{9,8},{10,11... | collective-permute-start | bytes 3145736 | tf_op jit(solution)/shard_map/ppermute | solution.py:26
  8.2 25.7 %collective-permute-start.2 = (bf16[2,2,128,1024]{3,2,1,0:T(8,128)(2,1)}, bf16[2,2,128,1024]{3,2,1,0:T(8,128)(2,1)}, u32[]{:S(2)}, u32[]{:S(2)}) collective-permute-start(bf16[2,2,128,1024]{3,2,1,0:T(8,128)(2,1)} %pad_maximum_fusion.2.refs_10_), channel_id=1, source_target_pairs={{0,8},{1,9},{2,10},{3,11},{4,12},{5,13},{6,14},{7,15},{8,16},{9,17... | collective-permute-start | bytes 3145736 | tf_op jit(solution)/shard_map/ppermute | solution.py:26
  35.4 24.5 %collective-permute-start.3 = (bf16[2,2,128,1024]{3,2,1,0:T(8,128)(2,1)S(1)}, bf16[2,2,128,1024]{3,2,1,0:T(8,128)(2,1)S(1)}, u32[]{:S(2)}, u32[]{:S(2)}) collective-permute-start(bf16[2,2,128,1024]{3,2,1,0:T(8,128)(2,1)S(1)} %get-tuple-element.19), channel_id=1, source_target_pairs={{0,6},{1,7},{8,14},{9,15},{16,22},{17,23},{24,30},{25,31},{2,0},{3... | collective-permute-start | bytes 3145736 | tf_op jit(solution)/shard_map/ppermute | solution.py:26
  35.7 46.8 %collective-permute-start.4 = (bf16[2,2,128,1024]{3,2,1,0:T(8,128)(2,1)S(1)}, bf16[2,2,128,1024]{3,2,1,0:T(8,128)(2,1)S(1)}, u32[]{:S(2)}, u32[]{:S(2)}) collective-permute-start(bf16[2,2,128,1024]{3,2,1,0:T(8,128)(2,1)S(1)} %get-tuple-element.18), channel_id=1, source_target_pairs={{0,4},{1,5},{2,6},{3,7},{8,12},{9,13},{10,14},{11,15},{16,20},{17,... | collective-permute-start | bytes 3145736 | tf_op jit(solution)/shard_map/ppermute | solution.py:26
  35.9 46.6 %collective-permute-start.5 = (bf16[2,2,128,1024]{3,2,1,0:T(8,128)(2,1)S(1)}, bf16[2,2,128,1024]{3,2,1,0:T(8,128)(2,1)S(1)}, u32[]{:S(2)}, u32[]{:S(2)}) collective-permute-start(bf16[2,2,128,1024]{3,2,1,0:T(8,128)(2,1)S(1)} %get-tuple-element.17), channel_id=1, source_target_pairs={{0,2},{1,3},{2,4},{3,5},{4,6},{5,7},{8,10},{9,11},{10,12},{11,13},... | collective-permute-start | bytes 3145736 | tf_op jit(solution)/shard_map/ppermute | solution.py:26
  59.8 22.7 %copy-start.8 = (bf16[2,2,128,1024]{3,2,1,0:T(8,128)(2,1)}, bf16[2,2,128,1024]{3,2,1,0:T(8,128)(2,1)S(1)}, u32[]{:S(2)}) copy-start(bf16[2,2,128,1024]{3,2,1,0:T(8,128)(2,1)S(1)} %collective-permute-done.3.refs_7_) | copy-start | bytes 3145732
  82.5 1.0 copy-start.9
  82.5 1.3 copy-start.10
  109.2 3.4 %copy-start.4 = (f32[2,2,128,1024]{3,2,1,0:T(8,128)S(1)}, f32[2,2,128,1024]{3,2,1,0:T(8,128)}, u32[]{:S(2)}) copy-start(f32[2,2,128,1024]{3,2,1,0:T(8,128)} %get-tuple-element.14) | copy-start | bytes 6291460
  111.1 3.1 %copy-start.3 = (f32[2,2,128,1024]{3,2,1,0:T(8,128)S(1)}, f32[2,2,128,1024]{3,2,1,0:T(8,128)}, u32[]{:S(2)}) copy-start(f32[2,2,128,1024]{3,2,1,0:T(8,128)} %get-tuple-element.12) | copy-start | bytes 6291460
  111.1 25.5 %collective-permute-start.10 = (bf16[2,2,128,1024]{3,2,1,0:T(8,128)(2,1)S(1)}, bf16[2,2,128,1024]{3,2,1,0:T(8,128)(2,1)S(1)}, u32[]{:S(2)}, u32[]{:S(2)}) collective-permute-start(bf16[2,2,128,1024]{3,2,1,0:T(8,128)(2,1)S(1)} %convert_element_type.65), channel_id=1, source_target_pairs={{0,4},{1,5},{2,6},{3,7},{8,12},{9,13},{10,14},{11,15},{16,20},{17,... | collective-permute-start | bytes 3145736 | tf_op jit(solution)/shard_map/ppermute | solution.py:26
  112.7 49.5 %copy-start.2 = (f32[2,2,128,1024]{3,2,1,0:T(8,128)S(1)}, f32[2,2,128,1024]{3,2,1,0:T(8,128)}, u32[]{:S(2)}) copy-start(f32[2,2,128,1024]{3,2,1,0:T(8,128)} %get-tuple-element.15) | copy-start | bytes 6291460
  112.7 43.6 %collective-permute-start.11 = (bf16[2,2,128,1024]{3,2,1,0:T(8,128)(2,1)S(1)}, bf16[2,2,128,1024]{3,2,1,0:T(8,128)(2,1)S(1)}, u32[]{:S(2)}, u32[]{:S(2)}) collective-permute-start(bf16[2,2,128,1024]{3,2,1,0:T(8,128)(2,1)S(1)} %convert_element_type.67), channel_id=1, source_target_pairs={{0,2},{1,3},{2,4},{3,5},{4,6},{5,7},{8,10},{9,11},{10,12},{11,13},... | collective-permute-start | bytes 3145736 | tf_op jit(solution)/shard_map/ppermute | solution.py:26
  114.3 47.9 %collective-permute-start.9 = (bf16[2,2,128,1024]{3,2,1,0:T(8,128)(2,1)S(1)}, bf16[2,2,128,1024]{3,2,1,0:T(8,128)(2,1)S(1)}, u32[]{:S(2)}, u32[]{:S(2)}) collective-permute-start(bf16[2,2,128,1024]{3,2,1,0:T(8,128)(2,1)S(1)} %convert_element_type.63), channel_id=1, source_target_pairs={{0,6},{1,7},{8,14},{9,15},{16,22},{17,23},{24,30},{25,31}} | collective-permute-start | bytes 3145736 | tf_op jit(solution)/shard_map/ppermute | solution.py:26
  115.6 48.7 %collective-permute-start.6 = (bf16[2,2,128,1024]{3,2,1,0:T(8,128)(2,1)S(1)}, bf16[2,2,128,1024]{3,2,1,0:T(8,128)(2,1)S(1)}, u32[]{:S(2)}, u32[]{:S(2)}) collective-permute-start(bf16[2,2,128,1024]{3,2,1,0:T(8,128)(2,1)S(1)} %convert_element_type.63), channel_id=1, source_target_pairs={{2,0},{3,1},{4,2},{5,3},{6,4},{7,5},{10,8},{11,9},{12,10},{13,11},... | collective-permute-start | bytes 3145736 | tf_op jit(solution)/shard_map/ppermute | solution.py:26
  119.1 47.5 %collective-permute-start.7 = (bf16[2,2,128,1024]{3,2,1,0:T(8,128)(2,1)S(1)}, bf16[2,2,128,1024]{3,2,1,0:T(8,128)(2,1)S(1)}, u32[]{:S(2)}, u32[]{:S(2)}) collective-permute-start(bf16[2,2,128,1024]{3,2,1,0:T(8,128)(2,1)S(1)} %convert_element_type.65), channel_id=1, source_target_pairs={{4,0},{5,1},{6,2},{7,3},{12,8},{13,9},{14,10},{15,11},{20,16},{21,... | collective-permute-start | bytes 3145736 | tf_op jit(solution)/shard_map/ppermute | solution.py:26
  136.5 37.6 %collective-permute-start.8 = (bf16[2,2,128,1024]{3,2,1,0:T(8,128)(2,1)S(1)}, bf16[2,2,128,1024]{3,2,1,0:T(8,128)(2,1)S(1)}, u32[]{:S(2)}, u32[]{:S(2)}) collective-permute-start(bf16[2,2,128,1024]{3,2,1,0:T(8,128)(2,1)S(1)} %convert_element_type.67), channel_id=1, source_target_pairs={{6,0},{7,1},{14,8},{15,9},{22,16},{23,17},{30,24},{31,25}} | collective-permute-start | bytes 3145736 | tf_op jit(solution)/shard_map/ppermute | solution.py:26
  162.2 26.0 %copy-start.1 = (f32[2,2,128,1024]{3,2,1,0:T(8,128)S(1)}, f32[2,2,128,1024]{3,2,1,0:T(8,128)}, u32[]{:S(2)}) copy-start(f32[2,2,128,1024]{3,2,1,0:T(8,128)} %get-tuple-element.11) | copy-start | bytes 6291460
  163.0 25.2 %collective-permute-start.12 = (bf16[2,2,128,1024]{3,2,1,0:T(8,128)(2,1)S(1)}, bf16[2,2,128,1024]{3,2,1,0:T(8,128)(2,1)S(1)}, u32[]{:S(2)}, u32[]{:S(2)}) collective-permute-start(bf16[2,2,128,1024]{3,2,1,0:T(8,128)(2,1)S(1)} %add_convert_fusion.1), channel_id=1, source_target_pairs={{8,0},{9,1},{10,2},{11,3},{12,4},{13,5},{14,6},{15,7},{16,8},{17,9... | collective-permute-start | bytes 3145736 | tf_op jit(solution)/shard_map/ppermute | solution.py:26
  189.2 1.0 copy-start.6
  190.4 5.4 %collective-permute-start.13 = (bf16[128,4096]{1,0:T(8,128)(2,1)S(1)}, bf16[128,4096]{1,0:T(8,128)(2,1)S(1)}, u32[]{:S(2)}, u32[]{:S(2)}) collective-permute-start(bf16[128,4096]{1,0:T(8,128)(2,1)S(1)} %pad_maximum_fusion.3), channel_id=1, source_target_pairs={{0,1},{1,0},{2,3},{3,2},{4,5},{5,4},{6,7},{7,6},{8,9},{9,8},{10,11... | collective-permute-start | bytes 3145736 | tf_op jit(solution)/shard_map/ppermute | solution.py:26
  193.5 4.2 %copy-start.5 = (bf16[128,2048]{1,0:T(8,128)(2,1)S(1)}, bf16[128,2048]{1,0:T(8,128)(2,1)}, u32[]{:S(2)}) copy-start(bf16[128,2048]{1,0:T(8,128)(2,1)} %get-tuple-element.10) | copy-start | bytes 1572868

commit v9 on v8

--- a/solution.py
+++ b/solution.py
@@ -55,16 +55,17 @@
     return [prev] + recv[::-1] + [own]
 
 
-def scatter_window(parts, routes):
+def scatter_window(parts, routes, chip_in_group):
     link = jnp.bfloat16
     chips = routes.chips
     prev, own = parts[0], parts[-1]
     recv = parts[1:-1][::-1]
-    sent = [r.astype(link) for r in recv]
     for e in range(1, chips):
-        prev = prev + moved(sent[e - 1], reverse(routes.down[e - 1])).astype(jnp.float32)
-    for e in range(1, chips):
-        own = own + moved(sent[e - 1], reverse(routes.up[e - 1])).astype(jnp.float32)
+        pairs = reverse(routes.up[e - 1] + routes.down[e - 1])
+        got = moved(recv[e - 1].astype(link), pairs).astype(jnp.float32)
+        upward = chip_in_group + e < chips
+        own = own + jnp.where(upward, got, 0.0)
+        prev = prev + jnp.where(upward, 0.0, got)
     return own + moved(prev.astype(link), reverse(routes.hop)).astype(jnp.float32)
 
 
@@ -201,7 +202,7 @@
         core[None].astype(jnp.int32), bias, queries[0], qd_sib[0], grad_out, qd_sib[1], payloads
     )
     dq_mine, dq_sib, parts = outs[0], outs[1], outs[2:]
-    summed = scatter_window(parts, routes)
+    summed = scatter_window(parts, routes, chip_in_group)
     sent = jnp.concatenate(
         [summed[0, 1].astype(jnp.bfloat16), summed[1, 1].astype(jnp.bfloat16), dq_sib], axis=-1
     )

time: 200 us -> 196 us (0.980)
  starting transfers between devices: 44.1 us -> 12.1 us
  waiting for transfers between devices: 107 us -> 134 us
    ppermute x14 -> x11, starting transfers between devices: 44.1 us -> 12.1 us  [moved(): return lax.ppermute(value, 'seq', pairs)]
    ppermute x14 -> x11, waiting for transfers between devices: 107 us -> 134 us  [moved(): return lax.ppermute(value, 'seq', pairs)]
  transfers between devices with their start and end apart: 14 -> 11, of which waited for: 9 -> 7; matrix products, arithmetic and copies ran while one was open for 5% -> 5% of each run, Pallas kernels for 0% -> 0%
where the time goes in v9:
time: 196 us
  waiting for transfers between devices  134 us (68%)
  Pallas kernels  25.4 us (13%)
  other arithmetic  14 us (7%)
  starting transfers between devices  12.1 us (6%)
  local copies, waits for them, and re-layouts  8.71 us (4%)
    ppermute x11, waiting for transfers between devices, moved(): return lax.ppermute(value, 'seq', pairs)  134 us
    pallas_call x1, Pallas kernels, attention_grads(): pl.pallas_call(lambda *refs: attention_kernel(chips, *refs), grid_spec=gr...  25.4 us
    ppermute x11, starting transfers between devices, moved(): return lax.ppermute(value, 'seq', pairs)  12.1 us
    unnamed x30, local copies, waits for them, and re-layouts  4.05 us
  transfers between devices with their start and end apart: 11, of which 7 were waited for; matrix products, arithmetic and copies ran while one was open for 5% of the time, Pallas kernels for 0%

profile of v9, /device:TPU:7, one launch (start us, length us, event | category | flops | bytes accessed | tf_op | source)
XLA Modules:
  0.0 195.5 jit_solution(1041999917641424763)
XLA Ops:
  0.6 0.0 copy-start
  0.6 0.0 copy-start.7
  0.7 2.0 %constant_dynamic-slice_fusion.2 = (bf16[1,128,1024]{2,1,0:T(8,128)(2,1)S(1)}, bf16[1,128,1024]{2,1,0:T(8,128)(2,1)S(1)}, bf16[1,128,1024]{2,1,0:T(8,128)(2,1)S(1)}, bf16[1,128,1024]{2,1,0:T(8,128)(2,1)}) fusion(bf16[1,128,2048]{2,1,0:T(8,128)(2,1)} %param.7, s32[]{:T(128)S(6)} %select_n.191, s32[]{:T(128)S(6)} %select_n.192, bf16[1,128,2048]{2,1,0:T(8,128)(2,1)} %param.6), kind=kLoop, calls=%fused_computation.79 | loop fusion | bytes 2097160 | tf_op jit(solution)/shard_map/dynamic_slice | solution.py:171
  2.7 0.8 pad_maximum_fusion.4
  3.6 0.7 collective-permute-start.1
  4.2 1.2 constant_dynamic-slice_fusion.4
  5.5 0.1 pad_maximum_fusion.1
  5.6 0.1 collective-permute-start
  5.9 0.0 copy-done
  5.9 0.1 broadcast_bitcast_fusion
  6.0 0.1 constant_dynamic-update-slice_fusion.19
  6.1 0.1 fusion.15
  6.2 1.0 maximum_bitcast_fusion
  7.2 0.0 collective-permute-done.1
  7.2 1.1 pad_maximum_fusion.2.refs_10_
  8.2 4.2 %collective-permute-start.2 = (bf16[2,2,128,1024]{3,2,1,0:T(8,128)(2,1)}, bf16[2,2,128,1024]{3,2,1,0:T(8,128)(2,1)}, u32[]{:S(2)}, u32[]{:S(2)}) collective-permute-start(bf16[2,2,128,1024]{3,2,1,0:T(8,128)(2,1)} %pad_maximum_fusion.2.refs_10_), channel_id=1, source_target_pairs={{0,8},{1,9},{2,10},{3,11},{4,12},{5,13},{6,14},{7,15},{8,16},{9,17... | collective-permute-start | bytes 3145736 | tf_op jit(solution)/shard_map/ppermute | solution.py:26
  12.4 0.1 constant_dynamic-update-slice_fusion.15
  12.5 0.1 constant_dynamic-update-slice_fusion.13
  12.6 0.1 constant_dynamic-update-slice_fusion.11
  12.7 0.1 constant_dynamic-update-slice_fusion.9
  12.7 0.1 constant_dynamic-update-slice_fusion.7
  12.8 0.1 constant_dynamic-update-slice_fusion.5
  12.9 0.1 constant_dynamic-update-slice_fusion.3
  13.0 0.1 constant_dynamic-update-slice_fusion
  13.1 20.8 %collective-permute-done.2.refs_6_ = bf16[2,2,128,1024]{3,2,1,0:T(8,128)(2,1)} collective-permute-done((bf16[2,2,128,1024]{3,2,1,0:T(8,128)(2,1)}, bf16[2,2,128,1024]{3,2,1,0:T(8,128)(2,1)}, u32[]{:S(2)}, u32[]{:S(2)}) %collective-permute-start.2) | collective-permute-done | bytes 1048608 | tf_op jit(solution)/shard_map/ppermute | solution.py:26
  33.9 1.4 broadcast_select_fusion
  35.4 0.3 collective-permute-start.3
  35.7 0.2 collective-permute-start.4
  35.9 2.1 %collective-permute-start.5 = (bf16[2,2,128,1024]{3,2,1,0:T(8,128)(2,1)S(1)}, bf16[2,2,128,1024]{3,2,1,0:T(8,128)(2,1)S(1)}, u32[]{:S(2)}, u32[]{:S(2)}) collective-permute-start(bf16[2,2,128,1024]{3,2,1,0:T(8,128)(2,1)S(1)} %get-tuple-element.17), channel_id=1, source_target_pairs={{0,2},{1,3},{2,4},{3,5},{4,6},{5,7},{8,10},{9,11},{10,12},{11,13},... | collective-permute-start | bytes 3145736 | tf_op jit(solution)/shard_map/ppermute | solution.py:26
  38.0 0.5 fusion.11
  38.5 1.7 pad_maximum_fusion.refs_1_
  40.2 0.0 collective-permute-done
  40.2 1.1 slice_bitcast_fusion.1
  41.3 18.6 %collective-permute-done.3.refs_7_ = bf16[2,2,128,1024]{3,2,1,0:T(8,128)(2,1)S(1)} collective-permute-done((bf16[2,2,128,1024]{3,2,1,0:T(8,128)(2,1)S(1)}, bf16[2,2,128,1024]{3,2,1,0:T(8,128)(2,1)S(1)}, u32[]{:S(2)}, u32[]{:S(2)}) %collective-permute-start.3) | collective-permute-done | bytes 1048608 | tf_op jit(solution)/shard_map/ppermute | solution.py:26
  59.8 22.7 %collective-permute-done.4.refs_8_ = bf16[2,2,128,1024]{3,2,1,0:T(8,128)(2,1)S(1)} collective-permute-done((bf16[2,2,128,1024]{3,2,1,0:T(8,128)(2,1)S(1)}, bf16[2,2,128,1024]{3,2,1,0:T(8,128)(2,1)S(1)}, u32[]{:S(2)}, u32[]{:S(2)}) %collective-permute-start.4) | collective-permute-done | bytes 1048608 | tf_op jit(solution)/shard_map/ppermute | solution.py:26
  82.5 0.0 collective-permute-done.5.refs_9_
  82.5 0.0 copy-done.8
  82.5 0.0 copy-start.10
  82.5 1.0 copy-done.9
  83.5 0.3 copy-done.10
  83.8 25.4 %shard_map.76 = (bf16[128,2048]{1,0:T(8,128)(2,1)}, bf16[128,2048]{1,0:T(8,128)(2,1)}, f32[2,2,128,1024]{3,2,1,0:T(8,128)}, f32[2,2,128,1024]{3,2,1,0:T(8,128)},...) custom-call(s32[1]{0:T(128)} %bitcast.refs_0_, ...), custom_call_target="tpu_custom_call" | custom-call | flops 6710886400 | bytes 21495808 | tf_op jit(solution)/shard_map/pallas_call | solution.py:133
  109.2 1.9 convert_element_type.54
  111.1 0.1 collective-permute-start.6
  111.2 0.2 copy-done.2
  111.4 0.2 convert_element_type.56
  111.6 0.3 collective-permute-start.7
  111.9 0.9 copy-done.1
  112.8 0.2 convert_element_type.58
  112.9 1.3 collective-permute-start.8
  114.2 21.4 %collective-permute-done.6 = bf16[2,2,128,1024]{3,2,1,0:T(8,128)(2,1)S(1)} collective-permute-done((bf16[2,2,128,1024]{3,2,1,0:T(8,128)(2,1)S(1)}, bf16[2,2,128,1024]{3,2,1,0:T(8,128)(2,1)S(1)}, u32[]{:S(2)}, u32[]{:S(2)}) %collective-permute-start.6) | collective-permute-done | bytes 1048608 | tf_op jit(solution)/shard_map/ppermute | solution.py:26
  135.6 23.1 %collective-permute-done.7 = bf16[2,2,128,1024]{3,2,1,0:T(8,128)(2,1)S(1)} collective-permute-done((bf16[2,2,128,1024]{3,2,1,0:T(8,128)(2,1)S(1)}, bf16[2,2,128,1024]{3,2,1,0:T(8,128)(2,1)S(1)}, u32[]{:S(2)}, u32[]{:S(2)}) %collective-permute-start.7) | collective-permute-done | bytes 1048608 | tf_op jit(solution)/shard_map/ppermute | solution.py:26
  158.7 0.0 collective-permute-done.8
  158.7 0.8 fusion.8
  159.6 1.3 collective-permute-start.9
  160.9 25.4 %collective-permute-done.9 = bf16[2,2,128,1024]{3,2,1,0:T(8,128)(2,1)S(1)} collective-permute-done((bf16[2,2,128,1024]{3,2,1,0:T(8,128)(2,1)S(1)}, bf16[2,2,128,1024]{3,2,1,0:T(8,128)(2,1)S(1)}, u32[]{:S(2)}, u32[]{:S(2)}) %collective-permute-start.9) | collective-permute-done | bytes 1048608 | tf_op jit(solution)/shard_map/ppermute | solution.py:26
  186.2 1.1 fusion.4
  187.3 0.1 slice_bitcast_fusion.4
  187.4 1.0 copy-done.6
  188.4 0.1 pad_maximum_fusion.3
  188.4 1.6 collective-permute-start.10
  190.1 2.3 %collective-permute-done.10 = bf16[128,4096]{1,0:T(8,128)(2,1)S(1)} collective-permute-done((bf16[128,4096]{1,0:T(8,128)(2,1)S(1)}, bf16[128,4096]{1,0:T(8,128)(2,1)S(1)}, u32[]{:S(2)}, u32[]{:S(2)}) %collective-permute-start.10) | collective-permute-done | bytes 1048608 | tf_op jit(solution)/shard_map/ppermute | solution.py:26
  192.4 0.9 maximum_select_fusion.2
  193.3 0.9 maximum_select_fusion.1
  194.3 1.2 maximum_select_fusion
  (26 shorter events, 0.2 us)
Async XLA Ops:
  0.6 5.3 %copy-start = (s32[1,32]{1,0:T(1,128)S(1)}, s32[1,32]{1,0:T(1,128)}, u32[]{:S(2)}) copy-start(s32[1,32]{1,0:T(1,128)} %param.9) | copy-start | bytes 388
  0.6 3.6 %copy-start.7 = (bf16[1,128,4096]{2,1,0:T(8,128)(2,1)S(1)}, bf16[1,128,4096]{2,1,0:T(8,128)(2,1)}, u32[]{:S(2)}) copy-start(bf16[1,128,4096]{2,1,0:T(8,128)(2,1)} %param.5) | copy-start | bytes 3145732
  3.6 3.6 %collective-permute-start.1 = (bf16[2,128,1024]{2,1,0:T(8,128)(2,1)}, bf16[2,128,1024]{2,1,0:T(8,128)(2,1)S(1)}, u32[]{:S(2)}, u32[]{:S(2)}) collective-permute-start(bf16[2,128,1024]{2,1,0:T(8,128)(2,1)} %pad_maximum_fusion.4), channel_id=1, source_target_pairs={{0,1},{1,0},{2,3},{3,2},{4,5},{5,4},{6,7},{7,6},{8,9},{9,8},{10,11... | collective-permute-start | bytes 1572872 | tf_op jit(solution)/shard_map/ppermute | solution.py:26
  5.6 34.6 %collective-permute-start = (bf16[2,128,2048]{2,1,0:T(8,128)(2,1)S(1)}, bf16[2,128,2048]{2,1,0:T(8,128)(2,1)S(1)}, u32[]{:S(2)}, u32[]{:S(2)}) collective-permute-start(bf16[2,128,2048]{2,1,0:T(8,128)(2,1)S(1)} %pad_maximum_fusion.1), channel_id=1, source_target_pairs={{0,1},{1,0},{2,3},{3,2},{4,5},{5,4},{6,7},{7,6},{8,9},{9,8},{10,11... | collective-permute-start | bytes 3145736 | tf_op jit(solution)/shard_map/ppermute | solution.py:26
  8.2 25.7 %collective-permute-start.2 = (bf16[2,2,128,1024]{3,2,1,0:T(8,128)(2,1)}, bf16[2,2,128,1024]{3,2,1,0:T(8,128)(2,1)}, u32[]{:S(2)}, u32[]{:S(2)}) collective-permute-start(bf16[2,2,128,1024]{3,2,1,0:T(8,128)(2,1)} %pad_maximum_fusion.2.refs_10_), channel_id=1, source_target_pairs={{0,8},{1,9},{2,10},{3,11},{4,12},{5,13},{6,14},{7,15},{8,16},{9,17... | collective-permute-start | bytes 3145736 | tf_op jit(solution)/shard_map/ppermute | solution.py:26
  35.4 24.5 %collective-permute-start.3 = (bf16[2,2,128,1024]{3,2,1,0:T(8,128)(2,1)S(1)}, bf16[2,2,128,1024]{3,2,1,0:T(8,128)(2,1)S(1)}, u32[]{:S(2)}, u32[]{:S(2)}) collective-permute-start(bf16[2,2,128,1024]{3,2,1,0:T(8,128)(2,1)S(1)} %get-tuple-element.19), channel_id=1, source_target_pairs={{0,6},{1,7},{8,14},{9,15},{16,22},{17,23},{24,30},{25,31},{2,0},{3... | collective-permute-start | bytes 3145736 | tf_op jit(solution)/shard_map/ppermute | solution.py:26
  35.7 46.8 %collective-permute-start.4 = (bf16[2,2,128,1024]{3,2,1,0:T(8,128)(2,1)S(1)}, bf16[2,2,128,1024]{3,2,1,0:T(8,128)(2,1)S(1)}, u32[]{:S(2)}, u32[]{:S(2)}) collective-permute-start(bf16[2,2,128,1024]{3,2,1,0:T(8,128)(2,1)S(1)} %get-tuple-element.18), channel_id=1, source_target_pairs={{0,4},{1,5},{2,6},{3,7},{8,12},{9,13},{10,14},{11,15},{16,20},{17,... | collective-permute-start | bytes 3145736 | tf_op jit(solution)/shard_map/ppermute | solution.py:26
  35.9 46.6 %collective-permute-start.5 = (bf16[2,2,128,1024]{3,2,1,0:T(8,128)(2,1)S(1)}, bf16[2,2,128,1024]{3,2,1,0:T(8,128)(2,1)S(1)}, u32[]{:S(2)}, u32[]{:S(2)}) collective-permute-start(bf16[2,2,128,1024]{3,2,1,0:T(8,128)(2,1)S(1)} %get-tuple-element.17), channel_id=1, source_target_pairs={{0,2},{1,3},{2,4},{3,5},{4,6},{5,7},{8,10},{9,11},{10,12},{11,13},... | collective-permute-start | bytes 3145736 | tf_op jit(solution)/shard_map/ppermute | solution.py:26
  59.8 22.7 %copy-start.8 = (bf16[2,2,128,1024]{3,2,1,0:T(8,128)(2,1)}, bf16[2,2,128,1024]{3,2,1,0:T(8,128)(2,1)S(1)}, u32[]{:S(2)}) copy-start(bf16[2,2,128,1024]{3,2,1,0:T(8,128)(2,1)S(1)} %collective-permute-done.3.refs_7_) | copy-start | bytes 3145732
  82.5 1.0 copy-start.9
  82.5 1.3 copy-start.10
  109.2 2.2 %copy-start.2 = (f32[2,2,128,1024]{3,2,1,0:T(8,128)S(1)}, f32[2,2,128,1024]{3,2,1,0:T(8,128)}, u32[]{:S(2)}) copy-start(f32[2,2,128,1024]{3,2,1,0:T(8,128)} %get-tuple-element.13) | copy-start | bytes 6291460
  111.1 1.7 copy-start.1
  111.1 24.5 %collective-permute-start.6 = (bf16[2,2,128,1024]{3,2,1,0:T(8,128)(2,1)S(1)}, bf16[2,2,128,1024]{3,2,1,0:T(8,128)(2,1)S(1)}, u32[]{:S(2)}, u32[]{:S(2)}) collective-permute-start(bf16[2,2,128,1024]{3,2,1,0:T(8,128)(2,1)S(1)} %convert_element_type.54), channel_id=1, source_target_pairs={{2,0},{3,1},{4,2},{5,3},{6,4},{7,5},{10,8},{11,9},{12,10},{13,11},... | collective-permute-start | bytes 3145736 | tf_op jit(solution)/shard_map/ppermute | solution.py:26
  111.6 47.2 %copy-start.3 = (f32[2,2,128,1024]{3,2,1,0:T(8,128)S(1)}, f32[2,2,128,1024]{3,2,1,0:T(8,128)}, u32[]{:S(2)}) copy-start(f32[2,2,128,1024]{3,2,1,0:T(8,128)} %get-tuple-element.15) | copy-start | bytes 6291460
  111.6 47.1 %collective-permute-start.7 = (bf16[2,2,128,1024]{3,2,1,0:T(8,128)(2,1)S(1)}, bf16[2,2,128,1024]{3,2,1,0:T(8,128)(2,1)S(1)}, u32[]{:S(2)}, u32[]{:S(2)}) collective-permute-start(bf16[2,2,128,1024]{3,2,1,0:T(8,128)(2,1)S(1)} %convert_element_type.56), channel_id=1, source_target_pairs={{4,0},{5,1},{6,2},{7,3},{12,8},{13,9},{14,10},{15,11},{20,16},{21,... | collective-permute-start | bytes 3145736 | tf_op jit(solution)/shard_map/ppermute | solution.py:26
  112.9 45.8 %collective-permute-start.8 = (bf16[2,2,128,1024]{3,2,1,0:T(8,128)(2,1)S(1)}, bf16[2,2,128,1024]{3,2,1,0:T(8,128)(2,1)S(1)}, u32[]{:S(2)}, u32[]{:S(2)}) collective-permute-start(bf16[2,2,128,1024]{3,2,1,0:T(8,128)(2,1)S(1)} %convert_element_type.58), channel_id=1, source_target_pairs={{6,0},{7,1},{14,8},{15,9},{22,16},{23,17},{30,24},{31,25},{0,2},{1... | collective-permute-start | bytes 3145736 | tf_op jit(solution)/shard_map/ppermute | solution.py:26
  158.7 27.5 %copy-start.4 = (f32[2,2,128,1024]{3,2,1,0:T(8,128)S(1)}, f32[2,2,128,1024]{3,2,1,0:T(8,128)}, u32[]{:S(2)}) copy-start(f32[2,2,128,1024]{3,2,1,0:T(8,128)} %get-tuple-element.11) | copy-start | bytes 6291460
  159.6 26.7 %collective-permute-start.9 = (bf16[2,2,128,1024]{3,2,1,0:T(8,128)(2,1)S(1)}, bf16[2,2,128,1024]{3,2,1,0:T(8,128)(2,1)S(1)}, u32[]{:S(2)}, u32[]{:S(2)}) collective-permute-start(bf16[2,2,128,1024]{3,2,1,0:T(8,128)(2,1)S(1)} %fusion.8), channel_id=1, source_target_pairs={{8,0},{9,1},{10,2},{11,3},{12,4},{13,5},{14,6},{15,7},{16,8},{17,9... | collective-permute-start | bytes 3145736 | tf_op jit(solution)/shard_map/ppermute | solution.py:26
  187.3 1.0 copy-start.6
  188.4 3.9 %collective-permute-start.10 = (bf16[128,4096]{1,0:T(8,128)(2,1)S(1)}, bf16[128,4096]{1,0:T(8,128)(2,1)S(1)}, u32[]{:S(2)}, u32[]{:S(2)}) collective-permute-start(bf16[128,4096]{1,0:T(8,128)(2,1)S(1)} %pad_maximum_fusion.3), channel_id=1, source_target_pairs={{0,1},{1,0},{2,3},{3,2},{4,5},{5,4},{6,7},{7,6},{8,9},{9,8},{10,11... | collective-permute-start | bytes 3145736 | tf_op jit(solution)/shard_map/ppermute | solution.py:26
  190.1 4.2 %copy-start.5 = (bf16[128,2048]{1,0:T(8,128)(2,1)S(1)}, bf16[128,2048]{1,0:T(8,128)(2,1)}, u32[]{:S(2)}) copy-start(bf16[128,2048]{1,0:T(8,128)(2,1)} %get-tuple-element.10) | copy-start | bytes 1572868

commit v10 on v9

--- a/solution.py
+++ b/solution.py
@@ -171,17 +171,20 @@
          lax.dynamic_slice_in_dim(values, core * key_width, key_width, 1)]
     )
     own = jnp.stack([kv_mine, kv_sib], axis=1)
+    payloads = gather_window(own, routes, chip_in_group)
+    (query_rows, grad_rows, doc_row), _ = lax.optimization_barrier(
+        ((queries[0], grad_out, doc_blocks[0]), payloads[0])
+    )
     qd_sent = jnp.stack(
-        [lax.dynamic_slice_in_dim(queries[0], other * query_width, query_width, 1),
-         lax.dynamic_slice_in_dim(grad_out, other * query_width, query_width, 1)]
+        [lax.dynamic_slice_in_dim(query_rows, other * query_width, query_width, 1),
+         lax.dynamic_slice_in_dim(grad_rows, other * query_width, query_width, 1)]
     )
     qd_sib = moved(qd_sent, routes.sibling)
-    payloads = gather_window(own, routes, chip_in_group)
 
     chip = position // 2
     block_of = lambda m, s: 2 * m + jnp.where(s == 0, core, other)
     key_blocks = [block_of(chip - chips + j, s) for j in range(chips + 1) for s in range(2)]
-    token_doc = jnp.repeat(doc_blocks[0], MBLK)
+    token_doc = jnp.repeat(doc_row, MBLK)
     pad = (reach_back + 2) * tokens
     doc_pad = jnp.concatenate([jnp.full((pad,), -1, jnp.int32), token_doc])
     key_doc = jnp.concatenate(

time: 196 us -> 191 us (0.974)
  other arithmetic: 14 us -> 10 us
    unnamed x30 -> x36, local copies, waits for them, and re-layouts: 4.05 us -> 4.82 us
  transfers between devices with their start and end apart: 11 -> 11, of which waited for: 7 -> 8; matrix products, arithmetic and copies ran while one was open for 5% -> 2% of each run, Pallas kernels for 0% -> 0%
where the time goes in v10:
time: 191 us
  waiting for transfers between devices  133 us (70%)
  Pallas kernels  25.4 us (13%)
  starting transfers between devices  13.2 us (7%)
  other arithmetic  10 us (5%)
  local copies, waits for them, and re-layouts  7.62 us (4%)
    ppermute x11, waiting for transfers between devices, moved(): return lax.ppermute(value, 'seq', pairs)  133 us
    pallas_call x1, Pallas kernels, attention_grads(): pl.pallas_call(lambda *refs: attention_kernel(chips, *refs), grid_spec=gr...  25.4 us
    ppermute x11, starting transfers between devices, moved(): return lax.ppermute(value, 'seq', pairs)  13.2 us
    unnamed x36, local copies, waits for them, and re-layouts  4.82 us
  transfers between devices with their start and end apart: 11, of which 8 were waited for; matrix products, arithmetic and copies ran while one was open for 2% of the time, Pallas kernels for 0%

profile of v10, /device:TPU:7, one launch (start us, length us, event | category | flops | bytes accessed | tf_op | source)
XLA Modules:
  0.0 190.9 jit_solution(8447462619496817872)
XLA Ops:
  0.6 0.0 copy-start
  0.7 1.3 constant_dynamic-slice_fusion.2
  1.9 0.1 pad_maximum_fusion.4
  2.0 0.7 collective-permute-start
  2.7 0.1 maximum_bitcast_fusion
  2.8 1.5 collective-permute-done
  4.3 0.1 pad_maximum_fusion.1.refs_10_
  4.4 3.3 %collective-permute-start.1 = (bf16[2,2,128,1024]{3,2,1,0:T(8,128)(2,1)S(1)}, bf16[2,2,128,1024]{3,2,1,0:T(8,128)(2,1)S(1)}, u32[]{:S(2)}, u32[]{:S(2)}) collective-permute-start(bf16[2,2,128,1024]{3,2,1,0:T(8,128)(2,1)S(1)} %pad_maximum_fusion.1.refs_10_), channel_id=1, source_target_pairs={{0,8},{1,9},{2,10},{3,11},{4,12},{5,13},{6,14},{7,15},{8,16},{9,17... | collective-permute-start | bytes 3145736 | tf_op jit(solution)/shard_map/ppermute | solution.py:26
  8.0 0.0 copy-start.10
  8.0 0.0 copy-start.9
  8.0 21.7 %collective-permute-done.1.refs_6_ = bf16[2,2,128,1024]{3,2,1,0:T(8,128)(2,1)S(1)} collective-permute-done((bf16[2,2,128,1024]{3,2,1,0:T(8,128)(2,1)S(1)}, bf16[2,2,128,1024]{3,2,1,0:T(8,128)(2,1)S(1)}, u32[]{:S(2)}, u32[]{:S(2)}) %collective-permute-start.1) | collective-permute-done | bytes 1048608 | tf_op jit(solution)/shard_map/ppermute | solution.py:26
  29.8 0.2 broadcast_select_fusion
  30.0 0.7 copy-done.6
  30.7 0.3 collective-permute-start.3
  31.0 0.2 collective-permute-start.4
  31.2 2.1 %collective-permute-start.5 = (bf16[2,2,128,1024]{3,2,1,0:T(8,128)(2,1)S(1)}, bf16[2,2,128,1024]{3,2,1,0:T(8,128)(2,1)S(1)}, u32[]{:S(2)}, u32[]{:S(2)}) collective-permute-start(bf16[2,2,128,1024]{3,2,1,0:T(8,128)(2,1)S(1)} %get-tuple-element.23), channel_id=1, source_target_pairs={{0,2},{1,3},{2,4},{3,5},{4,6},{5,7},{8,10},{9,11},{10,12},{11,13},... | collective-permute-start | bytes 3145736 | tf_op jit(solution)/shard_map/ppermute | solution.py:26
  33.4 0.0 copy-done.9
  33.4 0.1 pad_maximum_fusion.2
  33.5 2.1 %collective-permute-start.2 = (bf16[2,128,2048]{2,1,0:T(8,128)(2,1)S(1)}, bf16[2,128,2048]{2,1,0:T(8,128)(2,1)S(1)}, u32[]{:S(2)}, u32[]{:S(2)}) collective-permute-start(bf16[2,128,2048]{2,1,0:T(8,128)(2,1)S(1)} %pad_maximum_fusion.2), channel_id=1, source_target_pairs={{0,1},{1,0},{2,3},{3,2},{4,5},{5,4},{6,7},{7,6},{8,9},{9,8},{10,11... | collective-permute-start | bytes 3145736 | tf_op jit(solution)/shard_map/ppermute | solution.py:26
  35.6 0.1 broadcast_bitcast_fusion
  35.7 0.1 constant_dynamic-update-slice_fusion.19
  35.8 0.1 fusion.15
  35.9 0.1 constant_dynamic-update-slice_fusion.15
  35.9 0.1 constant_dynamic-update-slice_fusion.13
  36.0 0.1 constant_dynamic-update-slice_fusion.11
  36.1 0.1 constant_dynamic-update-slice_fusion.9
  36.2 0.1 constant_dynamic-update-slice_fusion.7
  36.3 0.1 constant_dynamic-update-slice_fusion.5
  36.4 0.1 constant_dynamic-update-slice_fusion.3
  36.4 0.1 constant_dynamic-update-slice_fusion.1
  36.5 0.5 fusion.11
  37.0 1.7 pad_maximum_fusion.refs_1_
  38.7 0.0 collective-permute-done.2
  38.7 1.1 slice_bitcast_fusion.1
  39.8 15.4 %collective-permute-done.3.refs_7_ = bf16[2,2,128,1024]{3,2,1,0:T(8,128)(2,1)S(1)} collective-permute-done((bf16[2,2,128,1024]{3,2,1,0:T(8,128)(2,1)S(1)}, bf16[2,2,128,1024]{3,2,1,0:T(8,128)(2,1)S(1)}, u32[]{:S(2)}, u32[]{:S(2)}) %collective-permute-start.3) | collective-permute-done | bytes 1048608 | tf_op jit(solution)/shard_map/ppermute | solution.py:26
  55.2 22.6 %collective-permute-done.4.refs_8_ = bf16[2,2,128,1024]{3,2,1,0:T(8,128)(2,1)S(1)} collective-permute-done((bf16[2,2,128,1024]{3,2,1,0:T(8,128)(2,1)S(1)}, bf16[2,2,128,1024]{3,2,1,0:T(8,128)(2,1)S(1)}, u32[]{:S(2)}, u32[]{:S(2)}) %collective-permute-start.4) | collective-permute-done | bytes 1048608 | tf_op jit(solution)/shard_map/ppermute | solution.py:26
  77.8 0.0 collective-permute-done.5.refs_9_
  77.8 1.0 copy-done.13
  78.8 0.3 copy-done.12
  79.1 25.4 %shard_map.76 = (bf16[128,2048]{1,0:T(8,128)(2,1)}, bf16[128,2048]{1,0:T(8,128)(2,1)}, f32[2,2,128,1024]{3,2,1,0:T(8,128)}, f32[2,2,128,1024]{3,2,1,0:T(8,128)},...) custom-call(s32[1]{0:T(128)} %bitcast.refs_0_, ...), custom_call_target="tpu_custom_call" | custom-call | flops 6710886400 | bytes 21495808 | tf_op jit(solution)/shard_map/pallas_call | solution.py:133
  104.5 1.9 convert_element_type.54
  106.4 0.1 collective-permute-start.6
  106.5 0.2 copy-done.2
  106.7 0.2 convert_element_type.56
  106.9 0.3 collective-permute-start.7
  107.2 0.9 copy-done.1
  108.1 0.2 convert_element_type.58
  108.3 1.3 collective-permute-start.8
  109.5 21.4 %collective-permute-done.6 = bf16[2,2,128,1024]{3,2,1,0:T(8,128)(2,1)S(1)} collective-permute-done((bf16[2,2,128,1024]{3,2,1,0:T(8,128)(2,1)S(1)}, bf16[2,2,128,1024]{3,2,1,0:T(8,128)(2,1)S(1)}, u32[]{:S(2)}, u32[]{:S(2)}) %collective-permute-start.6) | collective-permute-done | bytes 1048608 | tf_op jit(solution)/shard_map/ppermute | solution.py:26
  130.9 23.1 %collective-permute-done.7 = bf16[2,2,128,1024]{3,2,1,0:T(8,128)(2,1)S(1)} collective-permute-done((bf16[2,2,128,1024]{3,2,1,0:T(8,128)(2,1)S(1)}, bf16[2,2,128,1024]{3,2,1,0:T(8,128)(2,1)S(1)}, u32[]{:S(2)}, u32[]{:S(2)}) %collective-permute-start.7) | collective-permute-done | bytes 1048608 | tf_op jit(solution)/shard_map/ppermute | solution.py:26
  154.1 0.0 collective-permute-done.8
  154.1 0.9 fusion.8
  154.9 1.3 collective-permute-start.9
  156.2 25.4 %collective-permute-done.9 = bf16[2,2,128,1024]{3,2,1,0:T(8,128)(2,1)S(1)} collective-permute-done((bf16[2,2,128,1024]{3,2,1,0:T(8,128)(2,1)S(1)}, bf16[2,2,128,1024]{3,2,1,0:T(8,128)(2,1)S(1)}, u32[]{:S(2)}, u32[]{:S(2)}) %collective-permute-start.9) | collective-permute-done | bytes 1048608 | tf_op jit(solution)/shard_map/ppermute | solution.py:26
  181.6 1.1 fusion.4
  182.7 0.1 slice_bitcast_fusion.4
  182.8 0.9 copy-done.8
  183.7 0.1 pad_maximum_fusion.3
  183.8 1.6 collective-permute-start.10
  185.4 2.3 %collective-permute-done.10 = bf16[128,4096]{1,0:T(8,128)(2,1)S(1)} collective-permute-done((bf16[128,4096]{1,0:T(8,128)(2,1)S(1)}, bf16[128,4096]{1,0:T(8,128)(2,1)S(1)}, u32[]{:S(2)}, u32[]{:S(2)}) %collective-permute-start.10) | collective-permute-done | bytes 1048608 | tf_op jit(solution)/shard_map/ppermute | solution.py:26
  187.7 0.9 maximum_select_fusion.2
  188.7 0.9 maximum_select_fusion.1
  189.6 0.0 copy-done.7
  189.7 1.2 maximum_select_fusion
  (34 shorter events, 0.3 us)
Async XLA Ops:
  0.6 32.7 %copy-start = (s32[1,32]{1,0:T(1,128)S(1)}, s32[1,32]{1,0:T(1,128)}, u32[]{:S(2)}) copy-start(s32[1,32]{1,0:T(1,128)} %param.9) | copy-start | bytes 388
  2.0 2.3 %collective-permute-start = (bf16[2,128,1024]{2,1,0:T(8,128)(2,1)S(1)}, bf16[2,128,1024]{2,1,0:T(8,128)(2,1)S(1)}, u32[]{:S(2)}, u32[]{:S(2)}) collective-permute-start(bf16[2,128,1024]{2,1,0:T(8,128)(2,1)S(1)} %pad_maximum_fusion.4), channel_id=1, source_target_pairs={{0,1},{1,0},{2,3},{3,2},{4,5},{5,4},{6,7},{7,6},{8,9},{9,8},{10,11... | collective-permute-start | bytes 1572872 | tf_op jit(solution)/shard_map/ppermute | solution.py:26
  4.4 25.6 %copy-start.5 = (bf16[2,2,128,1024]{3,2,1,0:T(8,128)(2,1)}, bf16[2,2,128,1024]{3,2,1,0:T(8,128)(2,1)S(1)}, u32[]{:S(2)}) copy-start(bf16[2,2,128,1024]{3,2,1,0:T(8,128)(2,1)S(1)} %pad_maximum_fusion.1.refs_10_) | copy-start | bytes 3145732
  4.4 25.4 %collective-permute-start.1 = (bf16[2,2,128,1024]{3,2,1,0:T(8,128)(2,1)S(1)}, bf16[2,2,128,1024]{3,2,1,0:T(8,128)(2,1)S(1)}, u32[]{:S(2)}, u32[]{:S(2)}) collective-permute-start(bf16[2,2,128,1024]{3,2,1,0:T(8,128)(2,1)S(1)} %pad_maximum_fusion.1.refs_10_), channel_id=1, source_target_pairs={{0,8},{1,9},{2,10},{3,11},{4,12},{5,13},{6,14},{7,15},{8,16},{9,17... | collective-permute-start | bytes 3145736 | tf_op jit(solution)/shard_map/ppermute | solution.py:26
  8.0 25.3 %copy-start.10 = (bf16[1,128,4096]{2,1,0:T(8,128)(2,1)S(1)}, bf16[1,128,4096]{2,1,0:T(8,128)(2,1)}, u32[]{:S(2)}) copy-start(bf16[1,128,4096]{2,1,0:T(8,128)(2,1)} %param.8) | copy-start | bytes 3145732
  8.0 25.4 %copy-start.9 = (bf16[1,128,4096]{2,1,0:T(8,128)(2,1)S(1)}, bf16[1,128,4096]{2,1,0:T(8,128)(2,1)}, u32[]{:S(2)}) copy-start(bf16[1,128,4096]{2,1,0:T(8,128)(2,1)} %param.5) | copy-start | bytes 3145732
  29.8 1.0 copy-start.6
  30.7 24.4 %collective-permute-start.3 = (bf16[2,2,128,1024]{3,2,1,0:T(8,128)(2,1)S(1)}, bf16[2,2,128,1024]{3,2,1,0:T(8,128)(2,1)S(1)}, u32[]{:S(2)}, u32[]{:S(2)}) collective-permute-start(bf16[2,2,128,1024]{3,2,1,0:T(8,128)(2,1)S(1)} %get-tuple-element.25), channel_id=1, source_target_pairs={{0,6},{1,7},{8,14},{9,15},{16,22},{17,23},{24,30},{25,31},{2,0},{3... | collective-permute-start | bytes 3145736 | tf_op jit(solution)/shard_map/ppermute | solution.py:26
  31.0 46.8 %collective-permute-start.4 = (bf16[2,2,128,1024]{3,2,1,0:T(8,128)(2,1)S(1)}, bf16[2,2,128,1024]{3,2,1,0:T(8,128)(2,1)S(1)}, u32[]{:S(2)}, u32[]{:S(2)}) collective-permute-start(bf16[2,2,128,1024]{3,2,1,0:T(8,128)(2,1)S(1)} %get-tuple-element.24), channel_id=1, source_target_pairs={{0,4},{1,5},{2,6},{3,7},{8,12},{9,13},{10,14},{11,15},{16,20},{17,... | collective-permute-start | bytes 3145736 | tf_op jit(solution)/shard_map/ppermute | solution.py:26
  31.2 46.6 %collective-permute-start.5 = (bf16[2,2,128,1024]{3,2,1,0:T(8,128)(2,1)S(1)}, bf16[2,2,128,1024]{3,2,1,0:T(8,128)(2,1)S(1)}, u32[]{:S(2)}, u32[]{:S(2)}) collective-permute-start(bf16[2,2,128,1024]{3,2,1,0:T(8,128)(2,1)S(1)} %get-tuple-element.23), channel_id=1, source_target_pairs={{0,2},{1,3},{2,4},{3,5},{4,6},{5,7},{8,10},{9,11},{10,12},{11,13},... | collective-permute-start | bytes 3145736 | tf_op jit(solution)/shard_map/ppermute | solution.py:26
  33.5 5.2 %collective-permute-start.2 = (bf16[2,128,2048]{2,1,0:T(8,128)(2,1)S(1)}, bf16[2,128,2048]{2,1,0:T(8,128)(2,1)S(1)}, u32[]{:S(2)}, u32[]{:S(2)}) collective-permute-start(bf16[2,128,2048]{2,1,0:T(8,128)(2,1)S(1)} %pad_maximum_fusion.2), channel_id=1, source_target_pairs={{0,1},{1,0},{2,3},{3,2},{4,5},{5,4},{6,7},{7,6},{8,9},{9,8},{10,11... | collective-permute-start | bytes 3145736 | tf_op jit(solution)/shard_map/ppermute | solution.py:26
  55.2 23.7 %copy-start.11 = (bf16[2,2,128,1024]{3,2,1,0:T(8,128)(2,1)}, bf16[2,2,128,1024]{3,2,1,0:T(8,128)(2,1)S(1)}, u32[]{:S(2)}) copy-start(bf16[2,2,128,1024]{3,2,1,0:T(8,128)(2,1)S(1)} %collective-permute-done.3.refs_7_) | copy-start | bytes 3145732
  77.8 1.3 copy-start.12
  77.8 1.0 copy-start.13
  104.5 2.2 %copy-start.2 = (f32[2,2,128,1024]{3,2,1,0:T(8,128)S(1)}, f32[2,2,128,1024]{3,2,1,0:T(8,128)}, u32[]{:S(2)}) copy-start(f32[2,2,128,1024]{3,2,1,0:T(8,128)} %get-tuple-element.19) | copy-start | bytes 6291460
  106.4 1.7 copy-start.1
  106.4 24.5 %collective-permute-start.6 = (bf16[2,2,128,1024]{3,2,1,0:T(8,128)(2,1)S(1)}, bf16[2,2,128,1024]{3,2,1,0:T(8,128)(2,1)S(1)}, u32[]{:S(2)}, u32[]{:S(2)}) collective-permute-start(bf16[2,2,128,1024]{3,2,1,0:T(8,128)(2,1)S(1)} %convert_element_type.54), channel_id=1, source_target_pairs={{2,0},{3,1},{4,2},{5,3},{6,4},{7,5},{10,8},{11,9},{12,10},{13,11},... | collective-permute-start | bytes 3145736 | tf_op jit(solution)/shard_map/ppermute | solution.py:26
  106.9 47.2 %copy-start.3 = (f32[2,2,128,1024]{3,2,1,0:T(8,128)S(1)}, f32[2,2,128,1024]{3,2,1,0:T(8,128)}, u32[]{:S(2)}) copy-start(f32[2,2,128,1024]{3,2,1,0:T(8,128)} %get-tuple-element.21) | copy-start | bytes 6291460
  106.9 47.1 %collective-permute-start.7 = (bf16[2,2,128,1024]{3,2,1,0:T(8,128)(2,1)S(1)}, bf16[2,2,128,1024]{3,2,1,0:T(8,128)(2,1)S(1)}, u32[]{:S(2)}, u32[]{:S(2)}) collective-permute-start(bf16[2,2,128,1024]{3,2,1,0:T(8,128)(2,1)S(1)} %convert_element_type.56), channel_id=1, source_target_pairs={{4,0},{5,1},{6,2},{7,3},{12,8},{13,9},{14,10},{15,11},{20,16},{21,... | collective-permute-start | bytes 3145736 | tf_op jit(solution)/shard_map/ppermute | solution.py:26
  108.3 45.8 %collective-permute-start.8 = (bf16[2,2,128,1024]{3,2,1,0:T(8,128)(2,1)S(1)}, bf16[2,2,128,1024]{3,2,1,0:T(8,128)(2,1)S(1)}, u32[]{:S(2)}, u32[]{:S(2)}) collective-permute-start(bf16[2,2,128,1024]{3,2,1,0:T(8,128)(2,1)S(1)} %convert_element_type.58), channel_id=1, source_target_pairs={{6,0},{7,1},{14,8},{15,9},{22,16},{23,17},{30,24},{31,25},{0,2},{1... | collective-permute-start | bytes 3145736 | tf_op jit(solution)/shard_map/ppermute | solution.py:26
  154.1 27.5 %copy-start.4 = (f32[2,2,128,1024]{3,2,1,0:T(8,128)S(1)}, f32[2,2,128,1024]{3,2,1,0:T(8,128)}, u32[]{:S(2)}) copy-start(f32[2,2,128,1024]{3,2,1,0:T(8,128)} %get-tuple-element.17) | copy-start | bytes 6291460
  154.9 26.7 %collective-permute-start.9 = (bf16[2,2,128,1024]{3,2,1,0:T(8,128)(2,1)S(1)}, bf16[2,2,128,1024]{3,2,1,0:T(8,128)(2,1)S(1)}, u32[]{:S(2)}, u32[]{:S(2)}) collective-permute-start(bf16[2,2,128,1024]{3,2,1,0:T(8,128)(2,1)S(1)} %fusion.8), channel_id=1, source_target_pairs={{8,0},{9,1},{10,2},{11,3},{12,4},{13,5},{14,6},{15,7},{16,8},{17,9... | collective-permute-start | bytes 3145736 | tf_op jit(solution)/shard_map/ppermute | solution.py:26
  182.7 1.0 copy-start.8
  183.8 3.9 %collective-permute-start.10 = (bf16[128,4096]{1,0:T(8,128)(2,1)S(1)}, bf16[128,4096]{1,0:T(8,128)(2,1)S(1)}, u32[]{:S(2)}, u32[]{:S(2)}) collective-permute-start(bf16[128,4096]{1,0:T(8,128)(2,1)S(1)} %pad_maximum_fusion.3), channel_id=1, source_target_pairs={{0,1},{1,0},{2,3},{3,2},{4,5},{5,4},{6,7},{7,6},{8,9},{9,8},{10,11... | collective-permute-start | bytes 3145736 | tf_op jit(solution)/shard_map/ppermute | solution.py:26
  185.4 4.2 %copy-start.7 = (bf16[128,2048]{1,0:T(8,128)(2,1)S(1)}, bf16[128,2048]{1,0:T(8,128)(2,1)}, u32[]{:S(2)}) copy-start(bf16[128,2048]{1,0:T(8,128)(2,1)} %get-tuple-element.16) | copy-start | bytes 1572868

commit v11 on v10

--- a/solution.py
+++ b/solution.py
@@ -105,8 +105,8 @@
     )
     for j, out in enumerate(part_refs):
         for s in range(2):
-            out[0, s] = grad_k[rows(2 * j + s)]
-            out[1, s] = grad_v[rows(2 * j + s)]
+            out[0, s] = grad_k[rows(2 * j + s)].astype(out.dtype)
+            out[1, s] = grad_v[rows(2 * j + s)].astype(out.dtype)
 
 
 def attention_grads(core, bias, queries, query_sib, grad_out, grad_sib, payloads):
@@ -133,7 +133,10 @@
     return pl.pallas_call(
         lambda *refs: attention_kernel(chips, *refs),
         grid_spec=grid_spec,
-        out_shape=[jax.ShapeDtypeStruct(query_sib.shape, jnp.bfloat16)] * 2 + [part] * chips,
+        out_shape=[jax.ShapeDtypeStruct(query_sib.shape, jnp.bfloat16)] * 2
+        + [part]
+        + [jax.ShapeDtypeStruct(part.shape, jnp.bfloat16)] * (chips - 2)
+        + [part],
         cost_estimate=pl.CostEstimate(
             flops=flops, transcendentals=rows * key_count * heads, bytes_accessed=moved_bytes
         ),

time: 191 us -> 191 us (level)
    convert_element_type x3 -> x0, other arithmetic: 2.21 us -> none  [scatter_window(): got = moved(recv[e - 1].astype(link), pairs).astype(jnp.float32)]
    unnamed x36 -> x30, local copies, waits for them, and re-layouts: 4.82 us -> 3.78 us
where the time goes in v11:
time: 191 us; the launch traced here: 190 us
  waiting for transfers between devices  133 us (70%)
  Pallas kernels  25.3 us (13%)
  starting transfers between devices  14.7 us (8%)
  other arithmetic  9.49 us (5%)
  local copies, waits for them, and re-layouts  6.58 us (3%)
    ppermute x11, waiting for transfers between devices, moved(): return lax.ppermute(value, 'seq', pairs)  133 us
    pallas_call x1, Pallas kernels, attention_grads(): pl.pallas_call(lambda *refs: attention_kernel(chips, *refs), grid_spec=gr...  25.3 us
    ppermute x11, starting transfers between devices, moved(): return lax.ppermute(value, 'seq', pairs)  14.7 us
  transfers between devices with their start and end apart: 11, of which 8 were waited for; matrix products, arithmetic and copies ran while one was open for 2% of the time, Pallas kernels for 0%

profile of v11, /device:TPU:7, one launch (start us, length us, event | category | flops | bytes accessed | tf_op | source)
XLA Modules:
  0.0 190.0 jit_solution(8780751523602878154)
XLA Ops:
  0.6 0.0 copy-start
  0.7 1.3 constant_dynamic-slice_fusion.2
  1.9 0.1 pad_maximum_fusion.4
  2.0 0.7 collective-permute-start
  2.7 0.1 maximum_bitcast_fusion
  2.8 1.5 collective-permute-done
  4.3 0.1 pad_maximum_fusion.1.refs_10_
  4.4 0.0 copy-start.2
  4.4 3.3 %collective-permute-start.1 = (bf16[2,2,128,1024]{3,2,1,0:T(8,128)(2,1)S(1)}, bf16[2,2,128,1024]{3,2,1,0:T(8,128)(2,1)S(1)}, u32[]{:S(2)}, u32[]{:S(2)}) collective-permute-start(bf16[2,2,128,1024]{3,2,1,0:T(8,128)(2,1)S(1)} %pad_maximum_fusion.1.refs_10_), channel_id=1, source_target_pairs={{0,8},{1,9},{2,10},{3,11},{4,12},{5,13},{6,14},{7,15},{8,16},{9,17... | collective-permute-start | bytes 3145736 | tf_op jit(solution)/shard_map/ppermute | solution.py:26
  8.0 0.0 copy-start.7
  8.0 0.0 copy-start.6
  8.0 21.7 %collective-permute-done.1.refs_6_ = bf16[2,2,128,1024]{3,2,1,0:T(8,128)(2,1)S(1)} collective-permute-done((bf16[2,2,128,1024]{3,2,1,0:T(8,128)(2,1)S(1)}, bf16[2,2,128,1024]{3,2,1,0:T(8,128)(2,1)S(1)}, u32[]{:S(2)}, u32[]{:S(2)}) %collective-permute-start.1) | collective-permute-done | bytes 1048608 | tf_op jit(solution)/shard_map/ppermute | solution.py:26
  29.8 0.2 broadcast_select_fusion
  30.0 0.0 copy-done.2
  30.0 0.7 copy-done.3
  30.7 0.3 collective-permute-start.3
  31.0 0.2 collective-permute-start.4
  31.2 2.1 %collective-permute-start.5 = (bf16[2,2,128,1024]{3,2,1,0:T(8,128)(2,1)S(1)}, bf16[2,2,128,1024]{3,2,1,0:T(8,128)(2,1)S(1)}, u32[]{:S(2)}, u32[]{:S(2)}) collective-permute-start(bf16[2,2,128,1024]{3,2,1,0:T(8,128)(2,1)S(1)} %get-tuple-element.23), channel_id=1, source_target_pairs={{0,2},{1,3},{2,4},{3,5},{4,6},{5,7},{8,10},{9,11},{10,12},{11,13},... | collective-permute-start | bytes 3145736 | tf_op jit(solution)/shard_map/ppermute | solution.py:26
  33.3 0.0 copy-done
  33.3 0.0 copy-done.7
  33.4 0.1 pad_maximum_fusion.2
  33.5 2.1 %collective-permute-start.2 = (bf16[2,128,2048]{2,1,0:T(8,128)(2,1)S(1)}, bf16[2,128,2048]{2,1,0:T(8,128)(2,1)S(1)}, u32[]{:S(2)}, u32[]{:S(2)}) collective-permute-start(bf16[2,128,2048]{2,1,0:T(8,128)(2,1)S(1)} %pad_maximum_fusion.2), channel_id=1, source_target_pairs={{0,1},{1,0},{2,3},{3,2},{4,5},{5,4},{6,7},{7,6},{8,9},{9,8},{10,11... | collective-permute-start | bytes 3145736 | tf_op jit(solution)/shard_map/ppermute | solution.py:26
  35.6 0.1 broadcast_bitcast_fusion
  35.7 0.1 constant_dynamic-update-slice_fusion.19
  35.8 0.1 fusion.15
  35.9 0.1 constant_dynamic-update-slice_fusion.15
  35.9 0.1 constant_dynamic-update-slice_fusion.13
  36.0 0.1 constant_dynamic-update-slice_fusion.11
  36.1 0.1 constant_dynamic-update-slice_fusion.9
  36.2 0.1 constant_dynamic-update-slice_fusion.7
  36.3 0.1 constant_dynamic-update-slice_fusion.5
  36.4 0.1 constant_dynamic-update-slice_fusion.3
  36.4 0.1 constant_dynamic-update-slice_fusion.1
  36.5 0.5 fusion.11
  37.0 1.7 pad_maximum_fusion.refs_1_
  38.7 0.0 collective-permute-done.2
  38.7 1.1 slice_bitcast_fusion.1
  39.8 15.4 %collective-permute-done.3.refs_7_ = bf16[2,2,128,1024]{3,2,1,0:T(8,128)(2,1)S(1)} collective-permute-done((bf16[2,2,128,1024]{3,2,1,0:T(8,128)(2,1)S(1)}, bf16[2,2,128,1024]{3,2,1,0:T(8,128)(2,1)S(1)}, u32[]{:S(2)}, u32[]{:S(2)}) %collective-permute-start.3) | collective-permute-done | bytes 1048608 | tf_op jit(solution)/shard_map/ppermute | solution.py:26
  55.2 22.6 %collective-permute-done.4.refs_8_ = bf16[2,2,128,1024]{3,2,1,0:T(8,128)(2,1)S(1)} collective-permute-done((bf16[2,2,128,1024]{3,2,1,0:T(8,128)(2,1)S(1)}, bf16[2,2,128,1024]{3,2,1,0:T(8,128)(2,1)S(1)}, u32[]{:S(2)}, u32[]{:S(2)}) %collective-permute-start.4) | collective-permute-done | bytes 1048608 | tf_op jit(solution)/shard_map/ppermute | solution.py:26
  77.8 0.0 collective-permute-done.5.refs_9_
  77.8 1.0 copy-done.10
  78.8 0.0 copy-done.8
  78.8 0.4 copy-done.9
  79.2 25.3 %shard_map.76 = (bf16[128,2048]{1,0:T(8,128)(2,1)}, bf16[128,2048]{1,0:T(8,128)(2,1)}, f32[2,2,128,1024]{3,2,1,0:T(8,128)}, bf16[2,2,128,1024]{3,2,1,0:T(8,128)(...) custom-call(s32[1]{0:T(128)} %bitcast.refs_0_, ...), custom_call_target="tpu_custom_call" | custom-call | flops 6710886400 | bytes 21495808 | tf_op jit(solution)/shard_map/pallas_call | solution.py:133
  104.5 0.1 collective-permute-start.6
  104.6 0.3 collective-permute-start.7
  104.9 2.3 %collective-permute-start.8 = (bf16[2,2,128,1024]{3,2,1,0:T(8,128)(2,1)}, bf16[2,2,128,1024]{3,2,1,0:T(8,128)(2,1)S(1)}, u32[]{:S(2)}, u32[]{:S(2)}) collective-permute-start(bf16[2,2,128,1024]{3,2,1,0:T(8,128)(2,1)} %get-tuple-element.20), channel_id=1, source_target_pairs={{6,0},{7,1},{14,8},{15,9},{22,16},{23,17},{30,24},{31,25},{0,2},{1... | collective-permute-start | bytes 3145736 | tf_op jit(solution)/shard_map/ppermute | solution.py:26
  107.2 22.1 %collective-permute-done.6 = bf16[2,2,128,1024]{3,2,1,0:T(8,128)(2,1)S(1)} collective-permute-done((bf16[2,2,128,1024]{3,2,1,0:T(8,128)(2,1)}, bf16[2,2,128,1024]{3,2,1,0:T(8,128)(2,1)S(1)}, u32[]{:S(2)}, u32[]{:S(2)}) %collective-permute-start.6) | collective-permute-done | bytes 1048608 | tf_op jit(solution)/shard_map/ppermute | solution.py:26
  129.2 22.3 %collective-permute-done.7 = bf16[2,2,128,1024]{3,2,1,0:T(8,128)(2,1)S(1)} collective-permute-done((bf16[2,2,128,1024]{3,2,1,0:T(8,128)(2,1)}, bf16[2,2,128,1024]{3,2,1,0:T(8,128)(2,1)S(1)}, u32[]{:S(2)}, u32[]{:S(2)}) %collective-permute-start.7) | collective-permute-done | bytes 1048608 | tf_op jit(solution)/shard_map/ppermute | solution.py:26
  151.5 0.0 collective-permute-done.8
  151.5 2.5 %fusion.8 = bf16[2,2,128,1024]{3,2,1,0:T(8,128)(2,1)S(1)} fusion(f32[2,2,128,1024]{3,2,1,0:T(8,128)} %get-tuple-element.21, bf16[2,2,128,1024]{3,2,1,0:T(8,128)(2,1)S(1)} %collective-permute-done.6, bf16[2,2,128,1024]{3,2,1,0:T(8,128)(2,1)S(1)} %collective-permute-done.7, bf16[2,2,128,1024]{3,2,1,0:T(8,128)(2,1)S(1)} %collective-permute-done.8, pred[]{:T(512)S(6)} %lt.97, ...), kind=kLoop, calls=%fused_computation.15 | loop fusion | flops 5242880 | bytes 6291459 | tf_op jit(solution)/shard_map/convert_element_type | solution.py:69
  154.1 1.3 collective-permute-start.9
  155.4 24.9 %collective-permute-done.9 = bf16[2,2,128,1024]{3,2,1,0:T(8,128)(2,1)S(1)} collective-permute-done((bf16[2,2,128,1024]{3,2,1,0:T(8,128)(2,1)S(1)}, bf16[2,2,128,1024]{3,2,1,0:T(8,128)(2,1)S(1)}, u32[]{:S(2)}, u32[]{:S(2)}) %collective-permute-start.9) | collective-permute-done | bytes 1048608 | tf_op jit(solution)/shard_map/ppermute | solution.py:26
  180.3 0.0 copy-done.1
  180.3 1.1 fusion.4
  181.3 0.0 copy-start.5
  181.3 0.1 slice_bitcast_fusion.4
  181.4 0.9 copy-done.5
  182.4 0.1 pad_maximum_fusion.3
  182.5 2.1 %collective-permute-start.10 = (bf16[128,4096]{1,0:T(8,128)(2,1)S(1)}, bf16[128,4096]{1,0:T(8,128)(2,1)S(1)}, u32[]{:S(2)}, u32[]{:S(2)}) collective-permute-start(bf16[128,4096]{1,0:T(8,128)(2,1)S(1)} %pad_maximum_fusion.3), channel_id=1, source_target_pairs={{0,1},{1,0},{2,3},{3,2},{4,5},{5,4},{6,7},{7,6},{8,9},{9,8},{10,11... | collective-permute-start | bytes 3145736 | tf_op jit(solution)/shard_map/ppermute | solution.py:26
  184.5 2.3 %collective-permute-done.10 = bf16[128,4096]{1,0:T(8,128)(2,1)S(1)} collective-permute-done((bf16[128,4096]{1,0:T(8,128)(2,1)S(1)}, bf16[128,4096]{1,0:T(8,128)(2,1)S(1)}, u32[]{:S(2)}, u32[]{:S(2)}) %collective-permute-start.10) | collective-permute-done | bytes 1048608 | tf_op jit(solution)/shard_map/ppermute | solution.py:26
  186.9 0.9 maximum_select_fusion.2
  187.8 0.9 maximum_select_fusion.1
  188.8 1.2 maximum_select_fusion
  (25 shorter events, 0.2 us)
Async XLA Ops:
  0.6 32.7 %copy-start = (s32[1,32]{1,0:T(1,128)S(1)}, s32[1,32]{1,0:T(1,128)}, u32[]{:S(2)}) copy-start(s32[1,32]{1,0:T(1,128)} %param.9) | copy-start | bytes 388
  2.0 2.3 %collective-permute-start = (bf16[2,128,1024]{2,1,0:T(8,128)(2,1)S(1)}, bf16[2,128,1024]{2,1,0:T(8,128)(2,1)S(1)}, u32[]{:S(2)}, u32[]{:S(2)}) collective-permute-start(bf16[2,128,1024]{2,1,0:T(8,128)(2,1)S(1)} %pad_maximum_fusion.4), channel_id=1, source_target_pairs={{0,1},{1,0},{2,3},{3,2},{4,5},{5,4},{6,7},{7,6},{8,9},{9,8},{10,11... | collective-permute-start | bytes 1572872 | tf_op jit(solution)/shard_map/ppermute | solution.py:26
  4.4 25.6 %copy-start.2 = (bf16[2,2,128,1024]{3,2,1,0:T(8,128)(2,1)}, bf16[2,2,128,1024]{3,2,1,0:T(8,128)(2,1)S(1)}, u32[]{:S(2)}) copy-start(bf16[2,2,128,1024]{3,2,1,0:T(8,128)(2,1)S(1)} %pad_maximum_fusion.1.refs_10_) | copy-start | bytes 3145732
  4.4 25.4 %collective-permute-start.1 = (bf16[2,2,128,1024]{3,2,1,0:T(8,128)(2,1)S(1)}, bf16[2,2,128,1024]{3,2,1,0:T(8,128)(2,1)S(1)}, u32[]{:S(2)}, u32[]{:S(2)}) collective-permute-start(bf16[2,2,128,1024]{3,2,1,0:T(8,128)(2,1)S(1)} %pad_maximum_fusion.1.refs_10_), channel_id=1, source_target_pairs={{0,8},{1,9},{2,10},{3,11},{4,12},{5,13},{6,14},{7,15},{8,16},{9,17... | collective-permute-start | bytes 3145736 | tf_op jit(solution)/shard_map/ppermute | solution.py:26
  8.0 25.3 %copy-start.7 = (bf16[1,128,4096]{2,1,0:T(8,128)(2,1)S(1)}, bf16[1,128,4096]{2,1,0:T(8,128)(2,1)}, u32[]{:S(2)}) copy-start(bf16[1,128,4096]{2,1,0:T(8,128)(2,1)} %param.8) | copy-start | bytes 3145732
  8.0 25.4 %copy-start.6 = (bf16[1,128,4096]{2,1,0:T(8,128)(2,1)S(1)}, bf16[1,128,4096]{2,1,0:T(8,128)(2,1)}, u32[]{:S(2)}) copy-start(bf16[1,128,4096]{2,1,0:T(8,128)(2,1)} %param.5) | copy-start | bytes 3145732
  29.8 1.0 copy-start.3
  30.7 24.4 %collective-permute-start.3 = (bf16[2,2,128,1024]{3,2,1,0:T(8,128)(2,1)S(1)}, bf16[2,2,128,1024]{3,2,1,0:T(8,128)(2,1)S(1)}, u32[]{:S(2)}, u32[]{:S(2)}) collective-permute-start(bf16[2,2,128,1024]{3,2,1,0:T(8,128)(2,1)S(1)} %get-tuple-element.25), channel_id=1, source_target_pairs={{0,6},{1,7},{8,14},{9,15},{16,22},{17,23},{24,30},{25,31},{2,0},{3... | collective-permute-start | bytes 3145736 | tf_op jit(solution)/shard_map/ppermute | solution.py:26
  31.0 46.8 %collective-permute-start.4 = (bf16[2,2,128,1024]{3,2,1,0:T(8,128)(2,1)S(1)}, bf16[2,2,128,1024]{3,2,1,0:T(8,128)(2,1)S(1)}, u32[]{:S(2)}, u32[]{:S(2)}) collective-permute-start(bf16[2,2,128,1024]{3,2,1,0:T(8,128)(2,1)S(1)} %get-tuple-element.24), channel_id=1, source_target_pairs={{0,4},{1,5},{2,6},{3,7},{8,12},{9,13},{10,14},{11,15},{16,20},{17,... | collective-permute-start | bytes 3145736 | tf_op jit(solution)/shard_map/ppermute | solution.py:26
  31.2 46.6 %collective-permute-start.5 = (bf16[2,2,128,1024]{3,2,1,0:T(8,128)(2,1)S(1)}, bf16[2,2,128,1024]{3,2,1,0:T(8,128)(2,1)S(1)}, u32[]{:S(2)}, u32[]{:S(2)}) collective-permute-start(bf16[2,2,128,1024]{3,2,1,0:T(8,128)(2,1)S(1)} %get-tuple-element.23), channel_id=1, source_target_pairs={{0,2},{1,3},{2,4},{3,5},{4,6},{5,7},{8,10},{9,11},{10,12},{11,13},... | collective-permute-start | bytes 3145736 | tf_op jit(solution)/shard_map/ppermute | solution.py:26
  33.5 5.2 %collective-permute-start.2 = (bf16[2,128,2048]{2,1,0:T(8,128)(2,1)S(1)}, bf16[2,128,2048]{2,1,0:T(8,128)(2,1)S(1)}, u32[]{:S(2)}, u32[]{:S(2)}) collective-permute-start(bf16[2,128,2048]{2,1,0:T(8,128)(2,1)S(1)} %pad_maximum_fusion.2), channel_id=1, source_target_pairs={{0,1},{1,0},{2,3},{3,2},{4,5},{5,4},{6,7},{7,6},{8,9},{9,8},{10,11... | collective-permute-start | bytes 3145736 | tf_op jit(solution)/shard_map/ppermute | solution.py:26
  55.2 23.7 %copy-start.8 = (bf16[2,2,128,1024]{3,2,1,0:T(8,128)(2,1)}, bf16[2,2,128,1024]{3,2,1,0:T(8,128)(2,1)S(1)}, u32[]{:S(2)}) copy-start(bf16[2,2,128,1024]{3,2,1,0:T(8,128)(2,1)S(1)} %collective-permute-done.3.refs_7_) | copy-start | bytes 3145732
  77.8 1.4 copy-start.9
  77.8 1.0 copy-start.10
  104.5 24.7 %collective-permute-start.6 = (bf16[2,2,128,1024]{3,2,1,0:T(8,128)(2,1)}, bf16[2,2,128,1024]{3,2,1,0:T(8,128)(2,1)S(1)}, u32[]{:S(2)}, u32[]{:S(2)}) collective-permute-start(bf16[2,2,128,1024]{3,2,1,0:T(8,128)(2,1)} %get-tuple-element.18), channel_id=1, source_target_pairs={{2,0},{3,1},{4,2},{5,3},{6,4},{7,5},{10,8},{11,9},{12,10},{13,11},... | collective-permute-start | bytes 3145736 | tf_op jit(solution)/shard_map/ppermute | solution.py:26
  104.6 46.9 %collective-permute-start.7 = (bf16[2,2,128,1024]{3,2,1,0:T(8,128)(2,1)}, bf16[2,2,128,1024]{3,2,1,0:T(8,128)(2,1)S(1)}, u32[]{:S(2)}, u32[]{:S(2)}) collective-permute-start(bf16[2,2,128,1024]{3,2,1,0:T(8,128)(2,1)} %get-tuple-element.19), channel_id=1, source_target_pairs={{4,0},{5,1},{6,2},{7,3},{12,8},{13,9},{14,10},{15,11},{20,16},{21,... | collective-permute-start | bytes 3145736 | tf_op jit(solution)/shard_map/ppermute | solution.py:26
  104.9 46.6 %collective-permute-start.8 = (bf16[2,2,128,1024]{3,2,1,0:T(8,128)(2,1)}, bf16[2,2,128,1024]{3,2,1,0:T(8,128)(2,1)S(1)}, u32[]{:S(2)}, u32[]{:S(2)}) collective-permute-start(bf16[2,2,128,1024]{3,2,1,0:T(8,128)(2,1)} %get-tuple-element.20), channel_id=1, source_target_pairs={{6,0},{7,1},{14,8},{15,9},{22,16},{23,17},{30,24},{31,25},{0,2},{1... | collective-permute-start | bytes 3145736 | tf_op jit(solution)/shard_map/ppermute | solution.py:26
  151.5 28.7 %copy-start.1 = (f32[2,2,128,1024]{3,2,1,0:T(8,128)S(1)}, f32[2,2,128,1024]{3,2,1,0:T(8,128)}, u32[]{:S(2)}) copy-start(f32[2,2,128,1024]{3,2,1,0:T(8,128)} %get-tuple-element.17) | copy-start | bytes 6291460
  154.1 26.2 %collective-permute-start.9 = (bf16[2,2,128,1024]{3,2,1,0:T(8,128)(2,1)S(1)}, bf16[2,2,128,1024]{3,2,1,0:T(8,128)(2,1)S(1)}, u32[]{:S(2)}, u32[]{:S(2)}) collective-permute-start(bf16[2,2,128,1024]{3,2,1,0:T(8,128)(2,1)S(1)} %fusion.8), channel_id=1, source_target_pairs={{8,0},{9,1},{10,2},{11,3},{12,4},{13,5},{14,6},{15,7},{16,8},{17,9... | collective-permute-start | bytes 3145736 | tf_op jit(solution)/shard_map/ppermute | solution.py:26
  181.3 1.0 copy-start.5
  182.5 4.4 %collective-permute-start.10 = (bf16[128,4096]{1,0:T(8,128)(2,1)S(1)}, bf16[128,4096]{1,0:T(8,128)(2,1)S(1)}, u32[]{:S(2)}, u32[]{:S(2)}) collective-permute-start(bf16[128,4096]{1,0:T(8,128)(2,1)S(1)} %pad_maximum_fusion.3), channel_id=1, source_target_pairs={{0,1},{1,0},{2,3},{3,2},{4,5},{5,4},{6,7},{7,6},{8,9},{9,8},{10,11... | collective-permute-start | bytes 3145736 | tf_op jit(solution)/shard_map/ppermute | solution.py:26
  184.5 4.2 %copy-start.4 = (bf16[128,2048]{1,0:T(8,128)(2,1)S(1)}, bf16[128,2048]{1,0:T(8,128)(2,1)}, u32[]{:S(2)}) copy-start(bf16[128,2048]{1,0:T(8,128)(2,1)} %get-tuple-element.16) | copy-start | bytes 1572868

commit v12 on v11

--- a/solution.py
+++ b/solution.py
@@ -69,69 +69,78 @@
     return own + moved(prev.astype(link), reverse(routes.hop)).astype(jnp.float32)
 
 
-def attention_kernel(chips, core_ref, bias_ref, qm_ref, qs_ref, dm_ref, ds_ref, *refs):
+def attention_kernel(chips, heads, core_ref, bias_ref, qm_ref, qs_ref, dm_ref, ds_ref, *refs):
     del core_ref
     kv_refs = refs[:chips]
     dqm_ref, dqs_ref = refs[chips], refs[chips + 1]
     part_refs = refs[chips + 2 :]
     tokens = qm_ref.shape[0]
     d = HEAD_DIM
-    k = jnp.concatenate([r[0, s] for r in kv_refs for s in range(2)], axis=0)
-    v = jnp.concatenate([r[1, s] for r in kv_refs for s in range(2)], axis=0)
-    qs = jnp.concatenate([qm_ref[:, :d], qs_ref[:, :d], qm_ref[:, d:], qs_ref[:, d:]], axis=0)
-    dos = jnp.concatenate([dm_ref[:, :d], ds_ref[:, :d], dm_ref[:, d:], ds_ref[:, d:]], axis=0)
     contract_last = (((1,), (1,)), ((), ()))
     contract_first = (((0,), (0,)), ((), ()))
-    scores = lax.dot_general(qs, k, contract_last, preferred_element_type=jnp.float32)
-    scores = scores * SCORE_SCALE + bias_ref[...]
-    largest = jnp.max(scores, axis=1, keepdims=True)
-    unscaled = jnp.exp(scores - largest)
-    attn = unscaled * (1.0 / jnp.sum(unscaled, axis=1, keepdims=True))
-    dattn = lax.dot_general(dos, v, contract_last, preferred_element_type=jnp.float32)
-    row_delta = jnp.sum(attn * dattn, axis=1, keepdims=True)
-    dscores = (attn * (dattn - row_delta)).astype(jnp.bfloat16)
-    grad_q = jnp.dot(dscores, k, preferred_element_type=jnp.float32) * SCORE_SCALE
     rows = lambda j: slice(j * tokens, (j + 1) * tokens)
-    dqm_ref[:, :d] = grad_q[rows(0)].astype(dqm_ref.dtype)
-    dqs_ref[:, :d] = grad_q[rows(1)].astype(dqs_ref.dtype)
-    dqm_ref[:, d:] = grad_q[rows(2)].astype(dqm_ref.dtype)
-    dqs_ref[:, d:] = grad_q[rows(3)].astype(dqs_ref.dtype)
-    grad_k = (
-        lax.dot_general(dscores, qs, contract_first, preferred_element_type=jnp.float32)
-        * SCORE_SCALE
-    )
-    grad_v = lax.dot_general(
-        attn.astype(jnp.bfloat16), dos, contract_first, preferred_element_type=jnp.float32
-    )
-    for j, out in enumerate(part_refs):
-        for s in range(2):
-            out[0, s] = grad_k[rows(2 * j + s)].astype(out.dtype)
-            out[1, s] = grad_v[rows(2 * j + s)].astype(out.dtype)
-
-
-def attention_grads(core, bias, queries, query_sib, grad_out, grad_sib, payloads):
+    for h in range(heads):
+        cols = slice(h * d, (h + 1) * d)
+        first = slice(2 * h * d, (2 * h + 1) * d)
+        second = slice((2 * h + 1) * d, (2 * h + 2) * d)
+        k = jnp.concatenate([r[0, s, :, cols] for r in kv_refs for s in range(2)], axis=0)
+        v = jnp.concatenate([r[1, s, :, cols] for r in kv_refs for s in range(2)], axis=0)
+        qs = jnp.concatenate(
+            [qm_ref[:, first], qs_ref[:, first], qm_ref[:, second], qs_ref[:, second]], axis=0
+        )
+        dos = jnp.concatenate(
+            [dm_ref[:, first], ds_ref[:, first], dm_ref[:, second], ds_ref[:, second]], axis=0
+        )
+        scores = lax.dot_general(qs, k, contract_last, preferred_element_type=jnp.float32)
+        scores = scores * SCORE_SCALE + bias_ref[...]
+        largest = jnp.max(scores, axis=1, keepdims=True)
+        unscaled = jnp.exp(scores - largest)
+        attn = unscaled * (1.0 / jnp.sum(unscaled, axis=1, keepdims=True))
+        dattn = lax.dot_general(dos, v, contract_last, preferred_element_type=jnp.float32)
+        row_delta = jnp.sum(attn * dattn, axis=1, keepdims=True)
+        dscores = (attn * (dattn - row_delta)).astype(jnp.bfloat16)
+        grad_q = jnp.dot(dscores, k, preferred_element_type=jnp.float32) * SCORE_SCALE
+        dqm_ref[:, first] = grad_q[rows(0)].astype(dqm_ref.dtype)
+        dqs_ref[:, first] = grad_q[rows(1)].astype(dqs_ref.dtype)
+        dqm_ref[:, second] = grad_q[rows(2)].astype(dqm_ref.dtype)
+        dqs_ref[:, second] = grad_q[rows(3)].astype(dqs_ref.dtype)
+        grad_k = (
+            lax.dot_general(dscores, qs, contract_first, preferred_element_type=jnp.float32)
+            * SCORE_SCALE
+        )
+        grad_v = lax.dot_general(
+            attn.astype(jnp.bfloat16), dos, contract_first, preferred_element_type=jnp.float32
+        )
+        for j, out in enumerate(part_refs):
+            for s in range(2):
+                out[0, s, :, cols] = grad_k[rows(2 * j + s)].astype(out.dtype)
+                out[1, s, :, cols] = grad_v[rows(2 * j + s)].astype(out.dtype)
+
+
+def attention_grads(core, bias, queries, query_sib, grad_out, grad_sib, payloads, per_step=2):
     tokens = queries.shape[0]
     chips = len(payloads)
     key_count = bias.shape[1]
     half = payloads[0].shape[3]
     heads = half // HEAD_DIM
-    pair = 2 * HEAD_DIM
-    mine = pl.BlockSpec((tokens, pair), lambda g, c: (0, c[0] * heads + g))
+    pair = 2 * HEAD_DIM * per_step
+    steps = heads // per_step
+    mine = pl.BlockSpec((tokens, pair), lambda g, c: (0, c[0] * steps + g))
     other = pl.BlockSpec((tokens, pair), lambda g, c: (0, g))
-    chip = pl.BlockSpec((2, 2, tokens, HEAD_DIM), lambda g, c: (0, 0, 0, g))
+    chip = pl.BlockSpec((2, 2, tokens, HEAD_DIM * per_step), lambda g, c: (0, 0, 0, g))
     part = jax.ShapeDtypeStruct(payloads[0].shape, jnp.float32)
     rows = 4 * tokens
     flops = 2 * 5 * rows * key_count * HEAD_DIM * heads
     moved_bytes = 2 * 6 * tokens * half * 2 + 2 * 2 * key_count * half * 3 + bias.size * 4
     grid_spec = pltpu.PrefetchScalarGridSpec(
         num_scalar_prefetch=1,
-        grid=(heads,),
+        grid=(steps,),
         in_specs=[pl.BlockSpec(bias.shape, lambda g, c: (0, 0)), mine, other, mine, other]
         + [chip] * chips,
         out_specs=[other, other] + [chip] * chips,
     )
     return pl.pallas_call(
-        lambda *refs: attention_kernel(chips, *refs),
+        lambda *refs: attention_kernel(chips, per_step, *refs),
         grid_spec=grid_spec,
         out_shape=[jax.ShapeDtypeStruct(query_sib.shape, jnp.bfloat16)] * 2
         + [part]

time: 191 us -> 191 us (level)
  no operation moved by 1% of the time
where the time goes in v12:
time: 191 us; the launch traced here: 190 us
  waiting for transfers between devices  133 us (70%)
  Pallas kernels  25.8 us (14%)
  starting transfers between devices  14.7 us (8%)
  other arithmetic  9.49 us (5%)
  local copies, waits for them, and re-layouts  6.58 us (3%)
    ppermute x11, waiting for transfers between devices, moved(): return lax.ppermute(value, 'seq', pairs)  133 us
    pallas_call x1, Pallas kernels, attention_grads(): pl.pallas_call(lambda *refs: attention_kernel(chips, per_step, *refs), gr...  25.8 us
    ppermute x11, starting transfers between devices, moved(): return lax.ppermute(value, 'seq', pairs)  14.7 us
  transfers between devices with their start and end apart: 11, of which 8 were waited for; matrix products, arithmetic and copies ran while one was open for 2% of the time, Pallas kernels for 0%

profile of v12, /device:TPU:7, one launch (start us, length us, event | category | flops | bytes accessed | tf_op | source)
XLA Modules:
  0.0 190.5 jit_solution(8014901241762639742)
XLA Ops:
  0.6 0.0 copy-start
  0.7 1.3 constant_dynamic-slice_fusion.2
  1.9 0.1 pad_maximum_fusion.4
  2.0 0.7 collective-permute-start
  2.7 0.1 maximum_bitcast_fusion
  2.8 1.5 collective-permute-done
  4.3 0.1 pad_maximum_fusion.1.refs_10_
  4.4 0.0 copy-start.2
  4.4 3.3 %collective-permute-start.1 = (bf16[2,2,128,1024]{3,2,1,0:T(8,128)(2,1)S(1)}, bf16[2,2,128,1024]{3,2,1,0:T(8,128)(2,1)S(1)}, u32[]{:S(2)}, u32[]{:S(2)}) collective-permute-start(bf16[2,2,128,1024]{3,2,1,0:T(8,128)(2,1)S(1)} %pad_maximum_fusion.1.refs_10_), channel_id=1, source_target_pairs={{0,8},{1,9},{2,10},{3,11},{4,12},{5,13},{6,14},{7,15},{8,16},{9,17... | collective-permute-start | bytes 3145736 | tf_op jit(solution)/shard_map/ppermute | solution.py:26
  8.0 0.0 copy-start.7
  8.0 0.0 copy-start.6
  8.0 21.7 %collective-permute-done.1.refs_6_ = bf16[2,2,128,1024]{3,2,1,0:T(8,128)(2,1)S(1)} collective-permute-done((bf16[2,2,128,1024]{3,2,1,0:T(8,128)(2,1)S(1)}, bf16[2,2,128,1024]{3,2,1,0:T(8,128)(2,1)S(1)}, u32[]{:S(2)}, u32[]{:S(2)}) %collective-permute-start.1) | collective-permute-done | bytes 1048608 | tf_op jit(solution)/shard_map/ppermute | solution.py:26
  29.8 0.2 broadcast_select_fusion
  30.0 0.0 copy-done.2
  30.0 0.7 copy-done.3
  30.7 0.3 collective-permute-start.3
  31.0 0.2 collective-permute-start.4
  31.2 2.1 %collective-permute-start.5 = (bf16[2,2,128,1024]{3,2,1,0:T(8,128)(2,1)S(1)}, bf16[2,2,128,1024]{3,2,1,0:T(8,128)(2,1)S(1)}, u32[]{:S(2)}, u32[]{:S(2)}) collective-permute-start(bf16[2,2,128,1024]{3,2,1,0:T(8,128)(2,1)S(1)} %get-tuple-element.23), channel_id=1, source_target_pairs={{0,2},{1,3},{2,4},{3,5},{4,6},{5,7},{8,10},{9,11},{10,12},{11,13},... | collective-permute-start | bytes 3145736 | tf_op jit(solution)/shard_map/ppermute | solution.py:26
  33.3 0.0 copy-done
  33.3 0.0 copy-done.7
  33.4 0.1 pad_maximum_fusion.2
  33.5 2.1 %collective-permute-start.2 = (bf16[2,128,2048]{2,1,0:T(8,128)(2,1)S(1)}, bf16[2,128,2048]{2,1,0:T(8,128)(2,1)S(1)}, u32[]{:S(2)}, u32[]{:S(2)}) collective-permute-start(bf16[2,128,2048]{2,1,0:T(8,128)(2,1)S(1)} %pad_maximum_fusion.2), channel_id=1, source_target_pairs={{0,1},{1,0},{2,3},{3,2},{4,5},{5,4},{6,7},{7,6},{8,9},{9,8},{10,11... | collective-permute-start | bytes 3145736 | tf_op jit(solution)/shard_map/ppermute | solution.py:26
  35.6 0.1 broadcast_bitcast_fusion
  35.7 0.1 constant_dynamic-update-slice_fusion.19
  35.8 0.1 fusion.15
  35.9 0.1 constant_dynamic-update-slice_fusion.15
  35.9 0.1 constant_dynamic-update-slice_fusion.13
  36.0 0.1 constant_dynamic-update-slice_fusion.11
  36.1 0.1 constant_dynamic-update-slice_fusion.9
  36.2 0.1 constant_dynamic-update-slice_fusion.7
  36.3 0.1 constant_dynamic-update-slice_fusion.5
  36.4 0.1 constant_dynamic-update-slice_fusion.3
  36.4 0.1 constant_dynamic-update-slice_fusion.1
  36.5 0.5 fusion.11
  37.0 1.7 pad_maximum_fusion.refs_1_
  38.7 0.0 collective-permute-done.2
  38.7 1.1 slice_bitcast_fusion.1
  39.8 15.4 %collective-permute-done.3.refs_7_ = bf16[2,2,128,1024]{3,2,1,0:T(8,128)(2,1)S(1)} collective-permute-done((bf16[2,2,128,1024]{3,2,1,0:T(8,128)(2,1)S(1)}, bf16[2,2,128,1024]{3,2,1,0:T(8,128)(2,1)S(1)}, u32[]{:S(2)}, u32[]{:S(2)}) %collective-permute-start.3) | collective-permute-done | bytes 1048608 | tf_op jit(solution)/shard_map/ppermute | solution.py:26
  55.2 22.6 %collective-permute-done.4.refs_8_ = bf16[2,2,128,1024]{3,2,1,0:T(8,128)(2,1)S(1)} collective-permute-done((bf16[2,2,128,1024]{3,2,1,0:T(8,128)(2,1)S(1)}, bf16[2,2,128,1024]{3,2,1,0:T(8,128)(2,1)S(1)}, u32[]{:S(2)}, u32[]{:S(2)}) %collective-permute-start.4) | collective-permute-done | bytes 1048608 | tf_op jit(solution)/shard_map/ppermute | solution.py:26
  77.8 0.0 collective-permute-done.5.refs_9_
  77.8 1.0 copy-done.10
  78.8 0.0 copy-done.8
  78.8 0.4 copy-done.9
  79.2 25.8 %shard_map.76 = (bf16[128,2048]{1,0:T(8,128)(2,1)}, bf16[128,2048]{1,0:T(8,128)(2,1)}, f32[2,2,128,1024]{3,2,1,0:T(8,128)}, bf16[2,2,128,1024]{3,2,1,0:T(8,128)(...) custom-call(s32[1]{0:T(128)} %bitcast.refs_0_, ...), custom_call_target="tpu_custom_call" | custom-call | flops 6710886400 | bytes 21495808 | tf_op jit(solution)/shard_map/pallas_call | solution.py:142
  105.0 0.1 collective-permute-start.6
  105.1 0.3 collective-permute-start.7
  105.4 2.3 %collective-permute-start.8 = (bf16[2,2,128,1024]{3,2,1,0:T(8,128)(2,1)}, bf16[2,2,128,1024]{3,2,1,0:T(8,128)(2,1)S(1)}, u32[]{:S(2)}, u32[]{:S(2)}) collective-permute-start(bf16[2,2,128,1024]{3,2,1,0:T(8,128)(2,1)} %get-tuple-element.20), channel_id=1, source_target_pairs={{6,0},{7,1},{14,8},{15,9},{22,16},{23,17},{30,24},{31,25},{0,2},{1... | collective-permute-start | bytes 3145736 | tf_op jit(solution)/shard_map/ppermute | solution.py:26
  107.7 22.1 %collective-permute-done.6 = bf16[2,2,128,1024]{3,2,1,0:T(8,128)(2,1)S(1)} collective-permute-done((bf16[2,2,128,1024]{3,2,1,0:T(8,128)(2,1)}, bf16[2,2,128,1024]{3,2,1,0:T(8,128)(2,1)S(1)}, u32[]{:S(2)}, u32[]{:S(2)}) %collective-permute-start.6) | collective-permute-done | bytes 1048608 | tf_op jit(solution)/shard_map/ppermute | solution.py:26
  129.7 22.3 %collective-permute-done.7 = bf16[2,2,128,1024]{3,2,1,0:T(8,128)(2,1)S(1)} collective-permute-done((bf16[2,2,128,1024]{3,2,1,0:T(8,128)(2,1)}, bf16[2,2,128,1024]{3,2,1,0:T(8,128)(2,1)S(1)}, u32[]{:S(2)}, u32[]{:S(2)}) %collective-permute-start.7) | collective-permute-done | bytes 1048608 | tf_op jit(solution)/shard_map/ppermute | solution.py:26
  152.0 0.0 collective-permute-done.8
  152.0 2.5 %fusion.8 = bf16[2,2,128,1024]{3,2,1,0:T(8,128)(2,1)S(1)} fusion(f32[2,2,128,1024]{3,2,1,0:T(8,128)} %get-tuple-element.21, bf16[2,2,128,1024]{3,2,1,0:T(8,128)(2,1)S(1)} %collective-permute-done.6, bf16[2,2,128,1024]{3,2,1,0:T(8,128)(2,1)S(1)} %collective-permute-done.7, bf16[2,2,128,1024]{3,2,1,0:T(8,128)(2,1)S(1)} %collective-permute-done.8, pred[]{:T(512)S(6)} %lt.97, ...), kind=kLoop, calls=%fused_computation.15 | loop fusion | flops 5242880 | bytes 6291459 | tf_op jit(solution)/shard_map/convert_element_type | solution.py:69
  154.6 1.3 collective-permute-start.9
  155.9 24.9 %collective-permute-done.9 = bf16[2,2,128,1024]{3,2,1,0:T(8,128)(2,1)S(1)} collective-permute-done((bf16[2,2,128,1024]{3,2,1,0:T(8,128)(2,1)S(1)}, bf16[2,2,128,1024]{3,2,1,0:T(8,128)(2,1)S(1)}, u32[]{:S(2)}, u32[]{:S(2)}) %collective-permute-start.9) | collective-permute-done | bytes 1048608 | tf_op jit(solution)/shard_map/ppermute | solution.py:26
  180.8 1.1 fusion.4
  181.8 0.0 copy-start.5
  181.8 0.1 slice_bitcast_fusion.4
  181.9 0.9 copy-done.5
  182.9 0.1 pad_maximum_fusion.3
  182.9 2.1 %collective-permute-start.10 = (bf16[128,4096]{1,0:T(8,128)(2,1)S(1)}, bf16[128,4096]{1,0:T(8,128)(2,1)S(1)}, u32[]{:S(2)}, u32[]{:S(2)}) collective-permute-start(bf16[128,4096]{1,0:T(8,128)(2,1)S(1)} %pad_maximum_fusion.3), channel_id=1, source_target_pairs={{0,1},{1,0},{2,3},{3,2},{4,5},{5,4},{6,7},{7,6},{8,9},{9,8},{10,11... | collective-permute-start | bytes 3145736 | tf_op jit(solution)/shard_map/ppermute | solution.py:26
  185.0 2.3 %collective-permute-done.10 = bf16[128,4096]{1,0:T(8,128)(2,1)S(1)} collective-permute-done((bf16[128,4096]{1,0:T(8,128)(2,1)S(1)}, bf16[128,4096]{1,0:T(8,128)(2,1)S(1)}, u32[]{:S(2)}, u32[]{:S(2)}) %collective-permute-start.10) | collective-permute-done | bytes 1048608 | tf_op jit(solution)/shard_map/ppermute | solution.py:26
  187.4 0.9 maximum_select_fusion.2
  188.3 0.9 maximum_select_fusion.1
  189.3 0.0 copy-done.4
  189.3 1.2 maximum_select_fusion
  (25 shorter events, 0.2 us)
Async XLA Ops:
  0.6 32.7 %copy-start = (s32[1,32]{1,0:T(1,128)S(1)}, s32[1,32]{1,0:T(1,128)}, u32[]{:S(2)}) copy-start(s32[1,32]{1,0:T(1,128)} %param.9) | copy-start | bytes 388
  2.0 2.3 %collective-permute-start = (bf16[2,128,1024]{2,1,0:T(8,128)(2,1)S(1)}, bf16[2,128,1024]{2,1,0:T(8,128)(2,1)S(1)}, u32[]{:S(2)}, u32[]{:S(2)}) collective-permute-start(bf16[2,128,1024]{2,1,0:T(8,128)(2,1)S(1)} %pad_maximum_fusion.4), channel_id=1, source_target_pairs={{0,1},{1,0},{2,3},{3,2},{4,5},{5,4},{6,7},{7,6},{8,9},{9,8},{10,11... | collective-permute-start | bytes 1572872 | tf_op jit(solution)/shard_map/ppermute | solution.py:26
  4.4 25.6 %copy-start.2 = (bf16[2,2,128,1024]{3,2,1,0:T(8,128)(2,1)}, bf16[2,2,128,1024]{3,2,1,0:T(8,128)(2,1)S(1)}, u32[]{:S(2)}) copy-start(bf16[2,2,128,1024]{3,2,1,0:T(8,128)(2,1)S(1)} %pad_maximum_fusion.1.refs_10_) | copy-start | bytes 3145732
  4.4 25.4 %collective-permute-start.1 = (bf16[2,2,128,1024]{3,2,1,0:T(8,128)(2,1)S(1)}, bf16[2,2,128,1024]{3,2,1,0:T(8,128)(2,1)S(1)}, u32[]{:S(2)}, u32[]{:S(2)}) collective-permute-start(bf16[2,2,128,1024]{3,2,1,0:T(8,128)(2,1)S(1)} %pad_maximum_fusion.1.refs_10_), channel_id=1, source_target_pairs={{0,8},{1,9},{2,10},{3,11},{4,12},{5,13},{6,14},{7,15},{8,16},{9,17... | collective-permute-start | bytes 3145736 | tf_op jit(solution)/shard_map/ppermute | solution.py:26
  8.0 25.3 %copy-start.7 = (bf16[1,128,4096]{2,1,0:T(8,128)(2,1)S(1)}, bf16[1,128,4096]{2,1,0:T(8,128)(2,1)}, u32[]{:S(2)}) copy-start(bf16[1,128,4096]{2,1,0:T(8,128)(2,1)} %param.8) | copy-start | bytes 3145732
  8.0 25.4 %copy-start.6 = (bf16[1,128,4096]{2,1,0:T(8,128)(2,1)S(1)}, bf16[1,128,4096]{2,1,0:T(8,128)(2,1)}, u32[]{:S(2)}) copy-start(bf16[1,128,4096]{2,1,0:T(8,128)(2,1)} %param.5) | copy-start | bytes 3145732
  29.8 1.0 copy-start.3
  30.7 24.4 %collective-permute-start.3 = (bf16[2,2,128,1024]{3,2,1,0:T(8,128)(2,1)S(1)}, bf16[2,2,128,1024]{3,2,1,0:T(8,128)(2,1)S(1)}, u32[]{:S(2)}, u32[]{:S(2)}) collective-permute-start(bf16[2,2,128,1024]{3,2,1,0:T(8,128)(2,1)S(1)} %get-tuple-element.25), channel_id=1, source_target_pairs={{0,6},{1,7},{8,14},{9,15},{16,22},{17,23},{24,30},{25,31},{2,0},{3... | collective-permute-start | bytes 3145736 | tf_op jit(solution)/shard_map/ppermute | solution.py:26
  31.0 46.8 %collective-permute-start.4 = (bf16[2,2,128,1024]{3,2,1,0:T(8,128)(2,1)S(1)}, bf16[2,2,128,1024]{3,2,1,0:T(8,128)(2,1)S(1)}, u32[]{:S(2)}, u32[]{:S(2)}) collective-permute-start(bf16[2,2,128,1024]{3,2,1,0:T(8,128)(2,1)S(1)} %get-tuple-element.24), channel_id=1, source_target_pairs={{0,4},{1,5},{2,6},{3,7},{8,12},{9,13},{10,14},{11,15},{16,20},{17,... | collective-permute-start | bytes 3145736 | tf_op jit(solution)/shard_map/ppermute | solution.py:26
  31.2 46.6 %collective-permute-start.5 = (bf16[2,2,128,1024]{3,2,1,0:T(8,128)(2,1)S(1)}, bf16[2,2,128,1024]{3,2,1,0:T(8,128)(2,1)S(1)}, u32[]{:S(2)}, u32[]{:S(2)}) collective-permute-start(bf16[2,2,128,1024]{3,2,1,0:T(8,128)(2,1)S(1)} %get-tuple-element.23), channel_id=1, source_target_pairs={{0,2},{1,3},{2,4},{3,5},{4,6},{5,7},{8,10},{9,11},{10,12},{11,13},... | collective-permute-start | bytes 3145736 | tf_op jit(solution)/shard_map/ppermute | solution.py:26
  33.5 5.2 %collective-permute-start.2 = (bf16[2,128,2048]{2,1,0:T(8,128)(2,1)S(1)}, bf16[2,128,2048]{2,1,0:T(8,128)(2,1)S(1)}, u32[]{:S(2)}, u32[]{:S(2)}) collective-permute-start(bf16[2,128,2048]{2,1,0:T(8,128)(2,1)S(1)} %pad_maximum_fusion.2), channel_id=1, source_target_pairs={{0,1},{1,0},{2,3},{3,2},{4,5},{5,4},{6,7},{7,6},{8,9},{9,8},{10,11... | collective-permute-start | bytes 3145736 | tf_op jit(solution)/shard_map/ppermute | solution.py:26
  55.2 23.7 %copy-start.8 = (bf16[2,2,128,1024]{3,2,1,0:T(8,128)(2,1)}, bf16[2,2,128,1024]{3,2,1,0:T(8,128)(2,1)S(1)}, u32[]{:S(2)}) copy-start(bf16[2,2,128,1024]{3,2,1,0:T(8,128)(2,1)S(1)} %collective-permute-done.3.refs_7_) | copy-start | bytes 3145732
  77.8 1.4 copy-start.9
  77.8 1.0 copy-start.10
  105.0 24.7 %collective-permute-start.6 = (bf16[2,2,128,1024]{3,2,1,0:T(8,128)(2,1)}, bf16[2,2,128,1024]{3,2,1,0:T(8,128)(2,1)S(1)}, u32[]{:S(2)}, u32[]{:S(2)}) collective-permute-start(bf16[2,2,128,1024]{3,2,1,0:T(8,128)(2,1)} %get-tuple-element.18), channel_id=1, source_target_pairs={{2,0},{3,1},{4,2},{5,3},{6,4},{7,5},{10,8},{11,9},{12,10},{13,11},... | collective-permute-start | bytes 3145736 | tf_op jit(solution)/shard_map/ppermute | solution.py:26
  105.1 46.9 %collective-permute-start.7 = (bf16[2,2,128,1024]{3,2,1,0:T(8,128)(2,1)}, bf16[2,2,128,1024]{3,2,1,0:T(8,128)(2,1)S(1)}, u32[]{:S(2)}, u32[]{:S(2)}) collective-permute-start(bf16[2,2,128,1024]{3,2,1,0:T(8,128)(2,1)} %get-tuple-element.19), channel_id=1, source_target_pairs={{4,0},{5,1},{6,2},{7,3},{12,8},{13,9},{14,10},{15,11},{20,16},{21,... | collective-permute-start | bytes 3145736 | tf_op jit(solution)/shard_map/ppermute | solution.py:26
  105.4 46.6 %collective-permute-start.8 = (bf16[2,2,128,1024]{3,2,1,0:T(8,128)(2,1)}, bf16[2,2,128,1024]{3,2,1,0:T(8,128)(2,1)S(1)}, u32[]{:S(2)}, u32[]{:S(2)}) collective-permute-start(bf16[2,2,128,1024]{3,2,1,0:T(8,128)(2,1)} %get-tuple-element.20), channel_id=1, source_target_pairs={{6,0},{7,1},{14,8},{15,9},{22,16},{23,17},{30,24},{31,25},{0,2},{1... | collective-permute-start | bytes 3145736 | tf_op jit(solution)/shard_map/ppermute | solution.py:26
  152.0 28.7 %copy-start.1 = (f32[2,2,128,1024]{3,2,1,0:T(8,128)S(1)}, f32[2,2,128,1024]{3,2,1,0:T(8,128)}, u32[]{:S(2)}) copy-start(f32[2,2,128,1024]{3,2,1,0:T(8,128)} %get-tuple-element.17) | copy-start | bytes 6291460
  154.6 26.2 %collective-permute-start.9 = (bf16[2,2,128,1024]{3,2,1,0:T(8,128)(2,1)S(1)}, bf16[2,2,128,1024]{3,2,1,0:T(8,128)(2,1)S(1)}, u32[]{:S(2)}, u32[]{:S(2)}) collective-permute-start(bf16[2,2,128,1024]{3,2,1,0:T(8,128)(2,1)S(1)} %fusion.8), channel_id=1, source_target_pairs={{8,0},{9,1},{10,2},{11,3},{12,4},{13,5},{14,6},{15,7},{16,8},{17,9... | collective-permute-start | bytes 3145736 | tf_op jit(solution)/shard_map/ppermute | solution.py:26
  181.8 1.0 copy-start.5
  182.9 4.4 %collective-permute-start.10 = (bf16[128,4096]{1,0:T(8,128)(2,1)S(1)}, bf16[128,4096]{1,0:T(8,128)(2,1)S(1)}, u32[]{:S(2)}, u32[]{:S(2)}) collective-permute-start(bf16[128,4096]{1,0:T(8,128)(2,1)S(1)} %pad_maximum_fusion.3), channel_id=1, source_target_pairs={{0,1},{1,0},{2,3},{3,2},{4,5},{5,4},{6,7},{7,6},{8,9},{9,8},{10,11... | collective-permute-start | bytes 3145736 | tf_op jit(solution)/shard_map/ppermute | solution.py:26
  185.0 4.2 %copy-start.4 = (bf16[128,2048]{1,0:T(8,128)(2,1)S(1)}, bf16[128,2048]{1,0:T(8,128)(2,1)}, u32[]{:S(2)}) copy-start(bf16[128,2048]{1,0:T(8,128)(2,1)} %get-tuple-element.16) | copy-start | bytes 1572868

commit v13 on v11

--- a/solution.py
+++ b/solution.py
@@ -208,16 +208,11 @@
         core[None].astype(jnp.int32), bias, queries[0], qd_sib[0], grad_out, qd_sib[1], payloads
     )
     dq_mine, dq_sib, parts = outs[0], outs[1], outs[2:]
+    grad_query = in_core_order(core, dq_mine, moved(dq_sib, routes.sibling))
     summed = scatter_window(parts, routes, chip_in_group)
-    sent = jnp.concatenate(
-        [summed[0, 1].astype(jnp.bfloat16), summed[1, 1].astype(jnp.bfloat16), dq_sib], axis=-1
-    )
-    got = moved(sent, routes.sibling)
-    grad_key = in_core_order(core, summed[0, 0].astype(jnp.bfloat16), got[:, :key_width])
-    grad_value = in_core_order(
-        core, summed[1, 0].astype(jnp.bfloat16), got[:, key_width : 2 * key_width]
-    )
-    grad_query = in_core_order(core, dq_mine, got[:, 2 * key_width :])
+    got = moved(summed[:, 1].astype(jnp.bfloat16), routes.sibling)
+    grad_key = in_core_order(core, summed[0, 0].astype(jnp.bfloat16), got[0])
+    grad_value = in_core_order(core, summed[1, 0].astype(jnp.bfloat16), got[1])
     return (grad_query[None], grad_key[None], grad_value[None])
 
 

time: 191 us -> 191 us (level)
  waiting for transfers between devices: 133 us -> 130 us
  other arithmetic: 9.49 us -> 12.3 us
    ppermute x11 -> x12, waiting for transfers between devices: 133 us -> 130 us  [moved(): return lax.ppermute(value, 'seq', pairs)]
    another operation x1, other arithmetic: 1.05 us -> 3.04 us
    ppermute x11 -> x12, starting transfers between devices: 14.7 us -> 16.2 us  [moved(): return lax.ppermute(value, 'seq', pairs)]
  transfers between devices with their start and end apart: 11 -> 12, of which waited for: 8 -> 8; matrix products, arithmetic and copies ran while one was open for 2% -> 5% of each run, Pallas kernels for 0% -> 0%
where the time goes in v13:
time: 191 us; the launch traced here: 190 us
  waiting for transfers between devices  130 us (68%)
  Pallas kernels  25.3 us (13%)
  starting transfers between devices  16.2 us (8%)
  other arithmetic  12.3 us (6%)
  local copies, waits for them, and re-layouts  5.58 us (3%)
    ppermute x12, waiting for transfers between devices, moved(): return lax.ppermute(value, 'seq', pairs)  130 us
    pallas_call x1, Pallas kernels, attention_grads(): pl.pallas_call(lambda *refs: attention_kernel(chips, *refs), grid_spec=gr...  25.3 us
    ppermute x12, starting transfers between devices, moved(): return lax.ppermute(value, 'seq', pairs)  16.2 us
  transfers between devices with their start and end apart: 12, of which 8 were waited for; matrix products, arithmetic and copies ran while one was open for 5% of the time, Pallas kernels for 0%

profile of v13, /device:TPU:7, one launch (start us, length us, event | category | flops | bytes accessed | tf_op | source)
XLA Modules:
  0.0 190.1 jit_solution(6049785552505256990)
XLA Ops:
  0.6 0.0 copy-start
  0.7 1.3 constant_dynamic-slice_fusion.2
  2.0 0.1 pad_maximum_fusion.3
  2.0 0.7 collective-permute-start
  2.8 0.1 maximum_bitcast_fusion
  2.8 1.5 collective-permute-done
  4.3 0.1 pad_maximum_fusion.1.refs_10_
  4.4 0.0 copy-start.1
  4.4 3.3 %collective-permute-start.1 = (bf16[2,2,128,1024]{3,2,1,0:T(8,128)(2,1)S(1)}, bf16[2,2,128,1024]{3,2,1,0:T(8,128)(2,1)S(1)}, u32[]{:S(2)}, u32[]{:S(2)}) collective-permute-start(bf16[2,2,128,1024]{3,2,1,0:T(8,128)(2,1)S(1)} %pad_maximum_fusion.1.refs_10_), channel_id=1, source_target_pairs={{0,8},{1,9},{2,10},{3,11},{4,12},{5,13},{6,14},{7,15},{8,16},{9,17... | collective-permute-start | bytes 3145736 | tf_op jit(solution)/shard_map/ppermute | solution.py:26
  8.0 0.0 copy-start.5
  8.0 0.0 copy-start.4
  8.0 21.7 %collective-permute-done.1.refs_6_ = bf16[2,2,128,1024]{3,2,1,0:T(8,128)(2,1)S(1)} collective-permute-done((bf16[2,2,128,1024]{3,2,1,0:T(8,128)(2,1)S(1)}, bf16[2,2,128,1024]{3,2,1,0:T(8,128)(2,1)S(1)}, u32[]{:S(2)}, u32[]{:S(2)}) %collective-permute-start.1) | collective-permute-done | bytes 1048608 | tf_op jit(solution)/shard_map/ppermute | solution.py:26
  29.8 0.0 copy-start.2
  29.8 0.2 broadcast_select_fusion
  30.0 0.0 copy-done.1
  30.0 0.7 copy-done.2
  30.7 0.3 collective-permute-start.3
  31.0 0.2 collective-permute-start.4
  31.2 2.1 %collective-permute-start.5 = (bf16[2,2,128,1024]{3,2,1,0:T(8,128)(2,1)S(1)}, bf16[2,2,128,1024]{3,2,1,0:T(8,128)(2,1)S(1)}, u32[]{:S(2)}, u32[]{:S(2)}) collective-permute-start(bf16[2,2,128,1024]{3,2,1,0:T(8,128)(2,1)S(1)} %get-tuple-element.23), channel_id=1, source_target_pairs={{0,2},{1,3},{2,4},{3,5},{4,6},{5,7},{8,10},{9,11},{10,12},{11,13},... | collective-permute-start | bytes 3145736 | tf_op jit(solution)/shard_map/ppermute | solution.py:26
  33.3 0.0 copy-done
  33.3 0.0 copy-done.5
  33.4 0.0 copy-done.4
  33.4 0.1 pad_maximum_fusion.2
  33.5 2.1 %collective-permute-start.2 = (bf16[2,128,2048]{2,1,0:T(8,128)(2,1)S(1)}, bf16[2,128,2048]{2,1,0:T(8,128)(2,1)S(1)}, u32[]{:S(2)}, u32[]{:S(2)}) collective-permute-start(bf16[2,128,2048]{2,1,0:T(8,128)(2,1)S(1)} %pad_maximum_fusion.2), channel_id=1, source_target_pairs={{0,1},{1,0},{2,3},{3,2},{4,5},{5,4},{6,7},{7,6},{8,9},{9,8},{10,11... | collective-permute-start | bytes 3145736 | tf_op jit(solution)/shard_map/ppermute | solution.py:26
  35.7 0.1 broadcast_bitcast_fusion
  35.7 0.1 constant_dynamic-update-slice_fusion.19
  35.8 0.1 fusion.16
  35.9 0.1 constant_dynamic-update-slice_fusion.15
  36.0 0.1 constant_dynamic-update-slice_fusion.13
  36.0 0.1 constant_dynamic-update-slice_fusion.11
  36.1 0.1 constant_dynamic-update-slice_fusion.9
  36.2 0.1 constant_dynamic-update-slice_fusion.7
  36.3 0.1 constant_dynamic-update-slice_fusion.5
  36.4 0.1 constant_dynamic-update-slice_fusion.3
  36.5 0.1 constant_dynamic-update-slice_fusion.1
  36.5 0.5 fusion.11
  37.0 1.7 pad_maximum_fusion.refs_1_
  38.7 0.0 collective-permute-done.2
  38.7 1.1 slice_bitcast_fusion.1
  39.8 15.4 %collective-permute-done.3.refs_7_ = bf16[2,2,128,1024]{3,2,1,0:T(8,128)(2,1)S(1)} collective-permute-done((bf16[2,2,128,1024]{3,2,1,0:T(8,128)(2,1)S(1)}, bf16[2,2,128,1024]{3,2,1,0:T(8,128)(2,1)S(1)}, u32[]{:S(2)}, u32[]{:S(2)}) %collective-permute-start.3) | collective-permute-done | bytes 1048608 | tf_op jit(solution)/shard_map/ppermute | solution.py:26
  55.2 22.6 %collective-permute-done.4.refs_8_ = bf16[2,2,128,1024]{3,2,1,0:T(8,128)(2,1)S(1)} collective-permute-done((bf16[2,2,128,1024]{3,2,1,0:T(8,128)(2,1)S(1)}, bf16[2,2,128,1024]{3,2,1,0:T(8,128)(2,1)S(1)}, u32[]{:S(2)}, u32[]{:S(2)}) %collective-permute-start.4) | collective-permute-done | bytes 1048608 | tf_op jit(solution)/shard_map/ppermute | solution.py:26
  77.8 0.0 collective-permute-done.5.refs_9_
  77.8 0.0 copy-done.6
  77.8 1.1 copy-done.7
  78.9 0.3 copy-done.8
  79.2 25.3 %shard_map.76 = (bf16[128,2048]{1,0:T(8,128)(2,1)}, bf16[128,2048]{1,0:T(8,128)(2,1)}, f32[2,2,128,1024]{3,2,1,0:T(8,128)}, bf16[2,2,128,1024]{3,2,1,0:T(8,128)(...) custom-call(s32[1]{0:T(128)} %bitcast.refs_0_, ...), custom_call_target="tpu_custom_call" | custom-call | flops 6710886400 | bytes 21495808 | tf_op jit(solution)/shard_map/pallas_call | solution.py:133
  104.5 0.1 collective-permute-start.7
  104.6 0.3 collective-permute-start.8
  104.9 2.3 %collective-permute-start.9 = (bf16[2,2,128,1024]{3,2,1,0:T(8,128)(2,1)}, bf16[2,2,128,1024]{3,2,1,0:T(8,128)(2,1)S(1)}, u32[]{:S(2)}, u32[]{:S(2)}) collective-permute-start(bf16[2,2,128,1024]{3,2,1,0:T(8,128)(2,1)} %get-tuple-element.21), channel_id=1, source_target_pairs={{6,0},{7,1},{14,8},{15,9},{22,16},{23,17},{30,24},{31,25},{0,2},{1... | collective-permute-start | bytes 3145736 | tf_op jit(solution)/shard_map/ppermute | solution.py:26
  107.2 22.0 %collective-permute-done.7 = bf16[2,2,128,1024]{3,2,1,0:T(8,128)(2,1)S(1)} collective-permute-done((bf16[2,2,128,1024]{3,2,1,0:T(8,128)(2,1)}, bf16[2,2,128,1024]{3,2,1,0:T(8,128)(2,1)S(1)}, u32[]{:S(2)}, u32[]{:S(2)}) %collective-permute-start.7) | collective-permute-done | bytes 1048608 | tf_op jit(solution)/shard_map/ppermute | solution.py:26
  129.2 22.3 %collective-permute-done.8 = bf16[2,2,128,1024]{3,2,1,0:T(8,128)(2,1)S(1)} collective-permute-done((bf16[2,2,128,1024]{3,2,1,0:T(8,128)(2,1)}, bf16[2,2,128,1024]{3,2,1,0:T(8,128)(2,1)S(1)}, u32[]{:S(2)}, u32[]{:S(2)}) %collective-permute-start.8) | collective-permute-done | bytes 1048608 | tf_op jit(solution)/shard_map/ppermute | solution.py:26
  151.5 0.0 collective-permute-done.9
  151.5 3.4 %fusion.8 = bf16[2,2,128,1024]{3,2,1,0:T(8,128)(2,1)} fusion(f32[2,2,128,1024]{3,2,1,0:T(8,128)} %get-tuple-element.22, bf16[2,2,128,1024]{3,2,1,0:T(8,128)(2,1)S(1)} %collective-permute-done.7, bf16[2,2,128,1024]{3,2,1,0:T(8,128)(2,1)S(1)} %collective-permute-done.8, bf16[2,2,128,1024]{3,2,1,0:T(8,128)(2,1)S(1)} %collective-permute-done.9, pred[]{:T(512)S(6)} %lt.97, ...), kind=kLoop, calls=%fused_computation.15 | loop fusion | flops 5242880 | bytes 6291459 | tf_op jit(solution)/shard_map/convert_element_type | solution.py:69
  155.0 1.3 collective-permute-start.10
  156.3 1.4 collective-permute-start.6
  157.7 23.8 %collective-permute-done.10 = bf16[2,2,128,1024]{3,2,1,0:T(8,128)(2,1)} collective-permute-done((bf16[2,2,128,1024]{3,2,1,0:T(8,128)(2,1)}, bf16[2,2,128,1024]{3,2,1,0:T(8,128)(2,1)}, u32[]{:S(2)}, u32[]{:S(2)}) %collective-permute-start.10) | collective-permute-done | bytes 1048608 | tf_op jit(solution)/shard_map/ppermute | solution.py:26
  181.5 3.0 %fusion.4 = bf16[2,2,128,1024]{3,2,1,0:T(8,128)(2,1)S(1)} fusion(f32[2,2,128,1024]{3,2,1,0:T(8,128)} %get-tuple-element.18, bf16[2,2,128,1024]{3,2,1,0:T(8,128)(2,1)S(1)} %collective-permute-done.7, bf16[2,2,128,1024]{3,2,1,0:T(8,128)(2,1)S(1)} %collective-permute-done.8, bf16[2,2,128,1024]{3,2,1,0:T(8,128)(2,1)S(1)} %collective-permute-done.9, ...), kind=kLoop, calls=%fused_computation.11 | loop fusion | flops 6291456 | bytes 7340035 | tf_op jit(solution)/shard_map/convert.2
  184.6 2.1 %collective-permute-start.11 = (bf16[2,128,1024]{2,1,0:T(8,128)(2,1)S(1)}, bf16[2,128,1024]{2,1,0:T(8,128)(2,1)S(1)}, u32[]{:S(2)}, u32[]{:S(2)}) collective-permute-start(bf16[2,128,1024]{2,1,0:T(8,128)(2,1)S(1)} %slice_bitcast_fusion), channel_id=1, source_target_pairs={{0,1},{1,0},{2,3},{3,2},{4,5},{5,4},{6,7},{7,6},{8,9},{9,8},{10,11... | collective-permute-start | bytes 1572872 | tf_op jit(solution)/shard_map/ppermute | solution.py:26
  186.7 0.0 collective-permute-done.6
  186.7 0.0 copy-done.3
  186.7 1.2 maximum_select_fusion
  187.9 0.3 collective-permute-done.11
  188.2 0.9 maximum_select_fusion.2
  189.2 0.9 maximum_select_fusion.1
  (22 shorter events, 0.3 us)
Async XLA Ops:
  0.6 32.7 %copy-start = (s32[1,32]{1,0:T(1,128)S(1)}, s32[1,32]{1,0:T(1,128)}, u32[]{:S(2)}) copy-start(s32[1,32]{1,0:T(1,128)} %param.9) | copy-start | bytes 388
  2.0 2.3 %collective-permute-start = (bf16[2,128,1024]{2,1,0:T(8,128)(2,1)S(1)}, bf16[2,128,1024]{2,1,0:T(8,128)(2,1)S(1)}, u32[]{:S(2)}, u32[]{:S(2)}) collective-permute-start(bf16[2,128,1024]{2,1,0:T(8,128)(2,1)S(1)} %pad_maximum_fusion.3), channel_id=1, source_target_pairs={{0,1},{1,0},{2,3},{3,2},{4,5},{5,4},{6,7},{7,6},{8,9},{9,8},{10,11... | collective-permute-start | bytes 1572872 | tf_op jit(solution)/shard_map/ppermute | solution.py:26
  4.4 25.6 %copy-start.1 = (bf16[2,2,128,1024]{3,2,1,0:T(8,128)(2,1)}, bf16[2,2,128,1024]{3,2,1,0:T(8,128)(2,1)S(1)}, u32[]{:S(2)}) copy-start(bf16[2,2,128,1024]{3,2,1,0:T(8,128)(2,1)S(1)} %pad_maximum_fusion.1.refs_10_) | copy-start | bytes 3145732
  4.4 25.4 %collective-permute-start.1 = (bf16[2,2,128,1024]{3,2,1,0:T(8,128)(2,1)S(1)}, bf16[2,2,128,1024]{3,2,1,0:T(8,128)(2,1)S(1)}, u32[]{:S(2)}, u32[]{:S(2)}) collective-permute-start(bf16[2,2,128,1024]{3,2,1,0:T(8,128)(2,1)S(1)} %pad_maximum_fusion.1.refs_10_), channel_id=1, source_target_pairs={{0,8},{1,9},{2,10},{3,11},{4,12},{5,13},{6,14},{7,15},{8,16},{9,17... | collective-permute-start | bytes 3145736 | tf_op jit(solution)/shard_map/ppermute | solution.py:26
  8.0 25.3 %copy-start.5 = (bf16[1,128,4096]{2,1,0:T(8,128)(2,1)S(1)}, bf16[1,128,4096]{2,1,0:T(8,128)(2,1)}, u32[]{:S(2)}) copy-start(bf16[1,128,4096]{2,1,0:T(8,128)(2,1)} %param.8) | copy-start | bytes 3145732
  8.0 25.4 %copy-start.4 = (bf16[1,128,4096]{2,1,0:T(8,128)(2,1)S(1)}, bf16[1,128,4096]{2,1,0:T(8,128)(2,1)}, u32[]{:S(2)}) copy-start(bf16[1,128,4096]{2,1,0:T(8,128)(2,1)} %param.5) | copy-start | bytes 3145732
  29.8 1.0 copy-start.2
  30.7 24.4 %collective-permute-start.3 = (bf16[2,2,128,1024]{3,2,1,0:T(8,128)(2,1)S(1)}, bf16[2,2,128,1024]{3,2,1,0:T(8,128)(2,1)S(1)}, u32[]{:S(2)}, u32[]{:S(2)}) collective-permute-start(bf16[2,2,128,1024]{3,2,1,0:T(8,128)(2,1)S(1)} %get-tuple-element.25), channel_id=1, source_target_pairs={{0,6},{1,7},{8,14},{9,15},{16,22},{17,23},{24,30},{25,31},{2,0},{3... | collective-permute-start | bytes 3145736 | tf_op jit(solution)/shard_map/ppermute | solution.py:26
  31.0 46.8 %collective-permute-start.4 = (bf16[2,2,128,1024]{3,2,1,0:T(8,128)(2,1)S(1)}, bf16[2,2,128,1024]{3,2,1,0:T(8,128)(2,1)S(1)}, u32[]{:S(2)}, u32[]{:S(2)}) collective-permute-start(bf16[2,2,128,1024]{3,2,1,0:T(8,128)(2,1)S(1)} %get-tuple-element.24), channel_id=1, source_target_pairs={{0,4},{1,5},{2,6},{3,7},{8,12},{9,13},{10,14},{11,15},{16,20},{17,... | collective-permute-start | bytes 3145736 | tf_op jit(solution)/shard_map/ppermute | solution.py:26
  31.2 46.6 %collective-permute-start.5 = (bf16[2,2,128,1024]{3,2,1,0:T(8,128)(2,1)S(1)}, bf16[2,2,128,1024]{3,2,1,0:T(8,128)(2,1)S(1)}, u32[]{:S(2)}, u32[]{:S(2)}) collective-permute-start(bf16[2,2,128,1024]{3,2,1,0:T(8,128)(2,1)S(1)} %get-tuple-element.23), channel_id=1, source_target_pairs={{0,2},{1,3},{2,4},{3,5},{4,6},{5,7},{8,10},{9,11},{10,12},{11,13},... | collective-permute-start | bytes 3145736 | tf_op jit(solution)/shard_map/ppermute | solution.py:26
  33.5 5.2 %collective-permute-start.2 = (bf16[2,128,2048]{2,1,0:T(8,128)(2,1)S(1)}, bf16[2,128,2048]{2,1,0:T(8,128)(2,1)S(1)}, u32[]{:S(2)}, u32[]{:S(2)}) collective-permute-start(bf16[2,128,2048]{2,1,0:T(8,128)(2,1)S(1)} %pad_maximum_fusion.2), channel_id=1, source_target_pairs={{0,1},{1,0},{2,3},{3,2},{4,5},{5,4},{6,7},{7,6},{8,9},{9,8},{10,11... | collective-permute-start | bytes 3145736 | tf_op jit(solution)/shard_map/ppermute | solution.py:26
  55.2 22.7 %copy-start.6 = (bf16[2,2,128,1024]{3,2,1,0:T(8,128)(2,1)}, bf16[2,2,128,1024]{3,2,1,0:T(8,128)(2,1)S(1)}, u32[]{:S(2)}) copy-start(bf16[2,2,128,1024]{3,2,1,0:T(8,128)(2,1)S(1)} %collective-permute-done.3.refs_7_) | copy-start | bytes 3145732
  77.8 1.1 copy-start.7
  77.8 1.4 copy-start.8
  104.5 24.7 %collective-permute-start.7 = (bf16[2,2,128,1024]{3,2,1,0:T(8,128)(2,1)}, bf16[2,2,128,1024]{3,2,1,0:T(8,128)(2,1)S(1)}, u32[]{:S(2)}, u32[]{:S(2)}) collective-permute-start(bf16[2,2,128,1024]{3,2,1,0:T(8,128)(2,1)} %get-tuple-element.19), channel_id=1, source_target_pairs={{2,0},{3,1},{4,2},{5,3},{6,4},{7,5},{10,8},{11,9},{12,10},{13,11},... | collective-permute-start | bytes 3145736 | tf_op jit(solution)/shard_map/ppermute | solution.py:26
  104.6 46.9 %collective-permute-start.8 = (bf16[2,2,128,1024]{3,2,1,0:T(8,128)(2,1)}, bf16[2,2,128,1024]{3,2,1,0:T(8,128)(2,1)S(1)}, u32[]{:S(2)}, u32[]{:S(2)}) collective-permute-start(bf16[2,2,128,1024]{3,2,1,0:T(8,128)(2,1)} %get-tuple-element.20), channel_id=1, source_target_pairs={{4,0},{5,1},{6,2},{7,3},{12,8},{13,9},{14,10},{15,11},{20,16},{21,... | collective-permute-start | bytes 3145736 | tf_op jit(solution)/shard_map/ppermute | solution.py:26
  104.9 46.6 %collective-permute-start.9 = (bf16[2,2,128,1024]{3,2,1,0:T(8,128)(2,1)}, bf16[2,2,128,1024]{3,2,1,0:T(8,128)(2,1)S(1)}, u32[]{:S(2)}, u32[]{:S(2)}) collective-permute-start(bf16[2,2,128,1024]{3,2,1,0:T(8,128)(2,1)} %get-tuple-element.21), channel_id=1, source_target_pairs={{6,0},{7,1},{14,8},{15,9},{22,16},{23,17},{30,24},{31,25},{0,2},{1... | collective-permute-start | bytes 3145736 | tf_op jit(solution)/shard_map/ppermute | solution.py:26
  155.0 26.5 %collective-permute-start.10 = (bf16[2,2,128,1024]{3,2,1,0:T(8,128)(2,1)}, bf16[2,2,128,1024]{3,2,1,0:T(8,128)(2,1)}, u32[]{:S(2)}, u32[]{:S(2)}) collective-permute-start(bf16[2,2,128,1024]{3,2,1,0:T(8,128)(2,1)} %fusion.8), channel_id=1, source_target_pairs={{8,0},{9,1},{10,2},{11,3},{12,4},{13,5},{14,6},{15,7},{16,8},{17,9... | collective-permute-start | bytes 3145736 | tf_op jit(solution)/shard_map/ppermute | solution.py:26
  156.3 30.4 %collective-permute-start.6 = (bf16[128,2048]{1,0:T(8,128)(2,1)}, bf16[128,2048]{1,0:T(8,128)(2,1)S(1)}, u32[]{:S(2)}, u32[]{:S(2)}) collective-permute-start(bf16[128,2048]{1,0:T(8,128)(2,1)} %get-tuple-element.17), channel_id=1, source_target_pairs={{0,1},{1,0},{2,3},{3,2},{4,5},{5,4},{6,7},{7,6},{8,9},{9,8},{10,11... | collective-permute-start | bytes 1572872 | tf_op jit(solution)/shard_map/ppermute | solution.py:26
  181.5 5.2 %copy-start.3 = (bf16[128,2048]{1,0:T(8,128)(2,1)S(1)}, bf16[128,2048]{1,0:T(8,128)(2,1)}, u32[]{:S(2)}) copy-start(bf16[128,2048]{1,0:T(8,128)(2,1)} %get-tuple-element.16) | copy-start | bytes 1572868
  184.6 3.6 %collective-permute-start.11 = (bf16[2,128,1024]{2,1,0:T(8,128)(2,1)S(1)}, bf16[2,128,1024]{2,1,0:T(8,128)(2,1)S(1)}, u32[]{:S(2)}, u32[]{:S(2)}) collective-permute-start(bf16[2,128,1024]{2,1,0:T(8,128)(2,1)S(1)} %slice_bitcast_fusion), channel_id=1, source_target_pairs={{0,1},{1,0},{2,3},{3,2},{4,5},{5,4},{6,7},{7,6},{8,9},{9,8},{10,11... | collective-permute-start | bytes 1572872 | tf_op jit(solution)/shard_map/ppermute | solution.py:26

commit v14 on v11

--- a/solution.py
+++ b/solution.py
@@ -36,6 +36,7 @@
         self.chips = reach // 2
         group_chip = lambda i: (i % reach) // 2
         self.hop = [(i, i + reach) for i in range(count - reach)]
+        self.hop_cross = [(i, (i + reach) ^ 1) for i in range(count - reach)]
         self.up = []
         self.down = []
         for e in range(1, self.chips):
@@ -66,7 +67,7 @@
         upward = chip_in_group + e < chips
         own = own + jnp.where(upward, got, 0.0)
         prev = prev + jnp.where(upward, 0.0, got)
-    return own + moved(prev.astype(link), reverse(routes.hop)).astype(jnp.float32)
+    return own, prev
 
 
 def attention_kernel(chips, core_ref, bias_ref, qm_ref, qs_ref, dm_ref, ds_ref, *refs):
@@ -208,15 +209,19 @@
         core[None].astype(jnp.int32), bias, queries[0], qd_sib[0], grad_out, qd_sib[1], payloads
     )
     dq_mine, dq_sib, parts = outs[0], outs[1], outs[2:]
-    summed = scatter_window(parts, routes, chip_in_group)
+    summed, prev = scatter_window(parts, routes, chip_in_group)
+    link = jnp.bfloat16
     sent = jnp.concatenate(
-        [summed[0, 1].astype(jnp.bfloat16), summed[1, 1].astype(jnp.bfloat16), dq_sib], axis=-1
+        [summed[0, 1].astype(link), summed[1, 1].astype(link), dq_sib], axis=-1
     )
     got = moved(sent, routes.sibling)
-    grad_key = in_core_order(core, summed[0, 0].astype(jnp.bfloat16), got[:, :key_width])
-    grad_value = in_core_order(
-        core, summed[1, 0].astype(jnp.bfloat16), got[:, key_width : 2 * key_width]
-    )
+    back_same = moved(prev[:, 0].astype(link), reverse(routes.hop)).astype(jnp.float32)
+    back_cross = moved(prev[:, 1].astype(link), reverse(routes.hop_cross)).astype(jnp.float32)
+    mine = summed[:, 0] + back_same
+    theirs = jnp.stack([got[:, :key_width], got[:, key_width : 2 * key_width]])
+    theirs = theirs.astype(jnp.float32) + back_cross
+    grad_key = in_core_order(core, mine[0].astype(link), theirs[0].astype(link))
+    grad_value = in_core_order(core, mine[1].astype(link), theirs[1].astype(link))
     grad_query = in_core_order(core, dq_mine, got[:, 2 * key_width :])
     return (grad_query[None], grad_key[None], grad_value[None])
 

time: 191 us -> 195 us (1.021); the launches traced: 190 us -> 191 us
  local copies, waits for them, and re-layouts: 6.58 us -> 9.22 us
  waiting for transfers between devices: 133 us -> 131 us
    convert_element_type x1 -> x0, other arithmetic: 2.54 us -> none  [scatter_window(): prev.astype(link)]
    another operation x1 -> x4, other arithmetic: 1.05 us -> 3.17 us
    ppermute x11 -> x12, waiting for transfers between devices: 133 us -> 131 us  [moved(): return lax.ppermute(value, 'seq', pairs)]
    ppermute x11 -> x12, starting transfers between devices: 14.7 us -> 14.2 us  [moved(): return lax.ppermute(value, 'seq', pairs)]
  transfers between devices with their start and end apart: 11 -> 12, of which waited for: 8 -> 7; matrix products, arithmetic and copies ran while one was open for 2% -> 5% of each run, Pallas kernels for 0% -> 0%
where the time goes in v14:
time: 195 us; the launch traced here: 191 us
  waiting for transfers between devices  131 us (67%)
  Pallas kernels  25.3 us (13%)
  starting transfers between devices  14.2 us (7%)
  other arithmetic  10.4 us (5%)
  local copies, waits for them, and re-layouts  9.22 us (5%)
    ppermute x12, waiting for transfers between devices, moved(): return lax.ppermute(value, 'seq', pairs)  131 us
    pallas_call x1, Pallas kernels, attention_grads(): pl.pallas_call(lambda *refs: attention_kernel(chips, *refs), grid_spec=gr...  25.3 us
    ppermute x12, starting transfers between devices, moved(): return lax.ppermute(value, 'seq', pairs)  14.2 us
  transfers between devices with their start and end apart: 12, of which 7 were waited for; matrix products, arithmetic and copies ran while one was open for 5% of the time, Pallas kernels for 0%

profile of v14, /device:TPU:7, one launch (start us, length us, event | category | flops | bytes accessed | tf_op | source)
XLA Modules:
  0.0 191.5 jit_solution(843963207943825719)
XLA Ops:
  0.6 0.0 copy-start
  0.7 1.3 constant_dynamic-slice_fusion.2
  1.9 0.1 pad_maximum_fusion.4
  2.0 0.7 collective-permute-start
  2.7 0.1 maximum_bitcast_fusion
  2.8 1.5 collective-permute-done
  4.3 0.1 pad_maximum_fusion.1.refs_10_
  4.4 3.3 %collective-permute-start.1 = (bf16[2,2,128,1024]{3,2,1,0:T(8,128)(2,1)S(1)}, bf16[2,2,128,1024]{3,2,1,0:T(8,128)(2,1)S(1)}, u32[]{:S(2)}, u32[]{:S(2)}) collective-permute-start(bf16[2,2,128,1024]{3,2,1,0:T(8,128)(2,1)S(1)} %pad_maximum_fusion.1.refs_10_), channel_id=1, source_target_pairs={{0,8},{1,9},{2,10},{3,11},{4,12},{5,13},{6,14},{7,15},{8,16},{9,17... | collective-permute-start | bytes 3145736 | tf_op jit(solution)/shard_map/ppermute | solution.py:26
  8.0 21.8 %collective-permute-done.1.refs_6_ = bf16[2,2,128,1024]{3,2,1,0:T(8,128)(2,1)S(1)} collective-permute-done((bf16[2,2,128,1024]{3,2,1,0:T(8,128)(2,1)S(1)}, bf16[2,2,128,1024]{3,2,1,0:T(8,128)(2,1)S(1)}, u32[]{:S(2)}, u32[]{:S(2)}) %collective-permute-start.1) | collective-permute-done | bytes 1048608 | tf_op jit(solution)/shard_map/ppermute | solution.py:26
  29.8 0.1 broadcast_select_fusion
  29.9 0.0 copy-start.10
  29.9 0.3 collective-permute-start.4
  30.2 1.2 collective-permute-start.5
  31.4 0.0 copy-done.1
  31.4 0.4 copy_select_fusion.1
  31.8 0.3 collective-permute-start.3
  32.3 0.1 pad_maximum_fusion.2
  32.4 2.1 %collective-permute-start.2 = (bf16[2,128,2048]{2,1,0:T(8,128)(2,1)S(1)}, bf16[2,128,2048]{2,1,0:T(8,128)(2,1)S(1)}, u32[]{:S(2)}, u32[]{:S(2)}) collective-permute-start(bf16[2,128,2048]{2,1,0:T(8,128)(2,1)S(1)} %pad_maximum_fusion.2), channel_id=1, source_target_pairs={{0,1},{1,0},{2,3},{3,2},{4,5},{5,4},{6,7},{7,6},{8,9},{9,8},{10,11... | collective-permute-start | bytes 3145736 | tf_op jit(solution)/shard_map/ppermute | solution.py:26
  34.5 0.1 broadcast_bitcast_fusion
  34.6 0.1 constant_dynamic-update-slice_fusion.19
  34.6 0.1 fusion.17
  34.7 0.1 constant_dynamic-update-slice_fusion.15
  34.8 0.1 constant_dynamic-update-slice_fusion.13
  34.9 0.1 constant_dynamic-update-slice_fusion.11
  35.0 0.1 constant_dynamic-update-slice_fusion.9
  35.0 0.1 constant_dynamic-update-slice_fusion.7
  35.1 0.1 constant_dynamic-update-slice_fusion.5
  35.2 0.1 constant_dynamic-update-slice_fusion.3
  35.3 0.1 constant_dynamic-update-slice_fusion.1
  35.4 0.5 fusion.9
  35.8 1.7 pad_maximum_fusion.refs_1_
  37.5 39.3 %collective-permute-done.3 = bf16[2,2,128,1024]{3,2,0,1:T(8,128)(2,1)S(1)} collective-permute-done((bf16[2,2,128,1024]{3,2,0,1:T(8,128)(2,1)S(1)}, bf16[2,2,128,1024]{3,2,0,1:T(8,128)(2,1)S(1)}, u32[]{:S(2)}, u32[]{:S(2)}) %collective-permute-start.3) | collective-permute-done | bytes 1048608 | tf_op jit(solution)/shard_map/ppermute | solution.py:26
  76.8 1.1 copy.11.refs_7_
  77.9 0.0 collective-permute-done.2
  77.9 1.1 slice_bitcast_fusion.4
  79.0 0.0 collective-permute-done.4.refs_8_
  79.0 0.0 collective-permute-done.5.refs_9_
  79.0 1.0 copy-done.11
  80.0 1.0 copy-done.12
  81.0 25.3 %shard_map.76 = (bf16[128,2048]{1,0:T(8,128)(2,1)}, bf16[128,2048]{1,0:T(8,128)(2,1)}, f32[2,2,128,1024]{3,2,1,0:T(8,128)}, bf16[2,2,128,1024]{3,2,1,0:T(8,128)(...) custom-call(s32[1]{0:T(128)} %bitcast.refs_0_, ...), custom_call_target="tpu_custom_call" | custom-call | flops 6710886400 | bytes 21495808 | tf_op jit(solution)/shard_map/pallas_call | solution.py:134
  106.3 1.4 copy.12
  107.7 0.4 collective-permute-start.6
  108.1 0.1 copy.14
  108.2 0.3 collective-permute-start.7
  108.5 0.1 copy.16
  108.6 2.1 %collective-permute-start.8 = (bf16[2,2,128,1024]{3,2,0,1:T(8,128)(2,1)S(1)}, bf16[2,2,128,1024]{3,2,0,1:T(8,128)(2,1)S(1)}, u32[]{:S(2)}, u32[]{:S(2)}) collective-permute-start(bf16[2,2,128,1024]{3,2,0,1:T(8,128)(2,1)S(1)} %copy.16), channel_id=1, source_target_pairs={{6,0},{7,1},{14,8},{15,9},{22,16},{23,17},{30,24},{31,25},{0,2},{1... | collective-permute-start | bytes 3145736 | tf_op jit(solution)/shard_map/ppermute | solution.py:26
  110.6 20.4 %collective-permute-done.6 = bf16[2,2,128,1024]{3,2,0,1:T(8,128)(2,1)S(1)} collective-permute-done((bf16[2,2,128,1024]{3,2,0,1:T(8,128)(2,1)S(1)}, bf16[2,2,128,1024]{3,2,0,1:T(8,128)(2,1)S(1)}, u32[]{:S(2)}, u32[]{:S(2)}) %collective-permute-start.6) | collective-permute-done | bytes 1048608 | tf_op jit(solution)/shard_map/ppermute | solution.py:26
  131.0 24.3 %collective-permute-done.7 = bf16[2,2,128,1024]{3,2,0,1:T(8,128)(2,1)S(1)} collective-permute-done((bf16[2,2,128,1024]{3,2,0,1:T(8,128)(2,1)S(1)}, bf16[2,2,128,1024]{3,2,0,1:T(8,128)(2,1)S(1)}, u32[]{:S(2)}, u32[]{:S(2)}) %collective-permute-start.7) | collective-permute-done | bytes 1048608 | tf_op jit(solution)/shard_map/ppermute | solution.py:26
  155.3 0.0 collective-permute-done.8
  155.4 1.2 fusion.13
  156.6 1.1 pad_maximum_fusion.3
  157.7 1.0 collective-permute-start.9
  158.6 0.6 fusion.4
  159.2 1.0 slice_bitcast_fusion.2
  160.3 1.3 collective-permute-start.10
  161.6 1.3 collective-permute-start.11
  162.9 14.1 %collective-permute-done.10 = bf16[2,128,1024]{2,1,0:T(8,128)(2,1)} collective-permute-done((bf16[2,128,1024]{2,1,0:T(8,128)(2,1)}, bf16[2,128,1024]{2,1,0:T(8,128)(2,1)}, u32[]{:S(2)}, u32[]{:S(2)}) %collective-permute-start.10) | collective-permute-done | bytes 524320 | tf_op jit(solution)/shard_map/ppermute | solution.py:26
  177.0 1.2 fusion.6
  178.2 0.0 collective-permute-done.9
  178.3 9.8 %collective-permute-done.11 = bf16[2,128,1024]{2,1,0:T(8,128)(2,1)S(1)} collective-permute-done((bf16[2,128,1024]{2,1,0:T(8,128)(2,1)}, bf16[2,128,1024]{2,1,0:T(8,128)(2,1)S(1)}, u32[]{:S(2)}, u32[]{:S(2)}) %collective-permute-start.11) | collective-permute-done | bytes 524320 | tf_op jit(solution)/shard_map/ppermute | solution.py:26
  188.1 0.2 add_convert_fusion
  188.4 0.9 maximum_select_fusion.2
  189.3 0.9 maximum_select_fusion.1
  190.3 1.2 maximum_select_fusion
  (41 shorter events, 0.4 us)
Async XLA Ops:
  0.6 31.5 %copy-start = (s32[1,32]{1,0:T(1,128)S(1)}, s32[1,32]{1,0:T(1,128)}, u32[]{:S(2)}) copy-start(s32[1,32]{1,0:T(1,128)} %param.9) | copy-start | bytes 388
  2.0 2.3 %collective-permute-start = (bf16[2,128,1024]{2,1,0:T(8,128)(2,1)S(1)}, bf16[2,128,1024]{2,1,0:T(8,128)(2,1)S(1)}, u32[]{:S(2)}, u32[]{:S(2)}) collective-permute-start(bf16[2,128,1024]{2,1,0:T(8,128)(2,1)S(1)} %pad_maximum_fusion.4), channel_id=1, source_target_pairs={{0,1},{1,0},{2,3},{3,2},{4,5},{5,4},{6,7},{7,6},{8,9},{9,8},{10,11... | collective-permute-start | bytes 1572872 | tf_op jit(solution)/shard_map/ppermute | solution.py:26
  4.4 25.5 %copy-start.4 = (bf16[2,2,128,1024]{3,2,1,0:T(8,128)(2,1)}, bf16[2,2,128,1024]{3,2,1,0:T(8,128)(2,1)S(1)}, u32[]{:S(2)}) copy-start(bf16[2,2,128,1024]{3,2,1,0:T(8,128)(2,1)S(1)} %pad_maximum_fusion.1.refs_10_) | copy-start | bytes 3145732
  4.4 25.4 %collective-permute-start.1 = (bf16[2,2,128,1024]{3,2,1,0:T(8,128)(2,1)S(1)}, bf16[2,2,128,1024]{3,2,1,0:T(8,128)(2,1)S(1)}, u32[]{:S(2)}, u32[]{:S(2)}) collective-permute-start(bf16[2,2,128,1024]{3,2,1,0:T(8,128)(2,1)S(1)} %pad_maximum_fusion.1.refs_10_), channel_id=1, source_target_pairs={{0,8},{1,9},{2,10},{3,11},{4,12},{5,13},{6,14},{7,15},{8,16},{9,17... | collective-permute-start | bytes 3145736 | tf_op jit(solution)/shard_map/ppermute | solution.py:26
  29.8 1.7 copy-start.1
  29.9 2.2 %copy-start.10 = (bf16[1,128,4096]{2,1,0:T(8,128)(2,1)S(1)}, bf16[1,128,4096]{2,1,0:T(8,128)(2,1)}, u32[]{:S(2)}) copy-start(bf16[1,128,4096]{2,1,0:T(8,128)(2,1)} %param.8) | copy-start | bytes 3145732
  29.9 49.1 %collective-permute-start.4 = (bf16[2,2,128,1024]{3,2,1,0:T(8,128)(2,1)S(1)}, bf16[2,2,128,1024]{3,2,1,0:T(8,128)(2,1)S(1)}, u32[]{:S(2)}, u32[]{:S(2)}) collective-permute-start(bf16[2,2,128,1024]{3,2,1,0:T(8,128)(2,1)S(1)} %get-tuple-element.26), channel_id=1, source_target_pairs={{0,4},{1,5},{2,6},{3,7},{8,12},{9,13},{10,14},{11,15},{16,20},{17,... | collective-permute-start | bytes 3145736 | tf_op jit(solution)/shard_map/ppermute | solution.py:26
  30.2 2.0 %copy-start.9 = (bf16[1,128,4096]{2,1,0:T(8,128)(2,1)S(1)}, bf16[1,128,4096]{2,1,0:T(8,128)(2,1)}, u32[]{:S(2)}) copy-start(bf16[1,128,4096]{2,1,0:T(8,128)(2,1)} %param.5) | copy-start | bytes 3145732
  30.2 48.8 %collective-permute-start.5 = (bf16[2,2,128,1024]{3,2,1,0:T(8,128)(2,1)S(1)}, bf16[2,2,128,1024]{3,2,1,0:T(8,128)(2,1)S(1)}, u32[]{:S(2)}, u32[]{:S(2)}) collective-permute-start(bf16[2,2,128,1024]{3,2,1,0:T(8,128)(2,1)S(1)} %get-tuple-element.25), channel_id=1, source_target_pairs={{0,2},{1,3},{2,4},{3,5},{4,6},{5,7},{8,10},{9,11},{10,12},{11,13},... | collective-permute-start | bytes 3145736 | tf_op jit(solution)/shard_map/ppermute | solution.py:26
  31.8 45.0 %collective-permute-start.3 = (bf16[2,2,128,1024]{3,2,0,1:T(8,128)(2,1)S(1)}, bf16[2,2,128,1024]{3,2,0,1:T(8,128)(2,1)S(1)}, u32[]{:S(2)}, u32[]{:S(2)}) collective-permute-start(bf16[2,2,128,1024]{3,2,0,1:T(8,128)(2,1)S(1)} %copy_select_fusion.1), channel_id=1, source_target_pairs={{0,6},{1,7},{8,14},{9,15},{16,22},{17,23},{24,30},{25,31},{2,0},{3... | collective-permute-start | bytes 3145736 | tf_op jit(solution)/shard_map/ppermute | solution.py:26
  32.4 45.5 %collective-permute-start.2 = (bf16[2,128,2048]{2,1,0:T(8,128)(2,1)S(1)}, bf16[2,128,2048]{2,1,0:T(8,128)(2,1)S(1)}, u32[]{:S(2)}, u32[]{:S(2)}) collective-permute-start(bf16[2,128,2048]{2,1,0:T(8,128)(2,1)S(1)} %pad_maximum_fusion.2), channel_id=1, source_target_pairs={{0,1},{1,0},{2,3},{3,2},{4,5},{5,4},{6,7},{7,6},{8,9},{9,8},{10,11... | collective-permute-start | bytes 3145736 | tf_op jit(solution)/shard_map/ppermute | solution.py:26
  79.0 1.0 copy-start.11
  80.0 1.0 copy-start.12
  106.3 1.9 copy-start.6
  106.3 2.2 %copy-start.5 = (bf16[2,2,128,1024]{3,2,1,0:T(8,128)(2,1)S(1)}, bf16[2,2,128,1024]{3,2,1,0:T(8,128)(2,1)}, u32[]{:S(2)}) copy-start(bf16[2,2,128,1024]{3,2,1,0:T(8,128)(2,1)} %get-tuple-element.20) | copy-start | bytes 3145732
  107.7 23.3 %collective-permute-start.6 = (bf16[2,2,128,1024]{3,2,0,1:T(8,128)(2,1)S(1)}, bf16[2,2,128,1024]{3,2,0,1:T(8,128)(2,1)S(1)}, u32[]{:S(2)}, u32[]{:S(2)}) collective-permute-start(bf16[2,2,128,1024]{3,2,0,1:T(8,128)(2,1)S(1)} %copy.12), channel_id=1, source_target_pairs={{2,0},{3,1},{4,2},{5,3},{6,4},{7,5},{10,8},{11,9},{12,10},{13,11},... | collective-permute-start | bytes 3145736 | tf_op jit(solution)/shard_map/ppermute | solution.py:26
  108.1 47.2 %copy-start.2 = (f32[2,2,128,1024]{3,2,1,0:T(8,128)S(1)}, f32[2,2,128,1024]{3,2,1,0:T(8,128)}, u32[]{:S(2)}) copy-start(f32[2,2,128,1024]{3,2,1,0:T(8,128)} %get-tuple-element.22) | copy-start | bytes 6291460
  108.1 47.2 %copy-start.3 = (f32[2,2,128,1024]{3,2,1,0:T(8,128)S(1)}, f32[2,2,128,1024]{3,2,1,0:T(8,128)}, u32[]{:S(2)}) copy-start(f32[2,2,128,1024]{3,2,1,0:T(8,128)} %get-tuple-element.17) | copy-start | bytes 6291460
  108.2 47.1 %collective-permute-start.7 = (bf16[2,2,128,1024]{3,2,0,1:T(8,128)(2,1)S(1)}, bf16[2,2,128,1024]{3,2,0,1:T(8,128)(2,1)S(1)}, u32[]{:S(2)}, u32[]{:S(2)}) collective-permute-start(bf16[2,2,128,1024]{3,2,0,1:T(8,128)(2,1)S(1)} %copy.14), channel_id=1, source_target_pairs={{4,0},{5,1},{6,2},{7,3},{12,8},{13,9},{14,10},{15,11},{20,16},{21,... | collective-permute-start | bytes 3145736 | tf_op jit(solution)/shard_map/ppermute | solution.py:26
  108.6 46.8 %collective-permute-start.8 = (bf16[2,2,128,1024]{3,2,0,1:T(8,128)(2,1)S(1)}, bf16[2,2,128,1024]{3,2,0,1:T(8,128)(2,1)S(1)}, u32[]{:S(2)}, u32[]{:S(2)}) collective-permute-start(bf16[2,2,128,1024]{3,2,0,1:T(8,128)(2,1)S(1)} %copy.16), channel_id=1, source_target_pairs={{6,0},{7,1},{14,8},{15,9},{22,16},{23,17},{30,24},{31,25},{0,2},{1... | collective-permute-start | bytes 3145736 | tf_op jit(solution)/shard_map/ppermute | solution.py:26
  155.4 1.2 copy-start.8
  157.7 20.6 %collective-permute-start.9 = (bf16[128,4096]{1,0:T(8,128)(2,1)}, bf16[128,4096]{1,0:T(8,128)(2,1)S(1)}, u32[]{:S(2)}, u32[]{:S(2)}) collective-permute-start(bf16[128,4096]{1,0:T(8,128)(2,1)} %pad_maximum_fusion.3), channel_id=1, source_target_pairs={{0,1},{1,0},{2,3},{3,2},{4,5},{5,4},{6,7},{7,6},{8,9},{9,8},{10,11... | collective-permute-start | bytes 3145736 | tf_op jit(solution)/shard_map/ppermute | solution.py:26
  160.3 16.7 %collective-permute-start.10 = (bf16[2,128,1024]{2,1,0:T(8,128)(2,1)}, bf16[2,128,1024]{2,1,0:T(8,128)(2,1)}, u32[]{:S(2)}, u32[]{:S(2)}) collective-permute-start(bf16[2,128,1024]{2,1,0:T(8,128)(2,1)} %get-tuple-element.27), channel_id=1, source_target_pairs={{8,0},{9,1},{10,2},{11,3},{12,4},{13,5},{14,6},{15,7},{16,8},{17,9... | collective-permute-start | bytes 1572872 | tf_op jit(solution)/shard_map/ppermute | solution.py:26
  161.6 26.5 %collective-permute-start.11 = (bf16[2,128,1024]{2,1,0:T(8,128)(2,1)}, bf16[2,128,1024]{2,1,0:T(8,128)(2,1)S(1)}, u32[]{:S(2)}, u32[]{:S(2)}) collective-permute-start(bf16[2,128,1024]{2,1,0:T(8,128)(2,1)} %get-tuple-element.28), channel_id=1, source_target_pairs={{9,0},{8,1},{11,2},{10,3},{13,4},{12,5},{15,6},{14,7},{17,8},{16,9... | collective-permute-start | bytes 1572872 | tf_op jit(solution)/shard_map/ppermute | solution.py:26
  188.3 1.9 %copy-start.7 = (bf16[128,2048]{1,0:T(8,128)(2,1)S(1)}, bf16[128,2048]{1,0:T(8,128)(2,1)}, u32[]{:S(2)}) copy-start(bf16[128,2048]{1,0:T(8,128)(2,1)} %get-tuple-element.16) | copy-start | bytes 1572868

commit v15 on v11

--- a/solution.py
+++ b/solution.py
@@ -88,7 +88,9 @@
     unscaled = jnp.exp(scores - largest)
     attn = unscaled * (1.0 / jnp.sum(unscaled, axis=1, keepdims=True))
     dattn = lax.dot_general(dos, v, contract_last, preferred_element_type=jnp.float32)
-    row_delta = jnp.sum(attn * dattn, axis=1, keepdims=True)
+    attn_low = attn.astype(jnp.bfloat16)
+    mixed = jnp.dot(attn_low, v, preferred_element_type=jnp.float32)
+    row_delta = jnp.sum(dos.astype(jnp.float32) * mixed, axis=1, keepdims=True)
     dscores = (attn * (dattn - row_delta)).astype(jnp.bfloat16)
     grad_q = jnp.dot(dscores, k, preferred_element_type=jnp.float32) * SCORE_SCALE
     rows = lambda j: slice(j * tokens, (j + 1) * tokens)
@@ -100,9 +102,7 @@
         lax.dot_general(dscores, qs, contract_first, preferred_element_type=jnp.float32)
         * SCORE_SCALE
     )
-    grad_v = lax.dot_general(
-        attn.astype(jnp.bfloat16), dos, contract_first, preferred_element_type=jnp.float32
-    )
+    grad_v = lax.dot_general(attn_low, dos, contract_first, preferred_element_type=jnp.float32)
     for j, out in enumerate(part_refs):
         for s in range(2):
             out[0, s] = grad_k[rows(2 * j + s)].astype(out.dtype)

time: 191 us -> 195 us (1.021)
  Pallas kernels: 25.3 us -> 30 us
    pallas_call x1, Pallas kernels: 25.3 us -> 30 us  [attention_grads(): pl.pallas_call(lambda *refs: attention_kernel(chips, *refs), grid_spec=gr...]
where the time goes in v15:
time: 195 us
  waiting for transfers between devices  133 us (68%)
  Pallas kernels  30 us (15%)
  starting transfers between devices  14.7 us (8%)
  other arithmetic  9.49 us (5%)
  local copies, waits for them, and re-layouts  6.58 us (3%)
    ppermute x11, waiting for transfers between devices, moved(): return lax.ppermute(value, 'seq', pairs)  133 us
    pallas_call x1, Pallas kernels, attention_grads(): pl.pallas_call(lambda *refs: attention_kernel(chips, *refs), grid_spec=gr...  30 us
    ppermute x11, starting transfers between devices, moved(): return lax.ppermute(value, 'seq', pairs)  14.7 us
  transfers between devices with their start and end apart: 11, of which 8 were waited for; matrix products, arithmetic and copies ran while one was open for 2% of the time, Pallas kernels for 0%

profile of v15, /device:TPU:7, one launch (start us, length us, event | category | flops | bytes accessed | tf_op | source)
XLA Modules:
  0.0 194.7 jit_solution(425389247463309839)
XLA Ops:
  0.6 0.0 copy-start
  0.7 1.3 constant_dynamic-slice_fusion.2
  1.9 0.1 pad_maximum_fusion.4
  2.0 0.7 collective-permute-start
  2.7 0.1 maximum_bitcast_fusion
  2.8 1.5 collective-permute-done
  4.3 0.1 pad_maximum_fusion.1.refs_10_
  4.4 0.0 copy-start.2
  4.4 3.3 %collective-permute-start.1 = (bf16[2,2,128,1024]{3,2,1,0:T(8,128)(2,1)S(1)}, bf16[2,2,128,1024]{3,2,1,0:T(8,128)(2,1)S(1)}, u32[]{:S(2)}, u32[]{:S(2)}) collective-permute-start(bf16[2,2,128,1024]{3,2,1,0:T(8,128)(2,1)S(1)} %pad_maximum_fusion.1.refs_10_), channel_id=1, source_target_pairs={{0,8},{1,9},{2,10},{3,11},{4,12},{5,13},{6,14},{7,15},{8,16},{9,17... | collective-permute-start | bytes 3145736 | tf_op jit(solution)/shard_map/ppermute | solution.py:26
  8.0 0.0 copy-start.7
  8.0 0.0 copy-start.6
  8.0 21.7 %collective-permute-done.1.refs_6_ = bf16[2,2,128,1024]{3,2,1,0:T(8,128)(2,1)S(1)} collective-permute-done((bf16[2,2,128,1024]{3,2,1,0:T(8,128)(2,1)S(1)}, bf16[2,2,128,1024]{3,2,1,0:T(8,128)(2,1)S(1)}, u32[]{:S(2)}, u32[]{:S(2)}) %collective-permute-start.1) | collective-permute-done | bytes 1048608 | tf_op jit(solution)/shard_map/ppermute | solution.py:26
  29.8 0.2 broadcast_select_fusion
  30.0 0.0 copy-done.2
  30.0 0.7 copy-done.3
  30.7 0.3 collective-permute-start.3
  31.0 0.2 collective-permute-start.4
  31.2 2.1 %collective-permute-start.5 = (bf16[2,2,128,1024]{3,2,1,0:T(8,128)(2,1)S(1)}, bf16[2,2,128,1024]{3,2,1,0:T(8,128)(2,1)S(1)}, u32[]{:S(2)}, u32[]{:S(2)}) collective-permute-start(bf16[2,2,128,1024]{3,2,1,0:T(8,128)(2,1)S(1)} %get-tuple-element.23), channel_id=1, source_target_pairs={{0,2},{1,3},{2,4},{3,5},{4,6},{5,7},{8,10},{9,11},{10,12},{11,13},... | collective-permute-start | bytes 3145736 | tf_op jit(solution)/shard_map/ppermute | solution.py:26
  33.3 0.0 copy-done
  33.3 0.0 copy-done.7
  33.4 0.0 copy-done.6
  33.4 0.1 pad_maximum_fusion.2
  33.5 2.1 %collective-permute-start.2 = (bf16[2,128,2048]{2,1,0:T(8,128)(2,1)S(1)}, bf16[2,128,2048]{2,1,0:T(8,128)(2,1)S(1)}, u32[]{:S(2)}, u32[]{:S(2)}) collective-permute-start(bf16[2,128,2048]{2,1,0:T(8,128)(2,1)S(1)} %pad_maximum_fusion.2), channel_id=1, source_target_pairs={{0,1},{1,0},{2,3},{3,2},{4,5},{5,4},{6,7},{7,6},{8,9},{9,8},{10,11... | collective-permute-start | bytes 3145736 | tf_op jit(solution)/shard_map/ppermute | solution.py:26
  35.6 0.1 broadcast_bitcast_fusion
  35.7 0.1 constant_dynamic-update-slice_fusion.19
  35.8 0.1 fusion.15
  35.9 0.1 constant_dynamic-update-slice_fusion.15
  35.9 0.1 constant_dynamic-update-slice_fusion.13
  36.0 0.1 constant_dynamic-update-slice_fusion.11
  36.1 0.1 constant_dynamic-update-slice_fusion.9
  36.2 0.1 constant_dynamic-update-slice_fusion.7
  36.3 0.1 constant_dynamic-update-slice_fusion.5
  36.4 0.1 constant_dynamic-update-slice_fusion.3
  36.4 0.1 constant_dynamic-update-slice_fusion.1
  36.5 0.5 fusion.11
  37.0 1.7 pad_maximum_fusion.refs_1_
  38.7 0.0 collective-permute-done.2
  38.7 1.1 slice_bitcast_fusion.1
  39.8 15.4 %collective-permute-done.3.refs_7_ = bf16[2,2,128,1024]{3,2,1,0:T(8,128)(2,1)S(1)} collective-permute-done((bf16[2,2,128,1024]{3,2,1,0:T(8,128)(2,1)S(1)}, bf16[2,2,128,1024]{3,2,1,0:T(8,128)(2,1)S(1)}, u32[]{:S(2)}, u32[]{:S(2)}) %collective-permute-start.3) | collective-permute-done | bytes 1048608 | tf_op jit(solution)/shard_map/ppermute | solution.py:26
  55.2 22.6 %collective-permute-done.4.refs_8_ = bf16[2,2,128,1024]{3,2,1,0:T(8,128)(2,1)S(1)} collective-permute-done((bf16[2,2,128,1024]{3,2,1,0:T(8,128)(2,1)S(1)}, bf16[2,2,128,1024]{3,2,1,0:T(8,128)(2,1)S(1)}, u32[]{:S(2)}, u32[]{:S(2)}) %collective-permute-start.4) | collective-permute-done | bytes 1048608 | tf_op jit(solution)/shard_map/ppermute | solution.py:26
  77.8 0.0 collective-permute-done.5.refs_9_
  77.8 1.0 copy-done.10
  78.8 0.0 copy-done.8
  78.8 0.4 copy-done.9
  79.2 30.0 %shard_map.76 = (bf16[128,2048]{1,0:T(8,128)(2,1)}, bf16[128,2048]{1,0:T(8,128)(2,1)}, f32[2,2,128,1024]{3,2,1,0:T(8,128)}, bf16[2,2,128,1024]{3,2,1,0:T(8,128)(...) custom-call(s32[1]{0:T(128)} %bitcast.refs_0_, ...), custom_call_target="tpu_custom_call" | custom-call | flops 6710886400 | bytes 21495808 | tf_op jit(solution)/shard_map/pallas_call | solution.py:133
  109.3 0.1 collective-permute-start.6
  109.3 0.3 collective-permute-start.7
  109.6 2.3 %collective-permute-start.8 = (bf16[2,2,128,1024]{3,2,1,0:T(8,128)(2,1)}, bf16[2,2,128,1024]{3,2,1,0:T(8,128)(2,1)S(1)}, u32[]{:S(2)}, u32[]{:S(2)}) collective-permute-start(bf16[2,2,128,1024]{3,2,1,0:T(8,128)(2,1)} %get-tuple-element.20), channel_id=1, source_target_pairs={{6,0},{7,1},{14,8},{15,9},{22,16},{23,17},{30,24},{31,25},{0,2},{1... | collective-permute-start | bytes 3145736 | tf_op jit(solution)/shard_map/ppermute | solution.py:26
  111.9 22.1 %collective-permute-done.6 = bf16[2,2,128,1024]{3,2,1,0:T(8,128)(2,1)S(1)} collective-permute-done((bf16[2,2,128,1024]{3,2,1,0:T(8,128)(2,1)}, bf16[2,2,128,1024]{3,2,1,0:T(8,128)(2,1)S(1)}, u32[]{:S(2)}, u32[]{:S(2)}) %collective-permute-start.6) | collective-permute-done | bytes 1048608 | tf_op jit(solution)/shard_map/ppermute | solution.py:26
  134.0 22.3 %collective-permute-done.7 = bf16[2,2,128,1024]{3,2,1,0:T(8,128)(2,1)S(1)} collective-permute-done((bf16[2,2,128,1024]{3,2,1,0:T(8,128)(2,1)}, bf16[2,2,128,1024]{3,2,1,0:T(8,128)(2,1)S(1)}, u32[]{:S(2)}, u32[]{:S(2)}) %collective-permute-start.7) | collective-permute-done | bytes 1048608 | tf_op jit(solution)/shard_map/ppermute | solution.py:26
  156.3 0.0 collective-permute-done.8
  156.3 2.5 %fusion.8 = bf16[2,2,128,1024]{3,2,1,0:T(8,128)(2,1)S(1)} fusion(f32[2,2,128,1024]{3,2,1,0:T(8,128)} %get-tuple-element.21, bf16[2,2,128,1024]{3,2,1,0:T(8,128)(2,1)S(1)} %collective-permute-done.6, bf16[2,2,128,1024]{3,2,1,0:T(8,128)(2,1)S(1)} %collective-permute-done.7, bf16[2,2,128,1024]{3,2,1,0:T(8,128)(2,1)S(1)} %collective-permute-done.8, pred[]{:T(512)S(6)} %lt.97, ...), kind=kLoop, calls=%fused_computation.15 | loop fusion | flops 5242880 | bytes 6291459 | tf_op jit(solution)/shard_map/convert_element_type | solution.py:69
  158.8 1.3 collective-permute-start.9
  160.1 24.9 %collective-permute-done.9 = bf16[2,2,128,1024]{3,2,1,0:T(8,128)(2,1)S(1)} collective-permute-done((bf16[2,2,128,1024]{3,2,1,0:T(8,128)(2,1)S(1)}, bf16[2,2,128,1024]{3,2,1,0:T(8,128)(2,1)S(1)}, u32[]{:S(2)}, u32[]{:S(2)}) %collective-permute-start.9) | collective-permute-done | bytes 1048608 | tf_op jit(solution)/shard_map/ppermute | solution.py:26
  185.0 0.0 copy-done.1
  185.0 1.1 fusion.4
  186.1 0.1 slice_bitcast_fusion.4
  186.2 0.9 copy-done.5
  187.1 0.1 pad_maximum_fusion.3
  187.2 2.1 %collective-permute-start.10 = (bf16[128,4096]{1,0:T(8,128)(2,1)S(1)}, bf16[128,4096]{1,0:T(8,128)(2,1)S(1)}, u32[]{:S(2)}, u32[]{:S(2)}) collective-permute-start(bf16[128,4096]{1,0:T(8,128)(2,1)S(1)} %pad_maximum_fusion.3), channel_id=1, source_target_pairs={{0,1},{1,0},{2,3},{3,2},{4,5},{5,4},{6,7},{7,6},{8,9},{9,8},{10,11... | collective-permute-start | bytes 3145736 | tf_op jit(solution)/shard_map/ppermute | solution.py:26
  189.3 2.3 %collective-permute-done.10 = bf16[128,4096]{1,0:T(8,128)(2,1)S(1)} collective-permute-done((bf16[128,4096]{1,0:T(8,128)(2,1)S(1)}, bf16[128,4096]{1,0:T(8,128)(2,1)S(1)}, u32[]{:S(2)}, u32[]{:S(2)}) %collective-permute-start.10) | collective-permute-done | bytes 1048608 | tf_op jit(solution)/shard_map/ppermute | solution.py:26
  191.6 0.9 maximum_select_fusion.2
  192.5 0.9 maximum_select_fusion.1
  193.5 1.2 maximum_select_fusion
  (25 shorter events, 0.2 us)
Async XLA Ops:
  0.6 32.7 %copy-start = (s32[1,32]{1,0:T(1,128)S(1)}, s32[1,32]{1,0:T(1,128)}, u32[]{:S(2)}) copy-start(s32[1,32]{1,0:T(1,128)} %param.9) | copy-start | bytes 388
  2.0 2.3 %collective-permute-start = (bf16[2,128,1024]{2,1,0:T(8,128)(2,1)S(1)}, bf16[2,128,1024]{2,1,0:T(8,128)(2,1)S(1)}, u32[]{:S(2)}, u32[]{:S(2)}) collective-permute-start(bf16[2,128,1024]{2,1,0:T(8,128)(2,1)S(1)} %pad_maximum_fusion.4), channel_id=1, source_target_pairs={{0,1},{1,0},{2,3},{3,2},{4,5},{5,4},{6,7},{7,6},{8,9},{9,8},{10,11... | collective-permute-start | bytes 1572872 | tf_op jit(solution)/shard_map/ppermute | solution.py:26
  4.4 25.6 %copy-start.2 = (bf16[2,2,128,1024]{3,2,1,0:T(8,128)(2,1)}, bf16[2,2,128,1024]{3,2,1,0:T(8,128)(2,1)S(1)}, u32[]{:S(2)}) copy-start(bf16[2,2,128,1024]{3,2,1,0:T(8,128)(2,1)S(1)} %pad_maximum_fusion.1.refs_10_) | copy-start | bytes 3145732
  4.4 25.4 %collective-permute-start.1 = (bf16[2,2,128,1024]{3,2,1,0:T(8,128)(2,1)S(1)}, bf16[2,2,128,1024]{3,2,1,0:T(8,128)(2,1)S(1)}, u32[]{:S(2)}, u32[]{:S(2)}) collective-permute-start(bf16[2,2,128,1024]{3,2,1,0:T(8,128)(2,1)S(1)} %pad_maximum_fusion.1.refs_10_), channel_id=1, source_target_pairs={{0,8},{1,9},{2,10},{3,11},{4,12},{5,13},{6,14},{7,15},{8,16},{9,17... | collective-permute-start | bytes 3145736 | tf_op jit(solution)/shard_map/ppermute | solution.py:26
  8.0 25.3 %copy-start.7 = (bf16[1,128,4096]{2,1,0:T(8,128)(2,1)S(1)}, bf16[1,128,4096]{2,1,0:T(8,128)(2,1)}, u32[]{:S(2)}) copy-start(bf16[1,128,4096]{2,1,0:T(8,128)(2,1)} %param.8) | copy-start | bytes 3145732
  8.0 25.4 %copy-start.6 = (bf16[1,128,4096]{2,1,0:T(8,128)(2,1)S(1)}, bf16[1,128,4096]{2,1,0:T(8,128)(2,1)}, u32[]{:S(2)}) copy-start(bf16[1,128,4096]{2,1,0:T(8,128)(2,1)} %param.5) | copy-start | bytes 3145732
  29.8 1.0 copy-start.3
  30.7 24.4 %collective-permute-start.3 = (bf16[2,2,128,1024]{3,2,1,0:T(8,128)(2,1)S(1)}, bf16[2,2,128,1024]{3,2,1,0:T(8,128)(2,1)S(1)}, u32[]{:S(2)}, u32[]{:S(2)}) collective-permute-start(bf16[2,2,128,1024]{3,2,1,0:T(8,128)(2,1)S(1)} %get-tuple-element.25), channel_id=1, source_target_pairs={{0,6},{1,7},{8,14},{9,15},{16,22},{17,23},{24,30},{25,31},{2,0},{3... | collective-permute-start | bytes 3145736 | tf_op jit(solution)/shard_map/ppermute | solution.py:26
  31.0 46.8 %collective-permute-start.4 = (bf16[2,2,128,1024]{3,2,1,0:T(8,128)(2,1)S(1)}, bf16[2,2,128,1024]{3,2,1,0:T(8,128)(2,1)S(1)}, u32[]{:S(2)}, u32[]{:S(2)}) collective-permute-start(bf16[2,2,128,1024]{3,2,1,0:T(8,128)(2,1)S(1)} %get-tuple-element.24), channel_id=1, source_target_pairs={{0,4},{1,5},{2,6},{3,7},{8,12},{9,13},{10,14},{11,15},{16,20},{17,... | collective-permute-start | bytes 3145736 | tf_op jit(solution)/shard_map/ppermute | solution.py:26
  31.2 46.6 %collective-permute-start.5 = (bf16[2,2,128,1024]{3,2,1,0:T(8,128)(2,1)S(1)}, bf16[2,2,128,1024]{3,2,1,0:T(8,128)(2,1)S(1)}, u32[]{:S(2)}, u32[]{:S(2)}) collective-permute-start(bf16[2,2,128,1024]{3,2,1,0:T(8,128)(2,1)S(1)} %get-tuple-element.23), channel_id=1, source_target_pairs={{0,2},{1,3},{2,4},{3,5},{4,6},{5,7},{8,10},{9,11},{10,12},{11,13},... | collective-permute-start | bytes 3145736 | tf_op jit(solution)/shard_map/ppermute | solution.py:26
  33.5 5.2 %collective-permute-start.2 = (bf16[2,128,2048]{2,1,0:T(8,128)(2,1)S(1)}, bf16[2,128,2048]{2,1,0:T(8,128)(2,1)S(1)}, u32[]{:S(2)}, u32[]{:S(2)}) collective-permute-start(bf16[2,128,2048]{2,1,0:T(8,128)(2,1)S(1)} %pad_maximum_fusion.2), channel_id=1, source_target_pairs={{0,1},{1,0},{2,3},{3,2},{4,5},{5,4},{6,7},{7,6},{8,9},{9,8},{10,11... | collective-permute-start | bytes 3145736 | tf_op jit(solution)/shard_map/ppermute | solution.py:26
  55.2 23.7 %copy-start.8 = (bf16[2,2,128,1024]{3,2,1,0:T(8,128)(2,1)}, bf16[2,2,128,1024]{3,2,1,0:T(8,128)(2,1)S(1)}, u32[]{:S(2)}) copy-start(bf16[2,2,128,1024]{3,2,1,0:T(8,128)(2,1)S(1)} %collective-permute-done.3.refs_7_) | copy-start | bytes 3145732
  77.8 1.4 copy-start.9
  77.8 1.0 copy-start.10
  109.3 24.7 %collective-permute-start.6 = (bf16[2,2,128,1024]{3,2,1,0:T(8,128)(2,1)}, bf16[2,2,128,1024]{3,2,1,0:T(8,128)(2,1)S(1)}, u32[]{:S(2)}, u32[]{:S(2)}) collective-permute-start(bf16[2,2,128,1024]{3,2,1,0:T(8,128)(2,1)} %get-tuple-element.18), channel_id=1, source_target_pairs={{2,0},{3,1},{4,2},{5,3},{6,4},{7,5},{10,8},{11,9},{12,10},{13,11},... | collective-permute-start | bytes 3145736 | tf_op jit(solution)/shard_map/ppermute | solution.py:26
  109.3 46.9 %collective-permute-start.7 = (bf16[2,2,128,1024]{3,2,1,0:T(8,128)(2,1)}, bf16[2,2,128,1024]{3,2,1,0:T(8,128)(2,1)S(1)}, u32[]{:S(2)}, u32[]{:S(2)}) collective-permute-start(bf16[2,2,128,1024]{3,2,1,0:T(8,128)(2,1)} %get-tuple-element.19), channel_id=1, source_target_pairs={{4,0},{5,1},{6,2},{7,3},{12,8},{13,9},{14,10},{15,11},{20,16},{21,... | collective-permute-start | bytes 3145736 | tf_op jit(solution)/shard_map/ppermute | solution.py:26
  109.6 46.6 %collective-permute-start.8 = (bf16[2,2,128,1024]{3,2,1,0:T(8,128)(2,1)}, bf16[2,2,128,1024]{3,2,1,0:T(8,128)(2,1)S(1)}, u32[]{:S(2)}, u32[]{:S(2)}) collective-permute-start(bf16[2,2,128,1024]{3,2,1,0:T(8,128)(2,1)} %get-tuple-element.20), channel_id=1, source_target_pairs={{6,0},{7,1},{14,8},{15,9},{22,16},{23,17},{30,24},{31,25},{0,2},{1... | collective-permute-start | bytes 3145736 | tf_op jit(solution)/shard_map/ppermute | solution.py:26
  156.3 28.7 %copy-start.1 = (f32[2,2,128,1024]{3,2,1,0:T(8,128)S(1)}, f32[2,2,128,1024]{3,2,1,0:T(8,128)}, u32[]{:S(2)}) copy-start(f32[2,2,128,1024]{3,2,1,0:T(8,128)} %get-tuple-element.17) | copy-start | bytes 6291460
  158.8 26.2 %collective-permute-start.9 = (bf16[2,2,128,1024]{3,2,1,0:T(8,128)(2,1)S(1)}, bf16[2,2,128,1024]{3,2,1,0:T(8,128)(2,1)S(1)}, u32[]{:S(2)}, u32[]{:S(2)}) collective-permute-start(bf16[2,2,128,1024]{3,2,1,0:T(8,128)(2,1)S(1)} %fusion.8), channel_id=1, source_target_pairs={{8,0},{9,1},{10,2},{11,3},{12,4},{13,5},{14,6},{15,7},{16,8},{17,9... | collective-permute-start | bytes 3145736 | tf_op jit(solution)/shard_map/ppermute | solution.py:26
  186.1 1.0 copy-start.5
  187.2 4.4 %collective-permute-start.10 = (bf16[128,4096]{1,0:T(8,128)(2,1)S(1)}, bf16[128,4096]{1,0:T(8,128)(2,1)S(1)}, u32[]{:S(2)}, u32[]{:S(2)}) collective-permute-start(bf16[128,4096]{1,0:T(8,128)(2,1)S(1)} %pad_maximum_fusion.3), channel_id=1, source_target_pairs={{0,1},{1,0},{2,3},{3,2},{4,5},{5,4},{6,7},{7,6},{8,9},{9,8},{10,11... | collective-permute-start | bytes 3145736 | tf_op jit(solution)/shard_map/ppermute | solution.py:26
  189.3 4.2 %copy-start.4 = (bf16[128,2048]{1,0:T(8,128)(2,1)S(1)}, bf16[128,2048]{1,0:T(8,128)(2,1)}, u32[]{:S(2)}) copy-start(bf16[128,2048]{1,0:T(8,128)(2,1)} %get-tuple-element.16) | copy-start | bytes 1572868

commit v16 on v11

--- a/solution.py
+++ b/solution.py
@@ -144,7 +144,10 @@
 
 
 def in_core_order(core, mine, theirs):
-    return jnp.where(core == 0, jnp.concatenate([mine, theirs], -1), jnp.concatenate([theirs, mine], -1))
+    width = mine.shape[-1]
+    out = jnp.zeros(mine.shape[:-1] + (2 * width,), mine.dtype)
+    out = lax.dynamic_update_slice_in_dim(out, mine, core * width, out.ndim - 1)
+    return lax.dynamic_update_slice_in_dim(out, theirs, (1 - core) * width, out.ndim - 1)
 
 
 def local(queries, key_rows, value_rows, arriving_grad, doc_blocks):

time: 191 us -> 188 us (0.984)
  other arithmetic: 9.49 us -> 6.41 us
  waiting for transfers between devices: 133 us -> 131 us
    select_n x3 -> x0, other arithmetic: 3.07 us -> none  [in_core_order(): jnp.where(core == 0, jnp.concatenate([mine, theirs], -1), jnp.concatenate...]
    unnamed x30 -> x34, local copies, waits for them, and re-layouts: 3.78 us -> 4.04 us
  transfers between devices with their start and end apart: 11 -> 11, of which waited for: 8 -> 8; matrix products, arithmetic and copies ran while one was open for 2% -> 3% of each run, Pallas kernels for 0% -> 0%
where the time goes in v16:
time: 188 us; the launch traced here: 187 us
  waiting for transfers between devices  131 us (70%)
  Pallas kernels  25.3 us (13%)
  starting transfers between devices  14.7 us (8%)
  local copies, waits for them, and re-layouts  8.15 us (4%)
  other arithmetic  6.41 us (3%)
    ppermute x11, waiting for transfers between devices, moved(): return lax.ppermute(value, 'seq', pairs)  131 us
    pallas_call x1, Pallas kernels, attention_grads(): pl.pallas_call(lambda *refs: attention_kernel(chips, *refs), grid_spec=gr...  25.3 us
    ppermute x11, starting transfers between devices, moved(): return lax.ppermute(value, 'seq', pairs)  14.7 us
    unnamed x34, local copies, waits for them, and re-layouts  4.04 us
  transfers between devices with their start and end apart: 11, of which 8 were waited for; matrix products, arithmetic and copies ran while one was open for 3% of the time, Pallas kernels for 0%

profile of v16, /device:TPU:7, one launch (start us, length us, event | category | flops | bytes accessed | tf_op | source)
XLA Modules:
  0.0 187.2 jit_solution(3294742859837505725)
XLA Ops:
  0.6 0.0 copy-start
  0.7 1.3 constant_dynamic-slice_fusion.2
  1.9 0.1 pad_maximum_fusion.4
  2.0 0.7 collective-permute-start
  2.7 0.1 maximum_bitcast_fusion
  2.8 1.5 collective-permute-done
  4.3 0.1 pad_maximum_fusion.1.refs_10_
  4.4 3.3 %collective-permute-start.1 = (bf16[2,2,128,1024]{3,2,1,0:T(8,128)(2,1)S(1)}, bf16[2,2,128,1024]{3,2,1,0:T(8,128)(2,1)S(1)}, u32[]{:S(2)}, u32[]{:S(2)}) collective-permute-start(bf16[2,2,128,1024]{3,2,1,0:T(8,128)(2,1)S(1)} %pad_maximum_fusion.1.refs_10_), channel_id=1, source_target_pairs={{0,8},{1,9},{2,10},{3,11},{4,12},{5,13},{6,14},{7,15},{8,16},{9,17... | collective-permute-start | bytes 3145736 | tf_op jit(solution)/shard_map/ppermute | solution.py:26
  8.0 0.0 copy-start.9
  8.0 0.0 copy-start.8
  8.0 21.7 %collective-permute-done.1.refs_6_ = bf16[2,2,128,1024]{3,2,1,0:T(8,128)(2,1)S(1)} collective-permute-done((bf16[2,2,128,1024]{3,2,1,0:T(8,128)(2,1)S(1)}, bf16[2,2,128,1024]{3,2,1,0:T(8,128)(2,1)S(1)}, u32[]{:S(2)}, u32[]{:S(2)}) %collective-permute-start.1) | collective-permute-done | bytes 1048608 | tf_op jit(solution)/shard_map/ppermute | solution.py:26
  29.8 0.2 broadcast_select_fusion
  30.0 0.7 copy-done.4
  30.7 0.3 collective-permute-start.3
  31.0 0.2 collective-permute-start.4
  31.2 2.1 %collective-permute-start.5 = (bf16[2,2,128,1024]{3,2,1,0:T(8,128)(2,1)S(1)}, bf16[2,2,128,1024]{3,2,1,0:T(8,128)(2,1)S(1)}, u32[]{:S(2)}, u32[]{:S(2)}) collective-permute-start(bf16[2,2,128,1024]{3,2,1,0:T(8,128)(2,1)S(1)} %get-tuple-element.23), channel_id=1, source_target_pairs={{0,2},{1,3},{2,4},{3,5},{4,6},{5,7},{8,10},{9,11},{10,12},{11,13},... | collective-permute-start | bytes 3145736 | tf_op jit(solution)/shard_map/ppermute | solution.py:26
  33.3 0.0 copy-done.9
  33.4 0.0 copy-done.8
  33.4 0.1 pad_maximum_fusion.2
  33.5 2.1 %collective-permute-start.2 = (bf16[2,128,2048]{2,1,0:T(8,128)(2,1)S(1)}, bf16[2,128,2048]{2,1,0:T(8,128)(2,1)S(1)}, u32[]{:S(2)}, u32[]{:S(2)}) collective-permute-start(bf16[2,128,2048]{2,1,0:T(8,128)(2,1)S(1)} %pad_maximum_fusion.2), channel_id=1, source_target_pairs={{0,1},{1,0},{2,3},{3,2},{4,5},{5,4},{6,7},{7,6},{8,9},{9,8},{10,11... | collective-permute-start | bytes 3145736 | tf_op jit(solution)/shard_map/ppermute | solution.py:26
  35.6 0.1 broadcast_bitcast_fusion
  35.7 0.1 constant_dynamic-update-slice_fusion.19
  35.8 0.1 fusion.20
  35.9 0.1 constant_dynamic-update-slice_fusion.15
  35.9 0.1 constant_dynamic-update-slice_fusion.13
  36.0 0.1 constant_dynamic-update-slice_fusion.11
  36.1 0.1 constant_dynamic-update-slice_fusion.9
  36.2 0.1 constant_dynamic-update-slice_fusion.7
  36.3 0.1 constant_dynamic-update-slice_fusion.5
  36.4 0.1 constant_dynamic-update-slice_fusion.3
  36.4 0.1 constant_dynamic-update-slice_fusion.1
  36.5 0.5 fusion.11
  37.0 1.7 pad_maximum_fusion.refs_1_
  38.7 0.0 collective-permute-done.2
  38.7 1.1 slice_bitcast_fusion.1
  39.8 15.4 %collective-permute-done.3.refs_7_ = bf16[2,2,128,1024]{3,2,1,0:T(8,128)(2,1)S(1)} collective-permute-done((bf16[2,2,128,1024]{3,2,1,0:T(8,128)(2,1)S(1)}, bf16[2,2,128,1024]{3,2,1,0:T(8,128)(2,1)S(1)}, u32[]{:S(2)}, u32[]{:S(2)}) %collective-permute-start.3) | collective-permute-done | bytes 1048608 | tf_op jit(solution)/shard_map/ppermute | solution.py:26
  55.2 22.6 %collective-permute-done.4.refs_8_ = bf16[2,2,128,1024]{3,2,1,0:T(8,128)(2,1)S(1)} collective-permute-done((bf16[2,2,128,1024]{3,2,1,0:T(8,128)(2,1)S(1)}, bf16[2,2,128,1024]{3,2,1,0:T(8,128)(2,1)S(1)}, u32[]{:S(2)}, u32[]{:S(2)}) %collective-permute-start.4) | collective-permute-done | bytes 1048608 | tf_op jit(solution)/shard_map/ppermute | solution.py:26
  77.8 0.0 collective-permute-done.5.refs_9_
  77.8 1.0 copy-done.12
  78.8 0.4 copy-done.11
  79.2 25.3 %shard_map.76 = (bf16[128,2048]{1,0:T(8,128)(2,1)}, bf16[128,2048]{1,0:T(8,128)(2,1)}, f32[2,2,128,1024]{3,2,1,0:T(8,128)}, bf16[2,2,128,1024]{3,2,1,0:T(8,128)(...) custom-call(s32[1]{0:T(128)} %bitcast.refs_0_, ...), custom_call_target="tpu_custom_call" | custom-call | flops 6710886400 | bytes 21495808 | tf_op jit(solution)/shard_map/pallas_call | solution.py:133
  104.5 0.1 collective-permute-start.6
  104.6 0.3 collective-permute-start.7
  104.9 2.3 %collective-permute-start.8 = (bf16[2,2,128,1024]{3,2,1,0:T(8,128)(2,1)}, bf16[2,2,128,1024]{3,2,1,0:T(8,128)(2,1)S(1)}, u32[]{:S(2)}, u32[]{:S(2)}) collective-permute-start(bf16[2,2,128,1024]{3,2,1,0:T(8,128)(2,1)} %get-tuple-element.20), channel_id=1, source_target_pairs={{6,0},{7,1},{14,8},{15,9},{22,16},{23,17},{30,24},{31,25},{0,2},{1... | collective-permute-start | bytes 3145736 | tf_op jit(solution)/shard_map/ppermute | solution.py:26
  107.2 22.1 %collective-permute-done.6 = bf16[2,2,128,1024]{3,2,1,0:T(8,128)(2,1)S(1)} collective-permute-done((bf16[2,2,128,1024]{3,2,1,0:T(8,128)(2,1)}, bf16[2,2,128,1024]{3,2,1,0:T(8,128)(2,1)S(1)}, u32[]{:S(2)}, u32[]{:S(2)}) %collective-permute-start.6) | collective-permute-done | bytes 1048608 | tf_op jit(solution)/shard_map/ppermute | solution.py:26
  129.2 22.3 %collective-permute-done.7 = bf16[2,2,128,1024]{3,2,1,0:T(8,128)(2,1)S(1)} collective-permute-done((bf16[2,2,128,1024]{3,2,1,0:T(8,128)(2,1)}, bf16[2,2,128,1024]{3,2,1,0:T(8,128)(2,1)S(1)}, u32[]{:S(2)}, u32[]{:S(2)}) %collective-permute-start.7) | collective-permute-done | bytes 1048608 | tf_op jit(solution)/shard_map/ppermute | solution.py:26
  151.5 0.0 collective-permute-done.8
  151.5 2.5 %fusion.8 = bf16[2,2,128,1024]{3,2,1,0:T(8,128)(2,1)S(1)} fusion(f32[2,2,128,1024]{3,2,1,0:T(8,128)} %get-tuple-element.21, bf16[2,2,128,1024]{3,2,1,0:T(8,128)(2,1)S(1)} %collective-permute-done.6, bf16[2,2,128,1024]{3,2,1,0:T(8,128)(2,1)S(1)} %collective-permute-done.7, bf16[2,2,128,1024]{3,2,1,0:T(8,128)(2,1)S(1)} %collective-permute-done.8, ...), kind=kLoop, calls=%fused_computation.15 | loop fusion | flops 5242880 | bytes 6291459 | tf_op jit(solution)/shard_map/convert_element_type | solution.py:69
  154.1 1.3 collective-permute-start.9
  155.4 24.9 %collective-permute-done.9 = bf16[2,2,128,1024]{3,2,1,0:T(8,128)(2,1)S(1)} collective-permute-done((bf16[2,2,128,1024]{3,2,1,0:T(8,128)(2,1)S(1)}, bf16[2,2,128,1024]{3,2,1,0:T(8,128)(2,1)S(1)}, u32[]{:S(2)}, u32[]{:S(2)}) %collective-permute-start.9) | collective-permute-done | bytes 1048608 | tf_op jit(solution)/shard_map/ppermute | solution.py:26
  180.2 0.0 copy-done.1
  180.3 1.1 fusion.4
  181.4 0.1 pad_maximum_fusion.3
  181.5 2.1 %collective-permute-start.10 = (bf16[128,4096]{1,0:T(8,128)(2,1)S(1)}, bf16[128,4096]{1,0:T(8,128)(2,1)S(1)}, u32[]{:S(2)}, u32[]{:S(2)}) collective-permute-start(bf16[128,4096]{1,0:T(8,128)(2,1)S(1)} %pad_maximum_fusion.3), channel_id=1, source_target_pairs={{0,1},{1,0},{2,3},{3,2},{4,5},{5,4},{6,7},{7,6},{8,9},{9,8},{10,11... | collective-permute-start | bytes 3145736 | tf_op jit(solution)/shard_map/ppermute | solution.py:26
  183.5 0.1 broadcast_in_dim.51
  183.6 1.1 bitcast_dynamic-update-slice_fusion
  184.9 0.9 collective-permute-done.10
  185.9 0.0 copy-start.3
  185.9 0.1 fusion.16
  186.0 0.0 copy-start.5
  186.0 0.0 copy-start.6
  186.0 0.9 copy-done.3
  186.9 0.2 copy-done.5
  187.0 0.2 copy-done.6
  (32 shorter events, 0.4 us)
Async XLA Ops:
  0.6 32.7 %copy-start = (s32[1,32]{1,0:T(1,128)S(1)}, s32[1,32]{1,0:T(1,128)}, u32[]{:S(2)}) copy-start(s32[1,32]{1,0:T(1,128)} %param.9) | copy-start | bytes 388
  2.0 2.3 %collective-permute-start = (bf16[2,128,1024]{2,1,0:T(8,128)(2,1)S(1)}, bf16[2,128,1024]{2,1,0:T(8,128)(2,1)S(1)}, u32[]{:S(2)}, u32[]{:S(2)}) collective-permute-start(bf16[2,128,1024]{2,1,0:T(8,128)(2,1)S(1)} %pad_maximum_fusion.4), channel_id=1, source_target_pairs={{0,1},{1,0},{2,3},{3,2},{4,5},{5,4},{6,7},{7,6},{8,9},{9,8},{10,11... | collective-permute-start | bytes 1572872 | tf_op jit(solution)/shard_map/ppermute | solution.py:26
  4.4 25.6 %copy-start.2 = (bf16[2,2,128,1024]{3,2,1,0:T(8,128)(2,1)}, bf16[2,2,128,1024]{3,2,1,0:T(8,128)(2,1)S(1)}, u32[]{:S(2)}) copy-start(bf16[2,2,128,1024]{3,2,1,0:T(8,128)(2,1)S(1)} %pad_maximum_fusion.1.refs_10_) | copy-start | bytes 3145732
  4.4 25.4 %collective-permute-start.1 = (bf16[2,2,128,1024]{3,2,1,0:T(8,128)(2,1)S(1)}, bf16[2,2,128,1024]{3,2,1,0:T(8,128)(2,1)S(1)}, u32[]{:S(2)}, u32[]{:S(2)}) collective-permute-start(bf16[2,2,128,1024]{3,2,1,0:T(8,128)(2,1)S(1)} %pad_maximum_fusion.1.refs_10_), channel_id=1, source_target_pairs={{0,8},{1,9},{2,10},{3,11},{4,12},{5,13},{6,14},{7,15},{8,16},{9,17... | collective-permute-start | bytes 3145736 | tf_op jit(solution)/shard_map/ppermute | solution.py:26
  8.0 25.3 %copy-start.9 = (bf16[1,128,4096]{2,1,0:T(8,128)(2,1)S(1)}, bf16[1,128,4096]{2,1,0:T(8,128)(2,1)}, u32[]{:S(2)}) copy-start(bf16[1,128,4096]{2,1,0:T(8,128)(2,1)} %param.8) | copy-start | bytes 3145732
  8.0 25.4 %copy-start.8 = (bf16[1,128,4096]{2,1,0:T(8,128)(2,1)S(1)}, bf16[1,128,4096]{2,1,0:T(8,128)(2,1)}, u32[]{:S(2)}) copy-start(bf16[1,128,4096]{2,1,0:T(8,128)(2,1)} %param.5) | copy-start | bytes 3145732
  29.8 1.0 copy-start.4
  30.7 24.4 %collective-permute-start.3 = (bf16[2,2,128,1024]{3,2,1,0:T(8,128)(2,1)S(1)}, bf16[2,2,128,1024]{3,2,1,0:T(8,128)(2,1)S(1)}, u32[]{:S(2)}, u32[]{:S(2)}) collective-permute-start(bf16[2,2,128,1024]{3,2,1,0:T(8,128)(2,1)S(1)} %get-tuple-element.25), channel_id=1, source_target_pairs={{0,6},{1,7},{8,14},{9,15},{16,22},{17,23},{24,30},{25,31},{2,0},{3... | collective-permute-start | bytes 3145736 | tf_op jit(solution)/shard_map/ppermute | solution.py:26
  31.0 46.8 %collective-permute-start.4 = (bf16[2,2,128,1024]{3,2,1,0:T(8,128)(2,1)S(1)}, bf16[2,2,128,1024]{3,2,1,0:T(8,128)(2,1)S(1)}, u32[]{:S(2)}, u32[]{:S(2)}) collective-permute-start(bf16[2,2,128,1024]{3,2,1,0:T(8,128)(2,1)S(1)} %get-tuple-element.24), channel_id=1, source_target_pairs={{0,4},{1,5},{2,6},{3,7},{8,12},{9,13},{10,14},{11,15},{16,20},{17,... | collective-permute-start | bytes 3145736 | tf_op jit(solution)/shard_map/ppermute | solution.py:26
  31.2 46.6 %collective-permute-start.5 = (bf16[2,2,128,1024]{3,2,1,0:T(8,128)(2,1)S(1)}, bf16[2,2,128,1024]{3,2,1,0:T(8,128)(2,1)S(1)}, u32[]{:S(2)}, u32[]{:S(2)}) collective-permute-start(bf16[2,2,128,1024]{3,2,1,0:T(8,128)(2,1)S(1)} %get-tuple-element.23), channel_id=1, source_target_pairs={{0,2},{1,3},{2,4},{3,5},{4,6},{5,7},{8,10},{9,11},{10,12},{11,13},... | collective-permute-start | bytes 3145736 | tf_op jit(solution)/shard_map/ppermute | solution.py:26
  33.5 5.2 %collective-permute-start.2 = (bf16[2,128,2048]{2,1,0:T(8,128)(2,1)S(1)}, bf16[2,128,2048]{2,1,0:T(8,128)(2,1)S(1)}, u32[]{:S(2)}, u32[]{:S(2)}) collective-permute-start(bf16[2,128,2048]{2,1,0:T(8,128)(2,1)S(1)} %pad_maximum_fusion.2), channel_id=1, source_target_pairs={{0,1},{1,0},{2,3},{3,2},{4,5},{5,4},{6,7},{7,6},{8,9},{9,8},{10,11... | collective-permute-start | bytes 3145736 | tf_op jit(solution)/shard_map/ppermute | solution.py:26
  55.2 23.7 %copy-start.10 = (bf16[2,2,128,1024]{3,2,1,0:T(8,128)(2,1)}, bf16[2,2,128,1024]{3,2,1,0:T(8,128)(2,1)S(1)}, u32[]{:S(2)}) copy-start(bf16[2,2,128,1024]{3,2,1,0:T(8,128)(2,1)S(1)} %collective-permute-done.3.refs_7_) | copy-start | bytes 3145732
  77.8 1.4 copy-start.11
  77.8 1.0 copy-start.12
  104.5 24.7 %collective-permute-start.6 = (bf16[2,2,128,1024]{3,2,1,0:T(8,128)(2,1)}, bf16[2,2,128,1024]{3,2,1,0:T(8,128)(2,1)S(1)}, u32[]{:S(2)}, u32[]{:S(2)}) collective-permute-start(bf16[2,2,128,1024]{3,2,1,0:T(8,128)(2,1)} %get-tuple-element.18), channel_id=1, source_target_pairs={{2,0},{3,1},{4,2},{5,3},{6,4},{7,5},{10,8},{11,9},{12,10},{13,11},... | collective-permute-start | bytes 3145736 | tf_op jit(solution)/shard_map/ppermute | solution.py:26
  104.6 46.9 %collective-permute-start.7 = (bf16[2,2,128,1024]{3,2,1,0:T(8,128)(2,1)}, bf16[2,2,128,1024]{3,2,1,0:T(8,128)(2,1)S(1)}, u32[]{:S(2)}, u32[]{:S(2)}) collective-permute-start(bf16[2,2,128,1024]{3,2,1,0:T(8,128)(2,1)} %get-tuple-element.19), channel_id=1, source_target_pairs={{4,0},{5,1},{6,2},{7,3},{12,8},{13,9},{14,10},{15,11},{20,16},{21,... | collective-permute-start | bytes 3145736 | tf_op jit(solution)/shard_map/ppermute | solution.py:26
  104.9 46.6 %collective-permute-start.8 = (bf16[2,2,128,1024]{3,2,1,0:T(8,128)(2,1)}, bf16[2,2,128,1024]{3,2,1,0:T(8,128)(2,1)S(1)}, u32[]{:S(2)}, u32[]{:S(2)}) collective-permute-start(bf16[2,2,128,1024]{3,2,1,0:T(8,128)(2,1)} %get-tuple-element.20), channel_id=1, source_target_pairs={{6,0},{7,1},{14,8},{15,9},{22,16},{23,17},{30,24},{31,25},{0,2},{1... | collective-permute-start | bytes 3145736 | tf_op jit(solution)/shard_map/ppermute | solution.py:26
  151.5 28.7 %copy-start.1 = (f32[2,2,128,1024]{3,2,1,0:T(8,128)S(1)}, f32[2,2,128,1024]{3,2,1,0:T(8,128)}, u32[]{:S(2)}) copy-start(f32[2,2,128,1024]{3,2,1,0:T(8,128)} %get-tuple-element.17) | copy-start | bytes 6291460
  154.1 26.2 %collective-permute-start.9 = (bf16[2,2,128,1024]{3,2,1,0:T(8,128)(2,1)S(1)}, bf16[2,2,128,1024]{3,2,1,0:T(8,128)(2,1)S(1)}, u32[]{:S(2)}, u32[]{:S(2)}) collective-permute-start(bf16[2,2,128,1024]{3,2,1,0:T(8,128)(2,1)S(1)} %fusion.8), channel_id=1, source_target_pairs={{8,0},{9,1},{10,2},{11,3},{12,4},{13,5},{14,6},{15,7},{16,8},{17,9... | collective-permute-start | bytes 3145736 | tf_op jit(solution)/shard_map/ppermute | solution.py:26
  180.3 1.1 copy-start.7
  181.5 4.4 %collective-permute-start.10 = (bf16[128,4096]{1,0:T(8,128)(2,1)S(1)}, bf16[128,4096]{1,0:T(8,128)(2,1)S(1)}, u32[]{:S(2)}, u32[]{:S(2)}) collective-permute-start(bf16[128,4096]{1,0:T(8,128)(2,1)S(1)} %pad_maximum_fusion.3), channel_id=1, source_target_pairs={{0,1},{1,0},{2,3},{3,2},{4,5},{5,4},{6,7},{7,6},{8,9},{9,8},{10,11... | collective-permute-start | bytes 3145736 | tf_op jit(solution)/shard_map/ppermute | solution.py:26
  185.9 1.0 copy-start.3
  186.0 1.1 copy-start.5
  186.0 1.2 copy-start.6

commit v17 on v16

--- a/solution.py
+++ b/solution.py
@@ -49,8 +49,10 @@
 def gather_window(own, routes, chip_in_group):
     prev = moved(own, routes.hop)
     recv = []
+    both = lax.dynamic_update_index_in_dim(jnp.stack([own, own]), prev, 1, 0)
     for e in range(1, routes.chips):
-        sent = jnp.where(chip_in_group + e < routes.chips, own, prev)
+        pick = (chip_in_group + e >= routes.chips).astype(jnp.int32)
+        sent = lax.dynamic_index_in_dim(both, pick, 0, keepdims=False)
         recv.append(moved(sent, routes.up[e - 1] + routes.down[e - 1]))
     return [prev] + recv[::-1] + [own]
 

time: 188 us -> 190 us (1.011)
    unnamed x34 -> x36, local copies, waits for them, and re-layouts: 4.04 us -> 3.81 us
where the time goes in v17:
time: 190 us; the launch traced here: 189 us
  waiting for transfers between devices  131 us (69%)
  Pallas kernels  25.3 us (13%)
  starting transfers between devices  14.7 us (8%)
  local copies, waits for them, and re-layouts  8.38 us (4%)
  other arithmetic  8.1 us (4%)
    ppermute x11, waiting for transfers between devices, moved(): return lax.ppermute(value, 'seq', pairs)  131 us
    pallas_call x1, Pallas kernels, attention_grads(): pl.pallas_call(lambda *refs: attention_kernel(chips, *refs), grid_spec=gr...  25.3 us
    ppermute x11, starting transfers between devices, moved(): return lax.ppermute(value, 'seq', pairs)  14.7 us
    unnamed x36, local copies, waits for them, and re-layouts  3.81 us
  transfers between devices with their start and end apart: 11, of which 8 were waited for; matrix products, arithmetic and copies ran while one was open for 3% of the time, Pallas kernels for 0%

profile of v17, /device:TPU:7, one launch (start us, length us, event | category | flops | bytes accessed | tf_op | source)
XLA Modules:
  0.0 189.0 jit_solution(10320876143552286388)
XLA Ops:
  0.6 0.0 copy-start
  0.7 1.3 constant_dynamic-slice_fusion.2
  2.0 0.1 pad_maximum_fusion.5
  2.0 0.7 collective-permute-start
  2.8 0.1 maximum_bitcast_fusion
  2.8 1.5 collective-permute-done
  4.3 0.1 fusion.20
  4.4 0.0 copy-start.3
  4.4 3.3 %collective-permute-start.1 = (bf16[2,2,128,1024]{3,2,1,0:T(8,128)(2,1)S(1)}, bf16[2,2,128,1024]{3,2,1,0:T(8,128)(2,1)S(1)}, u32[]{:S(2)}, u32[]{:S(2)}) collective-permute-start(bf16[2,2,128,1024]{3,2,1,0:T(8,128)(2,1)S(1)} %get-tuple-element.31.refs_10_), channel_id=1, source_target_pairs={{0,8},{1,9},{2,10},{3,11},{4,12},{5,13},{6,14},{7,15},{8,16},{9,17... | collective-permute-start | bytes 3145736 | tf_op jit(solution)/shard_map/ppermute | solution.py:26
  7.8 0.2 pad_maximum_fusion.1
  8.0 21.8 %collective-permute-done.1.refs_6_ = bf16[2,2,128,1024]{3,2,1,0:T(8,128)(2,1)S(1)} collective-permute-done((bf16[2,2,128,1024]{3,2,1,0:T(8,128)(2,1)S(1)}, bf16[2,2,128,1024]{3,2,1,0:T(8,128)(2,1)S(1)}, u32[]{:S(2)}, u32[]{:S(2)}) %collective-permute-start.1) | collective-permute-done | bytes 1048608 | tf_op jit(solution)/shard_map/ppermute | solution.py:26
  29.8 0.1 bitcast_dynamic-update-slice_fusion
  29.9 0.0 copy-start.10
  29.9 0.0 copy-start.9
  29.9 0.4 dynamic-slice_bitcast_fusion
  30.3 0.5 copy-done.4
  30.8 0.3 collective-permute-start.3
  31.1 0.2 collective-permute-start.4
  31.3 2.1 %collective-permute-start.5 = (bf16[2,2,128,1024]{3,2,1,0:T(8,128)(2,1)S(1)}, bf16[2,2,128,1024]{3,2,1,0:T(8,128)(2,1)S(1)}, u32[]{:S(2)}, u32[]{:S(2)}) collective-permute-start(bf16[2,2,128,1024]{3,2,1,0:T(8,128)(2,1)S(1)} %get-tuple-element.23), channel_id=1, source_target_pairs={{0,2},{1,3},{2,4},{3,5},{4,6},{5,7},{8,10},{9,11},{10,12},{11,13},... | collective-permute-start | bytes 3145736 | tf_op jit(solution)/shard_map/ppermute | solution.py:26
  33.5 0.1 pad_maximum_fusion.3
  33.6 2.1 %collective-permute-start.2 = (bf16[2,128,2048]{2,1,0:T(8,128)(2,1)S(1)}, bf16[2,128,2048]{2,1,0:T(8,128)(2,1)S(1)}, u32[]{:S(2)}, u32[]{:S(2)}) collective-permute-start(bf16[2,128,2048]{2,1,0:T(8,128)(2,1)S(1)} %pad_maximum_fusion.3), channel_id=1, source_target_pairs={{0,1},{1,0},{2,3},{3,2},{4,5},{5,4},{6,7},{7,6},{8,9},{9,8},{10,11... | collective-permute-start | bytes 3145736 | tf_op jit(solution)/shard_map/ppermute | solution.py:26
  35.7 0.1 broadcast_bitcast_fusion
  35.8 0.1 constant_dynamic-update-slice_fusion.19
  35.9 0.1 fusion.21
  36.0 0.1 constant_dynamic-update-slice_fusion.15
  36.1 0.1 constant_dynamic-update-slice_fusion.13
  36.1 0.1 constant_dynamic-update-slice_fusion.11
  36.2 0.1 constant_dynamic-update-slice_fusion.9
  36.3 0.1 constant_dynamic-update-slice_fusion.7
  36.4 0.1 constant_dynamic-update-slice_fusion.5
  36.5 0.1 constant_dynamic-update-slice_fusion.3
  36.5 0.1 constant_dynamic-update-slice_fusion.1
  36.6 0.5 fusion.11
  37.1 1.7 pad_maximum_fusion.refs_1_
  38.8 0.0 collective-permute-done.2
  38.8 1.1 slice_bitcast_fusion.1
  39.9 15.4 %collective-permute-done.3.refs_7_ = bf16[2,2,128,1024]{3,2,1,0:T(8,128)(2,1)S(1)} collective-permute-done((bf16[2,2,128,1024]{3,2,1,0:T(8,128)(2,1)S(1)}, bf16[2,2,128,1024]{3,2,1,0:T(8,128)(2,1)S(1)}, u32[]{:S(2)}, u32[]{:S(2)}) %collective-permute-start.3) | collective-permute-done | bytes 1048608 | tf_op jit(solution)/shard_map/ppermute | solution.py:26
  55.3 22.6 %collective-permute-done.4.refs_8_ = bf16[2,2,128,1024]{3,2,1,0:T(8,128)(2,1)S(1)} collective-permute-done((bf16[2,2,128,1024]{3,2,1,0:T(8,128)(2,1)S(1)}, bf16[2,2,128,1024]{3,2,1,0:T(8,128)(2,1)S(1)}, u32[]{:S(2)}, u32[]{:S(2)}) %collective-permute-start.4) | collective-permute-done | bytes 1048608 | tf_op jit(solution)/shard_map/ppermute | solution.py:26
  77.9 0.0 collective-permute-done.5.refs_9_
  77.9 1.0 copy-done.13
  78.9 0.4 copy-done.12
  79.3 25.3 %shard_map.76 = (bf16[128,2048]{1,0:T(8,128)(2,1)}, bf16[128,2048]{1,0:T(8,128)(2,1)}, f32[2,2,128,1024]{3,2,1,0:T(8,128)}, bf16[2,2,128,1024]{3,2,1,0:T(8,128)(...) custom-call(s32[1]{0:T(128)} %bitcast.refs_0_, ...), custom_call_target="tpu_custom_call" | custom-call | flops 6710886400 | bytes 21495808 | tf_op jit(solution)/shard_map/pallas_call | solution.py:135
  104.6 0.1 collective-permute-start.6
  104.6 0.3 collective-permute-start.7
  104.9 2.3 %collective-permute-start.8 = (bf16[2,2,128,1024]{3,2,1,0:T(8,128)(2,1)}, bf16[2,2,128,1024]{3,2,1,0:T(8,128)(2,1)S(1)}, u32[]{:S(2)}, u32[]{:S(2)}) collective-permute-start(bf16[2,2,128,1024]{3,2,1,0:T(8,128)(2,1)} %get-tuple-element.20), channel_id=1, source_target_pairs={{6,0},{7,1},{14,8},{15,9},{22,16},{23,17},{30,24},{31,25},{0,2},{1... | collective-permute-start | bytes 3145736 | tf_op jit(solution)/shard_map/ppermute | solution.py:26
  107.2 22.0 %collective-permute-done.6 = bf16[2,2,128,1024]{3,2,1,0:T(8,128)(2,1)S(1)} collective-permute-done((bf16[2,2,128,1024]{3,2,1,0:T(8,128)(2,1)}, bf16[2,2,128,1024]{3,2,1,0:T(8,128)(2,1)S(1)}, u32[]{:S(2)}, u32[]{:S(2)}) %collective-permute-start.6) | collective-permute-done | bytes 1048608 | tf_op jit(solution)/shard_map/ppermute | solution.py:26
  129.3 22.3 %collective-permute-done.7 = bf16[2,2,128,1024]{3,2,1,0:T(8,128)(2,1)S(1)} collective-permute-done((bf16[2,2,128,1024]{3,2,1,0:T(8,128)(2,1)}, bf16[2,2,128,1024]{3,2,1,0:T(8,128)(2,1)S(1)}, u32[]{:S(2)}, u32[]{:S(2)}) %collective-permute-start.7) | collective-permute-done | bytes 1048608 | tf_op jit(solution)/shard_map/ppermute | solution.py:26
  151.6 0.0 collective-permute-done.8
  151.6 2.9 %fusion.8 = bf16[2,2,128,1024]{3,2,1,0:T(8,128)(2,1)S(1)} fusion(f32[2,2,128,1024]{3,2,1,0:T(8,128)} %get-tuple-element.21, bf16[2,2,128,1024]{3,2,1,0:T(8,128)(2,1)S(1)} %collective-permute-done.6, bf16[2,2,128,1024]{3,2,1,0:T(8,128)(2,1)S(1)} %collective-permute-done.7, bf16[2,2,128,1024]{3,2,1,0:T(8,128)(2,1)S(1)} %collective-permute-done.8, ...), kind=kLoop, calls=%fused_computation.15 | loop fusion | flops 5242880 | bytes 6291459 | tf_op jit(solution)/shard_map/convert_element_type | solution.py:71
  154.5 1.3 collective-permute-start.9
  155.8 24.9 %collective-permute-done.9 = bf16[2,2,128,1024]{3,2,1,0:T(8,128)(2,1)S(1)} collective-permute-done((bf16[2,2,128,1024]{3,2,1,0:T(8,128)(2,1)S(1)}, bf16[2,2,128,1024]{3,2,1,0:T(8,128)(2,1)S(1)}, u32[]{:S(2)}, u32[]{:S(2)}) %collective-permute-start.9) | collective-permute-done | bytes 1048608 | tf_op jit(solution)/shard_map/ppermute | solution.py:26
  180.7 2.4 %fusion.4 = bf16[2,2,128,1024]{3,2,1,0:T(8,128)(2,1)S(1)} fusion(f32[2,2,128,1024]{3,2,1,0:T(8,128)S(1)} %copy-done.2, bf16[2,2,128,1024]{3,2,1,0:T(8,128)(2,1)S(1)} %collective-permute-done.6, bf16[2,2,128,1024]{3,2,1,0:T(8,128)(2,1)S(1)} %collective-permute-done.7, bf16[2,2,128,1024]{3,2,1,0:T(8,128)(2,1)} %copy-done.1, ...), kind=kLoop, calls=%fused_computation.11 | loop fusion | flops 6291456 | bytes 7340035 | tf_op jit(solution)/shard_map/convert.3
  183.1 0.1 pad_maximum_fusion.4
  183.2 2.1 %collective-permute-start.10 = (bf16[128,4096]{1,0:T(8,128)(2,1)S(1)}, bf16[128,4096]{1,0:T(8,128)(2,1)S(1)}, u32[]{:S(2)}, u32[]{:S(2)}) collective-permute-start(bf16[128,4096]{1,0:T(8,128)(2,1)S(1)} %pad_maximum_fusion.4), channel_id=1, source_target_pairs={{0,1},{1,0},{2,3},{3,2},{4,5},{5,4},{6,7},{7,6},{8,9},{9,8},{10,11... | collective-permute-start | bytes 3145736 | tf_op jit(solution)/shard_map/ppermute | solution.py:26
  185.3 0.1 broadcast_in_dim.55
  185.4 1.1 bitcast_dynamic-update-slice_fusion.1
  186.7 0.9 collective-permute-done.10
  187.7 0.0 copy-start.5
  187.7 0.1 fusion.16
  187.7 0.0 copy-start.6
  187.7 0.0 copy-start.7
  187.7 0.9 copy-done.5
  188.6 0.2 copy-done.6
  188.8 0.2 copy-done.7
  (36 shorter events, 0.4 us)
Async XLA Ops:
  0.6 32.8 %copy-start = (s32[1,32]{1,0:T(1,128)S(1)}, s32[1,32]{1,0:T(1,128)}, u32[]{:S(2)}) copy-start(s32[1,32]{1,0:T(1,128)} %param.9) | copy-start | bytes 388
  2.0 2.3 %collective-permute-start = (bf16[2,128,1024]{2,1,0:T(8,128)(2,1)S(1)}, bf16[2,128,1024]{2,1,0:T(8,128)(2,1)S(1)}, u32[]{:S(2)}, u32[]{:S(2)}) collective-permute-start(bf16[2,128,1024]{2,1,0:T(8,128)(2,1)S(1)} %pad_maximum_fusion.5), channel_id=1, source_target_pairs={{0,1},{1,0},{2,3},{3,2},{4,5},{5,4},{6,7},{7,6},{8,9},{9,8},{10,11... | collective-permute-start | bytes 1572872 | tf_op jit(solution)/shard_map/ppermute | solution.py:26
  4.4 25.5 %copy-start.3 = (bf16[2,2,128,1024]{3,2,1,0:T(8,128)(2,1)}, bf16[2,2,128,1024]{3,2,1,0:T(8,128)(2,1)S(1)}, u32[]{:S(2)}) copy-start(bf16[2,2,128,1024]{3,2,1,0:T(8,128)(2,1)S(1)} %get-tuple-element.31.refs_10_) | copy-start | bytes 3145732
  4.4 25.4 %collective-permute-start.1 = (bf16[2,2,128,1024]{3,2,1,0:T(8,128)(2,1)S(1)}, bf16[2,2,128,1024]{3,2,1,0:T(8,128)(2,1)S(1)}, u32[]{:S(2)}, u32[]{:S(2)}) collective-permute-start(bf16[2,2,128,1024]{3,2,1,0:T(8,128)(2,1)S(1)} %get-tuple-element.31.refs_10_), channel_id=1, source_target_pairs={{0,8},{1,9},{2,10},{3,11},{4,12},{5,13},{6,14},{7,15},{8,16},{9,17... | collective-permute-start | bytes 3145736 | tf_op jit(solution)/shard_map/ppermute | solution.py:26
  29.8 1.0 copy-start.4
  29.9 3.5 %copy-start.10 = (bf16[1,128,4096]{2,1,0:T(8,128)(2,1)S(1)}, bf16[1,128,4096]{2,1,0:T(8,128)(2,1)}, u32[]{:S(2)}) copy-start(bf16[1,128,4096]{2,1,0:T(8,128)(2,1)} %param.8) | copy-start | bytes 3145732
  29.9 3.6 %copy-start.9 = (bf16[1,128,4096]{2,1,0:T(8,128)(2,1)S(1)}, bf16[1,128,4096]{2,1,0:T(8,128)(2,1)}, u32[]{:S(2)}) copy-start(bf16[1,128,4096]{2,1,0:T(8,128)(2,1)} %param.5) | copy-start | bytes 3145732
  30.8 24.4 %collective-permute-start.3 = (bf16[2,2,128,1024]{3,2,1,0:T(8,128)(2,1)S(1)}, bf16[2,2,128,1024]{3,2,1,0:T(8,128)(2,1)S(1)}, u32[]{:S(2)}, u32[]{:S(2)}) collective-permute-start(bf16[2,2,128,1024]{3,2,1,0:T(8,128)(2,1)S(1)} %get-tuple-element.25), channel_id=1, source_target_pairs={{0,6},{1,7},{8,14},{9,15},{16,22},{17,23},{24,30},{25,31},{2,0},{3... | collective-permute-start | bytes 3145736 | tf_op jit(solution)/shard_map/ppermute | solution.py:26
  31.1 46.8 %collective-permute-start.4 = (bf16[2,2,128,1024]{3,2,1,0:T(8,128)(2,1)S(1)}, bf16[2,2,128,1024]{3,2,1,0:T(8,128)(2,1)S(1)}, u32[]{:S(2)}, u32[]{:S(2)}) collective-permute-start(bf16[2,2,128,1024]{3,2,1,0:T(8,128)(2,1)S(1)} %get-tuple-element.24), channel_id=1, source_target_pairs={{0,4},{1,5},{2,6},{3,7},{8,12},{9,13},{10,14},{11,15},{16,20},{17,... | collective-permute-start | bytes 3145736 | tf_op jit(solution)/shard_map/ppermute | solution.py:26
  31.3 46.6 %collective-permute-start.5 = (bf16[2,2,128,1024]{3,2,1,0:T(8,128)(2,1)S(1)}, bf16[2,2,128,1024]{3,2,1,0:T(8,128)(2,1)S(1)}, u32[]{:S(2)}, u32[]{:S(2)}) collective-permute-start(bf16[2,2,128,1024]{3,2,1,0:T(8,128)(2,1)S(1)} %get-tuple-element.23), channel_id=1, source_target_pairs={{0,2},{1,3},{2,4},{3,5},{4,6},{5,7},{8,10},{9,11},{10,12},{11,13},... | collective-permute-start | bytes 3145736 | tf_op jit(solution)/shard_map/ppermute | solution.py:26
  33.6 5.2 %collective-permute-start.2 = (bf16[2,128,2048]{2,1,0:T(8,128)(2,1)S(1)}, bf16[2,128,2048]{2,1,0:T(8,128)(2,1)S(1)}, u32[]{:S(2)}, u32[]{:S(2)}) collective-permute-start(bf16[2,128,2048]{2,1,0:T(8,128)(2,1)S(1)} %pad_maximum_fusion.3), channel_id=1, source_target_pairs={{0,1},{1,0},{2,3},{3,2},{4,5},{5,4},{6,7},{7,6},{8,9},{9,8},{10,11... | collective-permute-start | bytes 3145736 | tf_op jit(solution)/shard_map/ppermute | solution.py:26
  55.3 23.7 %copy-start.11 = (bf16[2,2,128,1024]{3,2,1,0:T(8,128)(2,1)}, bf16[2,2,128,1024]{3,2,1,0:T(8,128)(2,1)S(1)}, u32[]{:S(2)}) copy-start(bf16[2,2,128,1024]{3,2,1,0:T(8,128)(2,1)S(1)} %collective-permute-done.3.refs_7_) | copy-start | bytes 3145732
  77.9 1.4 copy-start.12
  77.9 1.0 copy-start.13
  104.6 24.7 %collective-permute-start.6 = (bf16[2,2,128,1024]{3,2,1,0:T(8,128)(2,1)}, bf16[2,2,128,1024]{3,2,1,0:T(8,128)(2,1)S(1)}, u32[]{:S(2)}, u32[]{:S(2)}) collective-permute-start(bf16[2,2,128,1024]{3,2,1,0:T(8,128)(2,1)} %get-tuple-element.18), channel_id=1, source_target_pairs={{2,0},{3,1},{4,2},{5,3},{6,4},{7,5},{10,8},{11,9},{12,10},{13,11},... | collective-permute-start | bytes 3145736 | tf_op jit(solution)/shard_map/ppermute | solution.py:26
  104.6 46.9 %collective-permute-start.7 = (bf16[2,2,128,1024]{3,2,1,0:T(8,128)(2,1)}, bf16[2,2,128,1024]{3,2,1,0:T(8,128)(2,1)S(1)}, u32[]{:S(2)}, u32[]{:S(2)}) collective-permute-start(bf16[2,2,128,1024]{3,2,1,0:T(8,128)(2,1)} %get-tuple-element.19), channel_id=1, source_target_pairs={{4,0},{5,1},{6,2},{7,3},{12,8},{13,9},{14,10},{15,11},{20,16},{21,... | collective-permute-start | bytes 3145736 | tf_op jit(solution)/shard_map/ppermute | solution.py:26
  104.9 46.6 %collective-permute-start.8 = (bf16[2,2,128,1024]{3,2,1,0:T(8,128)(2,1)}, bf16[2,2,128,1024]{3,2,1,0:T(8,128)(2,1)S(1)}, u32[]{:S(2)}, u32[]{:S(2)}) collective-permute-start(bf16[2,2,128,1024]{3,2,1,0:T(8,128)(2,1)} %get-tuple-element.20), channel_id=1, source_target_pairs={{6,0},{7,1},{14,8},{15,9},{22,16},{23,17},{30,24},{31,25},{0,2},{1... | collective-permute-start | bytes 3145736 | tf_op jit(solution)/shard_map/ppermute | solution.py:26
  151.6 2.9 %copy-start.1 = (bf16[2,2,128,1024]{3,2,1,0:T(8,128)(2,1)}, bf16[2,2,128,1024]{3,2,1,0:T(8,128)(2,1)S(1)}, u32[]{:S(2)}) copy-start(bf16[2,2,128,1024]{3,2,1,0:T(8,128)(2,1)S(1)} %collective-permute-done.8) | copy-start | bytes 3145732
  151.6 29.1 %copy-start.2 = (f32[2,2,128,1024]{3,2,1,0:T(8,128)S(1)}, f32[2,2,128,1024]{3,2,1,0:T(8,128)}, u32[]{:S(2)}) copy-start(f32[2,2,128,1024]{3,2,1,0:T(8,128)} %get-tuple-element.17) | copy-start | bytes 6291460
  154.5 26.2 %collective-permute-start.9 = (bf16[2,2,128,1024]{3,2,1,0:T(8,128)(2,1)S(1)}, bf16[2,2,128,1024]{3,2,1,0:T(8,128)(2,1)S(1)}, u32[]{:S(2)}, u32[]{:S(2)}) collective-permute-start(bf16[2,2,128,1024]{3,2,1,0:T(8,128)(2,1)S(1)} %fusion.8), channel_id=1, source_target_pairs={{8,0},{9,1},{10,2},{11,3},{12,4},{13,5},{14,6},{15,7},{16,8},{17,9... | collective-permute-start | bytes 3145736 | tf_op jit(solution)/shard_map/ppermute | solution.py:26
  180.7 2.4 %copy-start.8 = (bf16[128,2048]{1,0:T(8,128)(2,1)S(1)}, bf16[128,2048]{1,0:T(8,128)(2,1)}, u32[]{:S(2)}) copy-start(bf16[128,2048]{1,0:T(8,128)(2,1)} %get-tuple-element.22) | copy-start | bytes 1572868
  183.2 4.4 %collective-permute-start.10 = (bf16[128,4096]{1,0:T(8,128)(2,1)S(1)}, bf16[128,4096]{1,0:T(8,128)(2,1)S(1)}, u32[]{:S(2)}, u32[]{:S(2)}) collective-permute-start(bf16[128,4096]{1,0:T(8,128)(2,1)S(1)} %pad_maximum_fusion.4), channel_id=1, source_target_pairs={{0,1},{1,0},{2,3},{3,2},{4,5},{5,4},{6,7},{7,6},{8,9},{9,8},{10,11... | collective-permute-start | bytes 3145736 | tf_op jit(solution)/shard_map/ppermute | solution.py:26
  187.7 1.0 copy-start.5
  187.7 1.1 copy-start.6
  187.7 1.2 copy-start.7

commit v18 on v16

--- a/solution.py
+++ b/solution.py
@@ -176,7 +176,9 @@
         [lax.dynamic_slice_in_dim(keys, core * key_width, key_width, 1),
          lax.dynamic_slice_in_dim(values, core * key_width, key_width, 1)]
     )
-    own = jnp.stack([kv_mine, kv_sib], axis=1)
+    own = jnp.zeros((2, 2) + kv_mine.shape[1:], kv_mine.dtype)
+    own = lax.dynamic_update_index_in_dim(own, kv_mine, 0, 1)
+    own = lax.dynamic_update_index_in_dim(own, kv_sib, 1, 1)
     payloads = gather_window(own, routes, chip_in_group)
     (query_rows, grad_rows, doc_row), _ = lax.optimization_barrier(
         ((queries[0], grad_out, doc_blocks[0]), payloads[0])

time: 188 us -> 188 us (level)
  no operation moved by 1% of the time
where the time goes in v18:
time: 188 us; the launch traced here: 187 us
  waiting for transfers between devices  131 us (70%)
  Pallas kernels  25.3 us (13%)
  starting transfers between devices  14.7 us (8%)
  local copies, waits for them, and re-layouts  8.15 us (4%)
  other arithmetic  6.41 us (3%)
    ppermute x11, waiting for transfers between devices, moved(): return lax.ppermute(value, 'seq', pairs)  131 us
    pallas_call x1, Pallas kernels, attention_grads(): pl.pallas_call(lambda *refs: attention_kernel(chips, *refs), grid_spec=gr...  25.3 us
    ppermute x11, starting transfers between devices, moved(): return lax.ppermute(value, 'seq', pairs)  14.7 us
    unnamed x34, local copies, waits for them, and re-layouts  4.04 us
  transfers between devices with their start and end apart: 11, of which 8 were waited for; matrix products, arithmetic and copies ran while one was open for 3% of the time, Pallas kernels for 0%

profile of v18, /device:TPU:7, one launch (start us, length us, event | category | flops | bytes accessed | tf_op | source)
XLA Modules:
  0.0 187.2 jit_solution(3294742859837505725)
XLA Ops:
  0.6 0.0 copy-start
  0.7 1.3 constant_dynamic-slice_fusion.2
  1.9 0.1 pad_maximum_fusion.4
  2.0 0.7 collective-permute-start
  2.7 0.1 maximum_bitcast_fusion
  2.8 1.5 collective-permute-done
  4.3 0.1 pad_maximum_fusion.1.refs_10_
  4.4 3.3 %collective-permute-start.1 = (bf16[2,2,128,1024]{3,2,1,0:T(8,128)(2,1)S(1)}, bf16[2,2,128,1024]{3,2,1,0:T(8,128)(2,1)S(1)}, u32[]{:S(2)}, u32[]{:S(2)}) collective-permute-start(bf16[2,2,128,1024]{3,2,1,0:T(8,128)(2,1)S(1)} %pad_maximum_fusion.1.refs_10_), channel_id=1, source_target_pairs={{0,8},{1,9},{2,10},{3,11},{4,12},{5,13},{6,14},{7,15},{8,16},{9,17... | collective-permute-start | bytes 3145736 | tf_op jit(solution)/shard_map/ppermute | solution.py:26
  8.0 0.0 copy-start.9
  8.0 0.0 copy-start.8
  8.0 21.7 %collective-permute-done.1.refs_6_ = bf16[2,2,128,1024]{3,2,1,0:T(8,128)(2,1)S(1)} collective-permute-done((bf16[2,2,128,1024]{3,2,1,0:T(8,128)(2,1)S(1)}, bf16[2,2,128,1024]{3,2,1,0:T(8,128)(2,1)S(1)}, u32[]{:S(2)}, u32[]{:S(2)}) %collective-permute-start.1) | collective-permute-done | bytes 1048608 | tf_op jit(solution)/shard_map/ppermute | solution.py:26
  29.8 0.2 broadcast_select_fusion
  30.0 0.7 copy-done.4
  30.7 0.3 collective-permute-start.3
  31.0 0.2 collective-permute-start.4
  31.2 2.1 %collective-permute-start.5 = (bf16[2,2,128,1024]{3,2,1,0:T(8,128)(2,1)S(1)}, bf16[2,2,128,1024]{3,2,1,0:T(8,128)(2,1)S(1)}, u32[]{:S(2)}, u32[]{:S(2)}) collective-permute-start(bf16[2,2,128,1024]{3,2,1,0:T(8,128)(2,1)S(1)} %get-tuple-element.23), channel_id=1, source_target_pairs={{0,2},{1,3},{2,4},{3,5},{4,6},{5,7},{8,10},{9,11},{10,12},{11,13},... | collective-permute-start | bytes 3145736 | tf_op jit(solution)/shard_map/ppermute | solution.py:26
  33.3 0.0 copy-done.9
  33.4 0.0 copy-done.8
  33.4 0.1 pad_maximum_fusion.2
  33.5 2.1 %collective-permute-start.2 = (bf16[2,128,2048]{2,1,0:T(8,128)(2,1)S(1)}, bf16[2,128,2048]{2,1,0:T(8,128)(2,1)S(1)}, u32[]{:S(2)}, u32[]{:S(2)}) collective-permute-start(bf16[2,128,2048]{2,1,0:T(8,128)(2,1)S(1)} %pad_maximum_fusion.2), channel_id=1, source_target_pairs={{0,1},{1,0},{2,3},{3,2},{4,5},{5,4},{6,7},{7,6},{8,9},{9,8},{10,11... | collective-permute-start | bytes 3145736 | tf_op jit(solution)/shard_map/ppermute | solution.py:26
  35.6 0.1 broadcast_bitcast_fusion
  35.7 0.1 constant_dynamic-update-slice_fusion.19
  35.8 0.1 fusion.20
  35.9 0.1 constant_dynamic-update-slice_fusion.15
  35.9 0.1 constant_dynamic-update-slice_fusion.13
  36.0 0.1 constant_dynamic-update-slice_fusion.11
  36.1 0.1 constant_dynamic-update-slice_fusion.9
  36.2 0.1 constant_dynamic-update-slice_fusion.7
  36.3 0.1 constant_dynamic-update-slice_fusion.5
  36.4 0.1 constant_dynamic-update-slice_fusion.3
  36.4 0.1 constant_dynamic-update-slice_fusion.1
  36.5 0.5 fusion.11
  37.0 1.7 pad_maximum_fusion.refs_1_
  38.7 0.0 collective-permute-done.2
  38.7 1.1 slice_bitcast_fusion.1
  39.8 15.4 %collective-permute-done.3.refs_7_ = bf16[2,2,128,1024]{3,2,1,0:T(8,128)(2,1)S(1)} collective-permute-done((bf16[2,2,128,1024]{3,2,1,0:T(8,128)(2,1)S(1)}, bf16[2,2,128,1024]{3,2,1,0:T(8,128)(2,1)S(1)}, u32[]{:S(2)}, u32[]{:S(2)}) %collective-permute-start.3) | collective-permute-done | bytes 1048608 | tf_op jit(solution)/shard_map/ppermute | solution.py:26
  55.2 22.6 %collective-permute-done.4.refs_8_ = bf16[2,2,128,1024]{3,2,1,0:T(8,128)(2,1)S(1)} collective-permute-done((bf16[2,2,128,1024]{3,2,1,0:T(8,128)(2,1)S(1)}, bf16[2,2,128,1024]{3,2,1,0:T(8,128)(2,1)S(1)}, u32[]{:S(2)}, u32[]{:S(2)}) %collective-permute-start.4) | collective-permute-done | bytes 1048608 | tf_op jit(solution)/shard_map/ppermute | solution.py:26
  77.8 0.0 collective-permute-done.5.refs_9_
  77.8 1.0 copy-done.12
  78.8 0.4 copy-done.11
  79.2 25.3 %shard_map.76 = (bf16[128,2048]{1,0:T(8,128)(2,1)}, bf16[128,2048]{1,0:T(8,128)(2,1)}, f32[2,2,128,1024]{3,2,1,0:T(8,128)}, bf16[2,2,128,1024]{3,2,1,0:T(8,128)(...) custom-call(s32[1]{0:T(128)} %bitcast.refs_0_, ...), custom_call_target="tpu_custom_call" | custom-call | flops 6710886400 | bytes 21495808 | tf_op jit(solution)/shard_map/pallas_call | solution.py:133
  104.5 0.1 collective-permute-start.6
  104.6 0.3 collective-permute-start.7
  104.9 2.3 %collective-permute-start.8 = (bf16[2,2,128,1024]{3,2,1,0:T(8,128)(2,1)}, bf16[2,2,128,1024]{3,2,1,0:T(8,128)(2,1)S(1)}, u32[]{:S(2)}, u32[]{:S(2)}) collective-permute-start(bf16[2,2,128,1024]{3,2,1,0:T(8,128)(2,1)} %get-tuple-element.20), channel_id=1, source_target_pairs={{6,0},{7,1},{14,8},{15,9},{22,16},{23,17},{30,24},{31,25},{0,2},{1... | collective-permute-start | bytes 3145736 | tf_op jit(solution)/shard_map/ppermute | solution.py:26
  107.2 22.1 %collective-permute-done.6 = bf16[2,2,128,1024]{3,2,1,0:T(8,128)(2,1)S(1)} collective-permute-done((bf16[2,2,128,1024]{3,2,1,0:T(8,128)(2,1)}, bf16[2,2,128,1024]{3,2,1,0:T(8,128)(2,1)S(1)}, u32[]{:S(2)}, u32[]{:S(2)}) %collective-permute-start.6) | collective-permute-done | bytes 1048608 | tf_op jit(solution)/shard_map/ppermute | solution.py:26
  129.2 22.3 %collective-permute-done.7 = bf16[2,2,128,1024]{3,2,1,0:T(8,128)(2,1)S(1)} collective-permute-done((bf16[2,2,128,1024]{3,2,1,0:T(8,128)(2,1)}, bf16[2,2,128,1024]{3,2,1,0:T(8,128)(2,1)S(1)}, u32[]{:S(2)}, u32[]{:S(2)}) %collective-permute-start.7) | collective-permute-done | bytes 1048608 | tf_op jit(solution)/shard_map/ppermute | solution.py:26
  151.5 0.0 collective-permute-done.8
  151.5 2.5 %fusion.8 = bf16[2,2,128,1024]{3,2,1,0:T(8,128)(2,1)S(1)} fusion(f32[2,2,128,1024]{3,2,1,0:T(8,128)} %get-tuple-element.21, bf16[2,2,128,1024]{3,2,1,0:T(8,128)(2,1)S(1)} %collective-permute-done.6, bf16[2,2,128,1024]{3,2,1,0:T(8,128)(2,1)S(1)} %collective-permute-done.7, bf16[2,2,128,1024]{3,2,1,0:T(8,128)(2,1)S(1)} %collective-permute-done.8, ...), kind=kLoop, calls=%fused_computation.15 | loop fusion | flops 5242880 | bytes 6291459 | tf_op jit(solution)/shard_map/convert_element_type | solution.py:69
  154.1 1.3 collective-permute-start.9
  155.4 24.9 %collective-permute-done.9 = bf16[2,2,128,1024]{3,2,1,0:T(8,128)(2,1)S(1)} collective-permute-done((bf16[2,2,128,1024]{3,2,1,0:T(8,128)(2,1)S(1)}, bf16[2,2,128,1024]{3,2,1,0:T(8,128)(2,1)S(1)}, u32[]{:S(2)}, u32[]{:S(2)}) %collective-permute-start.9) | collective-permute-done | bytes 1048608 | tf_op jit(solution)/shard_map/ppermute | solution.py:26
  180.2 0.0 copy-done.1
  180.3 1.1 fusion.4
  181.4 0.1 pad_maximum_fusion.3
  181.5 2.1 %collective-permute-start.10 = (bf16[128,4096]{1,0:T(8,128)(2,1)S(1)}, bf16[128,4096]{1,0:T(8,128)(2,1)S(1)}, u32[]{:S(2)}, u32[]{:S(2)}) collective-permute-start(bf16[128,4096]{1,0:T(8,128)(2,1)S(1)} %pad_maximum_fusion.3), channel_id=1, source_target_pairs={{0,1},{1,0},{2,3},{3,2},{4,5},{5,4},{6,7},{7,6},{8,9},{9,8},{10,11... | collective-permute-start | bytes 3145736 | tf_op jit(solution)/shard_map/ppermute | solution.py:26
  183.5 0.1 broadcast_in_dim.59
  183.6 1.1 bitcast_dynamic-update-slice_fusion
  184.9 0.9 collective-permute-done.10
  185.9 0.0 copy-start.3
  185.9 0.1 fusion.16
  186.0 0.0 copy-start.5
  186.0 0.0 copy-start.6
  186.0 0.9 copy-done.3
  186.9 0.2 copy-done.5
  187.0 0.2 copy-done.6
  (32 shorter events, 0.4 us)
Async XLA Ops:
  0.6 32.7 %copy-start = (s32[1,32]{1,0:T(1,128)S(1)}, s32[1,32]{1,0:T(1,128)}, u32[]{:S(2)}) copy-start(s32[1,32]{1,0:T(1,128)} %param.9) | copy-start | bytes 388
  2.0 2.3 %collective-permute-start = (bf16[2,128,1024]{2,1,0:T(8,128)(2,1)S(1)}, bf16[2,128,1024]{2,1,0:T(8,128)(2,1)S(1)}, u32[]{:S(2)}, u32[]{:S(2)}) collective-permute-start(bf16[2,128,1024]{2,1,0:T(8,128)(2,1)S(1)} %pad_maximum_fusion.4), channel_id=1, source_target_pairs={{0,1},{1,0},{2,3},{3,2},{4,5},{5,4},{6,7},{7,6},{8,9},{9,8},{10,11... | collective-permute-start | bytes 1572872 | tf_op jit(solution)/shard_map/ppermute | solution.py:26
  4.4 25.6 %copy-start.2 = (bf16[2,2,128,1024]{3,2,1,0:T(8,128)(2,1)}, bf16[2,2,128,1024]{3,2,1,0:T(8,128)(2,1)S(1)}, u32[]{:S(2)}) copy-start(bf16[2,2,128,1024]{3,2,1,0:T(8,128)(2,1)S(1)} %pad_maximum_fusion.1.refs_10_) | copy-start | bytes 3145732
  4.4 25.4 %collective-permute-start.1 = (bf16[2,2,128,1024]{3,2,1,0:T(8,128)(2,1)S(1)}, bf16[2,2,128,1024]{3,2,1,0:T(8,128)(2,1)S(1)}, u32[]{:S(2)}, u32[]{:S(2)}) collective-permute-start(bf16[2,2,128,1024]{3,2,1,0:T(8,128)(2,1)S(1)} %pad_maximum_fusion.1.refs_10_), channel_id=1, source_target_pairs={{0,8},{1,9},{2,10},{3,11},{4,12},{5,13},{6,14},{7,15},{8,16},{9,17... | collective-permute-start | bytes 3145736 | tf_op jit(solution)/shard_map/ppermute | solution.py:26
  8.0 25.3 %copy-start.9 = (bf16[1,128,4096]{2,1,0:T(8,128)(2,1)S(1)}, bf16[1,128,4096]{2,1,0:T(8,128)(2,1)}, u32[]{:S(2)}) copy-start(bf16[1,128,4096]{2,1,0:T(8,128)(2,1)} %param.8) | copy-start | bytes 3145732
  8.0 25.4 %copy-start.8 = (bf16[1,128,4096]{2,1,0:T(8,128)(2,1)S(1)}, bf16[1,128,4096]{2,1,0:T(8,128)(2,1)}, u32[]{:S(2)}) copy-start(bf16[1,128,4096]{2,1,0:T(8,128)(2,1)} %param.5) | copy-start | bytes 3145732
  29.8 1.0 copy-start.4
  30.7 24.4 %collective-permute-start.3 = (bf16[2,2,128,1024]{3,2,1,0:T(8,128)(2,1)S(1)}, bf16[2,2,128,1024]{3,2,1,0:T(8,128)(2,1)S(1)}, u32[]{:S(2)}, u32[]{:S(2)}) collective-permute-start(bf16[2,2,128,1024]{3,2,1,0:T(8,128)(2,1)S(1)} %get-tuple-element.25), channel_id=1, source_target_pairs={{0,6},{1,7},{8,14},{9,15},{16,22},{17,23},{24,30},{25,31},{2,0},{3... | collective-permute-start | bytes 3145736 | tf_op jit(solution)/shard_map/ppermute | solution.py:26
  31.0 46.8 %collective-permute-start.4 = (bf16[2,2,128,1024]{3,2,1,0:T(8,128)(2,1)S(1)}, bf16[2,2,128,1024]{3,2,1,0:T(8,128)(2,1)S(1)}, u32[]{:S(2)}, u32[]{:S(2)}) collective-permute-start(bf16[2,2,128,1024]{3,2,1,0:T(8,128)(2,1)S(1)} %get-tuple-element.24), channel_id=1, source_target_pairs={{0,4},{1,5},{2,6},{3,7},{8,12},{9,13},{10,14},{11,15},{16,20},{17,... | collective-permute-start | bytes 3145736 | tf_op jit(solution)/shard_map/ppermute | solution.py:26
  31.2 46.6 %collective-permute-start.5 = (bf16[2,2,128,1024]{3,2,1,0:T(8,128)(2,1)S(1)}, bf16[2,2,128,1024]{3,2,1,0:T(8,128)(2,1)S(1)}, u32[]{:S(2)}, u32[]{:S(2)}) collective-permute-start(bf16[2,2,128,1024]{3,2,1,0:T(8,128)(2,1)S(1)} %get-tuple-element.23), channel_id=1, source_target_pairs={{0,2},{1,3},{2,4},{3,5},{4,6},{5,7},{8,10},{9,11},{10,12},{11,13},... | collective-permute-start | bytes 3145736 | tf_op jit(solution)/shard_map/ppermute | solution.py:26
  33.5 5.2 %collective-permute-start.2 = (bf16[2,128,2048]{2,1,0:T(8,128)(2,1)S(1)}, bf16[2,128,2048]{2,1,0:T(8,128)(2,1)S(1)}, u32[]{:S(2)}, u32[]{:S(2)}) collective-permute-start(bf16[2,128,2048]{2,1,0:T(8,128)(2,1)S(1)} %pad_maximum_fusion.2), channel_id=1, source_target_pairs={{0,1},{1,0},{2,3},{3,2},{4,5},{5,4},{6,7},{7,6},{8,9},{9,8},{10,11... | collective-permute-start | bytes 3145736 | tf_op jit(solution)/shard_map/ppermute | solution.py:26
  55.2 23.7 %copy-start.10 = (bf16[2,2,128,1024]{3,2,1,0:T(8,128)(2,1)}, bf16[2,2,128,1024]{3,2,1,0:T(8,128)(2,1)S(1)}, u32[]{:S(2)}) copy-start(bf16[2,2,128,1024]{3,2,1,0:T(8,128)(2,1)S(1)} %collective-permute-done.3.refs_7_) | copy-start | bytes 3145732
  77.8 1.4 copy-start.11
  77.8 1.0 copy-start.12
  104.5 24.7 %collective-permute-start.6 = (bf16[2,2,128,1024]{3,2,1,0:T(8,128)(2,1)}, bf16[2,2,128,1024]{3,2,1,0:T(8,128)(2,1)S(1)}, u32[]{:S(2)}, u32[]{:S(2)}) collective-permute-start(bf16[2,2,128,1024]{3,2,1,0:T(8,128)(2,1)} %get-tuple-element.18), channel_id=1, source_target_pairs={{2,0},{3,1},{4,2},{5,3},{6,4},{7,5},{10,8},{11,9},{12,10},{13,11},... | collective-permute-start | bytes 3145736 | tf_op jit(solution)/shard_map/ppermute | solution.py:26
  104.6 46.9 %collective-permute-start.7 = (bf16[2,2,128,1024]{3,2,1,0:T(8,128)(2,1)}, bf16[2,2,128,1024]{3,2,1,0:T(8,128)(2,1)S(1)}, u32[]{:S(2)}, u32[]{:S(2)}) collective-permute-start(bf16[2,2,128,1024]{3,2,1,0:T(8,128)(2,1)} %get-tuple-element.19), channel_id=1, source_target_pairs={{4,0},{5,1},{6,2},{7,3},{12,8},{13,9},{14,10},{15,11},{20,16},{21,... | collective-permute-start | bytes 3145736 | tf_op jit(solution)/shard_map/ppermute | solution.py:26
  104.9 46.6 %collective-permute-start.8 = (bf16[2,2,128,1024]{3,2,1,0:T(8,128)(2,1)}, bf16[2,2,128,1024]{3,2,1,0:T(8,128)(2,1)S(1)}, u32[]{:S(2)}, u32[]{:S(2)}) collective-permute-start(bf16[2,2,128,1024]{3,2,1,0:T(8,128)(2,1)} %get-tuple-element.20), channel_id=1, source_target_pairs={{6,0},{7,1},{14,8},{15,9},{22,16},{23,17},{30,24},{31,25},{0,2},{1... | collective-permute-start | bytes 3145736 | tf_op jit(solution)/shard_map/ppermute | solution.py:26
  151.5 28.7 %copy-start.1 = (f32[2,2,128,1024]{3,2,1,0:T(8,128)S(1)}, f32[2,2,128,1024]{3,2,1,0:T(8,128)}, u32[]{:S(2)}) copy-start(f32[2,2,128,1024]{3,2,1,0:T(8,128)} %get-tuple-element.17) | copy-start | bytes 6291460
  154.1 26.2 %collective-permute-start.9 = (bf16[2,2,128,1024]{3,2,1,0:T(8,128)(2,1)S(1)}, bf16[2,2,128,1024]{3,2,1,0:T(8,128)(2,1)S(1)}, u32[]{:S(2)}, u32[]{:S(2)}) collective-permute-start(bf16[2,2,128,1024]{3,2,1,0:T(8,128)(2,1)S(1)} %fusion.8), channel_id=1, source_target_pairs={{8,0},{9,1},{10,2},{11,3},{12,4},{13,5},{14,6},{15,7},{16,8},{17,9... | collective-permute-start | bytes 3145736 | tf_op jit(solution)/shard_map/ppermute | solution.py:26
  180.3 1.1 copy-start.7
  181.5 4.4 %collective-permute-start.10 = (bf16[128,4096]{1,0:T(8,128)(2,1)S(1)}, bf16[128,4096]{1,0:T(8,128)(2,1)S(1)}, u32[]{:S(2)}, u32[]{:S(2)}) collective-permute-start(bf16[128,4096]{1,0:T(8,128)(2,1)S(1)} %pad_maximum_fusion.3), channel_id=1, source_target_pairs={{0,1},{1,0},{2,3},{3,2},{4,5},{5,4},{6,7},{7,6},{8,9},{9,8},{10,11... | collective-permute-start | bytes 3145736 | tf_op jit(solution)/shard_map/ppermute | solution.py:26
  185.9 1.0 copy-start.3
  186.0 1.1 copy-start.5
  186.0 1.2 copy-start.6

commit v19 on v18

--- a/solution.py
+++ b/solution.py
@@ -214,9 +214,10 @@
     )
     dq_mine, dq_sib, parts = outs[0], outs[1], outs[2:]
     summed = scatter_window(parts, routes, chip_in_group)
-    sent = jnp.concatenate(
-        [summed[0, 1].astype(jnp.bfloat16), summed[1, 1].astype(jnp.bfloat16), dq_sib], axis=-1
-    )
+    sent = jnp.zeros((tokens, 2 * key_width + dq_sib.shape[1]), jnp.bfloat16)
+    sent = lax.dynamic_update_slice_in_dim(sent, dq_sib, 2 * key_width, 1)
+    sent = lax.dynamic_update_slice_in_dim(sent, summed[0, 1].astype(jnp.bfloat16), 0, 1)
+    sent = lax.dynamic_update_slice_in_dim(sent, summed[1, 1].astype(jnp.bfloat16), key_width, 1)
     got = moved(sent, routes.sibling)
     grad_key = in_core_order(core, summed[0, 0].astype(jnp.bfloat16), got[:, :key_width])
     grad_value = in_core_order(

time: 188 us -> 188 us (level)
  no operation moved by 1% of the time
where the time goes in v19:
time: 188 us; the launch traced here: 187 us
  waiting for transfers between devices  131 us (70%)
  Pallas kernels  25.3 us (13%)
  starting transfers between devices  14.7 us (8%)
  local copies, waits for them, and re-layouts  8.26 us (4%)
  other arithmetic  6.34 us (3%)
    ppermute x11, waiting for transfers between devices, moved(): return lax.ppermute(value, 'seq', pairs)  131 us
    pallas_call x1, Pallas kernels, attention_grads(): pl.pallas_call(lambda *refs: attention_kernel(chips, *refs), grid_spec=gr...  25.3 us
    ppermute x11, starting transfers between devices, moved(): return lax.ppermute(value, 'seq', pairs)  14.7 us
    unnamed x34, local copies, waits for them, and re-layouts  4.04 us
  transfers between devices with their start and end apart: 11, of which 8 were waited for; matrix products, arithmetic and copies ran while one was open for 3% of the time, Pallas kernels for 0%

profile of v19, /device:TPU:7, one launch (start us, length us, event | category | flops | bytes accessed | tf_op | source)
XLA Modules:
  0.0 187.1 jit_solution(3688874482894153719)
XLA Ops:
  0.6 0.0 copy-start
  0.7 1.3 constant_dynamic-slice_fusion.2
  1.9 0.1 pad_maximum_fusion.3
  2.0 0.7 collective-permute-start
  2.7 0.1 maximum_bitcast_fusion
  2.8 1.5 collective-permute-done
  4.3 0.1 pad_maximum_fusion.1.refs_10_
  4.4 3.3 %collective-permute-start.1 = (bf16[2,2,128,1024]{3,2,1,0:T(8,128)(2,1)S(1)}, bf16[2,2,128,1024]{3,2,1,0:T(8,128)(2,1)S(1)}, u32[]{:S(2)}, u32[]{:S(2)}) collective-permute-start(bf16[2,2,128,1024]{3,2,1,0:T(8,128)(2,1)S(1)} %pad_maximum_fusion.1.refs_10_), channel_id=1, source_target_pairs={{0,8},{1,9},{2,10},{3,11},{4,12},{5,13},{6,14},{7,15},{8,16},{9,17... | collective-permute-start | bytes 3145736 | tf_op jit(solution)/shard_map/ppermute | solution.py:26
  8.0 0.0 copy-start.9
  8.0 0.0 copy-start.8
  8.0 21.7 %collective-permute-done.1.refs_6_ = bf16[2,2,128,1024]{3,2,1,0:T(8,128)(2,1)S(1)} collective-permute-done((bf16[2,2,128,1024]{3,2,1,0:T(8,128)(2,1)S(1)}, bf16[2,2,128,1024]{3,2,1,0:T(8,128)(2,1)S(1)}, u32[]{:S(2)}, u32[]{:S(2)}) %collective-permute-start.1) | collective-permute-done | bytes 1048608 | tf_op jit(solution)/shard_map/ppermute | solution.py:26
  29.8 0.2 broadcast_select_fusion
  30.0 0.7 copy-done.4
  30.7 0.3 collective-permute-start.3
  31.0 0.2 collective-permute-start.4
  31.2 2.1 %collective-permute-start.5 = (bf16[2,2,128,1024]{3,2,1,0:T(8,128)(2,1)S(1)}, bf16[2,2,128,1024]{3,2,1,0:T(8,128)(2,1)S(1)}, u32[]{:S(2)}, u32[]{:S(2)}) collective-permute-start(bf16[2,2,128,1024]{3,2,1,0:T(8,128)(2,1)S(1)} %get-tuple-element.23), channel_id=1, source_target_pairs={{0,2},{1,3},{2,4},{3,5},{4,6},{5,7},{8,10},{9,11},{10,12},{11,13},... | collective-permute-start | bytes 3145736 | tf_op jit(solution)/shard_map/ppermute | solution.py:26
  33.3 0.0 copy-done.9
  33.4 0.0 copy-done.8
  33.4 0.1 pad_maximum_fusion.2
  33.5 2.1 %collective-permute-start.2 = (bf16[2,128,2048]{2,1,0:T(8,128)(2,1)S(1)}, bf16[2,128,2048]{2,1,0:T(8,128)(2,1)S(1)}, u32[]{:S(2)}, u32[]{:S(2)}) collective-permute-start(bf16[2,128,2048]{2,1,0:T(8,128)(2,1)S(1)} %pad_maximum_fusion.2), channel_id=1, source_target_pairs={{0,1},{1,0},{2,3},{3,2},{4,5},{5,4},{6,7},{7,6},{8,9},{9,8},{10,11... | collective-permute-start | bytes 3145736 | tf_op jit(solution)/shard_map/ppermute | solution.py:26
  35.6 0.1 broadcast_bitcast_fusion
  35.7 0.1 constant_dynamic-update-slice_fusion.19
  35.8 0.1 fusion.22
  35.9 0.1 constant_dynamic-update-slice_fusion.15
  35.9 0.1 constant_dynamic-update-slice_fusion.13
  36.0 0.1 constant_dynamic-update-slice_fusion.11
  36.1 0.1 constant_dynamic-update-slice_fusion.9
  36.2 0.1 constant_dynamic-update-slice_fusion.7
  36.3 0.1 constant_dynamic-update-slice_fusion.5
  36.4 0.1 constant_dynamic-update-slice_fusion.3
  36.4 0.1 constant_dynamic-update-slice_fusion.1
  36.5 0.5 fusion.11
  37.0 1.7 pad_maximum_fusion.refs_1_
  38.7 0.0 collective-permute-done.2
  38.7 1.1 slice_bitcast_fusion.1
  39.8 15.4 %collective-permute-done.3.refs_7_ = bf16[2,2,128,1024]{3,2,1,0:T(8,128)(2,1)S(1)} collective-permute-done((bf16[2,2,128,1024]{3,2,1,0:T(8,128)(2,1)S(1)}, bf16[2,2,128,1024]{3,2,1,0:T(8,128)(2,1)S(1)}, u32[]{:S(2)}, u32[]{:S(2)}) %collective-permute-start.3) | collective-permute-done | bytes 1048608 | tf_op jit(solution)/shard_map/ppermute | solution.py:26
  55.2 22.6 %collective-permute-done.4.refs_8_ = bf16[2,2,128,1024]{3,2,1,0:T(8,128)(2,1)S(1)} collective-permute-done((bf16[2,2,128,1024]{3,2,1,0:T(8,128)(2,1)S(1)}, bf16[2,2,128,1024]{3,2,1,0:T(8,128)(2,1)S(1)}, u32[]{:S(2)}, u32[]{:S(2)}) %collective-permute-start.4) | collective-permute-done | bytes 1048608 | tf_op jit(solution)/shard_map/ppermute | solution.py:26
  77.8 0.0 collective-permute-done.5.refs_9_
  77.8 1.0 copy-done.12
  78.8 0.4 copy-done.11
  79.2 25.3 %shard_map.76 = (bf16[128,2048]{1,0:T(8,128)(2,1)}, bf16[128,2048]{1,0:T(8,128)(2,1)}, f32[2,2,128,1024]{3,2,1,0:T(8,128)}, bf16[2,2,128,1024]{3,2,1,0:T(8,128)(...) custom-call(s32[1]{0:T(128)} %bitcast.refs_0_, ...), custom_call_target="tpu_custom_call" | custom-call | flops 6710886400 | bytes 21495808 | tf_op jit(solution)/shard_map/pallas_call | solution.py:133
  104.5 0.1 collective-permute-start.6
  104.6 0.3 collective-permute-start.7
  104.9 2.3 %collective-permute-start.8 = (bf16[2,2,128,1024]{3,2,1,0:T(8,128)(2,1)}, bf16[2,2,128,1024]{3,2,1,0:T(8,128)(2,1)S(1)}, u32[]{:S(2)}, u32[]{:S(2)}) collective-permute-start(bf16[2,2,128,1024]{3,2,1,0:T(8,128)(2,1)} %get-tuple-element.21), channel_id=1, source_target_pairs={{6,0},{7,1},{14,8},{15,9},{22,16},{23,17},{30,24},{31,25},{0,2},{1... | collective-permute-start | bytes 3145736 | tf_op jit(solution)/shard_map/ppermute | solution.py:26
  107.2 22.1 %collective-permute-done.6 = bf16[2,2,128,1024]{3,2,1,0:T(8,128)(2,1)S(1)} collective-permute-done((bf16[2,2,128,1024]{3,2,1,0:T(8,128)(2,1)}, bf16[2,2,128,1024]{3,2,1,0:T(8,128)(2,1)S(1)}, u32[]{:S(2)}, u32[]{:S(2)}) %collective-permute-start.6) | collective-permute-done | bytes 1048608 | tf_op jit(solution)/shard_map/ppermute | solution.py:26
  129.2 22.3 %collective-permute-done.7 = bf16[2,2,128,1024]{3,2,1,0:T(8,128)(2,1)S(1)} collective-permute-done((bf16[2,2,128,1024]{3,2,1,0:T(8,128)(2,1)}, bf16[2,2,128,1024]{3,2,1,0:T(8,128)(2,1)S(1)}, u32[]{:S(2)}, u32[]{:S(2)}) %collective-permute-start.7) | collective-permute-done | bytes 1048608 | tf_op jit(solution)/shard_map/ppermute | solution.py:26
  151.5 0.0 collective-permute-done.8
  151.5 2.5 %fusion.8 = bf16[2,2,128,1024]{3,2,1,0:T(8,128)(2,1)S(1)} fusion(f32[2,2,128,1024]{3,2,1,0:T(8,128)} %get-tuple-element.22, bf16[2,2,128,1024]{3,2,1,0:T(8,128)(2,1)S(1)} %collective-permute-done.6, bf16[2,2,128,1024]{3,2,1,0:T(8,128)(2,1)S(1)} %collective-permute-done.7, bf16[2,2,128,1024]{3,2,1,0:T(8,128)(2,1)S(1)} %collective-permute-done.8, ...), kind=kLoop, calls=%fused_computation.15 | loop fusion | flops 5242880 | bytes 6291459 | tf_op jit(solution)/shard_map/convert_element_type | solution.py:69
  154.1 1.3 collective-permute-start.9
  155.4 0.1 dynamic_update_slice.40
  155.5 24.8 %collective-permute-done.9 = bf16[2,2,128,1024]{3,2,1,0:T(8,128)(2,1)S(1)} collective-permute-done((bf16[2,2,128,1024]{3,2,1,0:T(8,128)(2,1)S(1)}, bf16[2,2,128,1024]{3,2,1,0:T(8,128)(2,1)S(1)}, u32[]{:S(2)}, u32[]{:S(2)}) %collective-permute-start.9) | collective-permute-done | bytes 1048608 | tf_op jit(solution)/shard_map/ppermute | solution.py:26
  180.3 0.0 copy-done.1
  180.3 1.0 fusion.4
  181.4 2.1 %collective-permute-start.10 = (bf16[128,4096]{1,0:T(8,128)(2,1)S(1)}, bf16[128,4096]{1,0:T(8,128)(2,1)S(1)}, u32[]{:S(2)}, u32[]{:S(2)}) collective-permute-start(bf16[128,4096]{1,0:T(8,128)(2,1)S(1)} %fusion.20), channel_id=1, source_target_pairs={{0,1},{1,0},{2,3},{3,2},{4,5},{5,4},{6,7},{7,6},{8,9},{9,8},{10,11... | collective-permute-start | bytes 3145736 | tf_op jit(solution)/shard_map/ppermute | solution.py:26
  183.5 0.1 broadcast_in_dim.58
  183.6 1.1 bitcast_dynamic-update-slice_fusion
  184.8 0.9 collective-permute-done.10
  185.8 0.0 copy-start.3
  185.8 0.1 fusion.16
  185.9 0.0 copy-start.5
  185.9 0.0 copy-start.6
  185.9 0.9 copy-done.3
  186.8 0.2 copy-done.5
  187.0 0.2 copy-done.6
  (33 shorter events, 0.4 us)
Async XLA Ops:
  0.6 32.7 %copy-start = (s32[1,32]{1,0:T(1,128)S(1)}, s32[1,32]{1,0:T(1,128)}, u32[]{:S(2)}) copy-start(s32[1,32]{1,0:T(1,128)} %param.9) | copy-start | bytes 388
  2.0 2.3 %collective-permute-start = (bf16[2,128,1024]{2,1,0:T(8,128)(2,1)S(1)}, bf16[2,128,1024]{2,1,0:T(8,128)(2,1)S(1)}, u32[]{:S(2)}, u32[]{:S(2)}) collective-permute-start(bf16[2,128,1024]{2,1,0:T(8,128)(2,1)S(1)} %pad_maximum_fusion.3), channel_id=1, source_target_pairs={{0,1},{1,0},{2,3},{3,2},{4,5},{5,4},{6,7},{7,6},{8,9},{9,8},{10,11... | collective-permute-start | bytes 1572872 | tf_op jit(solution)/shard_map/ppermute | solution.py:26
  4.4 25.6 %copy-start.2 = (bf16[2,2,128,1024]{3,2,1,0:T(8,128)(2,1)}, bf16[2,2,128,1024]{3,2,1,0:T(8,128)(2,1)S(1)}, u32[]{:S(2)}) copy-start(bf16[2,2,128,1024]{3,2,1,0:T(8,128)(2,1)S(1)} %pad_maximum_fusion.1.refs_10_) | copy-start | bytes 3145732
  4.4 25.4 %collective-permute-start.1 = (bf16[2,2,128,1024]{3,2,1,0:T(8,128)(2,1)S(1)}, bf16[2,2,128,1024]{3,2,1,0:T(8,128)(2,1)S(1)}, u32[]{:S(2)}, u32[]{:S(2)}) collective-permute-start(bf16[2,2,128,1024]{3,2,1,0:T(8,128)(2,1)S(1)} %pad_maximum_fusion.1.refs_10_), channel_id=1, source_target_pairs={{0,8},{1,9},{2,10},{3,11},{4,12},{5,13},{6,14},{7,15},{8,16},{9,17... | collective-permute-start | bytes 3145736 | tf_op jit(solution)/shard_map/ppermute | solution.py:26
  8.0 25.3 %copy-start.9 = (bf16[1,128,4096]{2,1,0:T(8,128)(2,1)S(1)}, bf16[1,128,4096]{2,1,0:T(8,128)(2,1)}, u32[]{:S(2)}) copy-start(bf16[1,128,4096]{2,1,0:T(8,128)(2,1)} %param.8) | copy-start | bytes 3145732
  8.0 25.4 %copy-start.8 = (bf16[1,128,4096]{2,1,0:T(8,128)(2,1)S(1)}, bf16[1,128,4096]{2,1,0:T(8,128)(2,1)}, u32[]{:S(2)}) copy-start(bf16[1,128,4096]{2,1,0:T(8,128)(2,1)} %param.5) | copy-start | bytes 3145732
  29.8 1.0 copy-start.4
  30.7 24.4 %collective-permute-start.3 = (bf16[2,2,128,1024]{3,2,1,0:T(8,128)(2,1)S(1)}, bf16[2,2,128,1024]{3,2,1,0:T(8,128)(2,1)S(1)}, u32[]{:S(2)}, u32[]{:S(2)}) collective-permute-start(bf16[2,2,128,1024]{3,2,1,0:T(8,128)(2,1)S(1)} %get-tuple-element.25), channel_id=1, source_target_pairs={{0,6},{1,7},{8,14},{9,15},{16,22},{17,23},{24,30},{25,31},{2,0},{3... | collective-permute-start | bytes 3145736 | tf_op jit(solution)/shard_map/ppermute | solution.py:26
  31.0 46.8 %collective-permute-start.4 = (bf16[2,2,128,1024]{3,2,1,0:T(8,128)(2,1)S(1)}, bf16[2,2,128,1024]{3,2,1,0:T(8,128)(2,1)S(1)}, u32[]{:S(2)}, u32[]{:S(2)}) collective-permute-start(bf16[2,2,128,1024]{3,2,1,0:T(8,128)(2,1)S(1)} %get-tuple-element.24), channel_id=1, source_target_pairs={{0,4},{1,5},{2,6},{3,7},{8,12},{9,13},{10,14},{11,15},{16,20},{17,... | collective-permute-start | bytes 3145736 | tf_op jit(solution)/shard_map/ppermute | solution.py:26
  31.2 46.6 %collective-permute-start.5 = (bf16[2,2,128,1024]{3,2,1,0:T(8,128)(2,1)S(1)}, bf16[2,2,128,1024]{3,2,1,0:T(8,128)(2,1)S(1)}, u32[]{:S(2)}, u32[]{:S(2)}) collective-permute-start(bf16[2,2,128,1024]{3,2,1,0:T(8,128)(2,1)S(1)} %get-tuple-element.23), channel_id=1, source_target_pairs={{0,2},{1,3},{2,4},{3,5},{4,6},{5,7},{8,10},{9,11},{10,12},{11,13},... | collective-permute-start | bytes 3145736 | tf_op jit(solution)/shard_map/ppermute | solution.py:26
  33.5 5.2 %collective-permute-start.2 = (bf16[2,128,2048]{2,1,0:T(8,128)(2,1)S(1)}, bf16[2,128,2048]{2,1,0:T(8,128)(2,1)S(1)}, u32[]{:S(2)}, u32[]{:S(2)}) collective-permute-start(bf16[2,128,2048]{2,1,0:T(8,128)(2,1)S(1)} %pad_maximum_fusion.2), channel_id=1, source_target_pairs={{0,1},{1,0},{2,3},{3,2},{4,5},{5,4},{6,7},{7,6},{8,9},{9,8},{10,11... | collective-permute-start | bytes 3145736 | tf_op jit(solution)/shard_map/ppermute | solution.py:26
  55.2 23.7 %copy-start.10 = (bf16[2,2,128,1024]{3,2,1,0:T(8,128)(2,1)}, bf16[2,2,128,1024]{3,2,1,0:T(8,128)(2,1)S(1)}, u32[]{:S(2)}) copy-start(bf16[2,2,128,1024]{3,2,1,0:T(8,128)(2,1)S(1)} %collective-permute-done.3.refs_7_) | copy-start | bytes 3145732
  77.8 1.4 copy-start.11
  77.8 1.0 copy-start.12
  104.5 24.7 %collective-permute-start.6 = (bf16[2,2,128,1024]{3,2,1,0:T(8,128)(2,1)}, bf16[2,2,128,1024]{3,2,1,0:T(8,128)(2,1)S(1)}, u32[]{:S(2)}, u32[]{:S(2)}) collective-permute-start(bf16[2,2,128,1024]{3,2,1,0:T(8,128)(2,1)} %get-tuple-element.19), channel_id=1, source_target_pairs={{2,0},{3,1},{4,2},{5,3},{6,4},{7,5},{10,8},{11,9},{12,10},{13,11},... | collective-permute-start | bytes 3145736 | tf_op jit(solution)/shard_map/ppermute | solution.py:26
  104.6 46.9 %collective-permute-start.7 = (bf16[2,2,128,1024]{3,2,1,0:T(8,128)(2,1)}, bf16[2,2,128,1024]{3,2,1,0:T(8,128)(2,1)S(1)}, u32[]{:S(2)}, u32[]{:S(2)}) collective-permute-start(bf16[2,2,128,1024]{3,2,1,0:T(8,128)(2,1)} %get-tuple-element.20), channel_id=1, source_target_pairs={{4,0},{5,1},{6,2},{7,3},{12,8},{13,9},{14,10},{15,11},{20,16},{21,... | collective-permute-start | bytes 3145736 | tf_op jit(solution)/shard_map/ppermute | solution.py:26
  104.9 46.6 %collective-permute-start.8 = (bf16[2,2,128,1024]{3,2,1,0:T(8,128)(2,1)}, bf16[2,2,128,1024]{3,2,1,0:T(8,128)(2,1)S(1)}, u32[]{:S(2)}, u32[]{:S(2)}) collective-permute-start(bf16[2,2,128,1024]{3,2,1,0:T(8,128)(2,1)} %get-tuple-element.21), channel_id=1, source_target_pairs={{6,0},{7,1},{14,8},{15,9},{22,16},{23,17},{30,24},{31,25},{0,2},{1... | collective-permute-start | bytes 3145736 | tf_op jit(solution)/shard_map/ppermute | solution.py:26
  151.5 3.9 %copy-start.7 = (bf16[128,2048]{1,0:T(8,128)(2,1)S(1)}, bf16[128,2048]{1,0:T(8,128)(2,1)}, u32[]{:S(2)}) copy-start(bf16[128,2048]{1,0:T(8,128)(2,1)} %get-tuple-element.17) | copy-start | bytes 1572868
  151.5 28.7 %copy-start.1 = (f32[2,2,128,1024]{3,2,1,0:T(8,128)S(1)}, f32[2,2,128,1024]{3,2,1,0:T(8,128)}, u32[]{:S(2)}) copy-start(f32[2,2,128,1024]{3,2,1,0:T(8,128)} %get-tuple-element.18) | copy-start | bytes 6291460
  154.1 26.2 %collective-permute-start.9 = (bf16[2,2,128,1024]{3,2,1,0:T(8,128)(2,1)S(1)}, bf16[2,2,128,1024]{3,2,1,0:T(8,128)(2,1)S(1)}, u32[]{:S(2)}, u32[]{:S(2)}) collective-permute-start(bf16[2,2,128,1024]{3,2,1,0:T(8,128)(2,1)S(1)} %fusion.8), channel_id=1, source_target_pairs={{8,0},{9,1},{10,2},{11,3},{12,4},{13,5},{14,6},{15,7},{16,8},{17,9... | collective-permute-start | bytes 3145736 | tf_op jit(solution)/shard_map/ppermute | solution.py:26
  181.4 4.4 %collective-permute-start.10 = (bf16[128,4096]{1,0:T(8,128)(2,1)S(1)}, bf16[128,4096]{1,0:T(8,128)(2,1)S(1)}, u32[]{:S(2)}, u32[]{:S(2)}) collective-permute-start(bf16[128,4096]{1,0:T(8,128)(2,1)S(1)} %fusion.20), channel_id=1, source_target_pairs={{0,1},{1,0},{2,3},{3,2},{4,5},{5,4},{6,7},{7,6},{8,9},{9,8},{10,11... | collective-permute-start | bytes 3145736 | tf_op jit(solution)/shard_map/ppermute | solution.py:26
  185.8 1.0 copy-start.3
  185.9 1.1 copy-start.5
  185.9 1.2 copy-start.6
